TPU v7x, 512 devices: a whole 4x8x8 slice. The times are simulated.
512 devices in a mesh: col: 32 (over x_lo, z, core), rec: 16 (over x_hi, y).
Axes of the slice: x: 4 (x_hi: 2, x_lo: 2; x = x_hi * 2 + x_lo), y: 8, z: 8, core: 2. Of those that a mesh axis runs over, the one named last changes fastest.
Arguments:
- design: bfloat16 [4096, 16384], P('rec', 'col')
- record_weight: float32 [4096], P('rec'), may hold values from 0.5 to 3.47
Outputs:
- rotated_design: bfloat16 [4096, 16384], P('rec', 'col')
- column_rms: float32 [16384], P('col')
All inputs are finite; a program needn't handle non-finite values.
Results may differ from a plain program's by a relative error of at most 0.0088.
Values may be sent and summed in bfloat16 or wider, within the bound.
No kernel may reach another device: no remote copies, remote signals or barrier semaphores. Data moves between devices by JAX's collectives and lax.ppermute only.
A program may use at most 64 MiB of HBM per device.

v0:
```python
import jax
import jax.numpy as jnp
from jax import lax
from jax.sharding import PartitionSpec as P

ROUNDS = 3
SWEEPS = 6


eps_angle = 0.01


def from_behind(value, axis, steps):
    count = lax.axis_size(axis)
    leading, last = (max(0, -steps), min(count, count - steps))
    return lax.ppermute(value, axis, [(source, source + steps) for source in range(leading, last)])


def jacobi_sweeps(gram_matrix, width):
    top_left = gram_matrix[:width, :width]
    top_right = gram_matrix[:width, width:]
    low_left = gram_matrix[width:, :width]
    low_right = gram_matrix[width:, width:]
    identity = jnp.eye(2 * width, dtype=jnp.float32)
    rot_first = identity[:, :width]
    rot_second = identity[:, width:]
    for sweep_index in range(SWEEPS):
        if sweep_index > 0:
            top_right = jnp.roll(top_right, -1, axis=1)
            low_left = jnp.roll(low_left, -1, axis=0)
            low_right = jnp.roll(jnp.roll(low_right, -1, axis=0), -1, axis=1)
            rot_second = jnp.roll(rot_second, -1, axis=1)
        first_diag = jnp.diagonal(top_left)
        second_diag = jnp.diagonal(low_right)
        coupling = jnp.diagonal(top_right)
        spread = second_diag - first_diag
        tangent = (
            2.0
            * coupling
            * spread
            / (
                spread * spread
                + 4.0 * coupling * coupling
                + eps_angle * (first_diag + second_diag) ** 2
            )
        )
        half_angle = 0.5 * jnp.arctan(tangent)
        cosine = jnp.cos(half_angle)
        sine_value = jnp.sin(half_angle)
        cos_col = cosine[None, :]
        sin_col = sine_value[None, :]
        cos_row = cosine[:, None]
        sin_row = sine_value[:, None]
        left_a = top_left * cos_col - top_right * sin_col
        right_a = top_left * sin_col + top_right * cos_col
        left_b = low_left * cos_col - low_right * sin_col
        right_b = low_left * sin_col + low_right * cos_col
        top_left = cos_row * left_a - sin_row * left_b
        low_left = sin_row * left_a + cos_row * left_b
        top_right = cos_row * right_a - sin_row * right_b
        low_right = sin_row * right_a + cos_row * right_b
        rot_first, rot_second = (
            rot_first * cos_col - rot_second * sin_col,
            rot_first * sin_col + rot_second * cos_col,
        )
    rot_second = jnp.roll(rot_second, SWEEPS - 1, axis=1)
    return jnp.concatenate([rot_first, rot_second], axis=1)


def send_right(block):
    return from_behind(block, "col", 1)


def send_left(block):
    return from_behind(block, "col", -1)


def inner_products(left_part, right_part):
    return lax.dot_general(
        left_part, right_part, (((0,), (0,)), ((), ())), preferred_element_type=jnp.float32
    )


def local(design, record_weight):
    width = design.shape[1] // 2
    weighted = (design.astype(jnp.float32) * record_weight[:, None]).astype(jnp.bfloat16)
    upper_block = weighted[:, :width]
    lower_block = weighted[:, width:]
    position = lax.axis_index("col")
    device_count = lax.axis_size("col")
    for round_index in range(ROUNDS):
        moving = round_index + 1 < ROUNDS
        pair_data = jnp.concatenate([upper_block, lower_block], axis=1)
        gram_matrix = lax.psum(inner_products(pair_data, pair_data), "rec")
        rotation = jacobi_sweeps(gram_matrix, width).astype(jnp.bfloat16)
        rotated = jnp.dot(pair_data, rotation, preferred_element_type=jnp.float32).astype(
            jnp.bfloat16
        )
        new_upper = rotated[:, :width]
        new_lower = rotated[:, width:]
        if moving:
            from_right = send_left(new_lower)
            from_left = send_right(jnp.where(position == 0, new_lower, new_upper))
        if moving:
            upper_block = jnp.where(position == 0, new_upper, from_left)
            lower_block = jnp.where(position == device_count - 1, new_upper, from_right)
        else:
            upper_block = new_upper
            lower_block = new_lower
    rotated_design = jnp.concatenate([upper_block, lower_block], axis=1)
    squares = jnp.sum(jnp.square(rotated_design.astype(jnp.float32)), axis=0)
    totals = lax.psum(squares, "rec")
    record_total = design.shape[0] * lax.axis_size("rec")
    column_rms = jnp.sqrt(totals / record_total + 1e-06)
    return (rotated_design, column_rms)


def solution(mesh):
    placed = (P("rec", "col"), P("rec"))
    return jax.shard_map(
        local, mesh=mesh, in_specs=placed, out_specs=(P("rec", "col"), P("col")), check_vma=False
    )
```

profile of v0, /device:TPU:64, one launch (start us, length us, event | category | flops | bytes accessed | tf_op | source)
XLA Modules:
  0.0 738.1 jit_solution(11142493049382048583)
XLA Ops:
  7.2 2.5 fusion.33
  9.9 168.6 %all-reduce.4.cloned.1.call-done = f32[512,512]{1,0:T(8,128)} async-done(((f32[512,512]{1,0:T(8,128)}), f32[512,512]{1,0:T(8,128)}) %all-reduce.4.cloned.1.call-update) | async-done | bytes 1048592 | tf_op jit(solution)/shard_map/psum | solution.py:94
  179.6 2.3 gather_fusion
  182.0 2.3 gather_fusion.2
  184.3 2.3 gather_fusion.1
  187.3 2.3 gather_fusion.5
  189.9 2.3 gather_fusion.4
  192.3 2.3 gather_fusion.3
  195.2 2.3 gather_fusion.8
  197.7 2.3 gather_fusion.6
  200.3 2.3 gather_fusion.7
  203.3 2.3 gather_fusion.11
  205.7 2.3 gather_fusion.9
  208.3 2.3 gather_fusion.10
  211.3 2.3 gather_fusion.14
  213.8 2.3 gather_fusion.12
  216.4 2.5 gather_fusion.13
  223.2 2.9 gather_fusion.17
  227.2 2.3 gather_fusion.15
  229.9 2.3 gather_fusion.16
  234.0 1.9 collective-permute-start
  236.0 3.6 collective-permute-start.1
  240.3 1.8 collective-permute-done.1
  243.5 162.9 %all-reduce.6.cloned.1.call-done = f32[512,512]{1,0:T(8,128)} async-done(((f32[512,512]{1,0:T(8,128)}), f32[512,512]{1,0:T(8,128)}) %all-reduce.6.cloned.1.call-update) | async-done | bytes 1048592 | tf_op jit(solution)/shard_map/psum | solution.py:94
  407.6 2.3 gather_fusion.18
  410.0 2.3 gather_fusion.20
  412.3 2.3 gather_fusion.19
  415.3 2.3 gather_fusion.23
  417.8 2.3 gather_fusion.21
  420.4 2.3 gather_fusion.22
  423.3 2.3 gather_fusion.26
  425.8 2.3 gather_fusion.24
  428.4 2.3 gather_fusion.25
  431.4 2.3 gather_fusion.29
  433.9 2.3 gather_fusion.27
  436.5 2.3 gather_fusion.28
  439.5 2.3 gather_fusion.32
  441.9 2.3 gather_fusion.30
  444.5 2.6 gather_fusion.31
  452.1 2.9 gather_fusion.35
  456.1 2.9 gather_fusion.33
  459.3 2.9 gather_fusion.34
  464.7 1.9 collective-permute-start.2
  466.6 3.6 collective-permute-start.3
  474.1 163.0 %all-reduce.8.cloned.1.call-done = f32[512,512]{1,0:T(8,128)} async-done(((f32[512,512]{1,0:T(8,128)}), f32[512,512]{1,0:T(8,128)}) %all-reduce.8.cloned.1.call-update) | async-done | bytes 1048592 | tf_op jit(solution)/shard_map/psum | solution.py:94
  638.3 2.3 gather_fusion.36
  640.7 2.3 gather_fusion.38
  643.0 2.3 gather_fusion.37
  646.0 2.3 gather_fusion.41
  648.4 2.3 gather_fusion.39
  651.0 2.3 gather_fusion.40
  654.0 2.3 gather_fusion.44
  656.5 2.3 gather_fusion.42
  659.1 2.3 gather_fusion.43
  662.1 2.3 gather_fusion.47
  664.6 2.3 gather_fusion.45
  667.2 2.3 gather_fusion.46
  670.1 2.3 gather_fusion.50
  672.6 2.3 gather_fusion.48
  675.2 2.6 gather_fusion.49
  680.7 2.3 gather_fusion.53
  683.2 2.3 gather_fusion.51
  685.8 2.3 gather_fusion.52
  689.8 40.8 %psum.31 = f32[512]{0:T(512)S(1)} all-reduce(f32[512]{0:T(512)S(1)} %get-tuple-element.130), channel_id=1, replica_groups=mesh['col'=32,'rec'=16] {'rec'}, use_global_device_ids=true, to_apply=%region_4.5 | all-reduce | flops 512 | bytes 4096 | tf_op jit(solution)/shard_map/psum | solution.py:112
  (276 shorter events, 41.5 us)
Async XLA Ops:
  7.2 171.3 %all-reduce.4.cloned.1.call-start = ((), (), s32[]{:S(2)}) async-start(), calls=%async_computation | async-start | bytes 2097152 | tf_op jit(solution)/shard_map/psum | solution.py:94
  9.7 396.8 %all-reduce.6.cloned.1.call-start = ((), (), s32[]{:S(2)}) async-start(), calls=%async_computation.1 | async-start | bytes 2097152 | tf_op jit(solution)/shard_map/psum | solution.py:94
  182.0 4.8 copy-start
  229.8 2.4 copy-start.8
  229.8 2.5 copy-start.3
  232.7 1.0 copy-start.7
  232.8 0.8 copy-start.10
  234.0 6.3 collective-permute-start
  236.0 6.1 collective-permute-start.1
  242.1 1.3 copy-start.5
  243.5 393.7 %all-reduce.8.cloned.1.call-start = ((), (), s32[]{:S(2)}) async-start(), calls=%async_computation.2 | async-start | bytes 2097152 | tf_op jit(solution)/shard_map/psum | solution.py:94
  410.0 4.8 copy-start.1
  459.3 3.0 copy-start.9
  459.3 3.8 copy-start.4
  463.4 0.9 copy-start.6
  464.7 6.3 collective-permute-start.2
  466.6 6.1 collective-permute-start.3
  640.6 4.8 copy-start.2
Sparse Core Ops, SparseCore 0:
  10.9 167.4 all-reduce.3
  243.6 162.8 all-reduce.5
  474.2 162.8 all-reduce.7
where the time goes:
time: 746 us; the launch traced here: 738 us
  waiting for transfers between devices  500 us (67%)
  local copies, waits for them, and re-layouts  145 us (19%)
  blocking collectives  40.8 us (5%)
  other arithmetic  18.2 us (2%)
  between operations  16.3 us (2%)
  starting transfers between devices  11.2 us (2%)
    psum x3, waiting for transfers between devices, local(): gram_matrix = lax.psum(inner_products(pair_data, pair_data), 'rec')  495 us
    gather x18, local copies, waits for them, and re-layouts, jacobi_sweeps(): second_diag = jnp.diagonal(low_right)  43.4 us
    gather x18, local copies, waits for them, and re-layouts, jacobi_sweeps(): first_diag = jnp.diagonal(top_left)  43.4 us
    gather x18, local copies, waits for them, and re-layouts, jacobi_sweeps(): coupling = jnp.diagonal(top_right)  42.8 us
    psum x1, blocking collectives, local(): totals = lax.psum(squares, 'rec')  40.8 us
  transfers between devices with their start and end apart: 7, of which 7 were waited for; matrix products, arithmetic and copies ran while one was open for 0% of the time, Pallas kernels for 0%

commit v1 on v0

--- a/solution.py
+++ b/solution.py
@@ -16,6 +16,13 @@
     return lax.ppermute(value, axis, [(source, source + steps) for source in range(leading, last)])
 
 
+def diagonal_of(matrix):
+    size = matrix.shape[0]
+    rows = lax.broadcasted_iota(jnp.int32, (size, size), 0)
+    cols = lax.broadcasted_iota(jnp.int32, (size, size), 1)
+    return jnp.sum(jnp.where(rows == cols, matrix, 0.0), axis=0)
+
+
 def jacobi_sweeps(gram_matrix, width):
     top_left = gram_matrix[:width, :width]
     top_right = gram_matrix[:width, width:]
@@ -30,9 +37,9 @@
             low_left = jnp.roll(low_left, -1, axis=0)
             low_right = jnp.roll(jnp.roll(low_right, -1, axis=0), -1, axis=1)
             rot_second = jnp.roll(rot_second, -1, axis=1)
-        first_diag = jnp.diagonal(top_left)
-        second_diag = jnp.diagonal(low_right)
-        coupling = jnp.diagonal(top_right)
+        first_diag = diagonal_of(top_left)
+        second_diag = diagonal_of(low_right)
+        coupling = diagonal_of(top_right)
         spread = second_diag - first_diag
         tangent = (
             2.0
@@ -81,6 +88,50 @@
     )
 
 
+def reduce_over_records(rows_in):
+    count = lax.axis_size("rec")
+    total, width = rows_in.shape
+    chunks = rows_in.reshape(count, total // count, width)
+    mine = lax.all_to_all(chunks, "rec", 0, 0, tiled=False).sum(axis=0)
+    spread = jnp.broadcast_to(mine[None], (count,) + mine.shape)
+    return lax.all_to_all(spread, "rec", 0, 0, tiled=False).reshape(total, width)
+
+
+def summed_gram(pair_data, width):
+    gram_local = inner_products(pair_data, pair_data)
+    top_left = gram_local[:width, :width]
+    top_right = gram_local[:width, width:]
+    low_right = gram_local[width:, width:]
+    rows = lax.broadcasted_iota(jnp.int32, (width, width), 0)
+    cols = lax.broadcasted_iota(jnp.int32, (width, width), 1)
+    folded = jnp.where(rows <= cols, top_left, low_right)
+    count = lax.axis_size("rec")
+    padded = -(-(2 * width + 1) // (8 * count)) * 8 * count
+    packed = jnp.concatenate(
+        [
+            folded,
+            top_right,
+            diagonal_of(low_right)[None, :],
+            jnp.zeros((padded - 2 * width - 1, width), jnp.float32),
+        ],
+        axis=0,
+    )
+    summed = reduce_over_records(packed)
+    folded = summed[:width]
+    top_right = summed[width : 2 * width]
+    low_diag = summed[2 * width]
+    mirrored = folded.T
+    top_left = jnp.where(rows <= cols, folded, mirrored)
+    low_right = jnp.where(rows > cols, folded, jnp.where(rows < cols, mirrored, low_diag[None, :]))
+    return jnp.concatenate(
+        [
+            jnp.concatenate([top_left, top_right], axis=1),
+            jnp.concatenate([top_right.T, low_right], axis=1),
+        ],
+        axis=0,
+    )
+
+
 def local(design, record_weight):
     width = design.shape[1] // 2
     weighted = (design.astype(jnp.float32) * record_weight[:, None]).astype(jnp.bfloat16)
@@ -91,7 +142,7 @@
     for round_index in range(ROUNDS):
         moving = round_index + 1 < ROUNDS
         pair_data = jnp.concatenate([upper_block, lower_block], axis=1)
-        gram_matrix = lax.psum(inner_products(pair_data, pair_data), "rec")
+        gram_matrix = summed_gram(pair_data, width)
         rotation = jacobi_sweeps(gram_matrix, width).astype(jnp.bfloat16)
         rotated = jnp.dot(pair_data, rotation, preferred_element_type=jnp.float32).astype(
             jnp.bfloat16
@@ -109,7 +160,9 @@
             lower_block = new_lower
     rotated_design = jnp.concatenate([upper_block, lower_block], axis=1)
     squares = jnp.sum(jnp.square(rotated_design.astype(jnp.float32)), axis=0)
-    totals = lax.psum(squares, "rec")
+    count = lax.axis_size("rec")
+    spread = jnp.broadcast_to(squares[None], (count,) + squares.shape)
+    totals = lax.all_to_all(spread, "rec", 0, 0, tiled=False).sum(axis=0)
     record_total = design.shape[0] * lax.axis_size("rec")
     column_rms = jnp.sqrt(totals / record_total + 1e-06)
     return (rotated_design, column_rms)

time: 746 us -> 228 us (0.31)
  the two profiles are of different devices: /device:TPU:64 before, /device:TPU:192 now
where the time goes in v1:
time: 228 us; the launch traced here: 227 us
  blocking collectives  145 us (64%)
  waiting for transfers between devices  25.7 us (11%)
  other arithmetic  20.6 us (9%)
  local copies, waits for them, and re-layouts  15.2 us (7%)
  starting transfers between devices  14.7 us (6%)
  matrix products  3.92 us (2%)
  between operations  2.45 us (1%)
    all_to_all x3, blocking collectives, reduce_over_records(): mine = lax.all_to_all(chunks, 'rec', 0, 0, tiled=False).sum(axis=0)  73.3 us
    all_to_all x2, blocking collectives, reduce_over_records(): lax.all_to_all(spread, 'rec', 0, 0, tiled=False).reshape(total, width)  57.8 us
    all_to_all x1, waiting for transfers between devices, reduce_over_records(): lax.all_to_all(spread, 'rec', 0, 0, tiled=False).reshape(total, width)  19 us
    all_to_all x1, blocking collectives, local(): totals = lax.all_to_all(spread, 'rec', 0, 0, tiled=False).sum(axis=0)  13.8 us
    ppermute x4, starting transfers between devices, from_behind(): lax.ppermute(value, axis, [(source, source + steps) for source in range(l...  11.1 us
    ppermute x4, waiting for transfers between devices, from_behind(): lax.ppermute(value, axis, [(source, source + steps) for source in range(l...  6.64 us
    reduce_sum x41, other arithmetic, diagonal_of(): return jnp.sum(jnp.where(rows == cols, matrix, 0.0), axis=0)  5.64 us
  transfers between devices with their start and end apart: 5, of which 5 were waited for; matrix products, arithmetic and copies ran while one was open for 0% of the time, Pallas kernels for 0%

profile of v1, /device:TPU:192, one launch (start us, length us, event | category | flops | bytes accessed | tf_op | source)
XLA Modules:
  0.0 227.4 jit_solution(10846966492556842862)
XLA Ops:
  0.6 1.5 fusion.45
  2.4 30.8 %all_to_all.36 = f32[16,40,256]{2,1,0:T(8,128)S(1)} all-to-all(f32[16,40,256]{2,1,0:T(8,128)S(1)} %bitcast.64), channel_id=1, replica_groups=mesh['col'=32,'rec'=16] {'rec'}, dimensions={0} | all-to-all | bytes 1310720 | tf_op jit(solution)/shard_map/all_to_all | solution.py:95
  33.2 0.9 broadcast_in_dim.186
  34.1 3.6 %all-to-all-start.1 = ((f32[16,40,256]{2,1,0:T(8,128)}), f32[16,40,256]{2,1,0:T(8,128)S(1)}, u32[]{:S(2)}, u32[]{:S(2)}) async-start(f32[16,40,256]{2,1,0:T(8,128)} %broadcast_in_dim.186), calls=%async_computation.1 | async-start | bytes 1310720 | tf_op jit(solution)/shard_map/all_to_all | solution.py:97
  37.9 19.0 %all-to-all-done.1 = f32[16,40,256]{2,1,0:T(8,128)S(1)} async-done(((f32[16,40,256]{2,1,0:T(8,128)}), f32[16,40,256]{2,1,0:T(8,128)S(1)}, u32[]{:S(2)}, u32[]{:S(2)}) %all-to-all-start.1) | async-done | bytes 655392 | tf_op jit(solution)/shard_map/all_to_all | solution.py:97
  57.5 0.8 multiply_bitcast_fusion.5
  58.5 1.1 copy.60
  59.6 0.2 multiply_subtract_fusion.65
  60.7 0.2 select_reduce_fusion.41
  61.8 0.2 select_reduce_fusion.38
  63.0 0.3 select_reduce_fusion.35
  64.0 0.2 multiply_subtract_fusion.49
  64.8 0.3 multiply_add_fusion.12
  65.3 0.2 multiply_add_fusion.11
  65.8 0.3 multiply_add_fusion.10
  66.9 0.3 subtract_convert_fusion.2
  67.3 0.8 copy-done.8
  68.2 0.4 convolution_convert_fusion.2
  68.6 1.9 collective-permute-start
  70.5 3.6 %collective-permute-start.1 = (bf16[256,256]{1,0:T(8,128)(2,1)S(1)}, bf16[256,256]{1,0:T(8,128)(2,1)S(1)}, u32[]{:S(2)}, u32[]{:S(2)}) collective-permute-start(bf16[256,256]{1,0:T(8,128)(2,1)S(1)} %get-tuple-element.192), channel_id=1, source_target_pairs={{16,0},{32,16},{48,32},{64,48},{80,64},{96,80},{112,96},{128,112},... | collective-permute-start | bytes 393224 | tf_op jit(solution)/shard_map/ppermute | solution.py:16
  74.1 0.7 collective-permute-done
  74.9 2.1 collective-permute-done.1
  77.0 0.3 fusion.44
  77.3 0.3 copy-done.4
  77.9 22.0 %all_to_all.37 = f32[16,40,256]{2,1,0:T(8,128)S(1)} all-to-all(f32[16,40,256]{2,1,0:T(8,128)S(1)} %bitcast.65), channel_id=1, replica_groups=mesh['col'=32,'rec'=16] {'rec'}, dimensions={0} | all-to-all | bytes 1310720 | tf_op jit(solution)/shard_map/all_to_all | solution.py:95
  99.9 28.9 %all_to_all.38 = f32[16,40,256]{2,1,0:T(8,128)S(1)} all-to-all(f32[16,40,256]{2,1,0:T(8,128)S(1)} %broadcast_in_dim.190), channel_id=1, replica_groups=mesh['col'=32,'rec'=16] {'rec'}, dimensions={0} | all-to-all | bytes 1310720 | tf_op jit(solution)/shard_map/all_to_all | solution.py:97
  129.5 0.8 multiply_bitcast_fusion.3
  130.4 1.1 copy.65
  131.5 0.2 multiply_subtract_fusion.48
  132.7 0.2 select_reduce_fusion.24
  133.9 0.2 select_reduce_fusion.21
  135.0 0.3 select_reduce_fusion.18
  136.0 0.2 multiply_subtract_fusion.32
  136.8 0.3 multiply_add_fusion.7
  137.4 0.2 multiply_add_fusion.6
  137.7 0.2 slice.842
  137.8 0.3 multiply_add_fusion.5
  138.9 0.3 subtract_convert_fusion.1
  139.4 0.8 copy-done.5
  140.2 0.4 convolution_convert_fusion.1
  140.6 1.9 collective-permute-start.2
  142.5 3.6 %collective-permute-start.3 = (bf16[256,256]{1,0:T(8,128)(2,1)S(1)}, bf16[256,256]{1,0:T(8,128)(2,1)S(1)}, u32[]{:S(2)}, u32[]{:S(2)}) collective-permute-start(bf16[256,256]{1,0:T(8,128)(2,1)S(1)} %get-tuple-element.188), channel_id=1, source_target_pairs={{16,0},{32,16},{48,32},{64,48},{80,64},{96,80},{112,96},{128,112},... | collective-permute-start | bytes 393224 | tf_op jit(solution)/shard_map/ppermute | solution.py:16
  146.2 0.7 collective-permute-done.2
  146.9 3.2 %collective-permute-done.3 = bf16[256,256]{1,0:T(8,128)(2,1)S(1)} collective-permute-done((bf16[256,256]{1,0:T(8,128)(2,1)S(1)}, bf16[256,256]{1,0:T(8,128)(2,1)S(1)}, u32[]{:S(2)}, u32[]{:S(2)}) %collective-permute-start.3) | collective-permute-done | bytes 131104 | tf_op jit(solution)/shard_map/ppermute | solution.py:16
  150.1 0.3 fusion.43
  150.4 0.3 copy-done
  151.0 20.5 %all_to_all.39 = f32[16,40,256]{2,1,0:T(8,128)S(1)} all-to-all(f32[16,40,256]{2,1,0:T(8,128)S(1)} %bitcast.63), channel_id=1, replica_groups=mesh['col'=32,'rec'=16] {'rec'}, dimensions={0} | all-to-all | bytes 1310720 | tf_op jit(solution)/shard_map/all_to_all | solution.py:95
  171.6 28.9 %all_to_all.40 = f32[16,40,256]{2,1,0:T(8,128)S(1)} all-to-all(f32[16,40,256]{2,1,0:T(8,128)S(1)} %broadcast_in_dim.194), channel_id=1, replica_groups=mesh['col'=32,'rec'=16] {'rec'}, dimensions={0} | all-to-all | bytes 1310720 | tf_op jit(solution)/shard_map/all_to_all | solution.py:97
  201.2 0.8 multiply_bitcast_fusion.1
  202.1 1.1 copy.70
  203.2 0.2 multiply_subtract_fusion.31
  204.4 0.2 select_reduce_fusion.7
  205.5 0.2 select_reduce_fusion.4
  206.7 0.2 select_reduce_fusion.1
  207.7 0.2 multiply_subtract_fusion.15
  208.5 0.3 multiply_add_fusion.2
  209.0 0.3 multiply_add_fusion.1
  209.5 0.3 multiply_add_fusion
  209.9 0.2 slice.910
  210.6 0.3 subtract_convert_fusion
  211.0 0.8 copy-done.1
  211.9 1.1 multiply_reduce_fusion
  213.0 13.8 %all_to_all.41 = f32[16,1,512]{2,1,0:T(1,128)S(1)} all-to-all(f32[16,1,512]{2,1,0:T(1,128)S(1)} %broadcast_in_dim.197), channel_id=1, replica_groups=mesh['col'=32,'rec'=16] {'rec'}, dimensions={0} | all-to-all | bytes 65536 | tf_op jit(solution)/shard_map/all_to_all | solution.py:165
  226.8 0.6 add_sqrt_fusion
  (260 shorter events, 18.0 us)
Async XLA Ops:
  34.1 22.7 %all-to-all-start.1 = ((f32[16,40,256]{2,1,0:T(8,128)}), f32[16,40,256]{2,1,0:T(8,128)S(1)}, u32[]{:S(2)}, u32[]{:S(2)}) async-start(f32[16,40,256]{2,1,0:T(8,128)} %broadcast_in_dim.186), calls=%async_computation.1 | async-start | bytes 1310720 | tf_op jit(solution)/shard_map/all_to_all | solution.py:97
  67.2 1.0 copy-start.8
  67.3 0.8 copy-start.9
  68.6 6.3 %collective-permute-start = (bf16[256,256]{1,0:T(8,128)(2,1)S(1)}, bf16[256,256]{1,0:T(8,128)(2,1)S(1)}, u32[]{:S(2)}, u32[]{:S(2)}) collective-permute-start(bf16[256,256]{1,0:T(8,128)(2,1)S(1)} %get-tuple-element.191), channel_id=1, source_target_pairs={{0,16},{16,32},{32,48},{48,64},{64,80},{80,96},{96,112},{112,128},... | collective-permute-start | bytes 393224 | tf_op jit(solution)/shard_map/ppermute | solution.py:16
  70.5 6.4 %collective-permute-start.1 = (bf16[256,256]{1,0:T(8,128)(2,1)S(1)}, bf16[256,256]{1,0:T(8,128)(2,1)S(1)}, u32[]{:S(2)}, u32[]{:S(2)}) collective-permute-start(bf16[256,256]{1,0:T(8,128)(2,1)S(1)} %get-tuple-element.192), channel_id=1, source_target_pairs={{16,0},{32,16},{48,32},{64,48},{80,64},{96,80},{112,96},{128,112},... | collective-permute-start | bytes 393224 | tf_op jit(solution)/shard_map/ppermute | solution.py:16
  77.0 0.7 copy-start.4
  77.0 0.7 copy-start.6
  139.2 0.9 copy-start.5
  139.2 1.0 copy-start.7
  140.6 6.3 %collective-permute-start.2 = (bf16[256,256]{1,0:T(8,128)(2,1)S(1)}, bf16[256,256]{1,0:T(8,128)(2,1)S(1)}, u32[]{:S(2)}, u32[]{:S(2)}) collective-permute-start(bf16[256,256]{1,0:T(8,128)(2,1)S(1)} %get-tuple-element.187), channel_id=1, source_target_pairs={{0,16},{16,32},{32,48},{48,64},{64,80},{80,96},{96,112},{112,128},... | collective-permute-start | bytes 393224 | tf_op jit(solution)/shard_map/ppermute | solution.py:16
  142.5 7.5 %collective-permute-start.3 = (bf16[256,256]{1,0:T(8,128)(2,1)S(1)}, bf16[256,256]{1,0:T(8,128)(2,1)S(1)}, u32[]{:S(2)}, u32[]{:S(2)}) collective-permute-start(bf16[256,256]{1,0:T(8,128)(2,1)S(1)} %get-tuple-element.188), channel_id=1, source_target_pairs={{16,0},{32,16},{48,32},{64,48},{80,64},{96,80},{112,96},{128,112},... | collective-permute-start | bytes 393224 | tf_op jit(solution)/shard_map/ppermute | solution.py:16
  150.1 0.7 copy-start
  150.1 0.7 copy-start.2
  210.9 0.9 copy-start.1
  210.9 1.0 copy-start.3

commit v2 on v1

--- a/solution.py
+++ b/solution.py
@@ -1,6 +1,8 @@
 import jax
 import jax.numpy as jnp
 from jax import lax
+from jax.experimental import pallas as pl
+from jax.experimental.pallas import tpu as pltpu
 from jax.sharding import PartitionSpec as P
 
 ROUNDS = 3
@@ -23,41 +25,57 @@
     return jnp.sum(jnp.where(rows == cols, matrix, 0.0), axis=0)
 
 
-def jacobi_sweeps(gram_matrix, width):
-    top_left = gram_matrix[:width, :width]
-    top_right = gram_matrix[:width, width:]
-    low_left = gram_matrix[width:, :width]
-    low_right = gram_matrix[width:, width:]
-    identity = jnp.eye(2 * width, dtype=jnp.float32)
-    rot_first = identity[:, :width]
-    rot_second = identity[:, width:]
+def half_angle_terms(first_diag, second_diag, coupling):
+    spread = second_diag - first_diag
+    tangent = (
+        2.0
+        * coupling
+        * spread
+        / (
+            spread * spread
+            + 4.0 * coupling * coupling
+            + eps_angle * (first_diag + second_diag) ** 2
+        )
+    )
+    double_cos = 1.0 / jnp.sqrt(1.0 + tangent * tangent)
+    cosine = jnp.sqrt(0.5 + 0.5 * double_cos)
+    sine_value = tangent * double_cos / (2.0 * cosine)
+    return cosine, sine_value
+
+
+def sweeps_kernel(top_left_ref, top_right_ref, low_left_ref, low_right_ref, rotation_ref):
+    width = top_left_ref.shape[0]
+    top_left = top_left_ref[...]
+    top_right = top_right_ref[...]
+    low_left = low_left_ref[...]
+    low_right = low_right_ref[...]
+    rows = lax.broadcasted_iota(jnp.int32, (width, width), 0)
+    cols = lax.broadcasted_iota(jnp.int32, (width, width), 1)
+    on_diagonal = rows == cols
+    first_top = jnp.where(on_diagonal, 1.0, 0.0).astype(jnp.float32)
+    first_low = jnp.zeros((width, width), jnp.float32)
+    second_top = jnp.zeros((width, width), jnp.float32)
+    second_low = first_top
+
+    def both_diagonals(matrix):
+        masked = jnp.where(on_diagonal, matrix, 0.0)
+        return jnp.sum(masked, axis=0, keepdims=True), jnp.sum(masked, axis=1, keepdims=True)
+
+    def to_left(matrix, axis):
+        return pltpu.roll(matrix, width - 1, axis)
+
     for sweep_index in range(SWEEPS):
         if sweep_index > 0:
-            top_right = jnp.roll(top_right, -1, axis=1)
-            low_left = jnp.roll(low_left, -1, axis=0)
-            low_right = jnp.roll(jnp.roll(low_right, -1, axis=0), -1, axis=1)
-            rot_second = jnp.roll(rot_second, -1, axis=1)
-        first_diag = diagonal_of(top_left)
-        second_diag = diagonal_of(low_right)
-        coupling = diagonal_of(top_right)
-        spread = second_diag - first_diag
-        tangent = (
-            2.0
-            * coupling
-            * spread
-            / (
-                spread * spread
-                + 4.0 * coupling * coupling
-                + eps_angle * (first_diag + second_diag) ** 2
-            )
-        )
-        half_angle = 0.5 * jnp.arctan(tangent)
-        cosine = jnp.cos(half_angle)
-        sine_value = jnp.sin(half_angle)
-        cos_col = cosine[None, :]
-        sin_col = sine_value[None, :]
-        cos_row = cosine[:, None]
-        sin_row = sine_value[:, None]
+            top_right = to_left(top_right, 1)
+            low_left = to_left(low_left, 0)
+            low_right = to_left(to_left(low_right, 0), 1)
+            second_top = to_left(second_top, 1)
+            second_low = to_left(second_low, 1)
+        first_r, first_c = both_diagonals(top_left)
+        second_r, second_c = both_diagonals(low_right)
+        coupling_r, coupling_c = both_diagonals(top_right)
+        cos_col, sin_col = half_angle_terms(first_r, second_r, coupling_r)
+        cos_row, sin_row = half_angle_terms(first_c, second_c, coupling_c)
         left_a = top_left * cos_col - top_right * sin_col
         right_a = top_left * sin_col + top_right * cos_col
         left_b = low_left * cos_col - low_right * sin_col
@@ -66,12 +84,35 @@
         low_left = sin_row * left_a + cos_row * left_b
         top_right = cos_row * right_a - sin_row * right_b
         low_right = sin_row * right_a + cos_row * right_b
-        rot_first, rot_second = (
-            rot_first * cos_col - rot_second * sin_col,
-            rot_first * sin_col + rot_second * cos_col,
-        )
-    rot_second = jnp.roll(rot_second, SWEEPS - 1, axis=1)
-    return jnp.concatenate([rot_first, rot_second], axis=1)
+        first_top, second_top = (
+            first_top * cos_col - second_top * sin_col,
+            first_top * sin_col + second_top * cos_col,
+        )
+        first_low, second_low = (
+            first_low * cos_col - second_low * sin_col,
+            first_low * sin_col + second_low * cos_col,
+        )
+    second_top = pltpu.roll(second_top, SWEEPS - 1, 1)
+    second_low = pltpu.roll(second_low, SWEEPS - 1, 1)
+    out = rotation_ref.dtype
+    rotation_ref[:width, :width] = first_top.astype(out)
+    rotation_ref[width:, :width] = first_low.astype(out)
+    rotation_ref[:width, width:] = second_top.astype(out)
+    rotation_ref[width:, width:] = second_low.astype(out)
+
+
+def rotation_of(top_left, top_right, low_left, low_right):
+    width = top_left.shape[0]
+    vmem = pl.BlockSpec(memory_space=pltpu.VMEM)
+    return pl.pallas_call(
+        sweeps_kernel,
+        out_shape=jax.ShapeDtypeStruct((2 * width, 2 * width), jnp.bfloat16),
+        in_specs=[vmem] * 4,
+        out_specs=vmem,
+        cost_estimate=pl.CostEstimate(
+            flops=SWEEPS * 40 * width * width, transcendentals=SWEEPS * 8 * width, bytes_accessed=5 * 4 * width * width
+        ),
+    )(top_left, top_right, low_left, low_right)
 
 
 def send_right(block):
@@ -123,13 +164,7 @@
     mirrored = folded.T
     top_left = jnp.where(rows <= cols, folded, mirrored)
     low_right = jnp.where(rows > cols, folded, jnp.where(rows < cols, mirrored, low_diag[None, :]))
-    return jnp.concatenate(
-        [
-            jnp.concatenate([top_left, top_right], axis=1),
-            jnp.concatenate([top_right.T, low_right], axis=1),
-        ],
-        axis=0,
-    )
+    return top_left, top_right, top_right.T, low_right
 
 
 def local(design, record_weight):
@@ -142,8 +177,7 @@
     for round_index in range(ROUNDS):
         moving = round_index + 1 < ROUNDS
         pair_data = jnp.concatenate([upper_block, lower_block], axis=1)
-        gram_matrix = summed_gram(pair_data, width)
-        rotation = jacobi_sweeps(gram_matrix, width).astype(jnp.bfloat16)
+        rotation = rotation_of(*summed_gram(pair_data, width))
         rotated = jnp.dot(pair_data, rotation, preferred_element_type=jnp.float32).astype(
             jnp.bfloat16
         )

time: 228 us -> 220 us (0.965)
  Pallas kernels: 0 us -> 17.7 us
  other arithmetic: 20.6 us -> 4.25 us
  local copies, waits for them, and re-layouts: 15.2 us -> 4.07 us
  matrix products: 3.92 us -> 6.88 us
    pallas_call x0 -> x3, Pallas kernels: none -> 17.7 us  [rotation_of(): pl.pallas_call(sweeps_kernel, out_shape=jax.ShapeDtypeStruct((2 * width,...]
    slice x117 -> x0, local copies, waits for them, and re-layouts: 6.16 us -> none  [the longest x30 3.21 us: jacobi_sweeps(): rot_second = jnp.roll(rot_second, -1, axis=1)]
    reduce_sum x41 -> x0, other arithmetic: 5.64 us -> none  [diagonal_of(): return jnp.sum(jnp.where(rows == cols, matrix, 0.0), axis=0)]
    add x24 -> x0, other arithmetic: 5.04 us -> none  [the longest x15 3.44 us: jacobi_sweeps(): rot_first * sin_col + rot_second * cos_col]
    mul x6 -> x0, local copies, waits for them, and re-layouts: 3.62 us -> none  [the longest x3 3.24 us: jacobi_sweeps(): left_b = low_left * cos_col - low_right * sin_col]
    unnamed x23 -> x4, local copies, waits for them, and re-layouts: 3.61 us -> 0.01 us
    dot_general x3, matrix products: 1.8 us -> 4.76 us  [local(): jnp.dot(pair_data, rotation, preferred_element_type=jnp.float32)]
    select_n x0 -> x3, other arithmetic: none -> 2.75 us  [summed_gram(): jnp.where(rows > cols, folded, jnp.where(rows < cols, mirrored, low_diag[...]
where the time goes in v2:
time: 220 us; the launch traced here: 219 us
  blocking collectives  145 us (66%)
  waiting for transfers between devices  25.6 us (12%)
  Pallas kernels  17.7 us (8%)
  starting transfers between devices  14.9 us (7%)
  matrix products  6.88 us (3%)
  other arithmetic  4.25 us (2%)
  local copies, waits for them, and re-layouts  4.07 us (2%)
    all_to_all x3, blocking collectives, reduce_over_records(): mine = lax.all_to_all(chunks, 'rec', 0, 0, tiled=False).sum(axis=0)  73.3 us
    all_to_all x2, blocking collectives, reduce_over_records(): lax.all_to_all(spread, 'rec', 0, 0, tiled=False).reshape(total, width)  57.8 us
    all_to_all x1, waiting for transfers between devices, reduce_over_records(): lax.all_to_all(spread, 'rec', 0, 0, tiled=False).reshape(total, width)  19.1 us
    pallas_call x3, Pallas kernels, rotation_of(): pl.pallas_call(sweeps_kernel, out_shape=jax.ShapeDtypeStruct((2 * width,...  17.7 us
    all_to_all x1, blocking collectives, local(): totals = lax.all_to_all(spread, 'rec', 0, 0, tiled=False).sum(axis=0)  13.8 us
    ppermute x4, starting transfers between devices, from_behind(): lax.ppermute(value, axis, [(source, source + steps) for source in range(l...  11.3 us
    ppermute x4, waiting for transfers between devices, from_behind(): lax.ppermute(value, axis, [(source, source + steps) for source in range(l...  6.46 us
    dot_general x3, matrix products, local(): jnp.dot(pair_data, rotation, preferred_element_type=jnp.float32)  4.76 us
  transfers between devices with their start and end apart: 5, of which 5 were waited for; matrix products, arithmetic and copies ran while one was open for 0% of the time, Pallas kernels for 0%

profile of v2, /device:TPU:192, one launch (start us, length us, event | category | flops | bytes accessed | tf_op | source)
XLA Modules:
  0.0 219.1 jit_solution(11242061974929463792)
XLA Ops:
  0.6 1.5 fusion.5
  2.1 0.1 slice_select_fusion.2
  2.2 0.1 pad.15.clone
  2.3 0.2 maximum_maximum_fusion
  2.4 30.8 %all_to_all.36 = f32[16,40,256]{2,1,0:T(8,128)S(1)} all-to-all(f32[16,40,256]{2,1,0:T(8,128)S(1)} %bitcast.46), channel_id=1, replica_groups=mesh['col'=32,'rec'=16] {'rec'}, dimensions={0} | all-to-all | bytes 1310720 | tf_op jit(solution)/shard_map/all_to_all | solution.py:136
  33.2 0.9 broadcast_in_dim.66
  34.1 3.6 %all-to-all-start.1 = ((f32[16,40,256]{2,1,0:T(8,128)}), f32[16,40,256]{2,1,0:T(8,128)S(1)}, u32[]{:S(2)}, u32[]{:S(2)}) async-start(f32[16,40,256]{2,1,0:T(8,128)} %broadcast_in_dim.66), calls=%async_computation.1 | async-start | bytes 1310720 | tf_op jit(solution)/shard_map/all_to_all | solution.py:138
  37.7 19.1 %all-to-all-done.1 = f32[16,40,256]{2,1,0:T(8,128)S(1)} async-done(((f32[16,40,256]{2,1,0:T(8,128)}), f32[16,40,256]{2,1,0:T(8,128)S(1)}, u32[]{:S(2)}, u32[]{:S(2)}) %all-to-all-start.1) | async-done | bytes 655392 | tf_op jit(solution)/shard_map/all_to_all | solution.py:138
  56.9 0.1 copy.16
  57.0 0.9 fusion.2
  57.9 0.9 copy.17.low_left_ref
  58.8 0.0 copy-start
  58.8 0.0 copy-start.1
  58.8 5.9 %shard_map.41 = bf16[512,512]{1,0:T(8,128)(2,1)} custom-call(f32[256,256]{1,0:T(8,128)} %get-tuple-element.16.top_left_ref, f32[256,256]{1,0:T(8,128)} %get-tuple-element.22.top_right_ref, f32[256,256]{1,0:T(8,128)} %copy.17.low_left_ref, f32[256,256]{1,0:T(8,128)} %get-tuple-element.15.low_right_ref), custom_call_target="tpu_custom_call" | custom-call | flops 15728640 | bytes 1310720 | tf_op jit(solution)/shard_map/pallas_call | solution.py:107
  64.7 0.0 copy-done
  64.7 0.0 copy-done.1
  64.7 1.4 convolution_convert_fusion.2
  66.2 1.9 collective-permute-start
  68.1 3.6 %collective-permute-start.1 = (bf16[256,256]{1,0:T(8,128)(2,1)S(1)}, bf16[256,256]{1,0:T(8,128)(2,1)S(1)}, u32[]{:S(2)}, u32[]{:S(2)}) collective-permute-start(bf16[256,256]{1,0:T(8,128)(2,1)S(1)} %get-tuple-element.30), channel_id=1, source_target_pairs={{16,0},{32,16},{48,32},{64,48},{80,64},{96,80},{112,96},{128,112},... | collective-permute-start | bytes 393224 | tf_op jit(solution)/shard_map/ppermute | solution.py:18
  71.7 0.7 collective-permute-done
  72.4 2.1 collective-permute-done.1
  74.5 0.3 fusion.4
  74.9 0.1 slice_select_fusion.1
  74.9 0.1 maximum_maximum_fusion.1
  75.1 22.0 %all_to_all.37 = f32[16,40,256]{2,1,0:T(8,128)S(1)} all-to-all(f32[16,40,256]{2,1,0:T(8,128)S(1)} %bitcast.47), channel_id=1, replica_groups=mesh['col'=32,'rec'=16] {'rec'}, dimensions={0} | all-to-all | bytes 1310720 | tf_op jit(solution)/shard_map/all_to_all | solution.py:136
  97.2 28.9 %all_to_all.38 = f32[16,40,256]{2,1,0:T(8,128)S(1)} all-to-all(f32[16,40,256]{2,1,0:T(8,128)S(1)} %broadcast_in_dim.70), channel_id=1, replica_groups=mesh['col'=32,'rec'=16] {'rec'}, dimensions={0} | all-to-all | bytes 1310720 | tf_op jit(solution)/shard_map/all_to_all | solution.py:138
  126.1 0.1 copy.18
  126.2 0.9 fusion.1
  127.1 0.9 copy.19.low_left_ref
  128.0 5.9 %shard_map.42 = bf16[512,512]{1,0:T(8,128)(2,1)} custom-call(f32[256,256]{1,0:T(8,128)} %get-tuple-element.14.top_left_ref, f32[256,256]{1,0:T(8,128)} %get-tuple-element.20.top_right_ref, f32[256,256]{1,0:T(8,128)} %copy.19.low_left_ref, f32[256,256]{1,0:T(8,128)} %get-tuple-element.13.low_right_ref), custom_call_target="tpu_custom_call" | custom-call | flops 15728640 | bytes 1310720 | tf_op jit(solution)/shard_map/pallas_call | solution.py:107
  133.9 1.3 convolution_convert_fusion.1
  135.2 1.9 collective-permute-start.2
  137.2 3.8 %collective-permute-start.3 = (bf16[256,256]{1,0:T(8,128)(2,1)S(1)}, bf16[256,256]{1,0:T(8,128)(2,1)S(1)}, u32[]{:S(2)}, u32[]{:S(2)}) collective-permute-start(bf16[256,256]{1,0:T(8,128)(2,1)S(1)} %get-tuple-element.26), channel_id=1, source_target_pairs={{16,0},{32,16},{48,32},{64,48},{80,64},{96,80},{112,96},{128,112},... | collective-permute-start | bytes 393224 | tf_op jit(solution)/shard_map/ppermute | solution.py:18
  141.0 0.5 collective-permute-done.2
  141.5 3.2 %collective-permute-done.3 = bf16[256,256]{1,0:T(8,128)(2,1)S(1)} collective-permute-done((bf16[256,256]{1,0:T(8,128)(2,1)S(1)}, bf16[256,256]{1,0:T(8,128)(2,1)S(1)}, u32[]{:S(2)}, u32[]{:S(2)}) %collective-permute-start.3) | collective-permute-done | bytes 131104 | tf_op jit(solution)/shard_map/ppermute | solution.py:18
  144.7 0.3 fusion.3
  145.0 0.1 slice_select_fusion
  145.1 0.1 maximum_maximum_fusion.2
  145.3 20.5 %all_to_all.39 = f32[16,40,256]{2,1,0:T(8,128)S(1)} all-to-all(f32[16,40,256]{2,1,0:T(8,128)S(1)} %bitcast.45), channel_id=1, replica_groups=mesh['col'=32,'rec'=16] {'rec'}, dimensions={0} | all-to-all | bytes 1310720 | tf_op jit(solution)/shard_map/all_to_all | solution.py:136
  165.9 28.9 %all_to_all.40 = f32[16,40,256]{2,1,0:T(8,128)S(1)} all-to-all(f32[16,40,256]{2,1,0:T(8,128)S(1)} %broadcast_in_dim.74), channel_id=1, replica_groups=mesh['col'=32,'rec'=16] {'rec'}, dimensions={0} | all-to-all | bytes 1310720 | tf_op jit(solution)/shard_map/all_to_all | solution.py:138
  194.8 0.1 copy.20
  194.9 0.9 fusion
  195.8 0.9 copy.21.low_left_ref
  196.7 5.9 %shard_map.43 = bf16[512,512]{1,0:T(8,128)(2,1)} custom-call(f32[256,256]{1,0:T(8,128)} %get-tuple-element.12.top_left_ref, f32[256,256]{1,0:T(8,128)} %get-tuple-element.18.top_right_ref, f32[256,256]{1,0:T(8,128)} %copy.21.low_left_ref, f32[256,256]{1,0:T(8,128)} %get-tuple-element.11.low_right_ref), custom_call_target="tpu_custom_call" | custom-call | flops 15728640 | bytes 1310720 | tf_op jit(solution)/shard_map/pallas_call | solution.py:107
  202.6 2.0 multiply_reduce_fusion
  204.7 13.8 %all_to_all.41 = f32[16,1,512]{2,1,0:T(1,128)S(1)} all-to-all(f32[16,1,512]{2,1,0:T(1,128)S(1)} %broadcast_in_dim.77), channel_id=1, replica_groups=mesh['col'=32,'rec'=16] {'rec'}, dimensions={0} | all-to-all | bytes 65536 | tf_op jit(solution)/shard_map/all_to_all | solution.py:199
  218.5 0.6 add_sqrt_fusion
  (18 shorter events, 0.4 us)
Async XLA Ops:
  34.1 22.7 %all-to-all-start.1 = ((f32[16,40,256]{2,1,0:T(8,128)}), f32[16,40,256]{2,1,0:T(8,128)S(1)}, u32[]{:S(2)}, u32[]{:S(2)}) async-start(f32[16,40,256]{2,1,0:T(8,128)} %broadcast_in_dim.66), calls=%async_computation.1 | async-start | bytes 1310720 | tf_op jit(solution)/shard_map/all_to_all | solution.py:138
  58.8 5.9 %copy-start = (bf16[256,512]{1,0:T(8,128)(2,1)S(1)}, bf16[256,512]{1,0:T(8,128)(2,1)}, u32[]{:S(2)}) copy-start(bf16[256,512]{1,0:T(8,128)(2,1)} %param.2) | copy-start | bytes 786436
  58.8 5.9 %copy-start.1 = (f32[256]{0:T(256)S(1)}, f32[256]{0:T(256)}, u32[]{:S(2)}) copy-start(f32[256]{0:T(256)} %param.3) | copy-start | bytes 3076
  66.2 6.3 %collective-permute-start = (bf16[256,256]{1,0:T(8,128)(2,1)S(1)}, bf16[256,256]{1,0:T(8,128)(2,1)S(1)}, u32[]{:S(2)}, u32[]{:S(2)}) collective-permute-start(bf16[256,256]{1,0:T(8,128)(2,1)S(1)} %get-tuple-element.29), channel_id=1, source_target_pairs={{0,16},{16,32},{32,48},{48,64},{64,80},{80,96},{96,112},{112,128},... | collective-permute-start | bytes 393224 | tf_op jit(solution)/shard_map/ppermute | solution.py:18
  68.1 6.4 %collective-permute-start.1 = (bf16[256,256]{1,0:T(8,128)(2,1)S(1)}, bf16[256,256]{1,0:T(8,128)(2,1)S(1)}, u32[]{:S(2)}, u32[]{:S(2)}) collective-permute-start(bf16[256,256]{1,0:T(8,128)(2,1)S(1)} %get-tuple-element.30), channel_id=1, source_target_pairs={{16,0},{32,16},{48,32},{64,48},{80,64},{96,80},{112,96},{128,112},... | collective-permute-start | bytes 393224 | tf_op jit(solution)/shard_map/ppermute | solution.py:18
  135.2 6.3 %collective-permute-start.2 = (bf16[256,256]{1,0:T(8,128)(2,1)S(1)}, bf16[256,256]{1,0:T(8,128)(2,1)S(1)}, u32[]{:S(2)}, u32[]{:S(2)}) collective-permute-start(bf16[256,256]{1,0:T(8,128)(2,1)S(1)} %get-tuple-element.25), channel_id=1, source_target_pairs={{0,16},{16,32},{32,48},{48,64},{64,80},{80,96},{96,112},{112,128},... | collective-permute-start | bytes 393224 | tf_op jit(solution)/shard_map/ppermute | solution.py:18
  137.2 7.5 %collective-permute-start.3 = (bf16[256,256]{1,0:T(8,128)(2,1)S(1)}, bf16[256,256]{1,0:T(8,128)(2,1)S(1)}, u32[]{:S(2)}, u32[]{:S(2)}) collective-permute-start(bf16[256,256]{1,0:T(8,128)(2,1)S(1)} %get-tuple-element.26), channel_id=1, source_target_pairs={{16,0},{32,16},{48,32},{64,48},{80,64},{96,80},{112,96},{128,112},... | collective-permute-start | bytes 393224 | tf_op jit(solution)/shard_map/ppermute | solution.py:18

commit v3 on v2

--- a/solution.py
+++ b/solution.py
@@ -3,7 +3,7 @@
 from jax import lax
 from jax.experimental import pallas as pl
 from jax.experimental.pallas import tpu as pltpu
-from jax.sharding import PartitionSpec as P
+from jax.sharding import Mesh, PartitionSpec as P
 
 ROUNDS = 3
 SWEEPS = 6
@@ -12,10 +12,20 @@
 eps_angle = 0.01
 
 
-def from_behind(value, axis, steps):
-    count = lax.axis_size(axis)
+COLUMN_AXES = ("x_lo", "z", "core")
+GROUP_AXES = ("x_hi", "y_hi")
+PAIR_AXIS = "y_lo"
+RECORD_AXES = GROUP_AXES + (PAIR_AXIS,)
+
+
+def from_behind(value, steps):
+    count = lax.axis_size(COLUMN_AXES)
     leading, last = (max(0, -steps), min(count, count - steps))
-    return lax.ppermute(value, axis, [(source, source + steps) for source in range(leading, last)])
+    return lax.ppermute(value, COLUMN_AXES, [(source, source + steps) for source in range(leading, last)])
+
+
+def with_partner(value):
+    return value + lax.ppermute(value, PAIR_AXIS, [(0, 1), (1, 0)])
 
 
 def diagonal_of(matrix):
@@ -116,11 +126,11 @@
 
 
 def send_right(block):
-    return from_behind(block, "col", 1)
+    return from_behind(block, 1)
 
 
 def send_left(block):
-    return from_behind(block, "col", -1)
+    return from_behind(block, -1)
 
 
 def inner_products(left_part, right_part):
@@ -129,13 +139,11 @@
     )
 
 
-def reduce_over_records(rows_in):
-    count = lax.axis_size("rec")
-    total, width = rows_in.shape
-    chunks = rows_in.reshape(count, total // count, width)
-    mine = lax.all_to_all(chunks, "rec", 0, 0, tiled=False).sum(axis=0)
-    spread = jnp.broadcast_to(mine[None], (count,) + mine.shape)
-    return lax.all_to_all(spread, "rec", 0, 0, tiled=False).reshape(total, width)
+def gathered_records(block):
+    count = lax.axis_size(GROUP_AXES)
+    spread = jnp.broadcast_to(block[None], (count,) + block.shape)
+    gathered = lax.all_to_all(spread, GROUP_AXES, 0, 0, tiled=False)
+    return gathered.reshape(count * block.shape[0], block.shape[1])
 
 
 def summed_gram(pair_data, width):
@@ -146,8 +154,7 @@
     rows = lax.broadcasted_iota(jnp.int32, (width, width), 0)
     cols = lax.broadcasted_iota(jnp.int32, (width, width), 1)
     folded = jnp.where(rows <= cols, top_left, low_right)
-    count = lax.axis_size("rec")
-    padded = -(-(2 * width + 1) // (8 * count)) * 8 * count
+    padded = -(-(2 * width + 1) // 8) * 8
     packed = jnp.concatenate(
         [
             folded,
@@ -157,7 +164,7 @@
         ],
         axis=0,
     )
-    summed = reduce_over_records(packed)
+    summed = with_partner(packed)
     folded = summed[:width]
     top_right = summed[width : 2 * width]
     low_diag = summed[2 * width]
@@ -169,11 +176,13 @@
 
 def local(design, record_weight):
     width = design.shape[1] // 2
+    records = design.shape[0]
     weighted = (design.astype(jnp.float32) * record_weight[:, None]).astype(jnp.bfloat16)
+    weighted = gathered_records(weighted)
     upper_block = weighted[:, :width]
     lower_block = weighted[:, width:]
-    position = lax.axis_index("col")
-    device_count = lax.axis_size("col")
+    position = lax.axis_index(COLUMN_AXES)
+    device_count = lax.axis_size(COLUMN_AXES)
     for round_index in range(ROUNDS):
         moving = round_index + 1 < ROUNDS
         pair_data = jnp.concatenate([upper_block, lower_block], axis=1)
@@ -192,18 +201,23 @@
         else:
             upper_block = new_upper
             lower_block = new_lower
-    rotated_design = jnp.concatenate([upper_block, lower_block], axis=1)
-    squares = jnp.sum(jnp.square(rotated_design.astype(jnp.float32)), axis=0)
-    count = lax.axis_size("rec")
-    spread = jnp.broadcast_to(squares[None], (count,) + squares.shape)
-    totals = lax.all_to_all(spread, "rec", 0, 0, tiled=False).sum(axis=0)
-    record_total = design.shape[0] * lax.axis_size("rec")
-    column_rms = jnp.sqrt(totals / record_total + 1e-06)
+    gathered_design = jnp.concatenate([upper_block, lower_block], axis=1)
+    squares = with_partner(jnp.sum(jnp.square(gathered_design.astype(jnp.float32)), axis=0))
+    record_total = records * lax.axis_size(RECORD_AXES)
+    column_rms = jnp.sqrt(squares / record_total + 1e-06)
+    start = lax.axis_index(GROUP_AXES) * records
+    rotated_design = lax.dynamic_slice_in_dim(gathered_design, start, records, axis=0)
     return (rotated_design, column_rms)
 
 
 def solution(mesh):
-    placed = (P("rec", "col"), P("rec"))
+    devices = mesh.devices.reshape(2, mesh.devices.shape[0] // 4, 2, 2, mesh.devices.shape[1] // 4, 2)
+    view = Mesh(devices, COLUMN_AXES + RECORD_AXES)
+    placed = (P(RECORD_AXES, COLUMN_AXES), P(RECORD_AXES))
     return jax.shard_map(
-        local, mesh=mesh, in_specs=placed, out_specs=(P("rec", "col"), P("col")), check_vma=False
-    )
+        local,
+        mesh=view,
+        in_specs=placed,
+        out_specs=(P(RECORD_AXES, COLUMN_AXES), P(COLUMN_AXES)),
+        check_vma=False,
+    )

time: 220 us -> 197 us (0.90)
  the two profiles are of different devices: /device:TPU:192 before, /device:TPU:2 now
where the time goes in v3:
time: 197 us; the launch traced here: 196 us
  waiting for transfers between devices  112 us (57%)
  starting transfers between devices  38.9 us (20%)
  Pallas kernels  17.8 us (9%)
  matrix products  11.5 us (6%)
  other arithmetic  9.68 us (5%)
  local copies, waits for them, and re-layouts  5.34 us (3%)
    all_to_all x1, waiting for transfers between devices, gathered_records(): gathered = lax.all_to_all(spread, GROUP_AXES, 0, 0, tiled=False)  52.8 us
    ppermute x4, waiting for transfers between devices, with_partner(): return value + lax.ppermute(value, PAIR_AXIS, [(0, 1), (1, 0)])  34.6 us
    ppermute x4, waiting for transfers between devices, from_behind(): lax.ppermute(value, COLUMN_AXES, [(source, source + steps) for source in...  24.6 us
    ppermute x4, starting transfers between devices, from_behind(): lax.ppermute(value, COLUMN_AXES, [(source, source + steps) for source in...  20.9 us
    pallas_call x3, Pallas kernels, rotation_of(): pl.pallas_call(sweeps_kernel, out_shape=jax.ShapeDtypeStruct((2 * width,...  17.8 us
    ppermute x4, starting transfers between devices, with_partner(): return value + lax.ppermute(value, PAIR_AXIS, [(0, 1), (1, 0)])  9.4 us
    all_to_all x1, starting transfers between devices, gathered_records(): gathered = lax.all_to_all(spread, GROUP_AXES, 0, 0, tiled=False)  8.66 us
    dot_general x3, matrix products, local(): jnp.dot(pair_data, rotation, preferred_element_type=jnp.float32)  7.65 us
  transfers between devices with their start and end apart: 9, of which 9 were waited for; matrix products, arithmetic and copies ran while one was open for 0% of the time, Pallas kernels for 0%

profile of v3, /device:TPU:2, one launch (start us, length us, event | category | flops | bytes accessed | tf_op | source)
XLA Modules:
  0.0 196.1 jit_solution(11108166130843386713)
XLA Ops:
  0.6 1.1 multiply_convert_fusion
  1.7 1.5 broadcast_in_dim.46
  3.2 8.7 %all-to-all-start = ((bf16[8,256,512]{2,1,0:T(8,128)(2,1)}), bf16[8,256,512]{2,1,0:T(8,128)(2,1)S(1)}, u32[]{:S(2)}, u32[]{:S(2)}) async-start(bf16[8,256,512]{2,1,0:T(8,128)(2,1)} %broadcast_in_dim.46), calls=%async_computation | async-start | bytes 4194304 | tf_op jit(solution)/shard_map/all_to_all | solution.py:145
  11.9 0.1 pad.15.clone
  11.9 52.8 %all-to-all-done = bf16[8,256,512]{2,1,0:T(8,128)(2,1)S(1)} async-done(((bf16[8,256,512]{2,1,0:T(8,128)(2,1)}), bf16[8,256,512]{2,1,0:T(8,128)(2,1)S(1)}, u32[]{:S(2)}, u32[]{:S(2)}) %all-to-all-start) | async-done | bytes 2097184 | tf_op jit(solution)/shard_map/all_to_all | solution.py:145
  64.8 0.0 copy-start
  64.8 1.3 convolution_bitcast_fusion
  66.0 0.0 copy-done
  66.1 0.1 slice_select_fusion.2
  66.1 0.1 maximum_maximum_fusion
  66.3 2.7 %collective-permute-start = (f32[520,256]{1,0:T(8,128)S(1)}, f32[520,256]{1,0:T(8,128)S(1)}, u32[]{:S(2)}, u32[]{:S(2)}) collective-permute-start(f32[520,256]{1,0:T(8,128)S(1)} %maximum_maximum_fusion), channel_id=1, source_target_pairs={{0,1},{1,0},{2,3},{3,2},{4,5},{5,4},{6,7},{7,6},{8,9},{9,8},{10,11... | collective-permute-start | bytes 1597448 | tf_op jit(solution)/shard_map/ppermute | solution.py:28
  69.0 11.9 %collective-permute-done = f32[520,256]{1,0:T(8,128)S(1)} collective-permute-done((f32[520,256]{1,0:T(8,128)S(1)}, f32[520,256]{1,0:T(8,128)S(1)}, u32[]{:S(2)}, u32[]{:S(2)}) %collective-permute-start) | collective-permute-done | bytes 532512 | tf_op jit(solution)/shard_map/ppermute | solution.py:28
  80.9 0.1 fusion.11
  81.1 0.1 copy.5
  81.2 0.9 fusion.4
  82.2 0.8 copy.6.low_left_ref
  83.0 5.9 %shard_map.41 = bf16[512,512]{1,0:T(8,128)(2,1)} custom-call(f32[256,256]{1,0:T(8,128)} %get-tuple-element.24.top_left_ref, f32[256,256]{1,0:T(8,128)} %get-tuple-element.30.top_right_ref, f32[256,256]{1,0:T(8,128)} %copy.6.low_left_ref, f32[256,256]{1,0:T(8,128)} %get-tuple-element.23.low_right_ref), custom_call_target="tpu_custom_call" | custom-call | flops 15728640 | bytes 1310720 | tf_op jit(solution)/shard_map/pallas_call | solution.py:117
  88.9 3.0 %convolution_convert_fusion.2 = bf16[2048,512]{0,1:T(8,128)(2,1)S(1)} fusion(bf16[2048,512]{1,0:T(8,128)(2,1)} %bitcast.36, bf16[512,512]{1,0:T(8,128)(2,1)} %shard_map.41), kind=kOutput, calls=%fused_computation.3 | convolution fusion | flops 1074790400 | bytes 4718592 | tf_op jit(solution)/shard_map/dot_general | solution.py:190
  91.9 1.1 broadcast_select_fusion.5
  93.0 1.9 collective-permute-start.1
  94.9 9.2 %collective-permute-start.2 = (bf16[2048,256]{0,1:T(8,128)(2,1)S(1)}, bf16[2048,256]{0,1:T(8,128)(2,1)}, u32[]{:S(2)}, u32[]{:S(2)}) collective-permute-start(bf16[2048,256]{0,1:T(8,128)(2,1)S(1)} %get-tuple-element.9), channel_id=1, source_target_pairs={{16,0},{32,16},{48,32},{64,48},{80,64},{96,80},{112,96},{128,112},... | collective-permute-start | bytes 3145736 | tf_op jit(solution)/shard_map/ppermute | solution.py:24
  104.1 10.8 %collective-permute-done.1 = bf16[2048,256]{0,1:T(8,128)(2,1)} collective-permute-done((bf16[2048,256]{0,1:T(8,128)(2,1)}, bf16[2048,256]{0,1:T(8,128)(2,1)}, u32[]{:S(2)}, u32[]{:S(2)}) %collective-permute-start.1) | collective-permute-done | bytes 1048608 | tf_op jit(solution)/shard_map/ppermute | solution.py:24
  115.0 1.4 collective-permute-done.2
  116.4 1.7 broadcast_select_fusion.4
  118.1 0.0 copy-start.1
  118.1 1.3 fusion.1
  119.4 0.0 copy-done.1
  119.4 0.1 slice_select_fusion.1
  119.5 0.1 maximum_maximum_fusion.1
  119.7 2.1 %collective-permute-start.3 = (f32[520,256]{1,0:T(8,128)S(1)}, f32[520,256]{1,0:T(8,128)S(1)}, u32[]{:S(2)}, u32[]{:S(2)}) collective-permute-start(f32[520,256]{1,0:T(8,128)S(1)} %maximum_maximum_fusion.1), channel_id=1, source_target_pairs={{0,1},{1,0},{2,3},{3,2},{4,5},{5,4},{6,7},{7,6},{8,9},{9,8},{10,11... | collective-permute-start | bytes 1597448 | tf_op jit(solution)/shard_map/ppermute | solution.py:28
  121.8 11.3 %collective-permute-done.3 = f32[520,256]{1,0:T(8,128)S(1)} collective-permute-done((f32[520,256]{1,0:T(8,128)S(1)}, f32[520,256]{1,0:T(8,128)S(1)}, u32[]{:S(2)}, u32[]{:S(2)}) %collective-permute-start.3) | collective-permute-done | bytes 532512 | tf_op jit(solution)/shard_map/ppermute | solution.py:28
  133.0 0.1 fusion.10
  133.2 0.1 copy.7
  133.4 0.0 copy-start.2
  133.4 0.9 fusion.3
  134.3 0.8 copy.8.low_left_ref
  135.1 5.9 %shard_map.42 = bf16[512,512]{1,0:T(8,128)(2,1)} custom-call(f32[256,256]{1,0:T(8,128)} %get-tuple-element.22.top_left_ref, f32[256,256]{1,0:T(8,128)} %get-tuple-element.28.top_right_ref, f32[256,256]{1,0:T(8,128)} %copy.8.low_left_ref, f32[256,256]{1,0:T(8,128)} %get-tuple-element.21.low_right_ref), custom_call_target="tpu_custom_call" | custom-call | flops 15728640 | bytes 1310720 | tf_op jit(solution)/shard_map/pallas_call | solution.py:117
  141.1 0.0 copy-done.2
  141.1 2.3 %convolution_convert_fusion.1 = bf16[2048,512]{0,1:T(8,128)(2,1)S(1)} fusion(bf16[512,512]{1,0:T(8,128)(2,1)} %shard_map.42, bf16[2048,256]{0,1:T(8,128)(2,1)S(1)} %copy-done.2, bf16[2048,256]{0,1:T(8,128)(2,1)S(1)} %get-tuple-element.6), kind=kOutput, calls=%fused_computation.2 | convolution fusion | flops 1078984704 | bytes 4718592 | tf_op jit(solution)/shard_map/dot_general | solution.py:190
  143.4 0.1 broadcast_select_fusion.3
  143.6 1.9 collective-permute-start.4
  145.5 7.9 %collective-permute-start.5 = (bf16[2048,256]{0,1:T(8,128)(2,1)S(1)}, bf16[2048,256]{0,1:T(8,128)(2,1)S(1)}, u32[]{:S(2)}, u32[]{:S(2)}) collective-permute-start(bf16[2048,256]{0,1:T(8,128)(2,1)S(1)} %get-tuple-element.5), channel_id=1, source_target_pairs={{16,0},{32,16},{48,32},{64,48},{80,64},{96,80},{112,96},{128,112},... | collective-permute-start | bytes 3145736 | tf_op jit(solution)/shard_map/ppermute | solution.py:24
  153.3 10.5 %collective-permute-done.4 = bf16[2048,256]{0,1:T(8,128)(2,1)S(1)} collective-permute-done((bf16[2048,256]{0,1:T(8,128)(2,1)S(1)}, bf16[2048,256]{0,1:T(8,128)(2,1)S(1)}, u32[]{:S(2)}, u32[]{:S(2)}) %collective-permute-start.4) | collective-permute-done | bytes 1048608 | tf_op jit(solution)/shard_map/ppermute | solution.py:24
  163.9 1.8 collective-permute-done.5
  165.6 0.2 broadcast_select_fusion.2
  165.9 1.3 fusion
  167.1 0.1 slice_select_fusion
  167.2 0.1 maximum_maximum_fusion.2
  167.3 2.4 %collective-permute-start.6 = (f32[520,256]{1,0:T(8,128)S(1)}, f32[520,256]{1,0:T(8,128)}, u32[]{:S(2)}, u32[]{:S(2)}) collective-permute-start(f32[520,256]{1,0:T(8,128)S(1)} %maximum_maximum_fusion.2), channel_id=1, source_target_pairs={{0,1},{1,0},{2,3},{3,2},{4,5},{5,4},{6,7},{7,6},{8,9},{9,8},{10,11... | collective-permute-start | bytes 1597448 | tf_op jit(solution)/shard_map/ppermute | solution.py:28
  169.8 8.8 %collective-permute-done.6 = f32[520,256]{1,0:T(8,128)} collective-permute-done((f32[520,256]{1,0:T(8,128)S(1)}, f32[520,256]{1,0:T(8,128)}, u32[]{:S(2)}, u32[]{:S(2)}) %collective-permute-start.6) | collective-permute-done | bytes 532512 | tf_op jit(solution)/shard_map/ppermute | solution.py:28
  178.6 1.2 fusion.9
  179.8 0.1 copy.9
  180.0 0.9 fusion.2
  180.9 0.9 copy.10.low_left_ref
  181.7 5.9 %shard_map.43 = bf16[512,512]{1,0:T(8,128)(2,1)} custom-call(f32[256,256]{1,0:T(8,128)} %get-tuple-element.20.top_left_ref, f32[256,256]{1,0:T(8,128)} %get-tuple-element.26.top_right_ref, f32[256,256]{1,0:T(8,128)} %copy.10.low_left_ref, f32[256,256]{1,0:T(8,128)} %get-tuple-element.19.low_right_ref), custom_call_target="tpu_custom_call" | custom-call | flops 15728640 | bytes 1310720 | tf_op jit(solution)/shard_map/pallas_call | solution.py:117
  187.7 2.3 %multiply_reduce_fusion = (f32[512]{0:T(512)S(1)}, bf16[2048,512]{1,0:T(8,128)(2,1)S(1)}) fusion(bf16[512,512]{1,0:T(8,128)(2,1)} %shard_map.43, bf16[2048,256]{0,1:T(8,128)(2,1)S(1)} %get-tuple-element.3, bf16[2048,256]{0,1:T(8,128)(2,1)S(1)} %get-tuple-element.2), kind=kOutput, calls=%fused_computation | convolution fusion | flops 1082129920 | bytes 4720640 | tf_op jit(solution)/shard_map/dot_general | solution.py:190
  190.0 2.2 %collective-permute-start.7 = (f32[512]{0:T(512)S(1)}, f32[512]{0:T(512)S(1)}, u32[]{:S(2)}, u32[]{:S(2)}) collective-permute-start(f32[512]{0:T(512)S(1)} %get-tuple-element.31), channel_id=1, source_target_pairs={{0,1},{1,0},{2,3},{3,2},{4,5},{5,4},{6,7},{7,6},{8,9},{9,8},{10,11... | collective-permute-start | bytes 6152 | tf_op jit(solution)/shard_map/ppermute | solution.py:28
  192.2 0.7 constant_dynamic-slice_fusion
  192.9 2.6 %collective-permute-done.7 = f32[512]{0:T(512)S(1)} collective-permute-done((f32[512]{0:T(512)S(1)}, f32[512]{0:T(512)S(1)}, u32[]{:S(2)}, u32[]{:S(2)}) %collective-permute-start.7) | collective-permute-done | bytes 2080 | tf_op jit(solution)/shard_map/ppermute | solution.py:28
  195.5 0.6 add_sqrt_fusion
  (7 shorter events, 0.1 us)
Async XLA Ops:
  3.2 61.5 %all-to-all-start = ((bf16[8,256,512]{2,1,0:T(8,128)(2,1)}), bf16[8,256,512]{2,1,0:T(8,128)(2,1)S(1)}, u32[]{:S(2)}, u32[]{:S(2)}) async-start(bf16[8,256,512]{2,1,0:T(8,128)(2,1)} %broadcast_in_dim.46), calls=%async_computation | async-start | bytes 4194304 | tf_op jit(solution)/shard_map/all_to_all | solution.py:145
  64.8 1.3 copy-start
  66.3 14.6 %collective-permute-start = (f32[520,256]{1,0:T(8,128)S(1)}, f32[520,256]{1,0:T(8,128)S(1)}, u32[]{:S(2)}, u32[]{:S(2)}) collective-permute-start(f32[520,256]{1,0:T(8,128)S(1)} %maximum_maximum_fusion), channel_id=1, source_target_pairs={{0,1},{1,0},{2,3},{3,2},{4,5},{5,4},{6,7},{7,6},{8,9},{9,8},{10,11... | collective-permute-start | bytes 1597448 | tf_op jit(solution)/shard_map/ppermute | solution.py:28
  93.0 22.0 %collective-permute-start.1 = (bf16[2048,256]{0,1:T(8,128)(2,1)}, bf16[2048,256]{0,1:T(8,128)(2,1)}, u32[]{:S(2)}, u32[]{:S(2)}) collective-permute-start(bf16[2048,256]{0,1:T(8,128)(2,1)} %get-tuple-element.8), channel_id=1, source_target_pairs={{0,16},{16,32},{32,48},{48,64},{64,80},{80,96},{96,112},{112,128},... | collective-permute-start | bytes 3145736 | tf_op jit(solution)/shard_map/ppermute | solution.py:24
  94.9 21.5 %collective-permute-start.2 = (bf16[2048,256]{0,1:T(8,128)(2,1)S(1)}, bf16[2048,256]{0,1:T(8,128)(2,1)}, u32[]{:S(2)}, u32[]{:S(2)}) collective-permute-start(bf16[2048,256]{0,1:T(8,128)(2,1)S(1)} %get-tuple-element.9), channel_id=1, source_target_pairs={{16,0},{32,16},{48,32},{64,48},{80,64},{96,80},{112,96},{128,112},... | collective-permute-start | bytes 3145736 | tf_op jit(solution)/shard_map/ppermute | solution.py:24
  118.1 1.3 copy-start.1
  119.7 13.4 %collective-permute-start.3 = (f32[520,256]{1,0:T(8,128)S(1)}, f32[520,256]{1,0:T(8,128)S(1)}, u32[]{:S(2)}, u32[]{:S(2)}) collective-permute-start(f32[520,256]{1,0:T(8,128)S(1)} %maximum_maximum_fusion.1), channel_id=1, source_target_pairs={{0,1},{1,0},{2,3},{3,2},{4,5},{5,4},{6,7},{7,6},{8,9},{9,8},{10,11... | collective-permute-start | bytes 1597448 | tf_op jit(solution)/shard_map/ppermute | solution.py:28
  133.4 7.7 %copy-start.2 = (bf16[2048,256]{0,1:T(8,128)(2,1)S(1)}, bf16[2048,256]{0,1:T(8,128)(2,1)}, u32[]{:S(2)}) copy-start(bf16[2048,256]{0,1:T(8,128)(2,1)} %copy-done.1) | copy-start | bytes 3145732
  143.6 20.3 %collective-permute-start.4 = (bf16[2048,256]{0,1:T(8,128)(2,1)S(1)}, bf16[2048,256]{0,1:T(8,128)(2,1)S(1)}, u32[]{:S(2)}, u32[]{:S(2)}) collective-permute-start(bf16[2048,256]{0,1:T(8,128)(2,1)S(1)} %get-tuple-element.4), channel_id=1, source_target_pairs={{0,16},{16,32},{32,48},{48,64},{64,80},{80,96},{96,112},{112,128},... | collective-permute-start | bytes 3145736 | tf_op jit(solution)/shard_map/ppermute | solution.py:24
  145.5 20.2 %collective-permute-start.5 = (bf16[2048,256]{0,1:T(8,128)(2,1)S(1)}, bf16[2048,256]{0,1:T(8,128)(2,1)S(1)}, u32[]{:S(2)}, u32[]{:S(2)}) collective-permute-start(bf16[2048,256]{0,1:T(8,128)(2,1)S(1)} %get-tuple-element.5), channel_id=1, source_target_pairs={{16,0},{32,16},{48,32},{64,48},{80,64},{96,80},{112,96},{128,112},... | collective-permute-start | bytes 3145736 | tf_op jit(solution)/shard_map/ppermute | solution.py:24
  167.3 11.3 %collective-permute-start.6 = (f32[520,256]{1,0:T(8,128)S(1)}, f32[520,256]{1,0:T(8,128)}, u32[]{:S(2)}, u32[]{:S(2)}) collective-permute-start(f32[520,256]{1,0:T(8,128)S(1)} %maximum_maximum_fusion.2), channel_id=1, source_target_pairs={{0,1},{1,0},{2,3},{3,2},{4,5},{5,4},{6,7},{7,6},{8,9},{9,8},{10,11... | collective-permute-start | bytes 1597448 | tf_op jit(solution)/shard_map/ppermute | solution.py:28
  190.0 5.5 %collective-permute-start.7 = (f32[512]{0:T(512)S(1)}, f32[512]{0:T(512)S(1)}, u32[]{:S(2)}, u32[]{:S(2)}) collective-permute-start(f32[512]{0:T(512)S(1)} %get-tuple-element.31), channel_id=1, source_target_pairs={{0,1},{1,0},{2,3},{3,2},{4,5},{5,4},{6,7},{7,6},{8,9},{9,8},{10,11... | collective-permute-start | bytes 6152 | tf_op jit(solution)/shard_map/ppermute | solution.py:28

commit v4 on v3

--- a/solution.py
+++ b/solution.py
@@ -186,21 +186,28 @@
     for round_index in range(ROUNDS):
         moving = round_index + 1 < ROUNDS
         pair_data = jnp.concatenate([upper_block, lower_block], axis=1)
+        if moving:
+            pair_from_left = send_right(pair_data)
+            pair_from_right = send_left(pair_data)
         rotation = rotation_of(*summed_gram(pair_data, width))
-        rotated = jnp.dot(pair_data, rotation, preferred_element_type=jnp.float32).astype(
-            jnp.bfloat16
-        )
-        new_upper = rotated[:, :width]
-        new_lower = rotated[:, width:]
-        if moving:
-            from_right = send_left(new_lower)
-            from_left = send_right(jnp.where(position == 0, new_lower, new_upper))
-        if moving:
-            upper_block = jnp.where(position == 0, new_upper, from_left)
-            lower_block = jnp.where(position == device_count - 1, new_upper, from_right)
-        else:
-            upper_block = new_upper
-            lower_block = new_lower
+        if not moving:
+            rotated = jnp.dot(pair_data, rotation, preferred_element_type=jnp.float32)
+            upper_block = rotated[:, :width].astype(jnp.bfloat16)
+            lower_block = rotated[:, width:].astype(jnp.bfloat16)
+            break
+        first_columns = rotation[:, :width]
+        second_columns = rotation[:, width:]
+        kept = jnp.dot(pair_data, first_columns, preferred_element_type=jnp.float32).astype(jnp.bfloat16)
+        columns_from_left = send_right(jnp.where(position == 0, second_columns, first_columns))
+        columns_from_right = send_left(second_columns)
+        arriving_upper = jnp.dot(
+            pair_from_left, columns_from_left, preferred_element_type=jnp.float32
+        ).astype(jnp.bfloat16)
+        arriving_lower = jnp.dot(
+            pair_from_right, columns_from_right, preferred_element_type=jnp.float32
+        ).astype(jnp.bfloat16)
+        upper_block = jnp.where(position == 0, kept, arriving_upper)
+        lower_block = jnp.where(position == device_count - 1, kept, arriving_lower)
     gathered_design = jnp.concatenate([upper_block, lower_block], axis=1)
     squares = with_partner(jnp.sum(jnp.square(gathered_design.astype(jnp.float32)), axis=0))
     record_total = records * lax.axis_size(RECORD_AXES)

time: 197 us -> 199 us (1.010)
  waiting for transfers between devices: 112 us -> 86.8 us
  starting transfers between devices: 38.9 us -> 57.6 us
  matrix products: 11.5 us -> 19.3 us
    ppermute x4 -> x8, waiting for transfers between devices: 24.6 us -> 4.22 us  [from_behind(): lax.ppermute(value, COLUMN_AXES, [(source, source + steps) for source in...]
    ppermute x4 -> x8, starting transfers between devices: 20.9 us -> 38.6 us  [from_behind(): lax.ppermute(value, COLUMN_AXES, [(source, source + steps) for source in...]
    dot_general x3 -> x7, matrix products: 7.65 us -> 15.5 us  [the longest x2 4.71 us: local(): jnp.dot(pair_from_left, columns_from_left, preferred_element_type=jnp.flo...]
    ppermute x4, waiting for transfers between devices: 34.6 us -> 29.8 us  [with_partner(): return value + lax.ppermute(value, PAIR_AXIS, [(0, 1), (1, 0)])]
  transfers between devices with their start and end apart: 9 -> 13, of which waited for: 9 -> 8; matrix products, arithmetic and copies ran while one was open for 0% -> 10% of each run, Pallas kernels for 0% -> 6%
where the time goes in v4:
time: 199 us; the launch traced here: 198 us
  waiting for transfers between devices  86.8 us (44%)
  starting transfers between devices  57.6 us (29%)
  matrix products  19.3 us (10%)
  Pallas kernels  17.7 us (9%)
  other arithmetic  10.1 us (5%)
  local copies, waits for them, and re-layouts  5.25 us (3%)
    all_to_all x1, waiting for transfers between devices, gathered_records(): gathered = lax.all_to_all(spread, GROUP_AXES, 0, 0, tiled=False)  52.8 us
    ppermute x8, starting transfers between devices, from_behind(): lax.ppermute(value, COLUMN_AXES, [(source, source + steps) for source in...  38.6 us
    ppermute x4, waiting for transfers between devices, with_partner(): return value + lax.ppermute(value, PAIR_AXIS, [(0, 1), (1, 0)])  29.8 us
    pallas_call x3, Pallas kernels, rotation_of(): pl.pallas_call(sweeps_kernel, out_shape=jax.ShapeDtypeStruct((2 * width,...  17.7 us
    ppermute x4, starting transfers between devices, with_partner(): return value + lax.ppermute(value, PAIR_AXIS, [(0, 1), (1, 0)])  10.4 us
    all_to_all x1, starting transfers between devices, gathered_records(): gathered = lax.all_to_all(spread, GROUP_AXES, 0, 0, tiled=False)  8.66 us
    dot_general x2, matrix products, local(): jnp.dot(pair_from_left, columns_from_left, preferred_element_type=jnp.flo...  4.71 us
    dot_general x2, matrix products, local(): jnp.dot(pair_from_right, columns_from_right, preferred_element_type=jnp.f...  4.71 us
  transfers between devices with their start and end apart: 13, of which 8 were waited for; matrix products, arithmetic and copies ran while one was open for 10% of the time, Pallas kernels for 6%

profile of v4, /device:TPU:2, one launch (start us, length us, event | category | flops | bytes accessed | tf_op | source)
XLA Modules:
  0.0 197.8 jit_solution(17250561357673449771)
XLA Ops:
  0.6 1.1 multiply_convert_fusion
  1.7 1.5 broadcast_in_dim.46
  3.2 8.7 %all-to-all-start = ((bf16[8,256,512]{2,1,0:T(8,128)(2,1)}), bf16[8,256,512]{2,1,0:T(8,128)(2,1)S(1)}, u32[]{:S(2)}, u32[]{:S(2)}) async-start(bf16[8,256,512]{2,1,0:T(8,128)(2,1)} %broadcast_in_dim.46), calls=%async_computation | async-start | bytes 4194304 | tf_op jit(solution)/shard_map/all_to_all | solution.py:145
  11.9 0.1 pad.15.clone
  11.9 52.8 %all-to-all-done = bf16[8,256,512]{2,1,0:T(8,128)(2,1)S(1)} async-done(((bf16[8,256,512]{2,1,0:T(8,128)(2,1)}), bf16[8,256,512]{2,1,0:T(8,128)(2,1)S(1)}, u32[]{:S(2)}, u32[]{:S(2)}) %all-to-all-start) | async-done | bytes 2097184 | tf_op jit(solution)/shard_map/all_to_all | solution.py:145
  64.8 10.1 %collective-permute-start.3 = (bf16[2048,512]{1,0:T(8,128)(2,1)S(1)}, bf16[2048,512]{1,0:T(8,128)(2,1)}, u32[]{:S(2)}, u32[]{:S(2)}) collective-permute-start(bf16[2048,512]{1,0:T(8,128)(2,1)S(1)} %bitcast.42), channel_id=1, source_target_pairs={{16,0},{32,16},{48,32},{64,48},{80,64},{96,80},{112,96},{128,112},... | collective-permute-start | bytes 6291464 | tf_op jit(solution)/shard_map/ppermute | solution.py:24
  74.9 1.9 collective-permute-start.1
  76.8 1.3 convolution_bitcast_fusion
  78.1 0.1 slice_select_fusion.2
  78.1 0.1 maximum_maximum_fusion
  78.3 1.9 collective-permute-start
  80.2 9.3 %collective-permute-done = f32[520,256]{1,0:T(8,128)} collective-permute-done((f32[520,256]{1,0:T(8,128)S(1)}, f32[520,256]{1,0:T(8,128)}, u32[]{:S(2)}, u32[]{:S(2)}) %collective-permute-start) | collective-permute-done | bytes 532512 | tf_op jit(solution)/shard_map/ppermute | solution.py:28
  89.5 1.2 fusion.14
  90.8 0.1 copy.5
  90.9 0.9 fusion.7
  91.8 0.8 copy.6.low_left_ref
  92.7 5.9 %shard_map.41 = bf16[512,512]{1,0:T(8,128)(2,1)} custom-call(f32[256,256]{1,0:T(8,128)} %get-tuple-element.16.top_left_ref, f32[256,256]{1,0:T(8,128)} %get-tuple-element.22.top_right_ref, f32[256,256]{1,0:T(8,128)} %copy.6.low_left_ref, f32[256,256]{1,0:T(8,128)} %get-tuple-element.15.low_right_ref), custom_call_target="tpu_custom_call" | custom-call | flops 15728640 | bytes 1310720 | tf_op jit(solution)/shard_map/pallas_call | solution.py:117
  98.6 1.1 broadcast_select_fusion.1
  99.6 1.9 collective-permute-start.2
  101.6 9.5 %collective-permute-start.4 = (bf16[512,256]{1,0:T(8,128)(2,1)S(1)}, bf16[512,256]{1,0:T(8,128)(2,1)S(1)}, u32[]{:S(2)}, u32[]{:S(2)}) collective-permute-start(bf16[512,256]{1,0:T(8,128)(2,1)S(1)} %get-tuple-element.26), channel_id=1, source_target_pairs={{16,0},{32,16},{48,32},{64,48},{80,64},{96,80},{112,96},{128,112},... | collective-permute-start | bytes 786440 | tf_op jit(solution)/shard_map/ppermute | solution.py:24
  111.1 1.7 convolution_convert_fusion.6
  112.8 0.4 collective-permute-done.2
  113.2 0.0 collective-permute-done.1
  113.2 2.3 %fusion = bf16[2048,256]{0,1:T(8,128)(2,1)S(1)} fusion(bf16[2048,256]{0,1:T(8,128)(2,1)S(1)} %convolution_convert_fusion.6, bf16[2048,512]{1,0:T(8,128)(2,1)} %collective-permute-done.1, bf16[512,256]{1,0:T(8,128)(2,1)S(1)} %collective-permute-done.2, pred[]{:T(512)S(6)} %eq.19), kind=kOutput, calls=%fused_computation.8 | convolution fusion | flops 537919488 | bytes 4456449 | tf_op jit(solution)/shard_map/dot_general | solution.py:203
  115.6 0.0 collective-permute-done.4
  115.6 0.0 collective-permute-done.3
  115.6 2.3 %fusion.1 = bf16[2048,256]{0,1:T(8,128)(2,1)S(1)} fusion(bf16[2048,256]{0,1:T(8,128)(2,1)S(1)} %convolution_convert_fusion.6, bf16[2048,512]{1,0:T(8,128)(2,1)} %collective-permute-done.3, bf16[512,256]{1,0:T(8,128)(2,1)S(1)} %collective-permute-done.4, pred[]{:T(512)S(6)} %eq.21), kind=kOutput, calls=%fused_computation.9 | convolution fusion | flops 537919488 | bytes 4456449 | tf_op jit(solution)/shard_map/dot_general | solution.py:206
  118.0 1.5 pad_maximum_fusion
  119.4 5.3 %collective-permute-start.8 = (bf16[2048,512]{0,1:T(8,128)(2,1)}, bf16[2048,512]{0,1:T(8,128)(2,1)}, u32[]{:S(2)}, u32[]{:S(2)}) collective-permute-start(bf16[2048,512]{0,1:T(8,128)(2,1)} %pad_maximum_fusion), channel_id=1, source_target_pairs={{16,0},{32,16},{48,32},{64,48},{80,64},{96,80},{112,96},{128,112},... | collective-permute-start | bytes 6291464 | tf_op jit(solution)/shard_map/ppermute | solution.py:24
  124.7 1.3 fusion.15
  126.0 1.9 collective-permute-start.6
  127.9 0.1 slice_select_fusion.1
  128.0 0.1 maximum_maximum_fusion.1
  128.1 2.9 %collective-permute-start.5 = (f32[520,256]{1,0:T(8,128)S(1)}, f32[520,256]{1,0:T(8,128)S(1)}, u32[]{:S(2)}, u32[]{:S(2)}) collective-permute-start(f32[520,256]{1,0:T(8,128)S(1)} %maximum_maximum_fusion.1), channel_id=1, source_target_pairs={{0,1},{1,0},{2,3},{3,2},{4,5},{5,4},{6,7},{7,6},{8,9},{9,8},{10,11... | collective-permute-start | bytes 1597448 | tf_op jit(solution)/shard_map/ppermute | solution.py:28
  131.0 10.1 %collective-permute-done.5 = f32[520,256]{1,0:T(8,128)S(1)} collective-permute-done((f32[520,256]{1,0:T(8,128)S(1)}, f32[520,256]{1,0:T(8,128)S(1)}, u32[]{:S(2)}, u32[]{:S(2)}) %collective-permute-start.5) | collective-permute-done | bytes 532512 | tf_op jit(solution)/shard_map/ppermute | solution.py:28
  141.2 0.1 fusion.13
  141.3 0.1 copy.7
  141.5 0.9 fusion.6
  142.4 0.8 copy.8.low_left_ref
  143.2 5.9 %shard_map.42 = bf16[512,512]{1,0:T(8,128)(2,1)} custom-call(f32[256,256]{1,0:T(8,128)} %get-tuple-element.14.top_left_ref, f32[256,256]{1,0:T(8,128)} %get-tuple-element.20.top_right_ref, f32[256,256]{1,0:T(8,128)} %copy.8.low_left_ref, f32[256,256]{1,0:T(8,128)} %get-tuple-element.13.low_right_ref), custom_call_target="tpu_custom_call" | custom-call | flops 15728640 | bytes 1310720 | tf_op jit(solution)/shard_map/pallas_call | solution.py:117
  149.1 1.1 broadcast_select_fusion
  150.2 6.0 %collective-permute-start.9 = (bf16[512,256]{1,0:T(8,128)(2,1)S(1)}, bf16[512,256]{1,0:T(8,128)(2,1)S(1)}, u32[]{:S(2)}, u32[]{:S(2)}) collective-permute-start(bf16[512,256]{1,0:T(8,128)(2,1)S(1)} %get-tuple-element.24), channel_id=1, source_target_pairs={{16,0},{32,16},{48,32},{64,48},{80,64},{96,80},{112,96},{128,112},... | collective-permute-start | bytes 786440 | tf_op jit(solution)/shard_map/ppermute | solution.py:24
  156.2 1.9 collective-permute-start.7
  158.1 1.7 convolution_convert_fusion.3
  159.8 0.2 collective-permute-done.9
  160.1 0.0 collective-permute-done.8
  160.1 2.4 %fusion.3 = bf16[2048,256]{0,1:T(8,128)(2,1)S(1)} fusion(bf16[2048,256]{0,1:T(8,128)(2,1)S(1)} %convolution_convert_fusion.3, bf16[2048,512]{0,1:T(8,128)(2,1)} %collective-permute-done.8, bf16[512,256]{1,0:T(8,128)(2,1)S(1)} %collective-permute-done.9, pred[]{:T(512)S(6)} %eq.21), kind=kOutput, calls=%fused_computation.11 | convolution fusion | flops 537919488 | bytes 4456449 | tf_op jit(solution)/shard_map/dot_general | solution.py:206
  162.4 3.6 %collective-permute-done.7 = bf16[512,256]{1,0:T(8,128)(2,1)S(1)} collective-permute-done((bf16[512,256]{1,0:T(8,128)(2,1)S(1)}, bf16[512,256]{1,0:T(8,128)(2,1)S(1)}, u32[]{:S(2)}, u32[]{:S(2)}) %collective-permute-start.7) | collective-permute-done | bytes 262176 | tf_op jit(solution)/shard_map/ppermute | solution.py:24
  166.0 2.4 %fusion.2 = bf16[2048,256]{0,1:T(8,128)(2,1)S(1)} fusion(bf16[2048,256]{0,1:T(8,128)(2,1)S(1)} %convolution_convert_fusion.3, bf16[2048,512]{0,1:T(8,128)(2,1)} %collective-permute-done.6, bf16[512,256]{1,0:T(8,128)(2,1)S(1)} %collective-permute-done.7, pred[]{:T(512)S(6)} %eq.19), kind=kOutput, calls=%fused_computation.10 | convolution fusion | flops 537919488 | bytes 4456449 | tf_op jit(solution)/shard_map/dot_general | solution.py:203
  168.4 1.3 fusion.4
  169.7 0.1 slice_select_fusion
  169.7 0.1 maximum_maximum_fusion.2
  169.9 2.9 %collective-permute-start.10 = (f32[520,256]{1,0:T(8,128)S(1)}, f32[520,256]{1,0:T(8,128)S(1)}, u32[]{:S(2)}, u32[]{:S(2)}) collective-permute-start(f32[520,256]{1,0:T(8,128)S(1)} %maximum_maximum_fusion.2), channel_id=1, source_target_pairs={{0,1},{1,0},{2,3},{3,2},{4,5},{5,4},{6,7},{7,6},{8,9},{9,8},{10,11... | collective-permute-start | bytes 1597448 | tf_op jit(solution)/shard_map/ppermute | solution.py:28
  172.8 8.2 %collective-permute-done.10 = f32[520,256]{1,0:T(8,128)S(1)} collective-permute-done((f32[520,256]{1,0:T(8,128)S(1)}, f32[520,256]{1,0:T(8,128)S(1)}, u32[]{:S(2)}, u32[]{:S(2)}) %collective-permute-start.10) | collective-permute-done | bytes 532512 | tf_op jit(solution)/shard_map/ppermute | solution.py:28
  181.0 0.1 fusion.12
  181.2 0.1 copy.9
  181.4 0.9 fusion.5
  182.3 0.8 copy.10.low_left_ref
  183.1 5.9 %shard_map.43 = bf16[512,512]{1,0:T(8,128)(2,1)} custom-call(f32[256,256]{1,0:T(8,128)} %get-tuple-element.12.top_left_ref, f32[256,256]{1,0:T(8,128)} %get-tuple-element.18.top_right_ref, f32[256,256]{1,0:T(8,128)} %copy.10.low_left_ref, f32[256,256]{1,0:T(8,128)} %get-tuple-element.11.low_right_ref), custom_call_target="tpu_custom_call" | custom-call | flops 15728640 | bytes 1310720 | tf_op jit(solution)/shard_map/pallas_call | solution.py:117
  189.0 2.7 %multiply_reduce_fusion = (f32[512]{0:T(512)S(1)}, bf16[2048,512]{1,0:T(8,128)(2,1)S(1)}) fusion(bf16[512,512]{1,0:T(8,128)(2,1)} %shard_map.43, bf16[2048,256]{0,1:T(8,128)(2,1)S(1)} %fusion.3, bf16[2048,256]{0,1:T(8,128)(2,1)} %copy-done), kind=kOutput, calls=%fused_computation | convolution fusion | flops 1082129920 | bytes 4720640 | tf_op jit(solution)/shard_map/dot_general | solution.py:194
  191.7 2.7 %collective-permute-start.11 = (f32[512]{0:T(512)S(1)}, f32[512]{0:T(512)S(1)}, u32[]{:S(2)}, u32[]{:S(2)}) collective-permute-start(f32[512]{0:T(512)S(1)} %get-tuple-element.27), channel_id=1, source_target_pairs={{0,1},{1,0},{2,3},{3,2},{4,5},{5,4},{6,7},{7,6},{8,9},{9,8},{10,11... | collective-permute-start | bytes 6152 | tf_op jit(solution)/shard_map/ppermute | solution.py:28
  194.4 0.7 constant_dynamic-slice_fusion
  195.1 2.1 %collective-permute-done.11 = f32[512]{0:T(512)S(1)} collective-permute-done((f32[512]{0:T(512)S(1)}, f32[512]{0:T(512)S(1)}, u32[]{:S(2)}, u32[]{:S(2)}) %collective-permute-start.11) | collective-permute-done | bytes 2080 | tf_op jit(solution)/shard_map/ppermute | solution.py:28
  197.2 0.6 add_sqrt_fusion
  (10 shorter events, 0.1 us)
Async XLA Ops:
  3.2 61.5 %all-to-all-start = ((bf16[8,256,512]{2,1,0:T(8,128)(2,1)}), bf16[8,256,512]{2,1,0:T(8,128)(2,1)S(1)}, u32[]{:S(2)}, u32[]{:S(2)}) async-start(bf16[8,256,512]{2,1,0:T(8,128)(2,1)} %broadcast_in_dim.46), calls=%async_computation | async-start | bytes 4194304 | tf_op jit(solution)/shard_map/all_to_all | solution.py:145
  64.8 50.8 %collective-permute-start.3 = (bf16[2048,512]{1,0:T(8,128)(2,1)S(1)}, bf16[2048,512]{1,0:T(8,128)(2,1)}, u32[]{:S(2)}, u32[]{:S(2)}) collective-permute-start(bf16[2048,512]{1,0:T(8,128)(2,1)S(1)} %bitcast.42), channel_id=1, source_target_pairs={{16,0},{32,16},{48,32},{64,48},{80,64},{96,80},{112,96},{128,112},... | collective-permute-start | bytes 6291464 | tf_op jit(solution)/shard_map/ppermute | solution.py:24
  74.9 38.4 %collective-permute-start.1 = (bf16[2048,512]{1,0:T(8,128)(2,1)S(1)}, bf16[2048,512]{1,0:T(8,128)(2,1)}, u32[]{:S(2)}, u32[]{:S(2)}) collective-permute-start(bf16[2048,512]{1,0:T(8,128)(2,1)S(1)} %bitcast.43), channel_id=1, source_target_pairs={{0,16},{16,32},{32,48},{48,64},{64,80},{80,96},{96,112},{112,128},... | collective-permute-start | bytes 6291464 | tf_op jit(solution)/shard_map/ppermute | solution.py:24
  78.3 11.3 %collective-permute-start = (f32[520,256]{1,0:T(8,128)S(1)}, f32[520,256]{1,0:T(8,128)}, u32[]{:S(2)}, u32[]{:S(2)}) collective-permute-start(f32[520,256]{1,0:T(8,128)S(1)} %maximum_maximum_fusion), channel_id=1, source_target_pairs={{0,1},{1,0},{2,3},{3,2},{4,5},{5,4},{6,7},{7,6},{8,9},{9,8},{10,11... | collective-permute-start | bytes 1597448 | tf_op jit(solution)/shard_map/ppermute | solution.py:28
  99.6 13.6 %collective-permute-start.2 = (bf16[512,256]{1,0:T(8,128)(2,1)S(1)}, bf16[512,256]{1,0:T(8,128)(2,1)S(1)}, u32[]{:S(2)}, u32[]{:S(2)}) collective-permute-start(bf16[512,256]{1,0:T(8,128)(2,1)S(1)} %get-tuple-element.25), channel_id=1, source_target_pairs={{0,16},{16,32},{32,48},{48,64},{64,80},{80,96},{96,112},{112,128},... | collective-permute-start | bytes 786440 | tf_op jit(solution)/shard_map/ppermute | solution.py:24
  101.6 14.0 %collective-permute-start.4 = (bf16[512,256]{1,0:T(8,128)(2,1)S(1)}, bf16[512,256]{1,0:T(8,128)(2,1)S(1)}, u32[]{:S(2)}, u32[]{:S(2)}) collective-permute-start(bf16[512,256]{1,0:T(8,128)(2,1)S(1)} %get-tuple-element.26), channel_id=1, source_target_pairs={{16,0},{32,16},{48,32},{64,48},{80,64},{96,80},{112,96},{128,112},... | collective-permute-start | bytes 786440 | tf_op jit(solution)/shard_map/ppermute | solution.py:24
  119.4 40.6 %collective-permute-start.8 = (bf16[2048,512]{0,1:T(8,128)(2,1)}, bf16[2048,512]{0,1:T(8,128)(2,1)}, u32[]{:S(2)}, u32[]{:S(2)}) collective-permute-start(bf16[2048,512]{0,1:T(8,128)(2,1)} %pad_maximum_fusion), channel_id=1, source_target_pairs={{16,0},{32,16},{48,32},{64,48},{80,64},{96,80},{112,96},{128,112},... | collective-permute-start | bytes 6291464 | tf_op jit(solution)/shard_map/ppermute | solution.py:24
  126.0 40.0 %collective-permute-start.6 = (bf16[2048,512]{0,1:T(8,128)(2,1)}, bf16[2048,512]{0,1:T(8,128)(2,1)}, u32[]{:S(2)}, u32[]{:S(2)}) collective-permute-start(bf16[2048,512]{0,1:T(8,128)(2,1)} %pad_maximum_fusion), channel_id=1, source_target_pairs={{0,16},{16,32},{32,48},{48,64},{64,80},{80,96},{96,112},{112,128},... | collective-permute-start | bytes 6291464 | tf_op jit(solution)/shard_map/ppermute | solution.py:24
  128.1 13.0 %collective-permute-start.5 = (f32[520,256]{1,0:T(8,128)S(1)}, f32[520,256]{1,0:T(8,128)S(1)}, u32[]{:S(2)}, u32[]{:S(2)}) collective-permute-start(f32[520,256]{1,0:T(8,128)S(1)} %maximum_maximum_fusion.1), channel_id=1, source_target_pairs={{0,1},{1,0},{2,3},{3,2},{4,5},{5,4},{6,7},{7,6},{8,9},{9,8},{10,11... | collective-permute-start | bytes 1597448 | tf_op jit(solution)/shard_map/ppermute | solution.py:28
  150.2 9.9 %collective-permute-start.9 = (bf16[512,256]{1,0:T(8,128)(2,1)S(1)}, bf16[512,256]{1,0:T(8,128)(2,1)S(1)}, u32[]{:S(2)}, u32[]{:S(2)}) collective-permute-start(bf16[512,256]{1,0:T(8,128)(2,1)S(1)} %get-tuple-element.24), channel_id=1, source_target_pairs={{16,0},{32,16},{48,32},{64,48},{80,64},{96,80},{112,96},{128,112},... | collective-permute-start | bytes 786440 | tf_op jit(solution)/shard_map/ppermute | solution.py:24
  156.2 9.8 %collective-permute-start.7 = (bf16[512,256]{1,0:T(8,128)(2,1)S(1)}, bf16[512,256]{1,0:T(8,128)(2,1)S(1)}, u32[]{:S(2)}, u32[]{:S(2)}) collective-permute-start(bf16[512,256]{1,0:T(8,128)(2,1)S(1)} %get-tuple-element.23), channel_id=1, source_target_pairs={{0,16},{16,32},{32,48},{48,64},{64,80},{80,96},{96,112},{112,128},... | collective-permute-start | bytes 786440 | tf_op jit(solution)/shard_map/ppermute | solution.py:24
  168.4 1.3 copy-start
  169.9 11.2 %collective-permute-start.10 = (f32[520,256]{1,0:T(8,128)S(1)}, f32[520,256]{1,0:T(8,128)S(1)}, u32[]{:S(2)}, u32[]{:S(2)}) collective-permute-start(f32[520,256]{1,0:T(8,128)S(1)} %maximum_maximum_fusion.2), channel_id=1, source_target_pairs={{0,1},{1,0},{2,3},{3,2},{4,5},{5,4},{6,7},{7,6},{8,9},{9,8},{10,11... | collective-permute-start | bytes 1597448 | tf_op jit(solution)/shard_map/ppermute | solution.py:28
  191.7 5.5 %collective-permute-start.11 = (f32[512]{0:T(512)S(1)}, f32[512]{0:T(512)S(1)}, u32[]{:S(2)}, u32[]{:S(2)}) collective-permute-start(f32[512]{0:T(512)S(1)} %get-tuple-element.27), channel_id=1, source_target_pairs={{0,1},{1,0},{2,3},{3,2},{4,5},{5,4},{6,7},{7,6},{8,9},{9,8},{10,11... | collective-permute-start | bytes 6152 | tf_op jit(solution)/shard_map/ppermute | solution.py:28

commit v5 on v3

--- a/solution.py
+++ b/solution.py
@@ -53,23 +53,28 @@
     return cosine, sine_value
 
 
-def sweeps_kernel(top_left_ref, top_right_ref, low_left_ref, low_right_ref, rotation_ref):
-    width = top_left_ref.shape[0]
-    top_left = top_left_ref[...]
-    top_right = top_right_ref[...]
-    low_left = low_left_ref[...]
-    low_right = low_right_ref[...]
+def sweeps_kernel(packed_ref, rotation_ref):
+    width = packed_ref.shape[1]
     rows = lax.broadcasted_iota(jnp.int32, (width, width), 0)
     cols = lax.broadcasted_iota(jnp.int32, (width, width), 1)
     on_diagonal = rows == cols
+    folded = packed_ref[:width, :]
+    top_right = packed_ref[width : 2 * width, :]
+    low_diag = packed_ref[2 * width : 2 * width + 8, :][:1, :]
+    mirrored = folded.T
+    top_left = jnp.where(rows <= cols, folded, mirrored)
+    low_right = jnp.where(rows > cols, folded, jnp.where(rows < cols, mirrored, low_diag))
+    low_left = top_right.T
     first_top = jnp.where(on_diagonal, 1.0, 0.0).astype(jnp.float32)
     first_low = jnp.zeros((width, width), jnp.float32)
     second_top = jnp.zeros((width, width), jnp.float32)
     second_low = first_top
 
-    def both_diagonals(matrix):
-        masked = jnp.where(on_diagonal, matrix, 0.0)
-        return jnp.sum(masked, axis=0, keepdims=True), jnp.sum(masked, axis=1, keepdims=True)
+    def diagonal_row(matrix):
+        return jnp.sum(jnp.where(on_diagonal, matrix, 0.0), axis=0, keepdims=True)
+
+    def as_column(row):
+        return jnp.broadcast_to(row, (128, width)).T[:, :1]
 
     def to_left(matrix, axis):
         return pltpu.roll(matrix, width - 1, axis)
@@ -81,11 +86,11 @@
             low_right = to_left(to_left(low_right, 0), 1)
             second_top = to_left(second_top, 1)
             second_low = to_left(second_low, 1)
-        first_r, first_c = both_diagonals(top_left)
-        second_r, second_c = both_diagonals(low_right)
-        coupling_r, coupling_c = both_diagonals(top_right)
-        cos_col, sin_col = half_angle_terms(first_r, second_r, coupling_r)
-        cos_row, sin_row = half_angle_terms(first_c, second_c, coupling_c)
+        cos_col, sin_col = half_angle_terms(
+            diagonal_row(top_left), diagonal_row(low_right), diagonal_row(top_right)
+        )
+        cos_row = as_column(cos_col)
+        sin_row = as_column(sin_col)
         left_a = top_left * cos_col - top_right * sin_col
         right_a = top_left * sin_col + top_right * cos_col
         left_b = low_left * cos_col - low_right * sin_col
@@ -111,18 +116,18 @@
     rotation_ref[width:, width:] = second_low.astype(out)
 
 
-def rotation_of(top_left, top_right, low_left, low_right):
-    width = top_left.shape[0]
+def rotation_of(packed):
+    width = packed.shape[1]
     vmem = pl.BlockSpec(memory_space=pltpu.VMEM)
     return pl.pallas_call(
         sweeps_kernel,
         out_shape=jax.ShapeDtypeStruct((2 * width, 2 * width), jnp.bfloat16),
-        in_specs=[vmem] * 4,
+        in_specs=[vmem],
         out_specs=vmem,
         cost_estimate=pl.CostEstimate(
-            flops=SWEEPS * 40 * width * width, transcendentals=SWEEPS * 8 * width, bytes_accessed=5 * 4 * width * width
+            flops=SWEEPS * 40 * width * width, transcendentals=SWEEPS * 8 * width, bytes_accessed=4 * 4 * width * width
         ),
-    )(top_left, top_right, low_left, low_right)
+    )(packed)
 
 
 def send_right(block):
@@ -164,14 +169,7 @@
         ],
         axis=0,
     )
-    summed = with_partner(packed)
-    folded = summed[:width]
-    top_right = summed[width : 2 * width]
-    low_diag = summed[2 * width]
-    mirrored = folded.T
-    top_left = jnp.where(rows <= cols, folded, mirrored)
-    low_right = jnp.where(rows > cols, folded, jnp.where(rows < cols, mirrored, low_diag[None, :]))
-    return top_left, top_right, top_right.T, low_right
+    return with_partner(packed)
 
 
 def local(design, record_weight):
@@ -186,7 +184,7 @@
     for round_index in range(ROUNDS):
         moving = round_index + 1 < ROUNDS
         pair_data = jnp.concatenate([upper_block, lower_block], axis=1)
-        rotation = rotation_of(*summed_gram(pair_data, width))
+        rotation = rotation_of(summed_gram(pair_data, width))
         rotated = jnp.dot(pair_data, rotation, preferred_element_type=jnp.float32).astype(
             jnp.bfloat16
         )

time: 197 us -> 193 us (0.980)
  the two profiles are of different devices: /device:TPU:2 before, /device:TPU:256 now
where the time goes in v5:
time: 193 us; the launch traced here: 192 us
  waiting for transfers between devices  119 us (62%)
  starting transfers between devices  32.7 us (17%)
  Pallas kernels  16.9 us (9%)
  matrix products  11.5 us (6%)
  other arithmetic  9.26 us (5%)
  local copies, waits for them, and re-layouts  2.4 us (1%)
    all_to_all x1, waiting for transfers between devices, gathered_records(): gathered = lax.all_to_all(spread, GROUP_AXES, 0, 0, tiled=False)  52.8 us
    ppermute x4, waiting for transfers between devices, with_partner(): return value + lax.ppermute(value, PAIR_AXIS, [(0, 1), (1, 0)])  41.2 us
    ppermute x4, waiting for transfers between devices, from_behind(): lax.ppermute(value, COLUMN_AXES, [(source, source + steps) for source in...  24.6 us
    pallas_call x3, Pallas kernels, rotation_of(): pl.pallas_call(sweeps_kernel, out_shape=jax.ShapeDtypeStruct((2 * width,...  16.9 us
    ppermute x4, starting transfers between devices, from_behind(): lax.ppermute(value, COLUMN_AXES, [(source, source + steps) for source in...  13.5 us
    ppermute x4, starting transfers between devices, with_partner(): return value + lax.ppermute(value, PAIR_AXIS, [(0, 1), (1, 0)])  9.6 us
    all_to_all x1, starting transfers between devices, gathered_records(): gathered = lax.all_to_all(spread, GROUP_AXES, 0, 0, tiled=False)  9.56 us
    dot_general x3, matrix products, local(): jnp.dot(pair_data, rotation, preferred_element_type=jnp.float32)  7.65 us
  transfers between devices with their start and end apart: 9, of which 9 were waited for; matrix products, arithmetic and copies ran while one was open for 0% of the time, Pallas kernels for 0%

profile of v5, /device:TPU:256, one launch (start us, length us, event | category | flops | bytes accessed | tf_op | source)
XLA Modules:
  0.0 192.1 jit_solution(6701732015284724785)
XLA Ops:
  0.6 1.1 multiply_convert_fusion
  1.7 1.5 broadcast_in_dim.22
  3.2 9.6 %all-to-all-start = ((bf16[8,256,512]{2,1,0:T(8,128)(2,1)}), bf16[8,256,512]{2,1,0:T(8,128)(2,1)S(1)}, u32[]{:S(2)}, u32[]{:S(2)}) async-start(bf16[8,256,512]{2,1,0:T(8,128)(2,1)} %broadcast_in_dim.22), calls=%async_computation | async-start | bytes 4194304 | tf_op jit(solution)/shard_map/all_to_all | solution.py:150
  12.8 0.1 pad.15.clone
  12.9 52.8 %all-to-all-done = bf16[8,256,512]{2,1,0:T(8,128)(2,1)S(1)} async-done(((bf16[8,256,512]{2,1,0:T(8,128)(2,1)}), bf16[8,256,512]{2,1,0:T(8,128)(2,1)S(1)}, u32[]{:S(2)}, u32[]{:S(2)}) %all-to-all-start) | async-done | bytes 2097184 | tf_op jit(solution)/shard_map/all_to_all | solution.py:150
  65.7 0.0 copy-start
  65.7 1.3 convolution_bitcast_fusion
  66.9 0.1 copy-done
  67.0 0.1 slice_select_fusion.2
  67.1 0.1 maximum_maximum_fusion
  67.2 2.7 %collective-permute-start = (f32[520,256]{1,0:T(8,128)S(1)}, f32[520,256]{1,0:T(8,128)S(1)}, u32[]{:S(2)}, u32[]{:S(2)}) collective-permute-start(f32[520,256]{1,0:T(8,128)S(1)} %maximum_maximum_fusion), channel_id=1, source_target_pairs={{0,1},{1,0},{2,3},{3,2},{4,5},{5,4},{6,7},{7,6},{8,9},{9,8},{10,11... | collective-permute-start | bytes 1597448 | tf_op jit(solution)/shard_map/ppermute | solution.py:28
  69.9 11.9 %collective-permute-done = f32[520,256]{1,0:T(8,128)S(1)} collective-permute-done((f32[520,256]{1,0:T(8,128)S(1)}, f32[520,256]{1,0:T(8,128)S(1)}, u32[]{:S(2)}, u32[]{:S(2)}) %collective-permute-start) | collective-permute-done | bytes 532512 | tf_op jit(solution)/shard_map/ppermute | solution.py:28
  81.8 0.9 fusion.8.packed_ref
  82.7 5.6 %shard_map.41 = bf16[512,512]{1,0:T(8,128)(2,1)} custom-call(f32[520,256]{1,0:T(8,128)} %fusion.8.packed_ref), custom_call_target="tpu_custom_call" | custom-call | flops 15728640 | bytes 1048576 | tf_op jit(solution)/shard_map/pallas_call | solution.py:122
  88.4 3.0 %convolution_convert_fusion.2 = bf16[2048,512]{0,1:T(8,128)(2,1)S(1)} fusion(bf16[2048,512]{1,0:T(8,128)(2,1)} %bitcast.12, bf16[512,512]{1,0:T(8,128)(2,1)} %shard_map.41), kind=kOutput, calls=%fused_computation.3 | convolution fusion | flops 1074790400 | bytes 4718592 | tf_op jit(solution)/shard_map/dot_general | solution.py:188
  91.3 1.1 broadcast_select_fusion.5
  92.4 1.9 collective-permute-start.1
  94.4 4.9 %collective-permute-start.2 = (bf16[2048,256]{0,1:T(8,128)(2,1)S(1)}, bf16[2048,256]{0,1:T(8,128)(2,1)}, u32[]{:S(2)}, u32[]{:S(2)}) collective-permute-start(bf16[2048,256]{0,1:T(8,128)(2,1)S(1)} %get-tuple-element.9), channel_id=1, source_target_pairs={{16,0},{32,16},{48,32},{64,48},{80,64},{96,80},{112,96},{128,112},... | collective-permute-start | bytes 3145736 | tf_op jit(solution)/shard_map/ppermute | solution.py:24
  99.2 10.8 %collective-permute-done.1 = bf16[2048,256]{0,1:T(8,128)(2,1)} collective-permute-done((bf16[2048,256]{0,1:T(8,128)(2,1)}, bf16[2048,256]{0,1:T(8,128)(2,1)}, u32[]{:S(2)}, u32[]{:S(2)}) %collective-permute-start.1) | collective-permute-done | bytes 1048608 | tf_op jit(solution)/shard_map/ppermute | solution.py:24
  110.1 1.4 collective-permute-done.2
  111.5 1.7 broadcast_select_fusion.4
  113.2 0.0 copy-start.1
  113.2 1.3 fusion.1
  114.5 0.0 copy-done.1
  114.5 0.1 slice_select_fusion.1
  114.6 0.0 copy-start.2
  114.6 0.1 maximum_maximum_fusion.1
  114.7 2.5 %collective-permute-start.3 = (f32[520,256]{1,0:T(8,128)S(1)}, f32[520,256]{1,0:T(8,128)S(1)}, u32[]{:S(2)}, u32[]{:S(2)}) collective-permute-start(f32[520,256]{1,0:T(8,128)S(1)} %maximum_maximum_fusion.1), channel_id=1, source_target_pairs={{0,1},{1,0},{2,3},{3,2},{4,5},{5,4},{6,7},{7,6},{8,9},{9,8},{10,11... | collective-permute-start | bytes 1597448 | tf_op jit(solution)/shard_map/ppermute | solution.py:28
  117.3 14.2 %collective-permute-done.3 = f32[520,256]{1,0:T(8,128)S(1)} collective-permute-done((f32[520,256]{1,0:T(8,128)S(1)}, f32[520,256]{1,0:T(8,128)S(1)}, u32[]{:S(2)}, u32[]{:S(2)}) %collective-permute-start.3) | collective-permute-done | bytes 532512 | tf_op jit(solution)/shard_map/ppermute | solution.py:28
  131.4 0.9 fusion.7.packed_ref
  132.4 5.6 %shard_map.42 = bf16[512,512]{1,0:T(8,128)(2,1)} custom-call(f32[520,256]{1,0:T(8,128)} %fusion.7.packed_ref), custom_call_target="tpu_custom_call" | custom-call | flops 15728640 | bytes 1048576 | tf_op jit(solution)/shard_map/pallas_call | solution.py:122
  138.0 0.0 copy-done.2
  138.0 2.3 %convolution_convert_fusion.1 = bf16[2048,512]{0,1:T(8,128)(2,1)S(1)} fusion(bf16[512,512]{1,0:T(8,128)(2,1)} %shard_map.42, bf16[2048,256]{0,1:T(8,128)(2,1)S(1)} %copy-done.2, bf16[2048,256]{0,1:T(8,128)(2,1)S(1)} %get-tuple-element.6), kind=kOutput, calls=%fused_computation.2 | convolution fusion | flops 1078984704 | bytes 4718592 | tf_op jit(solution)/shard_map/dot_general | solution.py:188
  140.3 0.1 broadcast_select_fusion.3
  140.5 1.9 collective-permute-start.4
  142.4 4.9 %collective-permute-start.5 = (bf16[2048,256]{0,1:T(8,128)(2,1)S(1)}, bf16[2048,256]{0,1:T(8,128)(2,1)S(1)}, u32[]{:S(2)}, u32[]{:S(2)}) collective-permute-start(bf16[2048,256]{0,1:T(8,128)(2,1)S(1)} %get-tuple-element.5), channel_id=1, source_target_pairs={{16,0},{32,16},{48,32},{64,48},{80,64},{96,80},{112,96},{128,112},... | collective-permute-start | bytes 3145736 | tf_op jit(solution)/shard_map/ppermute | solution.py:24
  147.3 10.5 %collective-permute-done.4 = bf16[2048,256]{0,1:T(8,128)(2,1)S(1)} collective-permute-done((bf16[2048,256]{0,1:T(8,128)(2,1)S(1)}, bf16[2048,256]{0,1:T(8,128)(2,1)S(1)}, u32[]{:S(2)}, u32[]{:S(2)}) %collective-permute-start.4) | collective-permute-done | bytes 1048608 | tf_op jit(solution)/shard_map/ppermute | solution.py:24
  157.8 1.8 collective-permute-done.5
  159.6 0.2 broadcast_select_fusion.2
  159.8 1.3 fusion
  161.1 0.1 slice_select_fusion
  161.1 0.1 maximum_maximum_fusion.2
  161.3 2.2 %collective-permute-start.6 = (f32[520,256]{1,0:T(8,128)S(1)}, f32[520,256]{1,0:T(8,128)}, u32[]{:S(2)}, u32[]{:S(2)}) collective-permute-start(f32[520,256]{1,0:T(8,128)S(1)} %maximum_maximum_fusion.2), channel_id=1, source_target_pairs={{0,1},{1,0},{2,3},{3,2},{4,5},{5,4},{6,7},{7,6},{8,9},{9,8},{10,11... | collective-permute-start | bytes 1597448 | tf_op jit(solution)/shard_map/ppermute | solution.py:28
  163.5 12.6 %collective-permute-done.6 = f32[520,256]{1,0:T(8,128)} collective-permute-done((f32[520,256]{1,0:T(8,128)S(1)}, f32[520,256]{1,0:T(8,128)}, u32[]{:S(2)}, u32[]{:S(2)}) %collective-permute-start.6) | collective-permute-done | bytes 532512 | tf_op jit(solution)/shard_map/ppermute | solution.py:28
  176.1 2.0 %fusion.6.packed_ref = f32[520,256]{1,0:T(8,128)} fusion(f32[520,256]{1,0:T(8,128)} %collective-permute-done.6, f32[520]{0:T(1024)S(1)} %pad.15.clone, f32[1,256]{1,0:T(1,128)S(1)} %bitcast.16, f32[256,256]{1,0:T(8,128)S(1)} %get-tuple-element.11, f32[256,256]{1,0:T(8,128)S(1)} %get-tuple-element.10), kind=kLoop, calls=%fused_computation.33 | loop fusion | flops 532480 | bytes 1592352 | tf_op jit(solution)/shard_map/add | solution.py:28
  178.0 5.6 %shard_map.43 = bf16[512,512]{1,0:T(8,128)(2,1)} custom-call(f32[520,256]{1,0:T(8,128)} %fusion.6.packed_ref), custom_call_target="tpu_custom_call" | custom-call | flops 15728640 | bytes 1048576 | tf_op jit(solution)/shard_map/pallas_call | solution.py:122
  183.6 2.3 %multiply_reduce_fusion = (f32[512]{0:T(512)S(1)}, bf16[2048,512]{1,0:T(8,128)(2,1)S(1)}) fusion(bf16[512,512]{1,0:T(8,128)(2,1)} %shard_map.43, bf16[2048,256]{0,1:T(8,128)(2,1)S(1)} %get-tuple-element.3, bf16[2048,256]{0,1:T(8,128)(2,1)S(1)} %get-tuple-element.2), kind=kOutput, calls=%fused_computation | convolution fusion | flops 1082129920 | bytes 4720640 | tf_op jit(solution)/shard_map/dot_general | solution.py:188
  186.0 2.2 %collective-permute-start.7 = (f32[512]{0:T(512)S(1)}, f32[512]{0:T(512)S(1)}, u32[]{:S(2)}, u32[]{:S(2)}) collective-permute-start(f32[512]{0:T(512)S(1)} %get-tuple-element.19), channel_id=1, source_target_pairs={{0,1},{1,0},{2,3},{3,2},{4,5},{5,4},{6,7},{7,6},{8,9},{9,8},{10,11... | collective-permute-start | bytes 6152 | tf_op jit(solution)/shard_map/ppermute | solution.py:28
  188.2 0.7 constant_dynamic-slice_fusion
  188.9 2.5 %collective-permute-done.7 = f32[512]{0:T(512)S(1)} collective-permute-done((f32[512]{0:T(512)S(1)}, f32[512]{0:T(512)S(1)}, u32[]{:S(2)}, u32[]{:S(2)}) %collective-permute-start.7) | collective-permute-done | bytes 2080 | tf_op jit(solution)/shard_map/ppermute | solution.py:28
  191.5 0.6 add_sqrt_fusion
  (1 shorter events, 0.0 us)
Async XLA Ops:
  3.2 62.4 %all-to-all-start = ((bf16[8,256,512]{2,1,0:T(8,128)(2,1)}), bf16[8,256,512]{2,1,0:T(8,128)(2,1)S(1)}, u32[]{:S(2)}, u32[]{:S(2)}) async-start(bf16[8,256,512]{2,1,0:T(8,128)(2,1)} %broadcast_in_dim.22), calls=%async_computation | async-start | bytes 4194304 | tf_op jit(solution)/shard_map/all_to_all | solution.py:150
  65.7 1.3 copy-start
  67.2 14.6 %collective-permute-start = (f32[520,256]{1,0:T(8,128)S(1)}, f32[520,256]{1,0:T(8,128)S(1)}, u32[]{:S(2)}, u32[]{:S(2)}) collective-permute-start(f32[520,256]{1,0:T(8,128)S(1)} %maximum_maximum_fusion), channel_id=1, source_target_pairs={{0,1},{1,0},{2,3},{3,2},{4,5},{5,4},{6,7},{7,6},{8,9},{9,8},{10,11... | collective-permute-start | bytes 1597448 | tf_op jit(solution)/shard_map/ppermute | solution.py:28
  92.4 17.6 %collective-permute-start.1 = (bf16[2048,256]{0,1:T(8,128)(2,1)}, bf16[2048,256]{0,1:T(8,128)(2,1)}, u32[]{:S(2)}, u32[]{:S(2)}) collective-permute-start(bf16[2048,256]{0,1:T(8,128)(2,1)} %get-tuple-element.8), channel_id=1, source_target_pairs={{0,16},{16,32},{32,48},{48,64},{64,80},{80,96},{96,112},{112,128},... | collective-permute-start | bytes 3145736 | tf_op jit(solution)/shard_map/ppermute | solution.py:24
  94.4 17.2 %collective-permute-start.2 = (bf16[2048,256]{0,1:T(8,128)(2,1)S(1)}, bf16[2048,256]{0,1:T(8,128)(2,1)}, u32[]{:S(2)}, u32[]{:S(2)}) collective-permute-start(bf16[2048,256]{0,1:T(8,128)(2,1)S(1)} %get-tuple-element.9), channel_id=1, source_target_pairs={{16,0},{32,16},{48,32},{64,48},{80,64},{96,80},{112,96},{128,112},... | collective-permute-start | bytes 3145736 | tf_op jit(solution)/shard_map/ppermute | solution.py:24
  113.2 1.3 copy-start.1
  114.6 23.4 %copy-start.2 = (bf16[2048,256]{0,1:T(8,128)(2,1)S(1)}, bf16[2048,256]{0,1:T(8,128)(2,1)}, u32[]{:S(2)}) copy-start(bf16[2048,256]{0,1:T(8,128)(2,1)} %copy-done.1) | copy-start | bytes 3145732
  114.7 16.7 %collective-permute-start.3 = (f32[520,256]{1,0:T(8,128)S(1)}, f32[520,256]{1,0:T(8,128)S(1)}, u32[]{:S(2)}, u32[]{:S(2)}) collective-permute-start(f32[520,256]{1,0:T(8,128)S(1)} %maximum_maximum_fusion.1), channel_id=1, source_target_pairs={{0,1},{1,0},{2,3},{3,2},{4,5},{5,4},{6,7},{7,6},{8,9},{9,8},{10,11... | collective-permute-start | bytes 1597448 | tf_op jit(solution)/shard_map/ppermute | solution.py:28
  140.5 17.3 %collective-permute-start.4 = (bf16[2048,256]{0,1:T(8,128)(2,1)S(1)}, bf16[2048,256]{0,1:T(8,128)(2,1)S(1)}, u32[]{:S(2)}, u32[]{:S(2)}) collective-permute-start(bf16[2048,256]{0,1:T(8,128)(2,1)S(1)} %get-tuple-element.4), channel_id=1, source_target_pairs={{0,16},{16,32},{32,48},{48,64},{64,80},{80,96},{96,112},{112,128},... | collective-permute-start | bytes 3145736 | tf_op jit(solution)/shard_map/ppermute | solution.py:24
  142.4 17.2 %collective-permute-start.5 = (bf16[2048,256]{0,1:T(8,128)(2,1)S(1)}, bf16[2048,256]{0,1:T(8,128)(2,1)S(1)}, u32[]{:S(2)}, u32[]{:S(2)}) collective-permute-start(bf16[2048,256]{0,1:T(8,128)(2,1)S(1)} %get-tuple-element.5), channel_id=1, source_target_pairs={{16,0},{32,16},{48,32},{64,48},{80,64},{96,80},{112,96},{128,112},... | collective-permute-start | bytes 3145736 | tf_op jit(solution)/shard_map/ppermute | solution.py:24
  161.3 14.8 %collective-permute-start.6 = (f32[520,256]{1,0:T(8,128)S(1)}, f32[520,256]{1,0:T(8,128)}, u32[]{:S(2)}, u32[]{:S(2)}) collective-permute-start(f32[520,256]{1,0:T(8,128)S(1)} %maximum_maximum_fusion.2), channel_id=1, source_target_pairs={{0,1},{1,0},{2,3},{3,2},{4,5},{5,4},{6,7},{7,6},{8,9},{9,8},{10,11... | collective-permute-start | bytes 1597448 | tf_op jit(solution)/shard_map/ppermute | solution.py:28
  186.0 5.5 %collective-permute-start.7 = (f32[512]{0:T(512)S(1)}, f32[512]{0:T(512)S(1)}, u32[]{:S(2)}, u32[]{:S(2)}) collective-permute-start(f32[512]{0:T(512)S(1)} %get-tuple-element.19), channel_id=1, source_target_pairs={{0,1},{1,0},{2,3},{3,2},{4,5},{5,4},{6,7},{7,6},{8,9},{9,8},{10,11... | collective-permute-start | bytes 6152 | tf_op jit(solution)/shard_map/ppermute | solution.py:28

commit v6 on v5

--- a/solution.py
+++ b/solution.py
@@ -24,8 +24,20 @@
     return lax.ppermute(value, COLUMN_AXES, [(source, source + steps) for source in range(leading, last)])
 
 
+PARTNER_AXES = ("core", "y_hi", PAIR_AXIS)
+
+
+def partner_pairs(halves):
+    pairs = []
+    for half in range(halves):
+        for core, other in ((0, half), (1, (half - 1) % halves)):
+            even, odd = (core * halves + half) * 2, (core * halves + other) * 2 + 1
+            pairs += [(even, odd), (odd, even)]
+    return pairs
+
+
 def with_partner(value):
-    return value + lax.ppermute(value, PAIR_AXIS, [(0, 1), (1, 0)])
+    return value + lax.ppermute(value, PARTNER_AXES, partner_pairs(lax.axis_size("y_hi")))
 
 
 def diagonal_of(matrix):

time: 193 us -> 186 us (0.964)
  the two profiles are of different devices: /device:TPU:256 before, /device:TPU:2 now
where the time goes in v6:
time: 186 us; the launch traced here: 185 us
  waiting for transfers between devices  107 us (58%)
  starting transfers between devices  37.5 us (20%)
  Pallas kernels  16.9 us (9%)
  matrix products  11.5 us (6%)
  other arithmetic  9.26 us (5%)
  local copies, waits for them, and re-layouts  2.39 us (1%)
    all_to_all x1, waiting for transfers between devices, gathered_records(): gathered = lax.all_to_all(spread, GROUP_AXES, 0, 0, tiled=False)  52.8 us
    ppermute x4, waiting for transfers between devices, with_partner(): lax.ppermute(value, PARTNER_AXES, partner_pairs(lax.axis_size('y_hi')))  29.7 us
    ppermute x4, waiting for transfers between devices, from_behind(): lax.ppermute(value, COLUMN_AXES, [(source, source + steps) for source in...  24.6 us
    ppermute x4, starting transfers between devices, from_behind(): lax.ppermute(value, COLUMN_AXES, [(source, source + steps) for source in...  20.1 us
    pallas_call x3, Pallas kernels, rotation_of(): pl.pallas_call(sweeps_kernel, out_shape=jax.ShapeDtypeStruct((2 * width,...  16.9 us
    ppermute x4, starting transfers between devices, with_partner(): lax.ppermute(value, PARTNER_AXES, partner_pairs(lax.axis_size('y_hi')))  8.76 us
    all_to_all x1, starting transfers between devices, gathered_records(): gathered = lax.all_to_all(spread, GROUP_AXES, 0, 0, tiled=False)  8.66 us
    dot_general x3, matrix products, local(): jnp.dot(pair_data, rotation, preferred_element_type=jnp.float32)  7.65 us
  transfers between devices with their start and end apart: 9, of which 9 were waited for; matrix products, arithmetic and copies ran while one was open for 0% of the time, Pallas kernels for 0%

profile of v6, /device:TPU:2, one launch (start us, length us, event | category | flops | bytes accessed | tf_op | source)
XLA Modules:
  0.0 185.4 jit_solution(12138976208026809103)
XLA Ops:
  0.6 1.1 multiply_convert_fusion
  1.7 1.5 broadcast_in_dim.22
  3.2 8.7 %all-to-all-start = ((bf16[8,256,512]{2,1,0:T(8,128)(2,1)}), bf16[8,256,512]{2,1,0:T(8,128)(2,1)S(1)}, u32[]{:S(2)}, u32[]{:S(2)}) async-start(bf16[8,256,512]{2,1,0:T(8,128)(2,1)} %broadcast_in_dim.22), calls=%async_computation | async-start | bytes 4194304 | tf_op jit(solution)/shard_map/all_to_all | solution.py:162
  11.9 0.1 pad.15.clone
  12.0 52.8 %all-to-all-done = bf16[8,256,512]{2,1,0:T(8,128)(2,1)S(1)} async-done(((bf16[8,256,512]{2,1,0:T(8,128)(2,1)}), bf16[8,256,512]{2,1,0:T(8,128)(2,1)S(1)}, u32[]{:S(2)}, u32[]{:S(2)}) %all-to-all-start) | async-done | bytes 2097184 | tf_op jit(solution)/shard_map/all_to_all | solution.py:162
  64.8 0.0 copy-start
  64.8 1.3 convolution_bitcast_fusion
  66.0 0.1 copy-done
  66.1 0.1 slice_select_fusion.2
  66.2 0.1 maximum_maximum_fusion
  66.3 2.7 %collective-permute-start = (f32[520,256]{1,0:T(8,128)S(1)}, f32[520,256]{1,0:T(8,128)S(1)}, u32[]{:S(2)}, u32[]{:S(2)}) collective-permute-start(f32[520,256]{1,0:T(8,128)S(1)} %maximum_maximum_fusion), channel_id=1, source_target_pairs={{0,1},{1,0},{16,23},{23,16},{2,3},{3,2},{18,17},{17,18},{4,5},{5,4... | collective-permute-start | bytes 1597448 | tf_op jit(solution)/shard_map/ppermute | solution.py:40
  69.0 8.5 %collective-permute-done = f32[520,256]{1,0:T(8,128)S(1)} collective-permute-done((f32[520,256]{1,0:T(8,128)S(1)}, f32[520,256]{1,0:T(8,128)S(1)}, u32[]{:S(2)}, u32[]{:S(2)}) %collective-permute-start) | collective-permute-done | bytes 532512 | tf_op jit(solution)/shard_map/ppermute | solution.py:40
  77.5 0.9 fusion.8.packed_ref
  78.4 5.6 %shard_map.41 = bf16[512,512]{1,0:T(8,128)(2,1)} custom-call(f32[520,256]{1,0:T(8,128)} %fusion.8.packed_ref), custom_call_target="tpu_custom_call" | custom-call | flops 15728640 | bytes 1048576 | tf_op jit(solution)/shard_map/pallas_call | solution.py:134
  84.0 3.0 %convolution_convert_fusion.2 = bf16[2048,512]{0,1:T(8,128)(2,1)S(1)} fusion(bf16[2048,512]{1,0:T(8,128)(2,1)} %bitcast.12, bf16[512,512]{1,0:T(8,128)(2,1)} %shard_map.41), kind=kOutput, calls=%fused_computation.3 | convolution fusion | flops 1074790400 | bytes 4718592 | tf_op jit(solution)/shard_map/dot_general | solution.py:200
  87.0 1.1 broadcast_select_fusion.5
  88.1 1.9 %collective-permute-start.1 = (bf16[2048,256]{0,1:T(8,128)(2,1)}, bf16[2048,256]{0,1:T(8,128)(2,1)}, u32[]{:S(2)}, u32[]{:S(2)}) collective-permute-start(bf16[2048,256]{0,1:T(8,128)(2,1)} %get-tuple-element.8), channel_id=1, source_target_pairs={{0,16},{16,32},{32,48},{48,64},{64,80},{80,96},{96,112},{112,128},... | collective-permute-start | bytes 3145736 | tf_op jit(solution)/shard_map/ppermute | solution.py:24
  90.0 10.2 %collective-permute-start.2 = (bf16[2048,256]{0,1:T(8,128)(2,1)S(1)}, bf16[2048,256]{0,1:T(8,128)(2,1)}, u32[]{:S(2)}, u32[]{:S(2)}) collective-permute-start(bf16[2048,256]{0,1:T(8,128)(2,1)S(1)} %get-tuple-element.9), channel_id=1, source_target_pairs={{16,0},{32,16},{48,32},{64,48},{80,64},{96,80},{112,96},{128,112},... | collective-permute-start | bytes 3145736 | tf_op jit(solution)/shard_map/ppermute | solution.py:24
  100.2 10.8 %collective-permute-done.1 = bf16[2048,256]{0,1:T(8,128)(2,1)} collective-permute-done((bf16[2048,256]{0,1:T(8,128)(2,1)}, bf16[2048,256]{0,1:T(8,128)(2,1)}, u32[]{:S(2)}, u32[]{:S(2)}) %collective-permute-start.1) | collective-permute-done | bytes 1048608 | tf_op jit(solution)/shard_map/ppermute | solution.py:24
  111.1 1.4 collective-permute-done.2
  112.5 1.7 broadcast_select_fusion.4
  114.2 0.0 copy-start.1
  114.2 1.3 fusion.1
  115.5 0.0 copy-done.1
  115.5 0.1 slice_select_fusion.1
  115.6 0.0 copy-start.2
  115.6 0.1 maximum_maximum_fusion.1
  115.7 2.2 %collective-permute-start.3 = (f32[520,256]{1,0:T(8,128)S(1)}, f32[520,256]{1,0:T(8,128)S(1)}, u32[]{:S(2)}, u32[]{:S(2)}) collective-permute-start(f32[520,256]{1,0:T(8,128)S(1)} %maximum_maximum_fusion.1), channel_id=1, source_target_pairs={{0,1},{1,0},{16,23},{23,16},{2,3},{3,2},{18,17},{17,18},{4,5},{5,4... | collective-permute-start | bytes 1597448 | tf_op jit(solution)/shard_map/ppermute | solution.py:40
  118.0 9.1 %collective-permute-done.3 = f32[520,256]{1,0:T(8,128)S(1)} collective-permute-done((f32[520,256]{1,0:T(8,128)S(1)}, f32[520,256]{1,0:T(8,128)S(1)}, u32[]{:S(2)}, u32[]{:S(2)}) %collective-permute-start.3) | collective-permute-done | bytes 532512 | tf_op jit(solution)/shard_map/ppermute | solution.py:40
  127.0 0.9 fusion.7.packed_ref
  128.0 5.6 %shard_map.42 = bf16[512,512]{1,0:T(8,128)(2,1)} custom-call(f32[520,256]{1,0:T(8,128)} %fusion.7.packed_ref), custom_call_target="tpu_custom_call" | custom-call | flops 15728640 | bytes 1048576 | tf_op jit(solution)/shard_map/pallas_call | solution.py:134
  133.6 0.0 copy-done.2
  133.6 2.3 %convolution_convert_fusion.1 = bf16[2048,512]{0,1:T(8,128)(2,1)S(1)} fusion(bf16[512,512]{1,0:T(8,128)(2,1)} %shard_map.42, bf16[2048,256]{0,1:T(8,128)(2,1)S(1)} %copy-done.2, bf16[2048,256]{0,1:T(8,128)(2,1)S(1)} %get-tuple-element.6), kind=kOutput, calls=%fused_computation.2 | convolution fusion | flops 1078984704 | bytes 4718592 | tf_op jit(solution)/shard_map/dot_general | solution.py:200
  136.0 0.1 broadcast_select_fusion.3
  136.1 1.9 %collective-permute-start.4 = (bf16[2048,256]{0,1:T(8,128)(2,1)S(1)}, bf16[2048,256]{0,1:T(8,128)(2,1)S(1)}, u32[]{:S(2)}, u32[]{:S(2)}) collective-permute-start(bf16[2048,256]{0,1:T(8,128)(2,1)S(1)} %get-tuple-element.4), channel_id=1, source_target_pairs={{0,16},{16,32},{32,48},{48,64},{64,80},{80,96},{96,112},{112,128},... | collective-permute-start | bytes 3145736 | tf_op jit(solution)/shard_map/ppermute | solution.py:24
  138.0 6.1 %collective-permute-start.5 = (bf16[2048,256]{0,1:T(8,128)(2,1)S(1)}, bf16[2048,256]{0,1:T(8,128)(2,1)S(1)}, u32[]{:S(2)}, u32[]{:S(2)}) collective-permute-start(bf16[2048,256]{0,1:T(8,128)(2,1)S(1)} %get-tuple-element.5), channel_id=1, source_target_pairs={{16,0},{32,16},{48,32},{64,48},{80,64},{96,80},{112,96},{128,112},... | collective-permute-start | bytes 3145736 | tf_op jit(solution)/shard_map/ppermute | solution.py:24
  144.1 10.5 %collective-permute-done.4 = bf16[2048,256]{0,1:T(8,128)(2,1)S(1)} collective-permute-done((bf16[2048,256]{0,1:T(8,128)(2,1)S(1)}, bf16[2048,256]{0,1:T(8,128)(2,1)S(1)}, u32[]{:S(2)}, u32[]{:S(2)}) %collective-permute-start.4) | collective-permute-done | bytes 1048608 | tf_op jit(solution)/shard_map/ppermute | solution.py:24
  154.7 1.8 collective-permute-done.5
  156.4 0.2 broadcast_select_fusion.2
  156.6 1.3 fusion
  157.9 0.1 slice_select_fusion
  158.0 0.1 maximum_maximum_fusion.2
  158.1 1.9 %collective-permute-start.6 = (f32[520,256]{1,0:T(8,128)S(1)}, f32[520,256]{1,0:T(8,128)}, u32[]{:S(2)}, u32[]{:S(2)}) collective-permute-start(f32[520,256]{1,0:T(8,128)S(1)} %maximum_maximum_fusion.2), channel_id=1, source_target_pairs={{0,1},{1,0},{16,23},{23,16},{2,3},{3,2},{18,17},{17,18},{4,5},{5,4... | collective-permute-start | bytes 1597448 | tf_op jit(solution)/shard_map/ppermute | solution.py:40
  160.1 9.3 %collective-permute-done.6 = f32[520,256]{1,0:T(8,128)} collective-permute-done((f32[520,256]{1,0:T(8,128)S(1)}, f32[520,256]{1,0:T(8,128)}, u32[]{:S(2)}, u32[]{:S(2)}) %collective-permute-start.6) | collective-permute-done | bytes 532512 | tf_op jit(solution)/shard_map/ppermute | solution.py:40
  169.4 2.0 %fusion.6.packed_ref = f32[520,256]{1,0:T(8,128)} fusion(f32[520,256]{1,0:T(8,128)} %collective-permute-done.6, f32[520]{0:T(1024)S(1)} %pad.15.clone, f32[1,256]{1,0:T(1,128)S(1)} %bitcast.16, f32[256,256]{1,0:T(8,128)S(1)} %get-tuple-element.11, f32[256,256]{1,0:T(8,128)S(1)} %get-tuple-element.10), kind=kLoop, calls=%fused_computation.33 | loop fusion | flops 532480 | bytes 1592352 | tf_op jit(solution)/shard_map/add | solution.py:40
  171.4 5.6 %shard_map.43 = bf16[512,512]{1,0:T(8,128)(2,1)} custom-call(f32[520,256]{1,0:T(8,128)} %fusion.6.packed_ref), custom_call_target="tpu_custom_call" | custom-call | flops 15728640 | bytes 1048576 | tf_op jit(solution)/shard_map/pallas_call | solution.py:134
  177.0 2.3 %multiply_reduce_fusion = (f32[512]{0:T(512)S(1)}, bf16[2048,512]{1,0:T(8,128)(2,1)S(1)}) fusion(bf16[512,512]{1,0:T(8,128)(2,1)} %shard_map.43, bf16[2048,256]{0,1:T(8,128)(2,1)S(1)} %get-tuple-element.3, bf16[2048,256]{0,1:T(8,128)(2,1)S(1)} %get-tuple-element.2), kind=kOutput, calls=%fused_computation | convolution fusion | flops 1082129920 | bytes 4720640 | tf_op jit(solution)/shard_map/dot_general | solution.py:200
  179.3 1.9 %collective-permute-start.7 = (f32[512]{0:T(512)S(1)}, f32[512]{0:T(512)S(1)}, u32[]{:S(2)}, u32[]{:S(2)}) collective-permute-start(f32[512]{0:T(512)S(1)} %get-tuple-element.19), channel_id=1, source_target_pairs={{0,1},{1,0},{16,23},{23,16},{2,3},{3,2},{18,17},{17,18},{4,5},{5,4... | collective-permute-start | bytes 6152 | tf_op jit(solution)/shard_map/ppermute | solution.py:40
  181.2 0.7 constant_dynamic-slice_fusion
  182.0 2.8 %collective-permute-done.7 = f32[512]{0:T(512)S(1)} collective-permute-done((f32[512]{0:T(512)S(1)}, f32[512]{0:T(512)S(1)}, u32[]{:S(2)}, u32[]{:S(2)}) %collective-permute-start.7) | collective-permute-done | bytes 2080 | tf_op jit(solution)/shard_map/ppermute | solution.py:40
  184.8 0.6 add_sqrt_fusion
  (1 shorter events, 0.0 us)
Async XLA Ops:
  3.2 61.5 %all-to-all-start = ((bf16[8,256,512]{2,1,0:T(8,128)(2,1)}), bf16[8,256,512]{2,1,0:T(8,128)(2,1)S(1)}, u32[]{:S(2)}, u32[]{:S(2)}) async-start(bf16[8,256,512]{2,1,0:T(8,128)(2,1)} %broadcast_in_dim.22), calls=%async_computation | async-start | bytes 4194304 | tf_op jit(solution)/shard_map/all_to_all | solution.py:162
  64.8 1.3 copy-start
  66.3 11.2 %collective-permute-start = (f32[520,256]{1,0:T(8,128)S(1)}, f32[520,256]{1,0:T(8,128)S(1)}, u32[]{:S(2)}, u32[]{:S(2)}) collective-permute-start(f32[520,256]{1,0:T(8,128)S(1)} %maximum_maximum_fusion), channel_id=1, source_target_pairs={{0,1},{1,0},{16,23},{23,16},{2,3},{3,2},{18,17},{17,18},{4,5},{5,4... | collective-permute-start | bytes 1597448 | tf_op jit(solution)/shard_map/ppermute | solution.py:40
  88.1 23.0 %collective-permute-start.1 = (bf16[2048,256]{0,1:T(8,128)(2,1)}, bf16[2048,256]{0,1:T(8,128)(2,1)}, u32[]{:S(2)}, u32[]{:S(2)}) collective-permute-start(bf16[2048,256]{0,1:T(8,128)(2,1)} %get-tuple-element.8), channel_id=1, source_target_pairs={{0,16},{16,32},{32,48},{48,64},{64,80},{80,96},{96,112},{112,128},... | collective-permute-start | bytes 3145736 | tf_op jit(solution)/shard_map/ppermute | solution.py:24
  90.0 22.5 %collective-permute-start.2 = (bf16[2048,256]{0,1:T(8,128)(2,1)S(1)}, bf16[2048,256]{0,1:T(8,128)(2,1)}, u32[]{:S(2)}, u32[]{:S(2)}) collective-permute-start(bf16[2048,256]{0,1:T(8,128)(2,1)S(1)} %get-tuple-element.9), channel_id=1, source_target_pairs={{16,0},{32,16},{48,32},{64,48},{80,64},{96,80},{112,96},{128,112},... | collective-permute-start | bytes 3145736 | tf_op jit(solution)/shard_map/ppermute | solution.py:24
  114.2 1.3 copy-start.1
  115.6 18.0 %copy-start.2 = (bf16[2048,256]{0,1:T(8,128)(2,1)S(1)}, bf16[2048,256]{0,1:T(8,128)(2,1)}, u32[]{:S(2)}) copy-start(bf16[2048,256]{0,1:T(8,128)(2,1)} %copy-done.1) | copy-start | bytes 3145732
  115.7 11.3 %collective-permute-start.3 = (f32[520,256]{1,0:T(8,128)S(1)}, f32[520,256]{1,0:T(8,128)S(1)}, u32[]{:S(2)}, u32[]{:S(2)}) collective-permute-start(f32[520,256]{1,0:T(8,128)S(1)} %maximum_maximum_fusion.1), channel_id=1, source_target_pairs={{0,1},{1,0},{16,23},{23,16},{2,3},{3,2},{18,17},{17,18},{4,5},{5,4... | collective-permute-start | bytes 1597448 | tf_op jit(solution)/shard_map/ppermute | solution.py:40
  136.1 18.6 %collective-permute-start.4 = (bf16[2048,256]{0,1:T(8,128)(2,1)S(1)}, bf16[2048,256]{0,1:T(8,128)(2,1)S(1)}, u32[]{:S(2)}, u32[]{:S(2)}) collective-permute-start(bf16[2048,256]{0,1:T(8,128)(2,1)S(1)} %get-tuple-element.4), channel_id=1, source_target_pairs={{0,16},{16,32},{32,48},{48,64},{64,80},{80,96},{96,112},{112,128},... | collective-permute-start | bytes 3145736 | tf_op jit(solution)/shard_map/ppermute | solution.py:24
  138.0 18.4 %collective-permute-start.5 = (bf16[2048,256]{0,1:T(8,128)(2,1)S(1)}, bf16[2048,256]{0,1:T(8,128)(2,1)S(1)}, u32[]{:S(2)}, u32[]{:S(2)}) collective-permute-start(bf16[2048,256]{0,1:T(8,128)(2,1)S(1)} %get-tuple-element.5), channel_id=1, source_target_pairs={{16,0},{32,16},{48,32},{64,48},{80,64},{96,80},{112,96},{128,112},... | collective-permute-start | bytes 3145736 | tf_op jit(solution)/shard_map/ppermute | solution.py:24
  158.1 11.3 %collective-permute-start.6 = (f32[520,256]{1,0:T(8,128)S(1)}, f32[520,256]{1,0:T(8,128)}, u32[]{:S(2)}, u32[]{:S(2)}) collective-permute-start(f32[520,256]{1,0:T(8,128)S(1)} %maximum_maximum_fusion.2), channel_id=1, source_target_pairs={{0,1},{1,0},{16,23},{23,16},{2,3},{3,2},{18,17},{17,18},{4,5},{5,4... | collective-permute-start | bytes 1597448 | tf_op jit(solution)/shard_map/ppermute | solution.py:40
  179.3 5.5 %collective-permute-start.7 = (f32[512]{0:T(512)S(1)}, f32[512]{0:T(512)S(1)}, u32[]{:S(2)}, u32[]{:S(2)}) collective-permute-start(f32[512]{0:T(512)S(1)} %get-tuple-element.19), channel_id=1, source_target_pairs={{0,1},{1,0},{16,23},{23,16},{2,3},{3,2},{18,17},{17,18},{4,5},{5,4... | collective-permute-start | bytes 6152 | tf_op jit(solution)/shard_map/ppermute | solution.py:40

commit v7 on v6

--- a/solution.py
+++ b/solution.py
@@ -197,20 +197,27 @@
         moving = round_index + 1 < ROUNDS
         pair_data = jnp.concatenate([upper_block, lower_block], axis=1)
         rotation = rotation_of(summed_gram(pair_data, width))
-        rotated = jnp.dot(pair_data, rotation, preferred_element_type=jnp.float32).astype(
-            jnp.bfloat16
-        )
-        new_upper = rotated[:, :width]
-        new_lower = rotated[:, width:]
-        if moving:
-            from_right = send_left(new_lower)
-            from_left = send_right(jnp.where(position == 0, new_lower, new_upper))
-        if moving:
-            upper_block = jnp.where(position == 0, new_upper, from_left)
-            lower_block = jnp.where(position == device_count - 1, new_upper, from_right)
-        else:
-            upper_block = new_upper
-            lower_block = new_lower
+        if not moving:
+            rotated = jnp.dot(pair_data, rotation, preferred_element_type=jnp.float32)
+            upper_block = rotated[:, :width].astype(jnp.bfloat16)
+            lower_block = rotated[:, width:].astype(jnp.bfloat16)
+            break
+        first_columns = rotation[:, :width]
+        second_columns = rotation[:, width:]
+        going_right = jnp.dot(
+            pair_data,
+            jnp.where(position == 0, second_columns, first_columns),
+            preferred_element_type=jnp.float32,
+        ).astype(jnp.bfloat16)
+        going_left = jnp.dot(
+            pair_data,
+            jnp.where(position == 0, first_columns, second_columns),
+            preferred_element_type=jnp.float32,
+        ).astype(jnp.bfloat16)
+        from_left = send_right(going_right)
+        from_right = send_left(going_left)
+        upper_block = jnp.where(position == 0, going_left, from_left)
+        lower_block = jnp.where(position == device_count - 1, going_right, from_right)
     gathered_design = jnp.concatenate([upper_block, lower_block], axis=1)
     squares = with_partner(jnp.sum(jnp.square(gathered_design.astype(jnp.float32)), axis=0))
     record_total = records * lax.axis_size(RECORD_AXES)

time: 186 us -> 186 us (level)
    dot_general x3 -> x5, matrix products: 7.65 us -> 8.56 us  [the longest x2 3.68 us: local(): jnp.dot(pair_data, jnp.where(position == 0, second_columns, first_columns...]
  transfers between devices with their start and end apart: 9 -> 9, of which waited for: 9 -> 9; matrix products, arithmetic and copies ran while one was open for 0% -> 3% of each run, Pallas kernels for 0% -> 0%
where the time goes in v7:
time: 186 us
  waiting for transfers between devices  106 us (57%)
  starting transfers between devices  37.3 us (20%)
  Pallas kernels  16.8 us (9%)
  matrix products  12.4 us (7%)
  other arithmetic  10 us (5%)
  local copies, waits for them, and re-layouts  2.32 us (1%)
    all_to_all x1, waiting for transfers between devices, gathered_records(): gathered = lax.all_to_all(spread, GROUP_AXES, 0, 0, tiled=False)  52.8 us
    ppermute x4, waiting for transfers between devices, with_partner(): lax.ppermute(value, PARTNER_AXES, partner_pairs(lax.axis_size('y_hi')))  29.8 us
    ppermute x4, waiting for transfers between devices, from_behind(): lax.ppermute(value, COLUMN_AXES, [(source, source + steps) for source in...  23.4 us
    ppermute x4, starting transfers between devices, from_behind(): lax.ppermute(value, COLUMN_AXES, [(source, source + steps) for source in...  20 us
    pallas_call x3, Pallas kernels, rotation_of(): pl.pallas_call(sweeps_kernel, out_shape=jax.ShapeDtypeStruct((2 * width,...  16.8 us
    all_to_all x1, starting transfers between devices, gathered_records(): gathered = lax.all_to_all(spread, GROUP_AXES, 0, 0, tiled=False)  8.66 us
    ppermute x4, starting transfers between devices, with_partner(): lax.ppermute(value, PARTNER_AXES, partner_pairs(lax.axis_size('y_hi')))  8.64 us
    add x3, other arithmetic, with_partner(): value + lax.ppermute(value, PARTNER_AXES, partner_pairs(lax.axis_size('y_...  4.89 us
  transfers between devices with their start and end apart: 9, of which 9 were waited for; matrix products, arithmetic and copies ran while one was open for 3% of the time, Pallas kernels for 0%

profile of v7, /device:TPU:2, one launch (start us, length us, event | category | flops | bytes accessed | tf_op | source)
XLA Modules:
  0.0 185.7 jit_solution(3587405682294787426)
XLA Ops:
  0.6 1.1 multiply_convert_fusion
  1.7 1.5 broadcast_in_dim.22
  3.2 8.7 %all-to-all-start = ((bf16[8,256,512]{2,1,0:T(8,128)(2,1)}), bf16[8,256,512]{2,1,0:T(8,128)(2,1)S(1)}, u32[]{:S(2)}, u32[]{:S(2)}) async-start(bf16[8,256,512]{2,1,0:T(8,128)(2,1)} %broadcast_in_dim.22), calls=%async_computation | async-start | bytes 4194304 | tf_op jit(solution)/shard_map/all_to_all | solution.py:162
  11.9 0.1 pad.15.clone
  11.9 52.8 %all-to-all-done = bf16[8,256,512]{2,1,0:T(8,128)(2,1)S(1)} async-done(((bf16[8,256,512]{2,1,0:T(8,128)(2,1)}), bf16[8,256,512]{2,1,0:T(8,128)(2,1)S(1)}, u32[]{:S(2)}, u32[]{:S(2)}) %all-to-all-start) | async-done | bytes 2097184 | tf_op jit(solution)/shard_map/all_to_all | solution.py:162
  64.7 1.3 convolution_bitcast_fusion
  66.0 0.1 slice_select_fusion.2
  66.1 0.1 maximum_maximum_fusion
  66.2 2.7 %collective-permute-start = (f32[520,256]{1,0:T(8,128)S(1)}, f32[520,256]{1,0:T(8,128)}, u32[]{:S(2)}, u32[]{:S(2)}) collective-permute-start(f32[520,256]{1,0:T(8,128)S(1)} %maximum_maximum_fusion), channel_id=1, source_target_pairs={{0,1},{1,0},{16,23},{23,16},{2,3},{3,2},{18,17},{17,18},{4,5},{5,4... | collective-permute-start | bytes 1597448 | tf_op jit(solution)/shard_map/ppermute | solution.py:40
  68.9 8.6 %collective-permute-done = f32[520,256]{1,0:T(8,128)} collective-permute-done((f32[520,256]{1,0:T(8,128)S(1)}, f32[520,256]{1,0:T(8,128)}, u32[]{:S(2)}, u32[]{:S(2)}) %collective-permute-start) | collective-permute-done | bytes 532512 | tf_op jit(solution)/shard_map/ppermute | solution.py:40
  77.5 2.0 %fusion.25.packed_ref = f32[520,256]{1,0:T(8,128)} fusion(f32[520,256]{1,0:T(8,128)} %collective-permute-done, f32[520]{0:T(1024)S(1)} %pad.15.clone, f32[1,256]{1,0:T(1,128)S(1)} %bitcast.14, f32[256,256]{1,0:T(8,128)S(1)} %get-tuple-element.9, f32[256,256]{1,0:T(8,128)S(1)} %get-tuple-element.8), kind=kLoop, calls=%fused_computation.52 | loop fusion | flops 532480 | bytes 1592352 | tf_op jit(solution)/shard_map/add | solution.py:40
  79.5 5.6 %shard_map.41 = bf16[512,512]{1,0:T(8,128)(2,1)} custom-call(f32[520,256]{1,0:T(8,128)} %fusion.25.packed_ref), custom_call_target="tpu_custom_call" | custom-call | flops 15728640 | bytes 1048576 | tf_op jit(solution)/shard_map/pallas_call | solution.py:134
  85.1 0.0 copy-start
  85.1 1.8 convolution_convert_fusion.3
  87.0 1.9 %collective-permute-start.1 = (bf16[2048,256]{0,1:T(8,128)(2,1)S(1)}, bf16[2048,256]{0,1:T(8,128)(2,1)}, u32[]{:S(2)}, u32[]{:S(2)}) collective-permute-start(bf16[2048,256]{0,1:T(8,128)(2,1)S(1)} %convolution_convert_fusion.3), channel_id=1, source_target_pairs={{0,16},{16,32},{32,48},{48,64},{64,80},{80,96},{96,112},{112,128},... | collective-permute-start | bytes 3145736 | tf_op jit(solution)/shard_map/ppermute | solution.py:24
  88.9 0.0 copy-done
  88.9 1.8 convolution_convert_fusion.4
  90.7 10.2 %collective-permute-start.2 = (bf16[2048,256]{0,1:T(8,128)(2,1)}, bf16[2048,256]{0,1:T(8,128)(2,1)}, u32[]{:S(2)}, u32[]{:S(2)}) collective-permute-start(bf16[2048,256]{0,1:T(8,128)(2,1)} %convolution_convert_fusion.4), channel_id=1, source_target_pairs={{16,0},{32,16},{48,32},{64,48},{80,64},{96,80},{112,96},{128,112},... | collective-permute-start | bytes 3145736 | tf_op jit(solution)/shard_map/ppermute | solution.py:24
  100.8 8.9 %collective-permute-done.1 = bf16[2048,256]{0,1:T(8,128)(2,1)} collective-permute-done((bf16[2048,256]{0,1:T(8,128)(2,1)S(1)}, bf16[2048,256]{0,1:T(8,128)(2,1)}, u32[]{:S(2)}, u32[]{:S(2)}) %collective-permute-start.1) | collective-permute-done | bytes 1048608 | tf_op jit(solution)/shard_map/ppermute | solution.py:24
  109.7 1.3 broadcast_select_fusion.3
  111.1 2.4 %collective-permute-done.2 = bf16[2048,256]{0,1:T(8,128)(2,1)} collective-permute-done((bf16[2048,256]{0,1:T(8,128)(2,1)}, bf16[2048,256]{0,1:T(8,128)(2,1)}, u32[]{:S(2)}, u32[]{:S(2)}) %collective-permute-start.2) | collective-permute-done | bytes 1048608 | tf_op jit(solution)/shard_map/ppermute | solution.py:24
  113.5 1.3 broadcast_select_fusion.1
  114.8 1.3 fusion.1
  116.1 0.1 slice_select_fusion.1
  116.1 0.1 maximum_maximum_fusion.1
  116.3 2.1 %collective-permute-start.3 = (f32[520,256]{1,0:T(8,128)S(1)}, f32[520,256]{1,0:T(8,128)S(1)}, u32[]{:S(2)}, u32[]{:S(2)}) collective-permute-start(f32[520,256]{1,0:T(8,128)S(1)} %maximum_maximum_fusion.1), channel_id=1, source_target_pairs={{0,1},{1,0},{16,23},{23,16},{2,3},{3,2},{18,17},{17,18},{4,5},{5,4... | collective-permute-start | bytes 1597448 | tf_op jit(solution)/shard_map/ppermute | solution.py:40
  118.4 9.1 %collective-permute-done.3 = f32[520,256]{1,0:T(8,128)S(1)} collective-permute-done((f32[520,256]{1,0:T(8,128)S(1)}, f32[520,256]{1,0:T(8,128)S(1)}, u32[]{:S(2)}, u32[]{:S(2)}) %collective-permute-start.3) | collective-permute-done | bytes 532512 | tf_op jit(solution)/shard_map/ppermute | solution.py:40
  127.4 0.9 fusion.24.packed_ref
  128.4 5.6 %shard_map.42 = bf16[512,512]{1,0:T(8,128)(2,1)} custom-call(f32[520,256]{1,0:T(8,128)} %fusion.24.packed_ref), custom_call_target="tpu_custom_call" | custom-call | flops 15728640 | bytes 1048576 | tf_op jit(solution)/shard_map/pallas_call | solution.py:134
  134.0 0.0 copy-start.1
  134.0 1.8 convolution_convert_fusion.1
  135.8 1.9 %collective-permute-start.4 = (bf16[2048,256]{0,1:T(8,128)(2,1)S(1)}, bf16[2048,256]{0,1:T(8,128)(2,1)S(1)}, u32[]{:S(2)}, u32[]{:S(2)}) collective-permute-start(bf16[2048,256]{0,1:T(8,128)(2,1)S(1)} %convolution_convert_fusion.1), channel_id=1, source_target_pairs={{0,16},{16,32},{32,48},{48,64},{64,80},{80,96},{96,112},{112,128},... | collective-permute-start | bytes 3145736 | tf_op jit(solution)/shard_map/ppermute | solution.py:24
  137.8 0.0 copy-done.1
  137.8 0.8 convolution_convert_fusion.2
  138.5 6.0 %collective-permute-start.5 = (bf16[2048,256]{0,1:T(8,128)(2,1)S(1)}, bf16[2048,256]{0,1:T(8,128)(2,1)S(1)}, u32[]{:S(2)}, u32[]{:S(2)}) collective-permute-start(bf16[2048,256]{0,1:T(8,128)(2,1)S(1)} %convolution_convert_fusion.2), channel_id=1, source_target_pairs={{16,0},{32,16},{48,32},{64,48},{80,64},{96,80},{112,96},{128,112},... | collective-permute-start | bytes 3145736 | tf_op jit(solution)/shard_map/ppermute | solution.py:24
  144.5 9.8 %collective-permute-done.4 = bf16[2048,256]{0,1:T(8,128)(2,1)S(1)} collective-permute-done((bf16[2048,256]{0,1:T(8,128)(2,1)S(1)}, bf16[2048,256]{0,1:T(8,128)(2,1)S(1)}, u32[]{:S(2)}, u32[]{:S(2)}) %collective-permute-start.4) | collective-permute-done | bytes 1048608 | tf_op jit(solution)/shard_map/ppermute | solution.py:24
  154.3 0.1 broadcast_select_fusion.2
  154.4 2.4 %collective-permute-done.5 = bf16[2048,256]{0,1:T(8,128)(2,1)S(1)} collective-permute-done((bf16[2048,256]{0,1:T(8,128)(2,1)S(1)}, bf16[2048,256]{0,1:T(8,128)(2,1)S(1)}, u32[]{:S(2)}, u32[]{:S(2)}) %collective-permute-start.5) | collective-permute-done | bytes 1048608 | tf_op jit(solution)/shard_map/ppermute | solution.py:24
  156.8 0.1 broadcast_select_fusion
  156.9 1.3 fusion
  158.2 0.1 slice_select_fusion
  158.3 0.1 maximum_maximum_fusion.2
  158.4 1.9 %collective-permute-start.6 = (f32[520,256]{1,0:T(8,128)S(1)}, f32[520,256]{1,0:T(8,128)}, u32[]{:S(2)}, u32[]{:S(2)}) collective-permute-start(f32[520,256]{1,0:T(8,128)S(1)} %maximum_maximum_fusion.2), channel_id=1, source_target_pairs={{0,1},{1,0},{16,23},{23,16},{2,3},{3,2},{18,17},{17,18},{4,5},{5,4... | collective-permute-start | bytes 1597448 | tf_op jit(solution)/shard_map/ppermute | solution.py:40
  160.4 9.3 %collective-permute-done.6 = f32[520,256]{1,0:T(8,128)} collective-permute-done((f32[520,256]{1,0:T(8,128)S(1)}, f32[520,256]{1,0:T(8,128)}, u32[]{:S(2)}, u32[]{:S(2)}) %collective-permute-start.6) | collective-permute-done | bytes 532512 | tf_op jit(solution)/shard_map/ppermute | solution.py:40
  169.7 2.0 %fusion.23.packed_ref = f32[520,256]{1,0:T(8,128)} fusion(f32[520,256]{1,0:T(8,128)} %collective-permute-done.6, f32[520]{0:T(1024)S(1)} %pad.15.clone, f32[1,256]{1,0:T(1,128)S(1)} %bitcast.16, f32[256,256]{1,0:T(8,128)S(1)} %get-tuple-element.3, f32[256,256]{1,0:T(8,128)S(1)} %get-tuple-element.2), kind=kLoop, calls=%fused_computation.50 | loop fusion | flops 532480 | bytes 1592352 | tf_op jit(solution)/shard_map/add | solution.py:40
  171.7 5.6 %shard_map.43 = bf16[512,512]{1,0:T(8,128)(2,1)} custom-call(f32[520,256]{1,0:T(8,128)} %fusion.23.packed_ref), custom_call_target="tpu_custom_call" | custom-call | flops 15728640 | bytes 1048576 | tf_op jit(solution)/shard_map/pallas_call | solution.py:134
  177.3 2.3 %multiply_reduce_fusion = (f32[512]{0:T(512)S(1)}, bf16[2048,512]{1,0:T(8,128)(2,1)S(1)}) fusion(bf16[512,512]{1,0:T(8,128)(2,1)} %shard_map.43, bf16[2048,256]{0,1:T(8,128)(2,1)S(1)} %broadcast_select_fusion, bf16[2048,256]{0,1:T(8,128)(2,1)S(1)} %broadcast_select_fusion.2), kind=kOutput, calls=%fused_computation | convolution fusion | flops 1082129920 | bytes 4720640 | tf_op jit(solution)/shard_map/dot_general | solution.py:201
  179.6 1.9 %collective-permute-start.7 = (f32[512]{0:T(512)S(1)}, f32[512]{0:T(512)S(1)}, u32[]{:S(2)}, u32[]{:S(2)}) collective-permute-start(f32[512]{0:T(512)S(1)} %get-tuple-element.11), channel_id=1, source_target_pairs={{0,1},{1,0},{16,23},{23,16},{2,3},{3,2},{18,17},{17,18},{4,5},{5,4... | collective-permute-start | bytes 6152 | tf_op jit(solution)/shard_map/ppermute | solution.py:40
  181.6 0.7 constant_dynamic-slice_fusion
  182.3 2.8 %collective-permute-done.7 = f32[512]{0:T(512)S(1)} collective-permute-done((f32[512]{0:T(512)S(1)}, f32[512]{0:T(512)S(1)}, u32[]{:S(2)}, u32[]{:S(2)}) %collective-permute-start.7) | collective-permute-done | bytes 2080 | tf_op jit(solution)/shard_map/ppermute | solution.py:40
  185.1 0.6 add_sqrt_fusion
  (1 shorter events, 0.0 us)
Async XLA Ops:
  3.2 61.5 %all-to-all-start = ((bf16[8,256,512]{2,1,0:T(8,128)(2,1)}), bf16[8,256,512]{2,1,0:T(8,128)(2,1)S(1)}, u32[]{:S(2)}, u32[]{:S(2)}) async-start(bf16[8,256,512]{2,1,0:T(8,128)(2,1)} %broadcast_in_dim.22), calls=%async_computation | async-start | bytes 4194304 | tf_op jit(solution)/shard_map/all_to_all | solution.py:162
  66.2 11.3 %collective-permute-start = (f32[520,256]{1,0:T(8,128)S(1)}, f32[520,256]{1,0:T(8,128)}, u32[]{:S(2)}, u32[]{:S(2)}) collective-permute-start(f32[520,256]{1,0:T(8,128)S(1)} %maximum_maximum_fusion), channel_id=1, source_target_pairs={{0,1},{1,0},{16,23},{23,16},{2,3},{3,2},{18,17},{17,18},{4,5},{5,4... | collective-permute-start | bytes 1597448 | tf_op jit(solution)/shard_map/ppermute | solution.py:40
  85.1 3.8 %copy-start = (bf16[512,512]{1,0:T(8,128)(2,1)S(1)}, bf16[512,512]{1,0:T(8,128)(2,1)}, u32[]{:S(2)}) copy-start(bf16[512,512]{1,0:T(8,128)(2,1)} %shard_map.41) | copy-start | bytes 1572868
  87.0 22.8 %collective-permute-start.1 = (bf16[2048,256]{0,1:T(8,128)(2,1)S(1)}, bf16[2048,256]{0,1:T(8,128)(2,1)}, u32[]{:S(2)}, u32[]{:S(2)}) collective-permute-start(bf16[2048,256]{0,1:T(8,128)(2,1)S(1)} %convolution_convert_fusion.3), channel_id=1, source_target_pairs={{0,16},{16,32},{32,48},{48,64},{64,80},{80,96},{96,112},{112,128},... | collective-permute-start | bytes 3145736 | tf_op jit(solution)/shard_map/ppermute | solution.py:24
  90.7 22.8 %collective-permute-start.2 = (bf16[2048,256]{0,1:T(8,128)(2,1)}, bf16[2048,256]{0,1:T(8,128)(2,1)}, u32[]{:S(2)}, u32[]{:S(2)}) collective-permute-start(bf16[2048,256]{0,1:T(8,128)(2,1)} %convolution_convert_fusion.4), channel_id=1, source_target_pairs={{16,0},{32,16},{48,32},{64,48},{80,64},{96,80},{112,96},{128,112},... | collective-permute-start | bytes 3145736 | tf_op jit(solution)/shard_map/ppermute | solution.py:24
  116.3 11.2 %collective-permute-start.3 = (f32[520,256]{1,0:T(8,128)S(1)}, f32[520,256]{1,0:T(8,128)S(1)}, u32[]{:S(2)}, u32[]{:S(2)}) collective-permute-start(f32[520,256]{1,0:T(8,128)S(1)} %maximum_maximum_fusion.1), channel_id=1, source_target_pairs={{0,1},{1,0},{16,23},{23,16},{2,3},{3,2},{18,17},{17,18},{4,5},{5,4... | collective-permute-start | bytes 1597448 | tf_op jit(solution)/shard_map/ppermute | solution.py:40
  134.0 3.8 %copy-start.1 = (bf16[512,512]{1,0:T(8,128)(2,1)S(1)}, bf16[512,512]{1,0:T(8,128)(2,1)}, u32[]{:S(2)}) copy-start(bf16[512,512]{1,0:T(8,128)(2,1)} %shard_map.42) | copy-start | bytes 1572868
  135.8 18.5 %collective-permute-start.4 = (bf16[2048,256]{0,1:T(8,128)(2,1)S(1)}, bf16[2048,256]{0,1:T(8,128)(2,1)S(1)}, u32[]{:S(2)}, u32[]{:S(2)}) collective-permute-start(bf16[2048,256]{0,1:T(8,128)(2,1)S(1)} %convolution_convert_fusion.1), channel_id=1, source_target_pairs={{0,16},{16,32},{32,48},{48,64},{64,80},{80,96},{96,112},{112,128},... | collective-permute-start | bytes 3145736 | tf_op jit(solution)/shard_map/ppermute | solution.py:24
  138.5 18.3 %collective-permute-start.5 = (bf16[2048,256]{0,1:T(8,128)(2,1)S(1)}, bf16[2048,256]{0,1:T(8,128)(2,1)S(1)}, u32[]{:S(2)}, u32[]{:S(2)}) collective-permute-start(bf16[2048,256]{0,1:T(8,128)(2,1)S(1)} %convolution_convert_fusion.2), channel_id=1, source_target_pairs={{16,0},{32,16},{48,32},{64,48},{80,64},{96,80},{112,96},{128,112},... | collective-permute-start | bytes 3145736 | tf_op jit(solution)/shard_map/ppermute | solution.py:24
  158.4 11.3 %collective-permute-start.6 = (f32[520,256]{1,0:T(8,128)S(1)}, f32[520,256]{1,0:T(8,128)}, u32[]{:S(2)}, u32[]{:S(2)}) collective-permute-start(f32[520,256]{1,0:T(8,128)S(1)} %maximum_maximum_fusion.2), channel_id=1, source_target_pairs={{0,1},{1,0},{16,23},{23,16},{2,3},{3,2},{18,17},{17,18},{4,5},{5,4... | collective-permute-start | bytes 1597448 | tf_op jit(solution)/shard_map/ppermute | solution.py:40
  179.6 5.5 %collective-permute-start.7 = (f32[512]{0:T(512)S(1)}, f32[512]{0:T(512)S(1)}, u32[]{:S(2)}, u32[]{:S(2)}) collective-permute-start(f32[512]{0:T(512)S(1)} %get-tuple-element.11), channel_id=1, source_target_pairs={{0,1},{1,0},{16,23},{23,16},{2,3},{3,2},{18,17},{17,18},{4,5},{5,4... | collective-permute-start | bytes 6152 | tf_op jit(solution)/shard_map/ppermute | solution.py:40

commit v8 on v7

--- a/solution.py
+++ b/solution.py
@@ -193,6 +193,10 @@
     lower_block = weighted[:, width:]
     position = lax.axis_index(COLUMN_AXES)
     device_count = lax.axis_size(COLUMN_AXES)
+    core = lax.axis_index("core")
+    across_pairs = [(k, k + 1) for k in range(1, device_count - 1, 2)] + [
+        (k, k - 1) for k in range(2, device_count, 2)
+    ]
     for round_index in range(ROUNDS):
         moving = round_index + 1 < ROUNDS
         pair_data = jnp.concatenate([upper_block, lower_block], axis=1)
@@ -204,20 +208,25 @@
             break
         first_columns = rotation[:, :width]
         second_columns = rotation[:, width:]
-        going_right = jnp.dot(
+        right_columns = jnp.where(position == 0, second_columns, first_columns)
+        left_columns = jnp.where(position == 0, first_columns, second_columns)
+        core_zero = core == 0
+        within = jnp.dot(
             pair_data,
-            jnp.where(position == 0, second_columns, first_columns),
+            jnp.where(core_zero, right_columns, left_columns),
             preferred_element_type=jnp.float32,
         ).astype(jnp.bfloat16)
-        going_left = jnp.dot(
+        across = jnp.dot(
             pair_data,
-            jnp.where(position == 0, first_columns, second_columns),
+            jnp.where(core_zero, left_columns, right_columns),
             preferred_element_type=jnp.float32,
         ).astype(jnp.bfloat16)
-        from_left = send_right(going_right)
-        from_right = send_left(going_left)
-        upper_block = jnp.where(position == 0, going_left, from_left)
-        lower_block = jnp.where(position == device_count - 1, going_right, from_right)
+        within_in = lax.ppermute(within, "core", [(0, 1), (1, 0)])
+        across_in = lax.ppermute(across, COLUMN_AXES, across_pairs)
+        upper_block = jnp.where(position == 0, across, jnp.where(core_zero, across_in, within_in))
+        lower_block = jnp.where(
+            position == device_count - 1, across, jnp.where(core_zero, within_in, across_in)
+        )
     gathered_design = jnp.concatenate([upper_block, lower_block], axis=1)
     squares = with_partner(jnp.sum(jnp.square(gathered_design.astype(jnp.float32)), axis=0))
     record_total = records * lax.axis_size(RECORD_AXES)

time: 186 us -> 190 us (1.022)
  starting transfers between devices: 37.3 us -> 41 us
    ppermute x4, waiting for transfers between devices: 29.8 us -> 27.6 us  [with_partner(): lax.ppermute(value, PARTNER_AXES, partner_pairs(lax.axis_size('y_hi')))]
    ppermute x4, starting transfers between devices: 8.64 us -> 10.8 us  [with_partner(): lax.ppermute(value, PARTNER_AXES, partner_pairs(lax.axis_size('y_hi')))]
  transfers between devices with their start and end apart: 9 -> 9, of which waited for: 9 -> 7; matrix products, arithmetic and copies ran while one was open for 3% -> 0% of each run, Pallas kernels for 0% -> 0%
where the time goes in v8:
time: 190 us; the launch traced here: 189 us
  waiting for transfers between devices  106 us (56%)
  starting transfers between devices  41 us (22%)
  Pallas kernels  16.8 us (9%)
  matrix products  13.4 us (7%)
  other arithmetic  9.04 us (5%)
  local copies, waits for them, and re-layouts  2.35 us (1%)
    all_to_all x1, waiting for transfers between devices, gathered_records(): gathered = lax.all_to_all(spread, GROUP_AXES, 0, 0, tiled=False)  52.8 us
    ppermute x4, waiting for transfers between devices, with_partner(): lax.ppermute(value, PARTNER_AXES, partner_pairs(lax.axis_size('y_hi')))  27.6 us
    ppermute x2, waiting for transfers between devices, local(): across_in = lax.ppermute(across, COLUMN_AXES, across_pairs)  25.2 us
    ppermute x2, starting transfers between devices, local(): across_in = lax.ppermute(across, COLUMN_AXES, across_pairs)  17.7 us
    pallas_call x3, Pallas kernels, rotation_of(): pl.pallas_call(sweeps_kernel, out_shape=jax.ShapeDtypeStruct((2 * width,...  16.8 us
    ppermute x4, starting transfers between devices, with_partner(): lax.ppermute(value, PARTNER_AXES, partner_pairs(lax.axis_size('y_hi')))  10.8 us
    all_to_all x1, starting transfers between devices, gathered_records(): gathered = lax.all_to_all(spread, GROUP_AXES, 0, 0, tiled=False)  8.66 us
    add x3, other arithmetic, with_partner(): value + lax.ppermute(value, PARTNER_AXES, partner_pairs(lax.axis_size('y_...  4.91 us
  transfers between devices with their start and end apart: 9, of which 7 were waited for; matrix products, arithmetic and copies ran while one was open for 0% of the time, Pallas kernels for 0%

profile of v8, /device:TPU:2, one launch (start us, length us, event | category | flops | bytes accessed | tf_op | source)
XLA Modules:
  0.0 189.0 jit_solution(5604812981292392100)
XLA Ops:
  0.6 1.1 multiply_convert_fusion
  1.7 1.5 broadcast_in_dim.22
  3.2 8.7 %all-to-all-start = ((bf16[8,256,512]{2,1,0:T(8,128)(2,1)}), bf16[8,256,512]{2,1,0:T(8,128)(2,1)S(1)}, u32[]{:S(2)}, u32[]{:S(2)}) async-start(bf16[8,256,512]{2,1,0:T(8,128)(2,1)} %broadcast_in_dim.22), calls=%async_computation | async-start | bytes 4194304 | tf_op jit(solution)/shard_map/all_to_all | solution.py:162
  11.9 0.1 pad.15.clone
  12.0 52.8 %all-to-all-done = bf16[8,256,512]{2,1,0:T(8,128)(2,1)S(1)} async-done(((bf16[8,256,512]{2,1,0:T(8,128)(2,1)}), bf16[8,256,512]{2,1,0:T(8,128)(2,1)S(1)}, u32[]{:S(2)}, u32[]{:S(2)}) %all-to-all-start) | async-done | bytes 2097184 | tf_op jit(solution)/shard_map/all_to_all | solution.py:162
  64.8 1.3 convolution_bitcast_fusion
  66.1 0.1 slice_select_fusion.2
  66.1 0.1 maximum_maximum_fusion
  66.3 2.7 %collective-permute-start = (f32[520,256]{1,0:T(8,128)S(1)}, f32[520,256]{1,0:T(8,128)}, u32[]{:S(2)}, u32[]{:S(2)}) collective-permute-start(f32[520,256]{1,0:T(8,128)S(1)} %maximum_maximum_fusion), channel_id=1, source_target_pairs={{0,1},{1,0},{16,23},{23,16},{2,3},{3,2},{18,17},{17,18},{4,5},{5,4... | collective-permute-start | bytes 1597448 | tf_op jit(solution)/shard_map/ppermute | solution.py:40
  69.0 8.6 %collective-permute-done = f32[520,256]{1,0:T(8,128)} collective-permute-done((f32[520,256]{1,0:T(8,128)S(1)}, f32[520,256]{1,0:T(8,128)}, u32[]{:S(2)}, u32[]{:S(2)}) %collective-permute-start) | collective-permute-done | bytes 532512 | tf_op jit(solution)/shard_map/ppermute | solution.py:40
  77.5 2.0 %fusion.17.packed_ref = f32[520,256]{1,0:T(8,128)} fusion(f32[520,256]{1,0:T(8,128)} %collective-permute-done, f32[520]{0:T(1024)S(1)} %pad.15.clone, f32[1,256]{1,0:T(1,128)S(1)} %bitcast.14, f32[256,256]{1,0:T(8,128)S(1)} %get-tuple-element.13, f32[256,256]{1,0:T(8,128)S(1)} %get-tuple-element.12), kind=kLoop, calls=%fused_computation.48 | loop fusion | flops 532480 | bytes 1592352 | tf_op jit(solution)/shard_map/add | solution.py:40
  79.5 5.6 %shard_map.41 = bf16[512,512]{1,0:T(8,128)(2,1)} custom-call(f32[520,256]{1,0:T(8,128)} %fusion.17.packed_ref), custom_call_target="tpu_custom_call" | custom-call | flops 15728640 | bytes 1048576 | tf_op jit(solution)/shard_map/pallas_call | solution.py:134
  85.1 0.0 copy-start.1
  85.1 2.8 %convolution_convert_fusion.4 = bf16[2048,256]{0,1:T(8,128)(2,1)} fusion(bf16[2048,512]{1,0:T(8,128)(2,1)S(1)} %bitcast.11, pred[]{:T(512)S(6)} %eq.26, pred[]{:T(512)S(6)} %eq.12, bf16[512,512]{1,0:T(8,128)(2,1)} %shard_map.41), kind=kOutput, calls=%fused_computation.5 | convolution fusion | flops 537788416 | bytes 3670018 | tf_op jit(solution)/shard_map/dot_general | solution.py:219
  87.9 0.0 copy-done.1
  87.9 1.8 convolution_convert_fusion.3
  89.7 1.9 %collective-permute-start.2 = (bf16[2048,256]{0,1:T(8,128)(2,1)}, bf16[2048,256]{0,1:T(8,128)(2,1)S(1)}, u32[]{:S(2)}, u32[]{:S(2)}) collective-permute-start(bf16[2048,256]{0,1:T(8,128)(2,1)} %convolution_convert_fusion.3), channel_id=1, source_target_pairs={{0,16},{16,0},{1,17},{17,1},{2,18},{18,2},{3,19},{19,3},{4,20},{20... | collective-permute-start | bytes 3145736 | tf_op jit(solution)/shard_map/ppermute | solution.py:224
  91.6 11.9 %collective-permute-start.1 = (bf16[2048,256]{0,1:T(8,128)(2,1)}, bf16[2048,256]{0,1:T(8,128)(2,1)}, u32[]{:S(2)}, u32[]{:S(2)}) collective-permute-start(bf16[2048,256]{0,1:T(8,128)(2,1)} %convolution_convert_fusion.4), channel_id=1, source_target_pairs={{16,32},{48,64},{80,96},{112,128},{144,160},{176,192},{208,224},{2... | collective-permute-start | bytes 3145736 | tf_op jit(solution)/shard_map/ppermute | solution.py:225
  103.6 0.0 collective-permute-done.2
  103.6 12.8 %collective-permute-done.1 = bf16[2048,256]{0,1:T(8,128)(2,1)} collective-permute-done((bf16[2048,256]{0,1:T(8,128)(2,1)}, bf16[2048,256]{0,1:T(8,128)(2,1)}, u32[]{:S(2)}, u32[]{:S(2)}) %collective-permute-start.1) | collective-permute-done | bytes 1048608 | tf_op jit(solution)/shard_map/ppermute | solution.py:225
  116.3 1.7 select_select_fusion.3
  118.1 1.3 fusion.1
  119.3 0.1 slice_select_fusion.1
  119.4 0.1 maximum_maximum_fusion.1
  119.5 2.9 %collective-permute-start.3 = (f32[520,256]{1,0:T(8,128)S(1)}, f32[520,256]{1,0:T(8,128)S(1)}, u32[]{:S(2)}, u32[]{:S(2)}) collective-permute-start(f32[520,256]{1,0:T(8,128)S(1)} %maximum_maximum_fusion.1), channel_id=1, source_target_pairs={{0,1},{1,0},{16,23},{23,16},{2,3},{3,2},{18,17},{17,18},{4,5},{5,4... | collective-permute-start | bytes 1597448 | tf_op jit(solution)/shard_map/ppermute | solution.py:40
  122.4 8.3 %collective-permute-done.3 = f32[520,256]{1,0:T(8,128)S(1)} collective-permute-done((f32[520,256]{1,0:T(8,128)S(1)}, f32[520,256]{1,0:T(8,128)S(1)}, u32[]{:S(2)}, u32[]{:S(2)}) %collective-permute-start.3) | collective-permute-done | bytes 532512 | tf_op jit(solution)/shard_map/ppermute | solution.py:40
  130.7 0.9 fusion.16.packed_ref
  131.7 5.6 %shard_map.42 = bf16[512,512]{1,0:T(8,128)(2,1)} custom-call(f32[520,256]{1,0:T(8,128)} %fusion.16.packed_ref), custom_call_target="tpu_custom_call" | custom-call | flops 15728640 | bytes 1048576 | tf_op jit(solution)/shard_map/pallas_call | solution.py:134
  137.3 0.0 copy-start
  137.3 1.8 convolution_convert_fusion.2
  139.1 0.0 copy-done
  139.1 0.8 convolution_convert_fusion.1
  139.9 1.9 %collective-permute-start.5 = (bf16[2048,256]{0,1:T(8,128)(2,1)S(1)}, bf16[2048,256]{0,1:T(8,128)(2,1)S(1)}, u32[]{:S(2)}, u32[]{:S(2)}) collective-permute-start(bf16[2048,256]{0,1:T(8,128)(2,1)S(1)} %convolution_convert_fusion.1), channel_id=1, source_target_pairs={{0,16},{16,0},{1,17},{17,1},{2,18},{18,2},{3,19},{19,3},{4,20},{20... | collective-permute-start | bytes 3145736 | tf_op jit(solution)/shard_map/ppermute | solution.py:224
  141.8 5.8 %collective-permute-start.4 = (bf16[2048,256]{0,1:T(8,128)(2,1)S(1)}, bf16[2048,256]{0,1:T(8,128)(2,1)S(1)}, u32[]{:S(2)}, u32[]{:S(2)}) collective-permute-start(bf16[2048,256]{0,1:T(8,128)(2,1)S(1)} %convolution_convert_fusion.2), channel_id=1, source_target_pairs={{16,32},{48,64},{80,96},{112,128},{144,160},{176,192},{208,224},{2... | collective-permute-start | bytes 3145736 | tf_op jit(solution)/shard_map/ppermute | solution.py:225
  147.6 0.0 collective-permute-done.5
  147.6 12.5 %collective-permute-done.4 = bf16[2048,256]{0,1:T(8,128)(2,1)S(1)} collective-permute-done((bf16[2048,256]{0,1:T(8,128)(2,1)S(1)}, bf16[2048,256]{0,1:T(8,128)(2,1)S(1)}, u32[]{:S(2)}, u32[]{:S(2)}) %collective-permute-start.4) | collective-permute-done | bytes 1048608 | tf_op jit(solution)/shard_map/ppermute | solution.py:225
  160.1 0.2 select_select_fusion.1
  160.3 1.3 fusion
  161.6 0.1 slice_select_fusion
  161.6 0.1 maximum_maximum_fusion.2
  161.8 2.6 %collective-permute-start.6 = (f32[520,256]{1,0:T(8,128)S(1)}, f32[520,256]{1,0:T(8,128)}, u32[]{:S(2)}, u32[]{:S(2)}) collective-permute-start(f32[520,256]{1,0:T(8,128)S(1)} %maximum_maximum_fusion.2), channel_id=1, source_target_pairs={{0,1},{1,0},{16,23},{23,16},{2,3},{3,2},{18,17},{17,18},{4,5},{5,4... | collective-permute-start | bytes 1597448 | tf_op jit(solution)/shard_map/ppermute | solution.py:40
  164.4 8.6 %collective-permute-done.6 = f32[520,256]{1,0:T(8,128)} collective-permute-done((f32[520,256]{1,0:T(8,128)S(1)}, f32[520,256]{1,0:T(8,128)}, u32[]{:S(2)}, u32[]{:S(2)}) %collective-permute-start.6) | collective-permute-done | bytes 532512 | tf_op jit(solution)/shard_map/ppermute | solution.py:40
  173.0 2.0 %fusion.15.packed_ref = f32[520,256]{1,0:T(8,128)} fusion(f32[520,256]{1,0:T(8,128)} %collective-permute-done.6, f32[520]{0:T(1024)S(1)} %pad.15.clone, f32[1,256]{1,0:T(1,128)S(1)} %bitcast.16, f32[256,256]{1,0:T(8,128)S(1)} %get-tuple-element.7, f32[256,256]{1,0:T(8,128)S(1)} %get-tuple-element.6), kind=kLoop, calls=%fused_computation.46 | loop fusion | flops 532480 | bytes 1592352 | tf_op jit(solution)/shard_map/add | solution.py:40
  175.0 5.6 %shard_map.43 = bf16[512,512]{1,0:T(8,128)(2,1)} custom-call(f32[520,256]{1,0:T(8,128)} %fusion.15.packed_ref), custom_call_target="tpu_custom_call" | custom-call | flops 15728640 | bytes 1048576 | tf_op jit(solution)/shard_map/pallas_call | solution.py:134
  180.6 2.3 %multiply_reduce_fusion = (f32[512]{0:T(512)S(1)}, bf16[2048,512]{1,0:T(8,128)(2,1)S(1)}) fusion(bf16[512,512]{1,0:T(8,128)(2,1)} %shard_map.43, bf16[2048,256]{0,1:T(8,128)(2,1)S(1)} %get-tuple-element.3, bf16[2048,256]{0,1:T(8,128)(2,1)S(1)} %get-tuple-element.2), kind=kOutput, calls=%fused_computation | convolution fusion | flops 1082129920 | bytes 4720640 | tf_op jit(solution)/shard_map/dot_general | solution.py:205
  183.0 2.6 %collective-permute-start.7 = (f32[512]{0:T(512)S(1)}, f32[512]{0:T(512)S(1)}, u32[]{:S(2)}, u32[]{:S(2)}) collective-permute-start(f32[512]{0:T(512)S(1)} %get-tuple-element.15), channel_id=1, source_target_pairs={{0,1},{1,0},{16,23},{23,16},{2,3},{3,2},{18,17},{17,18},{4,5},{5,4... | collective-permute-start | bytes 6152 | tf_op jit(solution)/shard_map/ppermute | solution.py:40
  185.6 0.7 constant_dynamic-slice_fusion
  186.3 2.1 %collective-permute-done.7 = f32[512]{0:T(512)S(1)} collective-permute-done((f32[512]{0:T(512)S(1)}, f32[512]{0:T(512)S(1)}, u32[]{:S(2)}, u32[]{:S(2)}) %collective-permute-start.7) | collective-permute-done | bytes 2080 | tf_op jit(solution)/shard_map/ppermute | solution.py:40
  188.4 0.6 add_sqrt_fusion
  (1 shorter events, 0.0 us)
Async XLA Ops:
  3.2 61.5 %all-to-all-start = ((bf16[8,256,512]{2,1,0:T(8,128)(2,1)}), bf16[8,256,512]{2,1,0:T(8,128)(2,1)S(1)}, u32[]{:S(2)}, u32[]{:S(2)}) async-start(bf16[8,256,512]{2,1,0:T(8,128)(2,1)} %broadcast_in_dim.22), calls=%async_computation | async-start | bytes 4194304 | tf_op jit(solution)/shard_map/all_to_all | solution.py:162
  66.3 11.3 %collective-permute-start = (f32[520,256]{1,0:T(8,128)S(1)}, f32[520,256]{1,0:T(8,128)}, u32[]{:S(2)}, u32[]{:S(2)}) collective-permute-start(f32[520,256]{1,0:T(8,128)S(1)} %maximum_maximum_fusion), channel_id=1, source_target_pairs={{0,1},{1,0},{16,23},{23,16},{2,3},{3,2},{18,17},{17,18},{4,5},{5,4... | collective-permute-start | bytes 1597448 | tf_op jit(solution)/shard_map/ppermute | solution.py:40
  85.1 2.8 %copy-start.1 = (bf16[512,512]{1,0:T(8,128)(2,1)S(1)}, bf16[512,512]{1,0:T(8,128)(2,1)}, u32[]{:S(2)}) copy-start(bf16[512,512]{1,0:T(8,128)(2,1)} %shard_map.41) | copy-start | bytes 1572868
  89.7 13.9 %collective-permute-start.2 = (bf16[2048,256]{0,1:T(8,128)(2,1)}, bf16[2048,256]{0,1:T(8,128)(2,1)S(1)}, u32[]{:S(2)}, u32[]{:S(2)}) collective-permute-start(bf16[2048,256]{0,1:T(8,128)(2,1)} %convolution_convert_fusion.3), channel_id=1, source_target_pairs={{0,16},{16,0},{1,17},{17,1},{2,18},{18,2},{3,19},{19,3},{4,20},{20... | collective-permute-start | bytes 3145736 | tf_op jit(solution)/shard_map/ppermute | solution.py:224
  91.6 24.7 %collective-permute-start.1 = (bf16[2048,256]{0,1:T(8,128)(2,1)}, bf16[2048,256]{0,1:T(8,128)(2,1)}, u32[]{:S(2)}, u32[]{:S(2)}) collective-permute-start(bf16[2048,256]{0,1:T(8,128)(2,1)} %convolution_convert_fusion.4), channel_id=1, source_target_pairs={{16,32},{48,64},{80,96},{112,128},{144,160},{176,192},{208,224},{2... | collective-permute-start | bytes 3145736 | tf_op jit(solution)/shard_map/ppermute | solution.py:225
  119.5 11.2 %collective-permute-start.3 = (f32[520,256]{1,0:T(8,128)S(1)}, f32[520,256]{1,0:T(8,128)S(1)}, u32[]{:S(2)}, u32[]{:S(2)}) collective-permute-start(f32[520,256]{1,0:T(8,128)S(1)} %maximum_maximum_fusion.1), channel_id=1, source_target_pairs={{0,1},{1,0},{16,23},{23,16},{2,3},{3,2},{18,17},{17,18},{4,5},{5,4... | collective-permute-start | bytes 1597448 | tf_op jit(solution)/shard_map/ppermute | solution.py:40
  137.3 1.9 copy-start
  139.9 7.8 %collective-permute-start.5 = (bf16[2048,256]{0,1:T(8,128)(2,1)S(1)}, bf16[2048,256]{0,1:T(8,128)(2,1)S(1)}, u32[]{:S(2)}, u32[]{:S(2)}) collective-permute-start(bf16[2048,256]{0,1:T(8,128)(2,1)S(1)} %convolution_convert_fusion.1), channel_id=1, source_target_pairs={{0,16},{16,0},{1,17},{17,1},{2,18},{18,2},{3,19},{19,3},{4,20},{20... | collective-permute-start | bytes 3145736 | tf_op jit(solution)/shard_map/ppermute | solution.py:224
  141.8 18.3 %collective-permute-start.4 = (bf16[2048,256]{0,1:T(8,128)(2,1)S(1)}, bf16[2048,256]{0,1:T(8,128)(2,1)S(1)}, u32[]{:S(2)}, u32[]{:S(2)}) collective-permute-start(bf16[2048,256]{0,1:T(8,128)(2,1)S(1)} %convolution_convert_fusion.2), channel_id=1, source_target_pairs={{16,32},{48,64},{80,96},{112,128},{144,160},{176,192},{208,224},{2... | collective-permute-start | bytes 3145736 | tf_op jit(solution)/shard_map/ppermute | solution.py:225
  161.8 11.3 %collective-permute-start.6 = (f32[520,256]{1,0:T(8,128)S(1)}, f32[520,256]{1,0:T(8,128)}, u32[]{:S(2)}, u32[]{:S(2)}) collective-permute-start(f32[520,256]{1,0:T(8,128)S(1)} %maximum_maximum_fusion.2), channel_id=1, source_target_pairs={{0,1},{1,0},{16,23},{23,16},{2,3},{3,2},{18,17},{17,18},{4,5},{5,4... | collective-permute-start | bytes 1597448 | tf_op jit(solution)/shard_map/ppermute | solution.py:40
  183.0 5.5 %collective-permute-start.7 = (f32[512]{0:T(512)S(1)}, f32[512]{0:T(512)S(1)}, u32[]{:S(2)}, u32[]{:S(2)}) collective-permute-start(f32[512]{0:T(512)S(1)} %get-tuple-element.15), channel_id=1, source_target_pairs={{0,1},{1,0},{16,23},{23,16},{2,3},{3,2},{18,17},{17,18},{4,5},{5,4... | collective-permute-start | bytes 6152 | tf_op jit(solution)/shard_map/ppermute | solution.py:40

commit v9 on v7

--- a/solution.py
+++ b/solution.py
@@ -188,9 +188,8 @@
     width = design.shape[1] // 2
     records = design.shape[0]
     weighted = (design.astype(jnp.float32) * record_weight[:, None]).astype(jnp.bfloat16)
-    weighted = gathered_records(weighted)
-    upper_block = weighted[:, :width]
-    lower_block = weighted[:, width:]
+    upper_block = lax.all_gather(weighted[:, :width], GROUP_AXES, axis=0, tiled=True)
+    lower_block = gathered_records(weighted[:, width:])
     position = lax.axis_index(COLUMN_AXES)
     device_count = lax.axis_size(COLUMN_AXES)
     for round_index in range(ROUNDS):

time: 186 us -> 210 us (1.13)
  the two profiles are of different devices: /device:TPU:2 before, /device:TPU:193 now
where the time goes in v9:
time: 210 us; the launch traced here: 209 us
  waiting for transfers between devices  120 us (57%)
  starting transfers between devices  32.2 us (15%)
  Pallas kernels  16.8 us (8%)
  matrix products  14.3 us (7%)
  between operations  14.2 us (7%)
  other arithmetic  9.03 us (4%)
  local copies, waits for them, and re-layouts  2.58 us (1%)
    all_gather x1, waiting for transfers between devices, local(): lax.all_gather(weighted[:, :width], GROUP_AXES, axis=0, tiled=True)  62.7 us
    ppermute x4, waiting for transfers between devices, from_behind(): lax.ppermute(value, COLUMN_AXES, [(source, source + steps) for source in...  29.2 us
    ppermute x4, waiting for transfers between devices, with_partner(): lax.ppermute(value, PARTNER_AXES, partner_pairs(lax.axis_size('y_hi')))  28 us
    pallas_call x3, Pallas kernels, rotation_of(): pl.pallas_call(sweeps_kernel, out_shape=jax.ShapeDtypeStruct((2 * width,...  16.8 us
    ppermute x4, starting transfers between devices, from_behind(): lax.ppermute(value, COLUMN_AXES, [(source, source + steps) for source in...  12.4 us
    ppermute x4, starting transfers between devices, with_partner(): lax.ppermute(value, PARTNER_AXES, partner_pairs(lax.axis_size('y_hi')))  10.5 us
    all_to_all x1, starting transfers between devices, gathered_records(): gathered = lax.all_to_all(spread, GROUP_AXES, 0, 0, tiled=False)  9.28 us
    dot_general x3, matrix products, inner_products(): lax.dot_general(left_part, right_part, (((0,), (0,)), ((), ())), preferre...  5.38 us
  transfers between devices with their start and end apart: 10, of which 9 were waited for; matrix products, arithmetic and copies ran while one was open for 3% of the time, Pallas kernels for 0%

profile of v9, /device:TPU:193, one launch (start us, length us, event | category | flops | bytes accessed | tf_op | source)
XLA Modules:
  0.0 209.0 jit_solution(1145325040938099674)
XLA Ops:
  7.2 0.0 all-gather.2.cloned.1.call-start
  7.2 1.1 multiply_convert_fusion
  8.3 0.7 fusion.30
  8.9 0.0 all-gather.2.cloned.1.call-update
  9.0 1.1 broadcast_in_dim.22
  10.1 9.3 %all-to-all-start = ((bf16[8,256,256]{2,1,0:T(8,128)(2,1)}), bf16[8,256,256]{2,1,0:T(8,128)(2,1)S(1)}, u32[]{:S(2)}, u32[]{:S(2)}) async-start(bf16[8,256,256]{2,1,0:T(8,128)(2,1)} %broadcast_in_dim.22), calls=%async_computation | async-start | bytes 2097152 | tf_op jit(solution)/shard_map/all_to_all | solution.py:162
  19.4 0.1 pad.15.clone
  19.4 62.7 %all-gather.2.cloned.1.call-done = bf16[2048,256]{1,0:T(8,128)(2,1)} async-done(((bf16[256,256]{1,0:T(8,128)(2,1)}), bf16[2048,256]{1,0:T(8,128)(2,1)}) %all-gather.2.cloned.1.call-update) | async-done | bytes 1048592 | tf_op jit(solution)/shard_map/all_gather | solution.py:191
  82.1 0.0 all-to-all-done
  82.1 2.8 %fusion.2 = f32[512,512]{1,0:T(8,128)S(1)} fusion(bf16[2048,256]{1,0:T(8,128)(2,1)S(1)} %bitcast.5, bf16[2048,256]{1,0:T(8,128)(2,1)} %all-gather.2.cloned.1.call-done), kind=kOutput, calls=%fused_computation.15 | convolution fusion | flops 1077936128 | bytes 3145728 | tf_op jit(solution)/shard_map/dot_general | solution.py:154
  84.9 0.1 slice_select_fusion.2
  85.0 0.1 maximum_maximum_fusion
  85.1 2.3 %collective-permute-start = (f32[520,256]{1,0:T(8,128)S(1)}, f32[520,256]{1,0:T(8,128)S(1)}, u32[]{:S(2)}, u32[]{:S(2)}) collective-permute-start(f32[520,256]{1,0:T(8,128)S(1)} %maximum_maximum_fusion), channel_id=1, source_target_pairs={{0,1},{1,0},{16,23},{23,16},{2,3},{3,2},{18,17},{17,18},{4,5},{5,4... | collective-permute-start | bytes 1597448 | tf_op jit(solution)/shard_map/ppermute | solution.py:40
  87.4 8.9 %collective-permute-done = f32[520,256]{1,0:T(8,128)S(1)} collective-permute-done((f32[520,256]{1,0:T(8,128)S(1)}, f32[520,256]{1,0:T(8,128)S(1)}, u32[]{:S(2)}, u32[]{:S(2)}) %collective-permute-start) | collective-permute-done | bytes 532512 | tf_op jit(solution)/shard_map/ppermute | solution.py:40
  96.3 1.0 fusion.29.packed_ref
  97.3 5.6 %shard_map.41 = bf16[512,512]{1,0:T(8,128)(2,1)} custom-call(f32[520,256]{1,0:T(8,128)} %fusion.29.packed_ref), custom_call_target="tpu_custom_call" | custom-call | flops 15728640 | bytes 1048576 | tf_op jit(solution)/shard_map/pallas_call | solution.py:134
  102.9 0.0 copy-start
  102.9 0.0 copy-start.2
  102.9 2.2 %convolution_convert_fusion.3 = bf16[2048,256]{0,1:T(8,128)(2,1)S(1)} fusion(bf16[2048,256]{1,0:T(8,128)(2,1)S(1)} %bitcast.6, bf16[2048,256]{1,0:T(8,128)(2,1)} %all-gather.2.cloned.1.call-done, pred[]{:T(512)S(6)} %eq.10, bf16[512,512]{1,0:T(8,128)(2,1)} %shard_map.41), kind=kOutput, calls=%fused_computation.4 | convolution fusion | flops 541720576 | bytes 3670017 | tf_op jit(solution)/shard_map/dot_general | solution.py:206
  105.1 6.1 %collective-permute-start.1 = (bf16[2048,256]{0,1:T(8,128)(2,1)S(1)}, bf16[2048,256]{0,1:T(8,128)(2,1)}, u32[]{:S(2)}, u32[]{:S(2)}) collective-permute-start(bf16[2048,256]{0,1:T(8,128)(2,1)S(1)} %convolution_convert_fusion.3), channel_id=1, source_target_pairs={{0,16},{16,32},{32,48},{48,64},{64,80},{80,96},{96,112},{112,128},... | collective-permute-start | bytes 3145736 | tf_op jit(solution)/shard_map/ppermute | solution.py:24
  111.3 0.0 copy-done
  111.3 0.0 copy-done.2
  111.3 1.7 convolution_convert_fusion.4
  113.0 1.9 collective-permute-start.2
  115.0 8.0 %collective-permute-done.1 = bf16[2048,256]{0,1:T(8,128)(2,1)} collective-permute-done((bf16[2048,256]{0,1:T(8,128)(2,1)S(1)}, bf16[2048,256]{0,1:T(8,128)(2,1)}, u32[]{:S(2)}, u32[]{:S(2)}) %collective-permute-start.1) | collective-permute-done | bytes 1048608 | tf_op jit(solution)/shard_map/ppermute | solution.py:24
  123.0 1.3 broadcast_select_fusion.3
  124.3 6.3 %collective-permute-done.2 = bf16[2048,256]{0,1:T(8,128)(2,1)} collective-permute-done((bf16[2048,256]{0,1:T(8,128)(2,1)}, bf16[2048,256]{0,1:T(8,128)(2,1)}, u32[]{:S(2)}, u32[]{:S(2)}) %collective-permute-start.2) | collective-permute-done | bytes 1048608 | tf_op jit(solution)/shard_map/ppermute | solution.py:24
  130.7 1.3 broadcast_select_fusion.1
  132.0 1.3 fusion.1
  133.3 0.1 slice_select_fusion.1
  133.4 0.1 maximum_maximum_fusion.1
  133.5 2.9 %collective-permute-start.3 = (f32[520,256]{1,0:T(8,128)S(1)}, f32[520,256]{1,0:T(8,128)S(1)}, u32[]{:S(2)}, u32[]{:S(2)}) collective-permute-start(f32[520,256]{1,0:T(8,128)S(1)} %maximum_maximum_fusion.1), channel_id=1, source_target_pairs={{0,1},{1,0},{16,23},{23,16},{2,3},{3,2},{18,17},{17,18},{4,5},{5,4... | collective-permute-start | bytes 1597448 | tf_op jit(solution)/shard_map/ppermute | solution.py:40
  136.4 8.4 %collective-permute-done.3 = f32[520,256]{1,0:T(8,128)S(1)} collective-permute-done((f32[520,256]{1,0:T(8,128)S(1)}, f32[520,256]{1,0:T(8,128)S(1)}, u32[]{:S(2)}, u32[]{:S(2)}) %collective-permute-start.3) | collective-permute-done | bytes 532512 | tf_op jit(solution)/shard_map/ppermute | solution.py:40
  144.7 0.9 fusion.28.packed_ref
  145.7 5.6 %shard_map.42 = bf16[512,512]{1,0:T(8,128)(2,1)} custom-call(f32[520,256]{1,0:T(8,128)} %fusion.28.packed_ref), custom_call_target="tpu_custom_call" | custom-call | flops 15728640 | bytes 1048576 | tf_op jit(solution)/shard_map/pallas_call | solution.py:134
  151.3 0.0 copy-start.1
  151.3 1.8 convolution_convert_fusion.1
  153.1 1.9 collective-permute-start.4
  155.1 0.0 copy-done.1
  155.1 0.8 convolution_convert_fusion.2
  155.8 2.4 %collective-permute-start.5 = (bf16[2048,256]{0,1:T(8,128)(2,1)S(1)}, bf16[2048,256]{0,1:T(8,128)(2,1)S(1)}, u32[]{:S(2)}, u32[]{:S(2)}) collective-permute-start(bf16[2048,256]{0,1:T(8,128)(2,1)S(1)} %convolution_convert_fusion.2), channel_id=1, source_target_pairs={{16,0},{32,16},{48,32},{64,48},{80,64},{96,80},{112,96},{128,112},... | collective-permute-start | bytes 3145736 | tf_op jit(solution)/shard_map/ppermute | solution.py:24
  158.3 8.5 %collective-permute-done.4 = bf16[2048,256]{0,1:T(8,128)(2,1)S(1)} collective-permute-done((bf16[2048,256]{0,1:T(8,128)(2,1)S(1)}, bf16[2048,256]{0,1:T(8,128)(2,1)S(1)}, u32[]{:S(2)}, u32[]{:S(2)}) %collective-permute-start.4) | collective-permute-done | bytes 1048608 | tf_op jit(solution)/shard_map/ppermute | solution.py:24
  166.8 0.1 broadcast_select_fusion.2
  166.9 6.3 %collective-permute-done.5 = bf16[2048,256]{0,1:T(8,128)(2,1)S(1)} collective-permute-done((bf16[2048,256]{0,1:T(8,128)(2,1)S(1)}, bf16[2048,256]{0,1:T(8,128)(2,1)S(1)}, u32[]{:S(2)}, u32[]{:S(2)}) %collective-permute-start.5) | collective-permute-done | bytes 1048608 | tf_op jit(solution)/shard_map/ppermute | solution.py:24
  173.2 0.1 broadcast_select_fusion
  173.3 1.3 fusion
  174.6 0.1 slice_select_fusion
  174.6 0.1 maximum_maximum_fusion.2
  174.8 2.7 %collective-permute-start.6 = (f32[520,256]{1,0:T(8,128)S(1)}, f32[520,256]{1,0:T(8,128)}, u32[]{:S(2)}, u32[]{:S(2)}) collective-permute-start(f32[520,256]{1,0:T(8,128)S(1)} %maximum_maximum_fusion.2), channel_id=1, source_target_pairs={{0,1},{1,0},{16,23},{23,16},{2,3},{3,2},{18,17},{17,18},{4,5},{5,4... | collective-permute-start | bytes 1597448 | tf_op jit(solution)/shard_map/ppermute | solution.py:40
  177.5 8.6 %collective-permute-done.6 = f32[520,256]{1,0:T(8,128)} collective-permute-done((f32[520,256]{1,0:T(8,128)S(1)}, f32[520,256]{1,0:T(8,128)}, u32[]{:S(2)}, u32[]{:S(2)}) %collective-permute-start.6) | collective-permute-done | bytes 532512 | tf_op jit(solution)/shard_map/ppermute | solution.py:40
  186.1 2.0 fusion.27.packed_ref
  188.1 5.6 %shard_map.43 = bf16[512,512]{1,0:T(8,128)(2,1)} custom-call(f32[520,256]{1,0:T(8,128)} %fusion.27.packed_ref), custom_call_target="tpu_custom_call" | custom-call | flops 15728640 | bytes 1048576 | tf_op jit(solution)/shard_map/pallas_call | solution.py:134
  193.7 2.4 %multiply_reduce_fusion = (f32[512]{0:T(512)S(1)}, bf16[2048,512]{1,0:T(8,128)(2,1)S(1)}) fusion(bf16[512,512]{1,0:T(8,128)(2,1)} %shard_map.43, bf16[2048,256]{0,1:T(8,128)(2,1)S(1)} %broadcast_select_fusion, bf16[2048,256]{0,1:T(8,128)(2,1)S(1)} %broadcast_select_fusion.2), kind=kOutput, calls=%fused_computation | convolution fusion | flops 1082129920 | bytes 4720640 | tf_op jit(solution)/shard_map/dot_general | solution.py:200
  196.1 2.7 %collective-permute-start.7 = (f32[512]{0:T(512)S(1)}, f32[512]{0:T(512)S(1)}, u32[]{:S(2)}, u32[]{:S(2)}) collective-permute-start(f32[512]{0:T(512)S(1)} %get-tuple-element.13), channel_id=1, source_target_pairs={{0,1},{1,0},{16,23},{23,16},{2,3},{3,2},{18,17},{17,18},{4,5},{5,4... | collective-permute-start | bytes 6152 | tf_op jit(solution)/shard_map/ppermute | solution.py:40
  198.7 0.7 constant_dynamic-slice_fusion
  199.5 2.1 %collective-permute-done.7 = f32[512]{0:T(512)S(1)} collective-permute-done((f32[512]{0:T(512)S(1)}, f32[512]{0:T(512)S(1)}, u32[]{:S(2)}, u32[]{:S(2)}) %collective-permute-start.7) | collective-permute-done | bytes 2080 | tf_op jit(solution)/shard_map/ppermute | solution.py:40
  201.6 0.6 add_sqrt_fusion
  (1 shorter events, 0.0 us)
Async XLA Ops:
  7.2 74.9 %all-gather.2.cloned.1.call-start = ((), (), s32[]{:S(2)}) async-start(), calls=%async_computation.1 | async-start | bytes 1179648 | tf_op jit(solution)/shard_map/all_gather | solution.py:191
  10.1 72.0 %all-to-all-start = ((bf16[8,256,256]{2,1,0:T(8,128)(2,1)}), bf16[8,256,256]{2,1,0:T(8,128)(2,1)S(1)}, u32[]{:S(2)}, u32[]{:S(2)}) async-start(bf16[8,256,256]{2,1,0:T(8,128)(2,1)} %broadcast_in_dim.22), calls=%async_computation | async-start | bytes 2097152 | tf_op jit(solution)/shard_map/all_to_all | solution.py:162
  85.1 11.2 %collective-permute-start = (f32[520,256]{1,0:T(8,128)S(1)}, f32[520,256]{1,0:T(8,128)S(1)}, u32[]{:S(2)}, u32[]{:S(2)}) collective-permute-start(f32[520,256]{1,0:T(8,128)S(1)} %maximum_maximum_fusion), channel_id=1, source_target_pairs={{0,1},{1,0},{16,23},{23,16},{2,3},{3,2},{18,17},{17,18},{4,5},{5,4... | collective-permute-start | bytes 1597448 | tf_op jit(solution)/shard_map/ppermute | solution.py:40
  102.9 8.4 %copy-start = (bf16[512,512]{1,0:T(8,128)(2,1)S(1)}, bf16[512,512]{1,0:T(8,128)(2,1)}, u32[]{:S(2)}) copy-start(bf16[512,512]{1,0:T(8,128)(2,1)} %shard_map.41) | copy-start | bytes 1572868
  102.9 8.4 %copy-start.2 = (bf16[2048,256]{1,0:T(8,128)(2,1)S(1)}, bf16[2048,256]{1,0:T(8,128)(2,1)}, u32[]{:S(2)}) copy-start(bf16[2048,256]{1,0:T(8,128)(2,1)} %all-gather.2.cloned.1.call-done) | copy-start | bytes 3145732
  105.1 17.8 %collective-permute-start.1 = (bf16[2048,256]{0,1:T(8,128)(2,1)S(1)}, bf16[2048,256]{0,1:T(8,128)(2,1)}, u32[]{:S(2)}, u32[]{:S(2)}) collective-permute-start(bf16[2048,256]{0,1:T(8,128)(2,1)S(1)} %convolution_convert_fusion.3), channel_id=1, source_target_pairs={{0,16},{16,32},{32,48},{48,64},{64,80},{80,96},{96,112},{112,128},... | collective-permute-start | bytes 3145736 | tf_op jit(solution)/shard_map/ppermute | solution.py:24
  113.0 17.6 %collective-permute-start.2 = (bf16[2048,256]{0,1:T(8,128)(2,1)}, bf16[2048,256]{0,1:T(8,128)(2,1)}, u32[]{:S(2)}, u32[]{:S(2)}) collective-permute-start(bf16[2048,256]{0,1:T(8,128)(2,1)} %convolution_convert_fusion.4), channel_id=1, source_target_pairs={{16,0},{32,16},{48,32},{64,48},{80,64},{96,80},{112,96},{128,112},... | collective-permute-start | bytes 3145736 | tf_op jit(solution)/shard_map/ppermute | solution.py:24
  133.5 11.2 %collective-permute-start.3 = (f32[520,256]{1,0:T(8,128)S(1)}, f32[520,256]{1,0:T(8,128)S(1)}, u32[]{:S(2)}, u32[]{:S(2)}) collective-permute-start(f32[520,256]{1,0:T(8,128)S(1)} %maximum_maximum_fusion.1), channel_id=1, source_target_pairs={{0,1},{1,0},{16,23},{23,16},{2,3},{3,2},{18,17},{17,18},{4,5},{5,4... | collective-permute-start | bytes 1597448 | tf_op jit(solution)/shard_map/ppermute | solution.py:40
  151.3 3.8 %copy-start.1 = (bf16[512,512]{1,0:T(8,128)(2,1)S(1)}, bf16[512,512]{1,0:T(8,128)(2,1)}, u32[]{:S(2)}) copy-start(bf16[512,512]{1,0:T(8,128)(2,1)} %shard_map.42) | copy-start | bytes 1572868
  153.1 13.7 %collective-permute-start.4 = (bf16[2048,256]{0,1:T(8,128)(2,1)S(1)}, bf16[2048,256]{0,1:T(8,128)(2,1)S(1)}, u32[]{:S(2)}, u32[]{:S(2)}) collective-permute-start(bf16[2048,256]{0,1:T(8,128)(2,1)S(1)} %convolution_convert_fusion.1), channel_id=1, source_target_pairs={{0,16},{16,32},{32,48},{48,64},{64,80},{80,96},{96,112},{112,128},... | collective-permute-start | bytes 3145736 | tf_op jit(solution)/shard_map/ppermute | solution.py:24
  155.8 17.3 %collective-permute-start.5 = (bf16[2048,256]{0,1:T(8,128)(2,1)S(1)}, bf16[2048,256]{0,1:T(8,128)(2,1)S(1)}, u32[]{:S(2)}, u32[]{:S(2)}) collective-permute-start(bf16[2048,256]{0,1:T(8,128)(2,1)S(1)} %convolution_convert_fusion.2), channel_id=1, source_target_pairs={{16,0},{32,16},{48,32},{64,48},{80,64},{96,80},{112,96},{128,112},... | collective-permute-start | bytes 3145736 | tf_op jit(solution)/shard_map/ppermute | solution.py:24
  174.8 11.3 %collective-permute-start.6 = (f32[520,256]{1,0:T(8,128)S(1)}, f32[520,256]{1,0:T(8,128)}, u32[]{:S(2)}, u32[]{:S(2)}) collective-permute-start(f32[520,256]{1,0:T(8,128)S(1)} %maximum_maximum_fusion.2), channel_id=1, source_target_pairs={{0,1},{1,0},{16,23},{23,16},{2,3},{3,2},{18,17},{17,18},{4,5},{5,4... | collective-permute-start | bytes 1597448 | tf_op jit(solution)/shard_map/ppermute | solution.py:40
  196.1 5.5 %collective-permute-start.7 = (f32[512]{0:T(512)S(1)}, f32[512]{0:T(512)S(1)}, u32[]{:S(2)}, u32[]{:S(2)}) collective-permute-start(f32[512]{0:T(512)S(1)} %get-tuple-element.13), channel_id=1, source_target_pairs={{0,1},{1,0},{16,23},{23,16},{2,3},{3,2},{18,17},{17,18},{4,5},{5,4... | collective-permute-start | bytes 6152 | tf_op jit(solution)/shard_map/ppermute | solution.py:40
Sparse Core Ops, SparseCore 0:
  11.8 70.2 all-gather.1

commit v10 on v7

--- a/solution.py
+++ b/solution.py
@@ -36,8 +36,12 @@
     return pairs
 
 
+def from_partner(value):
+    return lax.ppermute(value, PARTNER_AXES, partner_pairs(lax.axis_size("y_hi")))
+
+
 def with_partner(value):
-    return value + lax.ppermute(value, PARTNER_AXES, partner_pairs(lax.axis_size("y_hi")))
+    return value + from_partner(value)
 
 
 def diagonal_of(matrix):
@@ -65,14 +69,14 @@
     return cosine, sine_value
 
 
-def sweeps_kernel(packed_ref, rotation_ref):
-    width = packed_ref.shape[1]
+def sweeps_kernel(local_ref, received_ref, rotation_ref):
+    width = local_ref.shape[1]
     rows = lax.broadcasted_iota(jnp.int32, (width, width), 0)
     cols = lax.broadcasted_iota(jnp.int32, (width, width), 1)
     on_diagonal = rows == cols
-    folded = packed_ref[:width, :]
-    top_right = packed_ref[width : 2 * width, :]
-    low_diag = packed_ref[2 * width : 2 * width + 8, :][:1, :]
+    folded = local_ref[:width, :] + received_ref[:width, :]
+    top_right = local_ref[width : 2 * width, :] + received_ref[width : 2 * width, :]
+    low_diag = (local_ref[2 * width : 2 * width + 8, :] + received_ref[2 * width : 2 * width + 8, :])[:1, :]
     mirrored = folded.T
     top_left = jnp.where(rows <= cols, folded, mirrored)
     low_right = jnp.where(rows > cols, folded, jnp.where(rows < cols, mirrored, low_diag))
@@ -128,18 +132,18 @@
     rotation_ref[width:, width:] = second_low.astype(out)
 
 
-def rotation_of(packed):
-    width = packed.shape[1]
+def rotation_of(local, received):
+    width = local.shape[1]
     vmem = pl.BlockSpec(memory_space=pltpu.VMEM)
     return pl.pallas_call(
         sweeps_kernel,
         out_shape=jax.ShapeDtypeStruct((2 * width, 2 * width), jnp.bfloat16),
-        in_specs=[vmem],
+        in_specs=[vmem, vmem],
         out_specs=vmem,
         cost_estimate=pl.CostEstimate(
             flops=SWEEPS * 40 * width * width, transcendentals=SWEEPS * 8 * width, bytes_accessed=4 * 4 * width * width
         ),
-    )(packed)
+    )(local, received)
 
 
 def send_right(block):
@@ -181,7 +185,7 @@
         ],
         axis=0,
     )
-    return with_partner(packed)
+    return packed, from_partner(packed)
 
 
 def local(design, record_weight):
@@ -196,7 +200,7 @@
     for round_index in range(ROUNDS):
         moving = round_index + 1 < ROUNDS
         pair_data = jnp.concatenate([upper_block, lower_block], axis=1)
-        rotation = rotation_of(summed_gram(pair_data, width))
+        rotation = rotation_of(*summed_gram(pair_data, width))
         if not moving:
             rotated = jnp.dot(pair_data, rotation, preferred_element_type=jnp.float32)
             upper_block = rotated[:, :width].astype(jnp.bfloat16)

time: 186 us -> 184 us (0.989)
  other arithmetic: 10 us -> 5.14 us
  local copies, waits for them, and re-layouts: 2.32 us -> 4.76 us
    add x3 -> x0, other arithmetic: 4.89 us -> none  [with_partner(): value + lax.ppermute(value, PARTNER_AXES, partner_pairs(lax.axis_size('y_...]
    unnamed x4 -> x20, local copies, waits for them, and re-layouts: 0.01 us -> 2.45 us
where the time goes in v10:
time: 184 us
  waiting for transfers between devices  106 us (58%)
  starting transfers between devices  37.4 us (20%)
  Pallas kernels  17.4 us (9%)
  matrix products  12.4 us (7%)
  other arithmetic  5.14 us (3%)
  local copies, waits for them, and re-layouts  4.76 us (3%)
    all_to_all x1, waiting for transfers between devices, gathered_records(): gathered = lax.all_to_all(spread, GROUP_AXES, 0, 0, tiled=False)  52.8 us
    ppermute x4, waiting for transfers between devices, from_partner(): lax.ppermute(value, PARTNER_AXES, partner_pairs(lax.axis_size('y_hi')))  29.5 us
    ppermute x4, waiting for transfers between devices, from_behind(): lax.ppermute(value, COLUMN_AXES, [(source, source + steps) for source in...  23.4 us
    ppermute x4, starting transfers between devices, from_behind(): lax.ppermute(value, COLUMN_AXES, [(source, source + steps) for source in...  20 us
    pallas_call x3, Pallas kernels, rotation_of(): pl.pallas_call(sweeps_kernel, out_shape=jax.ShapeDtypeStruct((2 * width,...  17.4 us
    ppermute x4, starting transfers between devices, from_partner(): lax.ppermute(value, PARTNER_AXES, partner_pairs(lax.axis_size('y_hi')))  8.77 us
    all_to_all x1, starting transfers between devices, gathered_records(): gathered = lax.all_to_all(spread, GROUP_AXES, 0, 0, tiled=False)  8.66 us
    dot_general x3, matrix products, inner_products(): lax.dot_general(left_part, right_part, (((0,), (0,)), ((), ())), preferre...  3.84 us
  transfers between devices with their start and end apart: 9, of which 9 were waited for; matrix products, arithmetic and copies ran while one was open for 3% of the time, Pallas kernels for 0%

profile of v10, /device:TPU:2, one launch (start us, length us, event | category | flops | bytes accessed | tf_op | source)
XLA Modules:
  0.0 183.8 jit_solution(14013246927280854796)
XLA Ops:
  0.6 1.1 multiply_convert_fusion
  1.7 1.5 broadcast_in_dim.22
  3.2 8.7 %all-to-all-start = ((bf16[8,256,512]{2,1,0:T(8,128)(2,1)}), bf16[8,256,512]{2,1,0:T(8,128)(2,1)S(1)}, u32[]{:S(2)}, u32[]{:S(2)}) async-start(bf16[8,256,512]{2,1,0:T(8,128)(2,1)} %broadcast_in_dim.22), calls=%async_computation | async-start | bytes 4194304 | tf_op jit(solution)/shard_map/all_to_all | solution.py:166
  11.9 0.1 pad.15.clone
  11.9 52.8 %all-to-all-done = bf16[8,256,512]{2,1,0:T(8,128)(2,1)S(1)} async-done(((bf16[8,256,512]{2,1,0:T(8,128)(2,1)}), bf16[8,256,512]{2,1,0:T(8,128)(2,1)S(1)}, u32[]{:S(2)}, u32[]{:S(2)}) %all-to-all-start) | async-done | bytes 2097184 | tf_op jit(solution)/shard_map/all_to_all | solution.py:166
  64.8 1.3 convolution_bitcast_fusion
  66.0 0.1 slice_select_fusion.2
  66.1 0.1 maximum_maximum_fusion.local_ref
  66.2 0.0 copy-start
  66.2 2.7 %collective-permute-start = (f32[520,256]{1,0:T(8,128)S(1)}, f32[520,256]{1,0:T(8,128)S(1)}, u32[]{:S(2)}, u32[]{:S(2)}) collective-permute-start(f32[520,256]{1,0:T(8,128)S(1)} %maximum_maximum_fusion.local_ref), channel_id=1, source_target_pairs={{0,1},{1,0},{16,23},{23,16},{2,3},{3,2},{18,17},{17,18},{4,5},{5,4... | collective-permute-start | bytes 1597448 | tf_op jit(solution)/shard_map/ppermute | solution.py:40
  69.0 8.4 %collective-permute-done.received_ref = f32[520,256]{1,0:T(8,128)S(1)} collective-permute-done((f32[520,256]{1,0:T(8,128)S(1)}, f32[520,256]{1,0:T(8,128)S(1)}, u32[]{:S(2)}, u32[]{:S(2)}) %collective-permute-start) | collective-permute-done | bytes 532512 | tf_op jit(solution)/shard_map/ppermute | solution.py:40
  77.4 0.0 copy-done
  77.4 0.0 copy-start.6
  77.4 0.8 copy-done.6
  78.2 5.8 %shard_map.41 = bf16[512,512]{1,0:T(8,128)(2,1)} custom-call(f32[520,256]{1,0:T(8,128)} %copy-done, f32[520,256]{1,0:T(8,128)} %copy-done.6), custom_call_target="tpu_custom_call" | custom-call | flops 15728640 | bytes 1048576 | tf_op jit(solution)/shard_map/pallas_call | solution.py:138
  84.0 0.0 copy-start.3
  84.0 1.8 %convolution_convert_fusion.3 = bf16[2048,256]{0,1:T(8,128)(2,1)S(1)} fusion(bf16[2048,512]{1,0:T(8,128)(2,1)S(1)} %bitcast.11, pred[]{:T(512)S(6)} %eq.10, bf16[512,512]{1,0:T(8,128)(2,1)} %shard_map.41), kind=kOutput, calls=%fused_computation.4 | convolution fusion | flops 537526272 | bytes 3670017 | tf_op jit(solution)/shard_map/dot_general | solution.py:211
  85.9 1.9 %collective-permute-start.1 = (bf16[2048,256]{0,1:T(8,128)(2,1)S(1)}, bf16[2048,256]{0,1:T(8,128)(2,1)}, u32[]{:S(2)}, u32[]{:S(2)}) collective-permute-start(bf16[2048,256]{0,1:T(8,128)(2,1)S(1)} %convolution_convert_fusion.3), channel_id=1, source_target_pairs={{0,16},{16,32},{32,48},{48,64},{64,80},{80,96},{96,112},{112,128},... | collective-permute-start | bytes 3145736 | tf_op jit(solution)/shard_map/ppermute | solution.py:24
  87.8 0.0 copy-done.3
  87.8 1.8 convolution_convert_fusion.4
  89.6 10.2 %collective-permute-start.2 = (bf16[2048,256]{0,1:T(8,128)(2,1)}, bf16[2048,256]{0,1:T(8,128)(2,1)}, u32[]{:S(2)}, u32[]{:S(2)}) collective-permute-start(bf16[2048,256]{0,1:T(8,128)(2,1)} %convolution_convert_fusion.4), channel_id=1, source_target_pairs={{16,0},{32,16},{48,32},{64,48},{80,64},{96,80},{112,96},{128,112},... | collective-permute-start | bytes 3145736 | tf_op jit(solution)/shard_map/ppermute | solution.py:24
  99.8 8.9 %collective-permute-done.1 = bf16[2048,256]{0,1:T(8,128)(2,1)} collective-permute-done((bf16[2048,256]{0,1:T(8,128)(2,1)S(1)}, bf16[2048,256]{0,1:T(8,128)(2,1)}, u32[]{:S(2)}, u32[]{:S(2)}) %collective-permute-start.1) | collective-permute-done | bytes 1048608 | tf_op jit(solution)/shard_map/ppermute | solution.py:24
  108.6 1.3 broadcast_select_fusion.3
  110.0 2.4 %collective-permute-done.2 = bf16[2048,256]{0,1:T(8,128)(2,1)} collective-permute-done((bf16[2048,256]{0,1:T(8,128)(2,1)}, bf16[2048,256]{0,1:T(8,128)(2,1)}, u32[]{:S(2)}, u32[]{:S(2)}) %collective-permute-start.2) | collective-permute-done | bytes 1048608 | tf_op jit(solution)/shard_map/ppermute | solution.py:24
  112.4 1.3 broadcast_select_fusion.1
  113.7 0.0 copy-start.4
  113.7 1.3 fusion.1
  115.0 0.0 copy-done.4
  115.0 0.1 slice_select_fusion.1
  115.1 0.0 copy-start.5
  115.1 0.1 maximum_maximum_fusion.1.local_ref
  115.2 0.0 copy-start.2
  115.2 2.2 %collective-permute-start.3 = (f32[520,256]{1,0:T(8,128)S(1)}, f32[520,256]{1,0:T(8,128)S(1)}, u32[]{:S(2)}, u32[]{:S(2)}) collective-permute-start(f32[520,256]{1,0:T(8,128)S(1)} %maximum_maximum_fusion.1.local_ref), channel_id=1, source_target_pairs={{0,1},{1,0},{16,23},{23,16},{2,3},{3,2},{18,17},{17,18},{4,5},{5,4... | collective-permute-start | bytes 1597448 | tf_op jit(solution)/shard_map/ppermute | solution.py:40
  117.5 9.1 %collective-permute-done.3.received_ref = f32[520,256]{1,0:T(8,128)S(1)} collective-permute-done((f32[520,256]{1,0:T(8,128)S(1)}, f32[520,256]{1,0:T(8,128)S(1)}, u32[]{:S(2)}, u32[]{:S(2)}) %collective-permute-start.3) | collective-permute-done | bytes 532512 | tf_op jit(solution)/shard_map/ppermute | solution.py:40
  126.5 0.0 copy-done.2
  126.5 0.0 copy-start.8
  126.5 0.8 copy-done.8
  127.3 5.8 %shard_map.42 = bf16[512,512]{1,0:T(8,128)(2,1)} custom-call(f32[520,256]{1,0:T(8,128)} %copy-done.2, f32[520,256]{1,0:T(8,128)} %copy-done.8), custom_call_target="tpu_custom_call" | custom-call | flops 15728640 | bytes 1048576 | tf_op jit(solution)/shard_map/pallas_call | solution.py:138
  133.1 0.0 copy-done.5
  133.1 0.0 copy-start.9
  133.1 1.8 %convolution_convert_fusion.1 = bf16[2048,256]{0,1:T(8,128)(2,1)S(1)} fusion(bf16[2048,256]{0,1:T(8,128)(2,1)S(1)} %copy-done.5, bf16[2048,256]{0,1:T(8,128)(2,1)S(1)} %broadcast_select_fusion.3, pred[]{:T(512)S(6)} %eq.10, bf16[512,512]{1,0:T(8,128)(2,1)} %shard_map.42), kind=kOutput, calls=%fused_computation.2 | convolution fusion | flops 541720576 | bytes 3670017 | tf_op jit(solution)/shard_map/dot_general | solution.py:211
  135.0 1.9 %collective-permute-start.4 = (bf16[2048,256]{0,1:T(8,128)(2,1)S(1)}, bf16[2048,256]{0,1:T(8,128)(2,1)S(1)}, u32[]{:S(2)}, u32[]{:S(2)}) collective-permute-start(bf16[2048,256]{0,1:T(8,128)(2,1)S(1)} %convolution_convert_fusion.1), channel_id=1, source_target_pairs={{0,16},{16,32},{32,48},{48,64},{64,80},{80,96},{96,112},{112,128},... | collective-permute-start | bytes 3145736 | tf_op jit(solution)/shard_map/ppermute | solution.py:24
  136.9 0.0 copy-done.9
  136.9 0.8 convolution_convert_fusion.2
  137.7 6.0 %collective-permute-start.5 = (bf16[2048,256]{0,1:T(8,128)(2,1)S(1)}, bf16[2048,256]{0,1:T(8,128)(2,1)S(1)}, u32[]{:S(2)}, u32[]{:S(2)}) collective-permute-start(bf16[2048,256]{0,1:T(8,128)(2,1)S(1)} %convolution_convert_fusion.2), channel_id=1, source_target_pairs={{16,0},{32,16},{48,32},{64,48},{80,64},{96,80},{112,96},{128,112},... | collective-permute-start | bytes 3145736 | tf_op jit(solution)/shard_map/ppermute | solution.py:24
  143.7 9.8 %collective-permute-done.4 = bf16[2048,256]{0,1:T(8,128)(2,1)S(1)} collective-permute-done((bf16[2048,256]{0,1:T(8,128)(2,1)S(1)}, bf16[2048,256]{0,1:T(8,128)(2,1)S(1)}, u32[]{:S(2)}, u32[]{:S(2)}) %collective-permute-start.4) | collective-permute-done | bytes 1048608 | tf_op jit(solution)/shard_map/ppermute | solution.py:24
  153.4 0.1 broadcast_select_fusion.2
  153.5 2.4 %collective-permute-done.5 = bf16[2048,256]{0,1:T(8,128)(2,1)S(1)} collective-permute-done((bf16[2048,256]{0,1:T(8,128)(2,1)S(1)}, bf16[2048,256]{0,1:T(8,128)(2,1)S(1)}, u32[]{:S(2)}, u32[]{:S(2)}) %collective-permute-start.5) | collective-permute-done | bytes 1048608 | tf_op jit(solution)/shard_map/ppermute | solution.py:24
  156.0 0.1 broadcast_select_fusion
  156.1 1.3 fusion
  157.4 0.1 slice_select_fusion
  157.4 0.1 maximum_maximum_fusion.2.local_ref
  157.6 0.0 copy-start.1
  157.6 1.9 %collective-permute-start.6 = (f32[520,256]{1,0:T(8,128)S(1)}, f32[520,256]{1,0:T(8,128)S(1)}, u32[]{:S(2)}, u32[]{:S(2)}) collective-permute-start(f32[520,256]{1,0:T(8,128)S(1)} %maximum_maximum_fusion.2.local_ref), channel_id=1, source_target_pairs={{0,1},{1,0},{16,23},{23,16},{2,3},{3,2},{18,17},{17,18},{4,5},{5,4... | collective-permute-start | bytes 1597448 | tf_op jit(solution)/shard_map/ppermute | solution.py:40
  159.5 9.2 %collective-permute-done.6.received_ref = f32[520,256]{1,0:T(8,128)S(1)} collective-permute-done((f32[520,256]{1,0:T(8,128)S(1)}, f32[520,256]{1,0:T(8,128)S(1)}, u32[]{:S(2)}, u32[]{:S(2)}) %collective-permute-start.6) | collective-permute-done | bytes 532512 | tf_op jit(solution)/shard_map/ppermute | solution.py:40
  168.7 0.0 copy-done.1
  168.7 0.0 copy-start.7
  168.7 0.8 copy-done.7
  169.5 5.8 %shard_map.43 = bf16[512,512]{1,0:T(8,128)(2,1)} custom-call(f32[520,256]{1,0:T(8,128)} %copy-done.1, f32[520,256]{1,0:T(8,128)} %copy-done.7), custom_call_target="tpu_custom_call" | custom-call | flops 15728640 | bytes 1048576 | tf_op jit(solution)/shard_map/pallas_call | solution.py:138
  175.3 2.3 %multiply_reduce_fusion = (f32[512]{0:T(512)S(1)}, bf16[2048,512]{1,0:T(8,128)(2,1)S(1)}) fusion(bf16[512,512]{1,0:T(8,128)(2,1)} %shard_map.43, bf16[2048,256]{0,1:T(8,128)(2,1)S(1)} %broadcast_select_fusion, bf16[2048,256]{0,1:T(8,128)(2,1)S(1)} %broadcast_select_fusion.2), kind=kOutput, calls=%fused_computation | convolution fusion | flops 1082129920 | bytes 4720640 | tf_op jit(solution)/shard_map/dot_general | solution.py:205
  177.7 1.9 %collective-permute-start.7 = (f32[512]{0:T(512)S(1)}, f32[512]{0:T(512)S(1)}, u32[]{:S(2)}, u32[]{:S(2)}) collective-permute-start(f32[512]{0:T(512)S(1)} %get-tuple-element.11), channel_id=1, source_target_pairs={{0,1},{1,0},{16,23},{23,16},{2,3},{3,2},{18,17},{17,18},{4,5},{5,4... | collective-permute-start | bytes 6152 | tf_op jit(solution)/shard_map/ppermute | solution.py:40
  179.6 0.7 constant_dynamic-slice_fusion
  180.4 2.8 %collective-permute-done.7 = f32[512]{0:T(512)S(1)} collective-permute-done((f32[512]{0:T(512)S(1)}, f32[512]{0:T(512)S(1)}, u32[]{:S(2)}, u32[]{:S(2)}) %collective-permute-start.7) | collective-permute-done | bytes 2080 | tf_op jit(solution)/shard_map/ppermute | solution.py:40
  183.2 0.6 add_sqrt_fusion
  (1 shorter events, 0.0 us)
Async XLA Ops:
  3.2 61.5 %all-to-all-start = ((bf16[8,256,512]{2,1,0:T(8,128)(2,1)}), bf16[8,256,512]{2,1,0:T(8,128)(2,1)S(1)}, u32[]{:S(2)}, u32[]{:S(2)}) async-start(bf16[8,256,512]{2,1,0:T(8,128)(2,1)} %broadcast_in_dim.22), calls=%async_computation | async-start | bytes 4194304 | tf_op jit(solution)/shard_map/all_to_all | solution.py:166
  66.2 11.2 %copy-start = (f32[520,256]{1,0:T(8,128)}, f32[520,256]{1,0:T(8,128)S(1)}, u32[]{:S(2)}) copy-start(f32[520,256]{1,0:T(8,128)S(1)} %maximum_maximum_fusion.local_ref) | copy-start | bytes 1597444
  66.2 11.2 %collective-permute-start = (f32[520,256]{1,0:T(8,128)S(1)}, f32[520,256]{1,0:T(8,128)S(1)}, u32[]{:S(2)}, u32[]{:S(2)}) collective-permute-start(f32[520,256]{1,0:T(8,128)S(1)} %maximum_maximum_fusion.local_ref), channel_id=1, source_target_pairs={{0,1},{1,0},{16,23},{23,16},{2,3},{3,2},{18,17},{17,18},{4,5},{5,4... | collective-permute-start | bytes 1597448 | tf_op jit(solution)/shard_map/ppermute | solution.py:40
  77.4 0.8 copy-start.6
  84.0 3.8 %copy-start.3 = (bf16[512,512]{1,0:T(8,128)(2,1)S(1)}, bf16[512,512]{1,0:T(8,128)(2,1)}, u32[]{:S(2)}) copy-start(bf16[512,512]{1,0:T(8,128)(2,1)} %shard_map.41) | copy-start | bytes 1572868
  85.9 22.8 %collective-permute-start.1 = (bf16[2048,256]{0,1:T(8,128)(2,1)S(1)}, bf16[2048,256]{0,1:T(8,128)(2,1)}, u32[]{:S(2)}, u32[]{:S(2)}) collective-permute-start(bf16[2048,256]{0,1:T(8,128)(2,1)S(1)} %convolution_convert_fusion.3), channel_id=1, source_target_pairs={{0,16},{16,32},{32,48},{48,64},{64,80},{80,96},{96,112},{112,128},... | collective-permute-start | bytes 3145736 | tf_op jit(solution)/shard_map/ppermute | solution.py:24
  89.6 22.8 %collective-permute-start.2 = (bf16[2048,256]{0,1:T(8,128)(2,1)}, bf16[2048,256]{0,1:T(8,128)(2,1)}, u32[]{:S(2)}, u32[]{:S(2)}) collective-permute-start(bf16[2048,256]{0,1:T(8,128)(2,1)} %convolution_convert_fusion.4), channel_id=1, source_target_pairs={{16,0},{32,16},{48,32},{64,48},{80,64},{96,80},{112,96},{128,112},... | collective-permute-start | bytes 3145736 | tf_op jit(solution)/shard_map/ppermute | solution.py:24
  113.7 1.3 copy-start.4
  115.1 18.0 %copy-start.5 = (bf16[2048,256]{0,1:T(8,128)(2,1)S(1)}, bf16[2048,256]{0,1:T(8,128)(2,1)}, u32[]{:S(2)}) copy-start(bf16[2048,256]{0,1:T(8,128)(2,1)} %copy-done.4) | copy-start | bytes 3145732
  115.2 11.3 %copy-start.2 = (f32[520,256]{1,0:T(8,128)}, f32[520,256]{1,0:T(8,128)S(1)}, u32[]{:S(2)}) copy-start(f32[520,256]{1,0:T(8,128)S(1)} %maximum_maximum_fusion.1.local_ref) | copy-start | bytes 1597444
  115.2 11.3 %collective-permute-start.3 = (f32[520,256]{1,0:T(8,128)S(1)}, f32[520,256]{1,0:T(8,128)S(1)}, u32[]{:S(2)}, u32[]{:S(2)}) collective-permute-start(f32[520,256]{1,0:T(8,128)S(1)} %maximum_maximum_fusion.1.local_ref), channel_id=1, source_target_pairs={{0,1},{1,0},{16,23},{23,16},{2,3},{3,2},{18,17},{17,18},{4,5},{5,4... | collective-permute-start | bytes 1597448 | tf_op jit(solution)/shard_map/ppermute | solution.py:40
  126.5 0.8 copy-start.8
  133.1 3.8 %copy-start.9 = (bf16[512,512]{1,0:T(8,128)(2,1)S(1)}, bf16[512,512]{1,0:T(8,128)(2,1)}, u32[]{:S(2)}) copy-start(bf16[512,512]{1,0:T(8,128)(2,1)} %shard_map.42) | copy-start | bytes 1572868
  135.0 18.5 %collective-permute-start.4 = (bf16[2048,256]{0,1:T(8,128)(2,1)S(1)}, bf16[2048,256]{0,1:T(8,128)(2,1)S(1)}, u32[]{:S(2)}, u32[]{:S(2)}) collective-permute-start(bf16[2048,256]{0,1:T(8,128)(2,1)S(1)} %convolution_convert_fusion.1), channel_id=1, source_target_pairs={{0,16},{16,32},{32,48},{48,64},{64,80},{80,96},{96,112},{112,128},... | collective-permute-start | bytes 3145736 | tf_op jit(solution)/shard_map/ppermute | solution.py:24
  137.7 18.3 %collective-permute-start.5 = (bf16[2048,256]{0,1:T(8,128)(2,1)S(1)}, bf16[2048,256]{0,1:T(8,128)(2,1)S(1)}, u32[]{:S(2)}, u32[]{:S(2)}) collective-permute-start(bf16[2048,256]{0,1:T(8,128)(2,1)S(1)} %convolution_convert_fusion.2), channel_id=1, source_target_pairs={{16,0},{32,16},{48,32},{64,48},{80,64},{96,80},{112,96},{128,112},... | collective-permute-start | bytes 3145736 | tf_op jit(solution)/shard_map/ppermute | solution.py:24
  157.6 11.2 %copy-start.1 = (f32[520,256]{1,0:T(8,128)}, f32[520,256]{1,0:T(8,128)S(1)}, u32[]{:S(2)}) copy-start(f32[520,256]{1,0:T(8,128)S(1)} %maximum_maximum_fusion.2.local_ref) | copy-start | bytes 1597444
  157.6 11.2 %collective-permute-start.6 = (f32[520,256]{1,0:T(8,128)S(1)}, f32[520,256]{1,0:T(8,128)S(1)}, u32[]{:S(2)}, u32[]{:S(2)}) collective-permute-start(f32[520,256]{1,0:T(8,128)S(1)} %maximum_maximum_fusion.2.local_ref), channel_id=1, source_target_pairs={{0,1},{1,0},{16,23},{23,16},{2,3},{3,2},{18,17},{17,18},{4,5},{5,4... | collective-permute-start | bytes 1597448 | tf_op jit(solution)/shard_map/ppermute | solution.py:40
  168.7 0.8 copy-start.7
  177.7 5.5 %collective-permute-start.7 = (f32[512]{0:T(512)S(1)}, f32[512]{0:T(512)S(1)}, u32[]{:S(2)}, u32[]{:S(2)}) collective-permute-start(f32[512]{0:T(512)S(1)} %get-tuple-element.11), channel_id=1, source_target_pairs={{0,1},{1,0},{16,23},{23,16},{2,3},{3,2},{18,17},{17,18},{4,5},{5,4... | collective-permute-start | bytes 6152 | tf_op jit(solution)/shard_map/ppermute | solution.py:40

commit v11 on v10

--- a/solution.py
+++ b/solution.py
@@ -191,8 +191,14 @@
 def local(design, record_weight):
     width = design.shape[1] // 2
     records = design.shape[0]
-    weighted = (design.astype(jnp.float32) * record_weight[:, None]).astype(jnp.bfloat16)
-    weighted = gathered_records(weighted)
+    count = lax.axis_size(GROUP_AXES)
+    spread = (
+        jnp.broadcast_to(design[None], (count,) + design.shape).astype(jnp.float32)
+        * record_weight[None, :, None]
+    ).astype(jnp.bfloat16)
+    weighted = lax.all_to_all(spread, GROUP_AXES, 0, 0, tiled=False).reshape(
+        count * records, design.shape[1]
+    )
     upper_block = weighted[:, :width]
     lower_block = weighted[:, width:]
     position = lax.axis_index(COLUMN_AXES)
@@ -202,9 +208,6 @@
         pair_data = jnp.concatenate([upper_block, lower_block], axis=1)
         rotation = rotation_of(*summed_gram(pair_data, width))
         if not moving:
-            rotated = jnp.dot(pair_data, rotation, preferred_element_type=jnp.float32)
-            upper_block = rotated[:, :width].astype(jnp.bfloat16)
-            lower_block = rotated[:, width:].astype(jnp.bfloat16)
             break
         first_columns = rotation[:, :width]
         second_columns = rotation[:, width:]
@@ -222,12 +225,13 @@
         from_right = send_left(going_left)
         upper_block = jnp.where(position == 0, going_left, from_left)
         lower_block = jnp.where(position == device_count - 1, going_right, from_right)
-    gathered_design = jnp.concatenate([upper_block, lower_block], axis=1)
-    squares = with_partner(jnp.sum(jnp.square(gathered_design.astype(jnp.float32)), axis=0))
+    rotated = jnp.dot(pair_data, rotation, preferred_element_type=jnp.float32).astype(jnp.bfloat16)
+    squares = with_partner(jnp.sum(jnp.square(rotated.astype(jnp.float32)), axis=0))
     record_total = records * lax.axis_size(RECORD_AXES)
     column_rms = jnp.sqrt(squares / record_total + 1e-06)
     start = lax.axis_index(GROUP_AXES) * records
-    rotated_design = lax.dynamic_slice_in_dim(gathered_design, start, records, axis=0)
+    own_rows = lax.dynamic_slice_in_dim(pair_data, start, records, axis=0)
+    rotated_design = jnp.dot(own_rows, rotation, preferred_element_type=jnp.float32).astype(jnp.bfloat16)
     return (rotated_design, column_rms)
 
 

time: 184 us -> 185 us (level)
  local copies, waits for them, and re-layouts: 4.76 us -> 2.53 us
  other arithmetic: 5.14 us -> 7.3 us
    convert_element_type x1 -> x2, other arithmetic: 1.06 us -> 3.22 us  [the longest x1 2.22 us: local(): spread = (jnp.broadcast_to(design[None], (count,) + design.shape).astype(...]
where the time goes in v11:
time: 185 us; the launch traced here: 184 us
  waiting for transfers between devices  105 us (57%)
  starting transfers between devices  37.4 us (20%)
  Pallas kernels  17.4 us (9%)
  matrix products  13.5 us (7%)
  other arithmetic  7.3 us (4%)
  local copies, waits for them, and re-layouts  2.53 us (1%)
    all_to_all x1, waiting for transfers between devices, local(): lax.all_to_all(spread, GROUP_AXES, 0, 0, tiled=False)  52.8 us
    ppermute x4, waiting for transfers between devices, from_partner(): lax.ppermute(value, PARTNER_AXES, partner_pairs(lax.axis_size('y_hi')))  29.2 us
    ppermute x4, waiting for transfers between devices, from_behind(): lax.ppermute(value, COLUMN_AXES, [(source, source + steps) for source in...  23.4 us
    ppermute x4, starting transfers between devices, from_behind(): lax.ppermute(value, COLUMN_AXES, [(source, source + steps) for source in...  20 us
    pallas_call x3, Pallas kernels, rotation_of(): pl.pallas_call(sweeps_kernel, out_shape=jax.ShapeDtypeStruct((2 * width,...  17.4 us
    ppermute x4, starting transfers between devices, from_partner(): lax.ppermute(value, PARTNER_AXES, partner_pairs(lax.axis_size('y_hi')))  8.76 us
    all_to_all x1, starting transfers between devices, local(): lax.all_to_all(spread, GROUP_AXES, 0, 0, tiled=False)  8.66 us
    dot_general x3, matrix products, inner_products(): lax.dot_general(left_part, right_part, (((0,), (0,)), ((), ())), preferre...  3.83 us
  transfers between devices with their start and end apart: 9, of which 9 were waited for; matrix products, arithmetic and copies ran while one was open for 3% of the time, Pallas kernels for 0%

profile of v11, /device:TPU:2, one launch (start us, length us, event | category | flops | bytes accessed | tf_op | source)
XLA Modules:
  0.0 184.5 jit_solution(15343275116398044137)
XLA Ops:
  0.6 1.0 convert_element_type.28
  1.6 2.2 %multiply_convert_fusion = bf16[8,256,512]{2,1,0:T(8,128)(2,1)} fusion(f32[256]{0:T(256)} %param.3, f32[256,512]{1,0:T(8,128)S(1)} %convert_element_type.28), kind=kLoop, calls=%fused_computation.1 | loop fusion | flops 2097152 | bytes 2622464 | tf_op jit(solution)/shard_map/convert_element_type | solution.py:198
  3.9 8.7 %all-to-all-start = ((bf16[8,256,512]{2,1,0:T(8,128)(2,1)}), bf16[8,256,512]{2,1,0:T(8,128)(2,1)S(1)}, u32[]{:S(2)}, u32[]{:S(2)}) async-start(bf16[8,256,512]{2,1,0:T(8,128)(2,1)} %multiply_convert_fusion), calls=%async_computation | async-start | bytes 4194304 | tf_op jit(solution)/shard_map/all_to_all | solution.py:199
  12.5 0.1 pad.15.clone
  12.6 52.8 %all-to-all-done = bf16[8,256,512]{2,1,0:T(8,128)(2,1)S(1)} async-done(((bf16[8,256,512]{2,1,0:T(8,128)(2,1)}), bf16[8,256,512]{2,1,0:T(8,128)(2,1)S(1)}, u32[]{:S(2)}, u32[]{:S(2)}) %all-to-all-start) | async-done | bytes 2097184 | tf_op jit(solution)/shard_map/all_to_all | solution.py:199
  65.4 1.3 convolution_bitcast_fusion
  66.7 0.1 slice_select_fusion.2
  66.7 0.1 maximum_maximum_fusion.local_ref
  66.9 0.0 copy-start
  66.9 2.7 %collective-permute-start = (f32[520,256]{1,0:T(8,128)S(1)}, f32[520,256]{1,0:T(8,128)S(1)}, u32[]{:S(2)}, u32[]{:S(2)}) collective-permute-start(f32[520,256]{1,0:T(8,128)S(1)} %maximum_maximum_fusion.local_ref), channel_id=1, source_target_pairs={{0,1},{1,0},{16,23},{23,16},{2,3},{3,2},{18,17},{17,18},{4,5},{5,4... | collective-permute-start | bytes 1597448 | tf_op jit(solution)/shard_map/ppermute | solution.py:40
  69.6 8.5 %collective-permute-done.received_ref = f32[520,256]{1,0:T(8,128)S(1)} collective-permute-done((f32[520,256]{1,0:T(8,128)S(1)}, f32[520,256]{1,0:T(8,128)S(1)}, u32[]{:S(2)}, u32[]{:S(2)}) %collective-permute-start) | collective-permute-done | bytes 532512 | tf_op jit(solution)/shard_map/ppermute | solution.py:40
  78.1 0.0 copy-done
  78.1 0.0 copy-start.7
  78.1 0.8 copy-done.7
  78.9 5.8 %shard_map.41 = bf16[512,512]{1,0:T(8,128)(2,1)} custom-call(f32[520,256]{1,0:T(8,128)} %copy-done, f32[520,256]{1,0:T(8,128)} %copy-done.7), custom_call_target="tpu_custom_call" | custom-call | flops 15728640 | bytes 1048576 | tf_op jit(solution)/shard_map/pallas_call | solution.py:138
  84.7 0.0 copy-start.3
  84.7 1.8 convolution_convert_fusion.3
  86.5 1.9 %collective-permute-start.1 = (bf16[2048,256]{0,1:T(8,128)(2,1)S(1)}, bf16[2048,256]{0,1:T(8,128)(2,1)}, u32[]{:S(2)}, u32[]{:S(2)}) collective-permute-start(bf16[2048,256]{0,1:T(8,128)(2,1)S(1)} %convolution_convert_fusion.3), channel_id=1, source_target_pairs={{0,16},{16,32},{32,48},{48,64},{64,80},{80,96},{96,112},{112,128},... | collective-permute-start | bytes 3145736 | tf_op jit(solution)/shard_map/ppermute | solution.py:24
  88.5 0.0 copy-done.3
  88.5 1.8 convolution_convert_fusion.4
  90.2 10.2 %collective-permute-start.2 = (bf16[2048,256]{0,1:T(8,128)(2,1)}, bf16[2048,256]{0,1:T(8,128)(2,1)}, u32[]{:S(2)}, u32[]{:S(2)}) collective-permute-start(bf16[2048,256]{0,1:T(8,128)(2,1)} %convolution_convert_fusion.4), channel_id=1, source_target_pairs={{16,0},{32,16},{48,32},{64,48},{80,64},{96,80},{112,96},{128,112},... | collective-permute-start | bytes 3145736 | tf_op jit(solution)/shard_map/ppermute | solution.py:24
  100.4 8.9 %collective-permute-done.1 = bf16[2048,256]{0,1:T(8,128)(2,1)} collective-permute-done((bf16[2048,256]{0,1:T(8,128)(2,1)S(1)}, bf16[2048,256]{0,1:T(8,128)(2,1)}, u32[]{:S(2)}, u32[]{:S(2)}) %collective-permute-start.1) | collective-permute-done | bytes 1048608 | tf_op jit(solution)/shard_map/ppermute | solution.py:24
  109.3 1.3 broadcast_select_fusion.3
  110.6 2.4 %collective-permute-done.2 = bf16[2048,256]{0,1:T(8,128)(2,1)} collective-permute-done((bf16[2048,256]{0,1:T(8,128)(2,1)}, bf16[2048,256]{0,1:T(8,128)(2,1)}, u32[]{:S(2)}, u32[]{:S(2)}) %collective-permute-start.2) | collective-permute-done | bytes 1048608 | tf_op jit(solution)/shard_map/ppermute | solution.py:24
  113.0 1.3 broadcast_select_fusion.1
  114.4 0.0 copy-start.5
  114.4 1.3 fusion.1
  115.7 0.0 copy-done.5
  115.7 0.1 slice_select_fusion.1
  115.7 0.0 copy-start.6
  115.7 0.1 maximum_maximum_fusion.1.local_ref
  115.9 0.0 copy-start.2
  115.9 2.2 %collective-permute-start.3 = (f32[520,256]{1,0:T(8,128)S(1)}, f32[520,256]{1,0:T(8,128)S(1)}, u32[]{:S(2)}, u32[]{:S(2)}) collective-permute-start(f32[520,256]{1,0:T(8,128)S(1)} %maximum_maximum_fusion.1.local_ref), channel_id=1, source_target_pairs={{0,1},{1,0},{16,23},{23,16},{2,3},{3,2},{18,17},{17,18},{4,5},{5,4... | collective-permute-start | bytes 1597448 | tf_op jit(solution)/shard_map/ppermute | solution.py:40
  118.1 9.1 %collective-permute-done.3.received_ref = f32[520,256]{1,0:T(8,128)S(1)} collective-permute-done((f32[520,256]{1,0:T(8,128)S(1)}, f32[520,256]{1,0:T(8,128)S(1)}, u32[]{:S(2)}, u32[]{:S(2)}) %collective-permute-start.3) | collective-permute-done | bytes 532512 | tf_op jit(solution)/shard_map/ppermute | solution.py:40
  127.2 0.0 copy-done.2
  127.2 0.0 copy-start.9
  127.2 0.8 copy-done.9
  128.0 5.8 %shard_map.42 = bf16[512,512]{1,0:T(8,128)(2,1)} custom-call(f32[520,256]{1,0:T(8,128)} %copy-done.2, f32[520,256]{1,0:T(8,128)} %copy-done.9), custom_call_target="tpu_custom_call" | custom-call | flops 15728640 | bytes 1048576 | tf_op jit(solution)/shard_map/pallas_call | solution.py:138
  133.8 0.0 copy-done.6
  133.8 0.0 copy-start.10
  133.8 1.8 convolution_convert_fusion.1
  135.6 1.9 %collective-permute-start.4 = (bf16[2048,256]{0,1:T(8,128)(2,1)S(1)}, bf16[2048,256]{0,1:T(8,128)(2,1)S(1)}, u32[]{:S(2)}, u32[]{:S(2)}) collective-permute-start(bf16[2048,256]{0,1:T(8,128)(2,1)S(1)} %convolution_convert_fusion.1), channel_id=1, source_target_pairs={{0,16},{16,32},{32,48},{48,64},{64,80},{80,96},{96,112},{112,128},... | collective-permute-start | bytes 3145736 | tf_op jit(solution)/shard_map/ppermute | solution.py:24
  137.5 0.0 copy-done.10
  137.5 0.8 convolution_convert_fusion.2
  138.3 6.0 %collective-permute-start.5 = (bf16[2048,256]{0,1:T(8,128)(2,1)S(1)}, bf16[2048,256]{0,1:T(8,128)(2,1)S(1)}, u32[]{:S(2)}, u32[]{:S(2)}) collective-permute-start(bf16[2048,256]{0,1:T(8,128)(2,1)S(1)} %convolution_convert_fusion.2), channel_id=1, source_target_pairs={{16,0},{32,16},{48,32},{64,48},{80,64},{96,80},{112,96},{128,112},... | collective-permute-start | bytes 3145736 | tf_op jit(solution)/shard_map/ppermute | solution.py:24
  144.3 9.8 %collective-permute-done.4 = bf16[2048,256]{0,1:T(8,128)(2,1)S(1)} collective-permute-done((bf16[2048,256]{0,1:T(8,128)(2,1)S(1)}, bf16[2048,256]{0,1:T(8,128)(2,1)S(1)}, u32[]{:S(2)}, u32[]{:S(2)}) %collective-permute-start.4) | collective-permute-done | bytes 1048608 | tf_op jit(solution)/shard_map/ppermute | solution.py:24
  154.1 0.1 broadcast_select_fusion.2
  154.2 2.4 %collective-permute-done.5 = bf16[2048,256]{0,1:T(8,128)(2,1)S(1)} collective-permute-done((bf16[2048,256]{0,1:T(8,128)(2,1)S(1)}, bf16[2048,256]{0,1:T(8,128)(2,1)S(1)}, u32[]{:S(2)}, u32[]{:S(2)}) %collective-permute-start.5) | collective-permute-done | bytes 1048608 | tf_op jit(solution)/shard_map/ppermute | solution.py:24
  156.6 0.1 broadcast_select_fusion
  156.7 1.3 fusion
  158.0 0.1 slice_select_fusion
  158.1 0.1 maximum_maximum_fusion.2.local_ref
  158.2 0.0 copy-start.1
  158.2 1.9 %collective-permute-start.6 = (f32[520,256]{1,0:T(8,128)S(1)}, f32[520,256]{1,0:T(8,128)S(1)}, u32[]{:S(2)}, u32[]{:S(2)}) collective-permute-start(f32[520,256]{1,0:T(8,128)S(1)} %maximum_maximum_fusion.2.local_ref), channel_id=1, source_target_pairs={{0,1},{1,0},{16,23},{23,16},{2,3},{3,2},{18,17},{17,18},{4,5},{5,4... | collective-permute-start | bytes 1597448 | tf_op jit(solution)/shard_map/ppermute | solution.py:40
  160.2 9.2 %collective-permute-done.6.received_ref = f32[520,256]{1,0:T(8,128)S(1)} collective-permute-done((f32[520,256]{1,0:T(8,128)S(1)}, f32[520,256]{1,0:T(8,128)S(1)}, u32[]{:S(2)}, u32[]{:S(2)}) %collective-permute-start.6) | collective-permute-done | bytes 532512 | tf_op jit(solution)/shard_map/ppermute | solution.py:40
  169.4 0.0 copy-done.1
  169.4 0.8 copy-done.8
  170.2 5.8 %shard_map.43 = bf16[512,512]{1,0:T(8,128)(2,1)} custom-call(f32[520,256]{1,0:T(8,128)} %copy-done.1, f32[520,256]{1,0:T(8,128)} %copy-done.8), custom_call_target="tpu_custom_call" | custom-call | flops 15728640 | bytes 1048576 | tf_op jit(solution)/shard_map/pallas_call | solution.py:138
  176.0 2.4 %multiply_reduce_fusion = f32[512]{0:T(512)S(1)} fusion(bf16[512,512]{1,0:T(8,128)(2,1)} %shard_map.43, bf16[2048,256]{0,1:T(8,128)(2,1)S(1)} %broadcast_select_fusion, bf16[2048,256]{0,1:T(8,128)(2,1)S(1)} %broadcast_select_fusion.2), kind=kOutput, calls=%fused_computation | convolution fusion | flops 1082129920 | bytes 2623488 | tf_op jit(solution)/shard_map/dot_general | solution.py:228
  178.4 1.9 %collective-permute-start.7 = (f32[512]{0:T(512)S(1)}, f32[512]{0:T(512)S(1)}, u32[]{:S(2)}, u32[]{:S(2)}) collective-permute-start(f32[512]{0:T(512)S(1)} %multiply_reduce_fusion), channel_id=1, source_target_pairs={{0,1},{1,0},{16,23},{23,16},{2,3},{3,2},{18,17},{17,18},{4,5},{5,4... | collective-permute-start | bytes 6152 | tf_op jit(solution)/shard_map/ppermute | solution.py:40
  180.3 0.0 copy-done.4
  180.3 1.0 convolution_convert_fusion.5
  181.4 2.5 %collective-permute-done.7 = f32[512]{0:T(512)S(1)} collective-permute-done((f32[512]{0:T(512)S(1)}, f32[512]{0:T(512)S(1)}, u32[]{:S(2)}, u32[]{:S(2)}) %collective-permute-start.7) | collective-permute-done | bytes 2080 | tf_op jit(solution)/shard_map/ppermute | solution.py:40
  183.9 0.6 add_sqrt_fusion
  (3 shorter events, 0.0 us)
Async XLA Ops:
  3.9 61.5 %all-to-all-start = ((bf16[8,256,512]{2,1,0:T(8,128)(2,1)}), bf16[8,256,512]{2,1,0:T(8,128)(2,1)S(1)}, u32[]{:S(2)}, u32[]{:S(2)}) async-start(bf16[8,256,512]{2,1,0:T(8,128)(2,1)} %multiply_convert_fusion), calls=%async_computation | async-start | bytes 4194304 | tf_op jit(solution)/shard_map/all_to_all | solution.py:199
  66.9 11.2 %copy-start = (f32[520,256]{1,0:T(8,128)}, f32[520,256]{1,0:T(8,128)S(1)}, u32[]{:S(2)}) copy-start(f32[520,256]{1,0:T(8,128)S(1)} %maximum_maximum_fusion.local_ref) | copy-start | bytes 1597444
  66.9 11.2 %collective-permute-start = (f32[520,256]{1,0:T(8,128)S(1)}, f32[520,256]{1,0:T(8,128)S(1)}, u32[]{:S(2)}, u32[]{:S(2)}) collective-permute-start(f32[520,256]{1,0:T(8,128)S(1)} %maximum_maximum_fusion.local_ref), channel_id=1, source_target_pairs={{0,1},{1,0},{16,23},{23,16},{2,3},{3,2},{18,17},{17,18},{4,5},{5,4... | collective-permute-start | bytes 1597448 | tf_op jit(solution)/shard_map/ppermute | solution.py:40
  78.1 0.8 copy-start.7
  84.7 3.8 %copy-start.3 = (bf16[512,512]{1,0:T(8,128)(2,1)S(1)}, bf16[512,512]{1,0:T(8,128)(2,1)}, u32[]{:S(2)}) copy-start(bf16[512,512]{1,0:T(8,128)(2,1)} %shard_map.41) | copy-start | bytes 1572868
  86.5 22.8 %collective-permute-start.1 = (bf16[2048,256]{0,1:T(8,128)(2,1)S(1)}, bf16[2048,256]{0,1:T(8,128)(2,1)}, u32[]{:S(2)}, u32[]{:S(2)}) collective-permute-start(bf16[2048,256]{0,1:T(8,128)(2,1)S(1)} %convolution_convert_fusion.3), channel_id=1, source_target_pairs={{0,16},{16,32},{32,48},{48,64},{64,80},{80,96},{96,112},{112,128},... | collective-permute-start | bytes 3145736 | tf_op jit(solution)/shard_map/ppermute | solution.py:24
  90.2 22.8 %collective-permute-start.2 = (bf16[2048,256]{0,1:T(8,128)(2,1)}, bf16[2048,256]{0,1:T(8,128)(2,1)}, u32[]{:S(2)}, u32[]{:S(2)}) collective-permute-start(bf16[2048,256]{0,1:T(8,128)(2,1)} %convolution_convert_fusion.4), channel_id=1, source_target_pairs={{16,0},{32,16},{48,32},{64,48},{80,64},{96,80},{112,96},{128,112},... | collective-permute-start | bytes 3145736 | tf_op jit(solution)/shard_map/ppermute | solution.py:24
  114.4 1.3 copy-start.5
  115.7 18.0 %copy-start.6 = (bf16[2048,256]{0,1:T(8,128)(2,1)S(1)}, bf16[2048,256]{0,1:T(8,128)(2,1)}, u32[]{:S(2)}) copy-start(bf16[2048,256]{0,1:T(8,128)(2,1)} %copy-done.5) | copy-start | bytes 3145732
  115.9 11.3 %copy-start.2 = (f32[520,256]{1,0:T(8,128)}, f32[520,256]{1,0:T(8,128)S(1)}, u32[]{:S(2)}) copy-start(f32[520,256]{1,0:T(8,128)S(1)} %maximum_maximum_fusion.1.local_ref) | copy-start | bytes 1597444
  115.9 11.3 %collective-permute-start.3 = (f32[520,256]{1,0:T(8,128)S(1)}, f32[520,256]{1,0:T(8,128)S(1)}, u32[]{:S(2)}, u32[]{:S(2)}) collective-permute-start(f32[520,256]{1,0:T(8,128)S(1)} %maximum_maximum_fusion.1.local_ref), channel_id=1, source_target_pairs={{0,1},{1,0},{16,23},{23,16},{2,3},{3,2},{18,17},{17,18},{4,5},{5,4... | collective-permute-start | bytes 1597448 | tf_op jit(solution)/shard_map/ppermute | solution.py:40
  127.2 0.8 copy-start.9
  133.8 3.8 %copy-start.10 = (bf16[512,512]{1,0:T(8,128)(2,1)S(1)}, bf16[512,512]{1,0:T(8,128)(2,1)}, u32[]{:S(2)}) copy-start(bf16[512,512]{1,0:T(8,128)(2,1)} %shard_map.42) | copy-start | bytes 1572868
  135.6 18.5 %collective-permute-start.4 = (bf16[2048,256]{0,1:T(8,128)(2,1)S(1)}, bf16[2048,256]{0,1:T(8,128)(2,1)S(1)}, u32[]{:S(2)}, u32[]{:S(2)}) collective-permute-start(bf16[2048,256]{0,1:T(8,128)(2,1)S(1)} %convolution_convert_fusion.1), channel_id=1, source_target_pairs={{0,16},{16,32},{32,48},{48,64},{64,80},{80,96},{96,112},{112,128},... | collective-permute-start | bytes 3145736 | tf_op jit(solution)/shard_map/ppermute | solution.py:24
  138.3 18.3 %collective-permute-start.5 = (bf16[2048,256]{0,1:T(8,128)(2,1)S(1)}, bf16[2048,256]{0,1:T(8,128)(2,1)S(1)}, u32[]{:S(2)}, u32[]{:S(2)}) collective-permute-start(bf16[2048,256]{0,1:T(8,128)(2,1)S(1)} %convolution_convert_fusion.2), channel_id=1, source_target_pairs={{16,0},{32,16},{48,32},{64,48},{80,64},{96,80},{112,96},{128,112},... | collective-permute-start | bytes 3145736 | tf_op jit(solution)/shard_map/ppermute | solution.py:24
  158.2 11.2 %copy-start.1 = (f32[520,256]{1,0:T(8,128)}, f32[520,256]{1,0:T(8,128)S(1)}, u32[]{:S(2)}) copy-start(f32[520,256]{1,0:T(8,128)S(1)} %maximum_maximum_fusion.2.local_ref) | copy-start | bytes 1597444
  158.2 11.2 %collective-permute-start.6 = (f32[520,256]{1,0:T(8,128)S(1)}, f32[520,256]{1,0:T(8,128)S(1)}, u32[]{:S(2)}, u32[]{:S(2)}) collective-permute-start(f32[520,256]{1,0:T(8,128)S(1)} %maximum_maximum_fusion.2.local_ref), channel_id=1, source_target_pairs={{0,1},{1,0},{16,23},{23,16},{2,3},{3,2},{18,17},{17,18},{4,5},{5,4... | collective-permute-start | bytes 1597448 | tf_op jit(solution)/shard_map/ppermute | solution.py:40
  169.4 0.8 copy-start.8
  176.0 4.3 %copy-start.4 = (bf16[512,512]{1,0:T(8,128)(2,1)S(1)}, bf16[512,512]{1,0:T(8,128)(2,1)}, u32[]{:S(2)}) copy-start(bf16[512,512]{1,0:T(8,128)(2,1)} %shard_map.43) | copy-start | bytes 1572868
  178.4 5.5 %collective-permute-start.7 = (f32[512]{0:T(512)S(1)}, f32[512]{0:T(512)S(1)}, u32[]{:S(2)}, u32[]{:S(2)}) collective-permute-start(f32[512]{0:T(512)S(1)} %multiply_reduce_fusion), channel_id=1, source_target_pairs={{0,1},{1,0},{16,23},{23,16},{2,3},{3,2},{18,17},{17,18},{4,5},{5,4... | collective-permute-start | bytes 6152 | tf_op jit(solution)/shard_map/ppermute | solution.py:40

commit v12 on v10

--- a/solution.py
+++ b/solution.py
@@ -69,18 +69,20 @@
     return cosine, sine_value
 
 
-def sweeps_kernel(local_ref, received_ref, rotation_ref):
+def sweeps_kernel(local_ref, received_hbm, rotation_ref, received_ref, copy_sem):
     width = local_ref.shape[1]
+    arrival = pltpu.make_async_copy(received_hbm, received_ref, copy_sem)
+    arrival.start()
     rows = lax.broadcasted_iota(jnp.int32, (width, width), 0)
     cols = lax.broadcasted_iota(jnp.int32, (width, width), 1)
     on_diagonal = rows == cols
+    arrival.wait()
     folded = local_ref[:width, :] + received_ref[:width, :]
     top_right = local_ref[width : 2 * width, :] + received_ref[width : 2 * width, :]
     low_diag = (local_ref[2 * width : 2 * width + 8, :] + received_ref[2 * width : 2 * width + 8, :])[:1, :]
     mirrored = folded.T
     top_left = jnp.where(rows <= cols, folded, mirrored)
     low_right = jnp.where(rows > cols, folded, jnp.where(rows < cols, mirrored, low_diag))
-    low_left = top_right.T
     first_top = jnp.where(on_diagonal, 1.0, 0.0).astype(jnp.float32)
     first_low = jnp.zeros((width, width), jnp.float32)
     second_top = jnp.zeros((width, width), jnp.float32)
@@ -98,10 +100,10 @@
     for sweep_index in range(SWEEPS):
         if sweep_index > 0:
             top_right = to_left(top_right, 1)
-            low_left = to_left(low_left, 0)
             low_right = to_left(to_left(low_right, 0), 1)
             second_top = to_left(second_top, 1)
             second_low = to_left(second_low, 1)
+        low_left = top_right.T
         cos_col, sin_col = half_angle_terms(
             diagonal_row(top_left), diagonal_row(low_right), diagonal_row(top_right)
         )
@@ -112,7 +114,6 @@
         left_b = low_left * cos_col - low_right * sin_col
         right_b = low_left * sin_col + low_right * cos_col
         top_left = cos_row * left_a - sin_row * left_b
-        low_left = sin_row * left_a + cos_row * left_b
         top_right = cos_row * right_a - sin_row * right_b
         low_right = sin_row * right_a + cos_row * right_b
         first_top, second_top = (
@@ -138,8 +139,9 @@
     return pl.pallas_call(
         sweeps_kernel,
         out_shape=jax.ShapeDtypeStruct((2 * width, 2 * width), jnp.bfloat16),
-        in_specs=[vmem, vmem],
+        in_specs=[vmem, pl.BlockSpec(memory_space=pl.ANY)],
         out_specs=vmem,
+        scratch_shapes=[pltpu.VMEM(received.shape, received.dtype), pltpu.SemaphoreType.DMA(())],
         cost_estimate=pl.CostEstimate(
             flops=SWEEPS * 40 * width * width, transcendentals=SWEEPS * 8 * width, bytes_accessed=4 * 4 * width * width
         ),

time: 184 us -> 187 us (1.016)
  Pallas kernels: 17.4 us -> 20 us
    pallas_call x3, Pallas kernels: 17.4 us -> 20 us  [rotation_of(): pl.pallas_call(sweeps_kernel, out_shape=jax.ShapeDtypeStruct((2 * width,...]
where the time goes in v12:
time: 187 us; the launch traced here: 186 us
  waiting for transfers between devices  106 us (57%)
  starting transfers between devices  37.4 us (20%)
  Pallas kernels  20 us (11%)
  matrix products  12.4 us (7%)
  other arithmetic  5.14 us (3%)
  local copies, waits for them, and re-layouts  4.77 us (3%)
    all_to_all x1, waiting for transfers between devices, gathered_records(): gathered = lax.all_to_all(spread, GROUP_AXES, 0, 0, tiled=False)  52.8 us
    ppermute x4, waiting for transfers between devices, from_partner(): lax.ppermute(value, PARTNER_AXES, partner_pairs(lax.axis_size('y_hi')))  29.5 us
    ppermute x4, waiting for transfers between devices, from_behind(): lax.ppermute(value, COLUMN_AXES, [(source, source + steps) for source in...  23.4 us
    pallas_call x3, Pallas kernels, rotation_of(): pl.pallas_call(sweeps_kernel, out_shape=jax.ShapeDtypeStruct((2 * width,...  20 us
    ppermute x4, starting transfers between devices, from_behind(): lax.ppermute(value, COLUMN_AXES, [(source, source + steps) for source in...  20 us
    ppermute x4, starting transfers between devices, from_partner(): lax.ppermute(value, PARTNER_AXES, partner_pairs(lax.axis_size('y_hi')))  8.77 us
    all_to_all x1, starting transfers between devices, gathered_records(): gathered = lax.all_to_all(spread, GROUP_AXES, 0, 0, tiled=False)  8.66 us
    dot_general x3, matrix products, inner_products(): lax.dot_general(left_part, right_part, (((0,), (0,)), ((), ())), preferre...  3.83 us
  transfers between devices with their start and end apart: 9, of which 9 were waited for; matrix products, arithmetic and copies ran while one was open for 3% of the time, Pallas kernels for 0%

profile of v12, /device:TPU:2, one launch (start us, length us, event | category | flops | bytes accessed | tf_op | source)
XLA Modules:
  0.0 186.5 jit_solution(7190737964280372482)
XLA Ops:
  0.6 1.1 multiply_convert_fusion
  1.7 1.5 broadcast_in_dim.22
  3.2 8.7 %all-to-all-start = ((bf16[8,256,512]{2,1,0:T(8,128)(2,1)}), bf16[8,256,512]{2,1,0:T(8,128)(2,1)S(1)}, u32[]{:S(2)}, u32[]{:S(2)}) async-start(bf16[8,256,512]{2,1,0:T(8,128)(2,1)} %broadcast_in_dim.22), calls=%async_computation | async-start | bytes 4194304 | tf_op jit(solution)/shard_map/all_to_all | solution.py:168
  11.9 0.1 pad.15.clone
  11.9 52.8 %all-to-all-done = bf16[8,256,512]{2,1,0:T(8,128)(2,1)S(1)} async-done(((bf16[8,256,512]{2,1,0:T(8,128)(2,1)}), bf16[8,256,512]{2,1,0:T(8,128)(2,1)S(1)}, u32[]{:S(2)}, u32[]{:S(2)}) %all-to-all-start) | async-done | bytes 2097184 | tf_op jit(solution)/shard_map/all_to_all | solution.py:168
  64.8 1.3 convolution_bitcast_fusion
  66.0 0.1 slice_select_fusion.2
  66.1 0.1 maximum_maximum_fusion.local_ref
  66.2 0.0 copy-start
  66.2 2.7 %collective-permute-start = (f32[520,256]{1,0:T(8,128)S(1)}, f32[520,256]{1,0:T(8,128)S(1)}, u32[]{:S(2)}, u32[]{:S(2)}) collective-permute-start(f32[520,256]{1,0:T(8,128)S(1)} %maximum_maximum_fusion.local_ref), channel_id=1, source_target_pairs={{0,1},{1,0},{16,23},{23,16},{2,3},{3,2},{18,17},{17,18},{4,5},{5,4... | collective-permute-start | bytes 1597448 | tf_op jit(solution)/shard_map/ppermute | solution.py:40
  69.0 8.4 %collective-permute-done.received_hbm = f32[520,256]{1,0:T(8,128)S(1)} collective-permute-done((f32[520,256]{1,0:T(8,128)S(1)}, f32[520,256]{1,0:T(8,128)S(1)}, u32[]{:S(2)}, u32[]{:S(2)}) %collective-permute-start) | collective-permute-done | bytes 532512 | tf_op jit(solution)/shard_map/ppermute | solution.py:40
  77.4 0.0 copy-done
  77.4 0.0 copy-start.6
  77.4 0.8 copy-done.6
  78.2 6.7 %shard_map.41 = bf16[512,512]{1,0:T(8,128)(2,1)} custom-call(f32[520,256]{1,0:T(8,128)} %copy-done, f32[520,256]{1,0:T(8,128)} %copy-done.6), custom_call_target="tpu_custom_call" | custom-call | flops 15728640 | bytes 1048576 | tf_op jit(solution)/shard_map/pallas_call | solution.py:139
  84.9 0.0 copy-start.3
  84.9 1.8 convolution_convert_fusion.3
  86.8 1.9 %collective-permute-start.1 = (bf16[2048,256]{0,1:T(8,128)(2,1)S(1)}, bf16[2048,256]{0,1:T(8,128)(2,1)}, u32[]{:S(2)}, u32[]{:S(2)}) collective-permute-start(bf16[2048,256]{0,1:T(8,128)(2,1)S(1)} %convolution_convert_fusion.3), channel_id=1, source_target_pairs={{0,16},{16,32},{32,48},{48,64},{64,80},{80,96},{96,112},{112,128},... | collective-permute-start | bytes 3145736 | tf_op jit(solution)/shard_map/ppermute | solution.py:24
  88.7 0.0 copy-done.3
  88.7 1.8 convolution_convert_fusion.4
  90.5 10.2 %collective-permute-start.2 = (bf16[2048,256]{0,1:T(8,128)(2,1)}, bf16[2048,256]{0,1:T(8,128)(2,1)}, u32[]{:S(2)}, u32[]{:S(2)}) collective-permute-start(bf16[2048,256]{0,1:T(8,128)(2,1)} %convolution_convert_fusion.4), channel_id=1, source_target_pairs={{16,0},{32,16},{48,32},{64,48},{80,64},{96,80},{112,96},{128,112},... | collective-permute-start | bytes 3145736 | tf_op jit(solution)/shard_map/ppermute | solution.py:24
  100.7 8.9 %collective-permute-done.1 = bf16[2048,256]{0,1:T(8,128)(2,1)} collective-permute-done((bf16[2048,256]{0,1:T(8,128)(2,1)S(1)}, bf16[2048,256]{0,1:T(8,128)(2,1)}, u32[]{:S(2)}, u32[]{:S(2)}) %collective-permute-start.1) | collective-permute-done | bytes 1048608 | tf_op jit(solution)/shard_map/ppermute | solution.py:24
  109.5 1.3 broadcast_select_fusion.3
  110.9 2.4 %collective-permute-done.2 = bf16[2048,256]{0,1:T(8,128)(2,1)} collective-permute-done((bf16[2048,256]{0,1:T(8,128)(2,1)}, bf16[2048,256]{0,1:T(8,128)(2,1)}, u32[]{:S(2)}, u32[]{:S(2)}) %collective-permute-start.2) | collective-permute-done | bytes 1048608 | tf_op jit(solution)/shard_map/ppermute | solution.py:24
  113.3 1.3 broadcast_select_fusion.1
  114.6 0.0 copy-start.4
  114.6 1.3 fusion.1
  115.9 0.0 copy-done.4
  115.9 0.1 slice_select_fusion.1
  116.0 0.0 copy-start.5
  116.0 0.1 maximum_maximum_fusion.1.local_ref
  116.1 0.0 copy-start.2
  116.1 2.2 %collective-permute-start.3 = (f32[520,256]{1,0:T(8,128)S(1)}, f32[520,256]{1,0:T(8,128)S(1)}, u32[]{:S(2)}, u32[]{:S(2)}) collective-permute-start(f32[520,256]{1,0:T(8,128)S(1)} %maximum_maximum_fusion.1.local_ref), channel_id=1, source_target_pairs={{0,1},{1,0},{16,23},{23,16},{2,3},{3,2},{18,17},{17,18},{4,5},{5,4... | collective-permute-start | bytes 1597448 | tf_op jit(solution)/shard_map/ppermute | solution.py:40
  118.4 9.1 %collective-permute-done.3.received_hbm = f32[520,256]{1,0:T(8,128)S(1)} collective-permute-done((f32[520,256]{1,0:T(8,128)S(1)}, f32[520,256]{1,0:T(8,128)S(1)}, u32[]{:S(2)}, u32[]{:S(2)}) %collective-permute-start.3) | collective-permute-done | bytes 532512 | tf_op jit(solution)/shard_map/ppermute | solution.py:40
  127.4 0.0 copy-done.2
  127.4 0.0 copy-start.8
  127.4 0.8 copy-done.8
  128.2 6.7 %shard_map.42 = bf16[512,512]{1,0:T(8,128)(2,1)} custom-call(f32[520,256]{1,0:T(8,128)} %copy-done.2, f32[520,256]{1,0:T(8,128)} %copy-done.8), custom_call_target="tpu_custom_call" | custom-call | flops 15728640 | bytes 1048576 | tf_op jit(solution)/shard_map/pallas_call | solution.py:139
  134.9 0.0 copy-done.5
  134.9 0.0 copy-start.9
  134.9 1.8 convolution_convert_fusion.1
  136.8 1.9 %collective-permute-start.4 = (bf16[2048,256]{0,1:T(8,128)(2,1)S(1)}, bf16[2048,256]{0,1:T(8,128)(2,1)S(1)}, u32[]{:S(2)}, u32[]{:S(2)}) collective-permute-start(bf16[2048,256]{0,1:T(8,128)(2,1)S(1)} %convolution_convert_fusion.1), channel_id=1, source_target_pairs={{0,16},{16,32},{32,48},{48,64},{64,80},{80,96},{96,112},{112,128},... | collective-permute-start | bytes 3145736 | tf_op jit(solution)/shard_map/ppermute | solution.py:24
  138.7 0.0 copy-done.9
  138.7 0.8 convolution_convert_fusion.2
  139.5 6.0 %collective-permute-start.5 = (bf16[2048,256]{0,1:T(8,128)(2,1)S(1)}, bf16[2048,256]{0,1:T(8,128)(2,1)S(1)}, u32[]{:S(2)}, u32[]{:S(2)}) collective-permute-start(bf16[2048,256]{0,1:T(8,128)(2,1)S(1)} %convolution_convert_fusion.2), channel_id=1, source_target_pairs={{16,0},{32,16},{48,32},{64,48},{80,64},{96,80},{112,96},{128,112},... | collective-permute-start | bytes 3145736 | tf_op jit(solution)/shard_map/ppermute | solution.py:24
  145.5 9.8 %collective-permute-done.4 = bf16[2048,256]{0,1:T(8,128)(2,1)S(1)} collective-permute-done((bf16[2048,256]{0,1:T(8,128)(2,1)S(1)}, bf16[2048,256]{0,1:T(8,128)(2,1)S(1)}, u32[]{:S(2)}, u32[]{:S(2)}) %collective-permute-start.4) | collective-permute-done | bytes 1048608 | tf_op jit(solution)/shard_map/ppermute | solution.py:24
  155.2 0.1 broadcast_select_fusion.2
  155.3 2.4 %collective-permute-done.5 = bf16[2048,256]{0,1:T(8,128)(2,1)S(1)} collective-permute-done((bf16[2048,256]{0,1:T(8,128)(2,1)S(1)}, bf16[2048,256]{0,1:T(8,128)(2,1)S(1)}, u32[]{:S(2)}, u32[]{:S(2)}) %collective-permute-start.5) | collective-permute-done | bytes 1048608 | tf_op jit(solution)/shard_map/ppermute | solution.py:24
  157.8 0.1 broadcast_select_fusion
  157.9 1.3 fusion
  159.2 0.1 slice_select_fusion
  159.2 0.1 maximum_maximum_fusion.2.local_ref
  159.4 0.0 copy-start.1
  159.4 1.9 %collective-permute-start.6 = (f32[520,256]{1,0:T(8,128)S(1)}, f32[520,256]{1,0:T(8,128)S(1)}, u32[]{:S(2)}, u32[]{:S(2)}) collective-permute-start(f32[520,256]{1,0:T(8,128)S(1)} %maximum_maximum_fusion.2.local_ref), channel_id=1, source_target_pairs={{0,1},{1,0},{16,23},{23,16},{2,3},{3,2},{18,17},{17,18},{4,5},{5,4... | collective-permute-start | bytes 1597448 | tf_op jit(solution)/shard_map/ppermute | solution.py:40
  161.3 9.2 %collective-permute-done.6.received_hbm = f32[520,256]{1,0:T(8,128)S(1)} collective-permute-done((f32[520,256]{1,0:T(8,128)S(1)}, f32[520,256]{1,0:T(8,128)S(1)}, u32[]{:S(2)}, u32[]{:S(2)}) %collective-permute-start.6) | collective-permute-done | bytes 532512 | tf_op jit(solution)/shard_map/ppermute | solution.py:40
  170.5 0.0 copy-done.1
  170.5 0.0 copy-start.7
  170.5 0.8 copy-done.7
  171.3 6.7 %shard_map.43 = bf16[512,512]{1,0:T(8,128)(2,1)} custom-call(f32[520,256]{1,0:T(8,128)} %copy-done.1, f32[520,256]{1,0:T(8,128)} %copy-done.7), custom_call_target="tpu_custom_call" | custom-call | flops 15728640 | bytes 1048576 | tf_op jit(solution)/shard_map/pallas_call | solution.py:139
  178.0 2.3 %multiply_reduce_fusion = (f32[512]{0:T(512)S(1)}, bf16[2048,512]{1,0:T(8,128)(2,1)S(1)}) fusion(bf16[512,512]{1,0:T(8,128)(2,1)} %shard_map.43, bf16[2048,256]{0,1:T(8,128)(2,1)S(1)} %broadcast_select_fusion, bf16[2048,256]{0,1:T(8,128)(2,1)S(1)} %broadcast_select_fusion.2), kind=kOutput, calls=%fused_computation | convolution fusion | flops 1082129920 | bytes 4720640 | tf_op jit(solution)/shard_map/dot_general | solution.py:207
  180.4 1.9 %collective-permute-start.7 = (f32[512]{0:T(512)S(1)}, f32[512]{0:T(512)S(1)}, u32[]{:S(2)}, u32[]{:S(2)}) collective-permute-start(f32[512]{0:T(512)S(1)} %get-tuple-element.11), channel_id=1, source_target_pairs={{0,1},{1,0},{16,23},{23,16},{2,3},{3,2},{18,17},{17,18},{4,5},{5,4... | collective-permute-start | bytes 6152 | tf_op jit(solution)/shard_map/ppermute | solution.py:40
  182.3 0.7 constant_dynamic-slice_fusion
  183.1 2.8 %collective-permute-done.7 = f32[512]{0:T(512)S(1)} collective-permute-done((f32[512]{0:T(512)S(1)}, f32[512]{0:T(512)S(1)}, u32[]{:S(2)}, u32[]{:S(2)}) %collective-permute-start.7) | collective-permute-done | bytes 2080 | tf_op jit(solution)/shard_map/ppermute | solution.py:40
  185.9 0.6 add_sqrt_fusion
  (1 shorter events, 0.0 us)
Async XLA Ops:
  3.2 61.5 %all-to-all-start = ((bf16[8,256,512]{2,1,0:T(8,128)(2,1)}), bf16[8,256,512]{2,1,0:T(8,128)(2,1)S(1)}, u32[]{:S(2)}, u32[]{:S(2)}) async-start(bf16[8,256,512]{2,1,0:T(8,128)(2,1)} %broadcast_in_dim.22), calls=%async_computation | async-start | bytes 4194304 | tf_op jit(solution)/shard_map/all_to_all | solution.py:168
  66.2 11.2 %copy-start = (f32[520,256]{1,0:T(8,128)}, f32[520,256]{1,0:T(8,128)S(1)}, u32[]{:S(2)}) copy-start(f32[520,256]{1,0:T(8,128)S(1)} %maximum_maximum_fusion.local_ref) | copy-start | bytes 1597444
  66.2 11.2 %collective-permute-start = (f32[520,256]{1,0:T(8,128)S(1)}, f32[520,256]{1,0:T(8,128)S(1)}, u32[]{:S(2)}, u32[]{:S(2)}) collective-permute-start(f32[520,256]{1,0:T(8,128)S(1)} %maximum_maximum_fusion.local_ref), channel_id=1, source_target_pairs={{0,1},{1,0},{16,23},{23,16},{2,3},{3,2},{18,17},{17,18},{4,5},{5,4... | collective-permute-start | bytes 1597448 | tf_op jit(solution)/shard_map/ppermute | solution.py:40
  77.4 0.8 copy-start.6
  84.9 3.8 %copy-start.3 = (bf16[512,512]{1,0:T(8,128)(2,1)S(1)}, bf16[512,512]{1,0:T(8,128)(2,1)}, u32[]{:S(2)}) copy-start(bf16[512,512]{1,0:T(8,128)(2,1)} %shard_map.41) | copy-start | bytes 1572868
  86.8 22.8 %collective-permute-start.1 = (bf16[2048,256]{0,1:T(8,128)(2,1)S(1)}, bf16[2048,256]{0,1:T(8,128)(2,1)}, u32[]{:S(2)}, u32[]{:S(2)}) collective-permute-start(bf16[2048,256]{0,1:T(8,128)(2,1)S(1)} %convolution_convert_fusion.3), channel_id=1, source_target_pairs={{0,16},{16,32},{32,48},{48,64},{64,80},{80,96},{96,112},{112,128},... | collective-permute-start | bytes 3145736 | tf_op jit(solution)/shard_map/ppermute | solution.py:24
  90.5 22.8 %collective-permute-start.2 = (bf16[2048,256]{0,1:T(8,128)(2,1)}, bf16[2048,256]{0,1:T(8,128)(2,1)}, u32[]{:S(2)}, u32[]{:S(2)}) collective-permute-start(bf16[2048,256]{0,1:T(8,128)(2,1)} %convolution_convert_fusion.4), channel_id=1, source_target_pairs={{16,0},{32,16},{48,32},{64,48},{80,64},{96,80},{112,96},{128,112},... | collective-permute-start | bytes 3145736 | tf_op jit(solution)/shard_map/ppermute | solution.py:24
  114.6 1.3 copy-start.4
  116.0 18.9 %copy-start.5 = (bf16[2048,256]{0,1:T(8,128)(2,1)S(1)}, bf16[2048,256]{0,1:T(8,128)(2,1)}, u32[]{:S(2)}) copy-start(bf16[2048,256]{0,1:T(8,128)(2,1)} %copy-done.4) | copy-start | bytes 3145732
  116.1 11.3 %copy-start.2 = (f32[520,256]{1,0:T(8,128)}, f32[520,256]{1,0:T(8,128)S(1)}, u32[]{:S(2)}) copy-start(f32[520,256]{1,0:T(8,128)S(1)} %maximum_maximum_fusion.1.local_ref) | copy-start | bytes 1597444
  116.1 11.3 %collective-permute-start.3 = (f32[520,256]{1,0:T(8,128)S(1)}, f32[520,256]{1,0:T(8,128)S(1)}, u32[]{:S(2)}, u32[]{:S(2)}) collective-permute-start(f32[520,256]{1,0:T(8,128)S(1)} %maximum_maximum_fusion.1.local_ref), channel_id=1, source_target_pairs={{0,1},{1,0},{16,23},{23,16},{2,3},{3,2},{18,17},{17,18},{4,5},{5,4... | collective-permute-start | bytes 1597448 | tf_op jit(solution)/shard_map/ppermute | solution.py:40
  127.4 0.8 copy-start.8
  134.9 3.8 %copy-start.9 = (bf16[512,512]{1,0:T(8,128)(2,1)S(1)}, bf16[512,512]{1,0:T(8,128)(2,1)}, u32[]{:S(2)}) copy-start(bf16[512,512]{1,0:T(8,128)(2,1)} %shard_map.42) | copy-start | bytes 1572868
  136.8 18.5 %collective-permute-start.4 = (bf16[2048,256]{0,1:T(8,128)(2,1)S(1)}, bf16[2048,256]{0,1:T(8,128)(2,1)S(1)}, u32[]{:S(2)}, u32[]{:S(2)}) collective-permute-start(bf16[2048,256]{0,1:T(8,128)(2,1)S(1)} %convolution_convert_fusion.1), channel_id=1, source_target_pairs={{0,16},{16,32},{32,48},{48,64},{64,80},{80,96},{96,112},{112,128},... | collective-permute-start | bytes 3145736 | tf_op jit(solution)/shard_map/ppermute | solution.py:24
  139.5 18.3 %collective-permute-start.5 = (bf16[2048,256]{0,1:T(8,128)(2,1)S(1)}, bf16[2048,256]{0,1:T(8,128)(2,1)S(1)}, u32[]{:S(2)}, u32[]{:S(2)}) collective-permute-start(bf16[2048,256]{0,1:T(8,128)(2,1)S(1)} %convolution_convert_fusion.2), channel_id=1, source_target_pairs={{16,0},{32,16},{48,32},{64,48},{80,64},{96,80},{112,96},{128,112},... | collective-permute-start | bytes 3145736 | tf_op jit(solution)/shard_map/ppermute | solution.py:24
  159.4 11.2 %copy-start.1 = (f32[520,256]{1,0:T(8,128)}, f32[520,256]{1,0:T(8,128)S(1)}, u32[]{:S(2)}) copy-start(f32[520,256]{1,0:T(8,128)S(1)} %maximum_maximum_fusion.2.local_ref) | copy-start | bytes 1597444
  159.4 11.2 %collective-permute-start.6 = (f32[520,256]{1,0:T(8,128)S(1)}, f32[520,256]{1,0:T(8,128)S(1)}, u32[]{:S(2)}, u32[]{:S(2)}) collective-permute-start(f32[520,256]{1,0:T(8,128)S(1)} %maximum_maximum_fusion.2.local_ref), channel_id=1, source_target_pairs={{0,1},{1,0},{16,23},{23,16},{2,3},{3,2},{18,17},{17,18},{4,5},{5,4... | collective-permute-start | bytes 1597448 | tf_op jit(solution)/shard_map/ppermute | solution.py:40
  170.5 0.8 copy-start.7
  180.4 5.5 %collective-permute-start.7 = (f32[512]{0:T(512)S(1)}, f32[512]{0:T(512)S(1)}, u32[]{:S(2)}, u32[]{:S(2)}) collective-permute-start(f32[512]{0:T(512)S(1)} %get-tuple-element.11), channel_id=1, source_target_pairs={{0,1},{1,0},{16,23},{23,16},{2,3},{3,2},{18,17},{17,18},{4,5},{5,4... | collective-permute-start | bytes 6152 | tf_op jit(solution)/shard_map/ppermute | solution.py:40

commit v13 on v11

--- a/solution.py
+++ b/solution.py
@@ -191,14 +191,8 @@
 def local(design, record_weight):
     width = design.shape[1] // 2
     records = design.shape[0]
-    count = lax.axis_size(GROUP_AXES)
-    spread = (
-        jnp.broadcast_to(design[None], (count,) + design.shape).astype(jnp.float32)
-        * record_weight[None, :, None]
-    ).astype(jnp.bfloat16)
-    weighted = lax.all_to_all(spread, GROUP_AXES, 0, 0, tiled=False).reshape(
-        count * records, design.shape[1]
-    )
+    weighted = (design.astype(jnp.float32) * record_weight[:, None]).astype(jnp.bfloat16)
+    weighted = gathered_records(weighted)
     upper_block = weighted[:, :width]
     lower_block = weighted[:, width:]
     position = lax.axis_index(COLUMN_AXES)

time: 185 us -> 184 us (level)
  other arithmetic: 7.3 us -> 5.14 us
    convert_element_type x2 -> x1, other arithmetic: 3.22 us -> 1.06 us  [local(): (design.astype(jnp.float32) * record_weight[:, None]).astype(jnp.bfloat16)]
where the time goes in v13:
time: 184 us
  waiting for transfers between devices  105 us (57%)
  starting transfers between devices  37.4 us (20%)
  Pallas kernels  17.4 us (9%)
  matrix products  13.5 us (7%)
  other arithmetic  5.14 us (3%)
  local copies, waits for them, and re-layouts  4.04 us (2%)
    all_to_all x1, waiting for transfers between devices, gathered_records(): gathered = lax.all_to_all(spread, GROUP_AXES, 0, 0, tiled=False)  52.8 us
    ppermute x4, waiting for transfers between devices, from_partner(): lax.ppermute(value, PARTNER_AXES, partner_pairs(lax.axis_size('y_hi')))  29.2 us
    ppermute x4, waiting for transfers between devices, from_behind(): lax.ppermute(value, COLUMN_AXES, [(source, source + steps) for source in...  23.4 us
    ppermute x4, starting transfers between devices, from_behind(): lax.ppermute(value, COLUMN_AXES, [(source, source + steps) for source in...  20 us
    pallas_call x3, Pallas kernels, rotation_of(): pl.pallas_call(sweeps_kernel, out_shape=jax.ShapeDtypeStruct((2 * width,...  17.4 us
    ppermute x4, starting transfers between devices, from_partner(): lax.ppermute(value, PARTNER_AXES, partner_pairs(lax.axis_size('y_hi')))  8.77 us
    all_to_all x1, starting transfers between devices, gathered_records(): gathered = lax.all_to_all(spread, GROUP_AXES, 0, 0, tiled=False)  8.66 us
    dot_general x3, matrix products, inner_products(): lax.dot_general(left_part, right_part, (((0,), (0,)), ((), ())), preferre...  3.84 us
  transfers between devices with their start and end apart: 9, of which 9 were waited for; matrix products, arithmetic and copies ran while one was open for 3% of the time, Pallas kernels for 0%

profile of v13, /device:TPU:2, one launch (start us, length us, event | category | flops | bytes accessed | tf_op | source)
XLA Modules:
  0.0 183.8 jit_solution(7484449513052243222)
XLA Ops:
  0.6 1.1 multiply_convert_fusion
  1.7 1.5 broadcast_in_dim.22
  3.2 8.7 %all-to-all-start = ((bf16[8,256,512]{2,1,0:T(8,128)(2,1)}), bf16[8,256,512]{2,1,0:T(8,128)(2,1)S(1)}, u32[]{:S(2)}, u32[]{:S(2)}) async-start(bf16[8,256,512]{2,1,0:T(8,128)(2,1)} %broadcast_in_dim.22), calls=%async_computation | async-start | bytes 4194304 | tf_op jit(solution)/shard_map/all_to_all | solution.py:166
  11.9 0.1 pad.15.clone
  11.9 52.8 %all-to-all-done = bf16[8,256,512]{2,1,0:T(8,128)(2,1)S(1)} async-done(((bf16[8,256,512]{2,1,0:T(8,128)(2,1)}), bf16[8,256,512]{2,1,0:T(8,128)(2,1)S(1)}, u32[]{:S(2)}, u32[]{:S(2)}) %all-to-all-start) | async-done | bytes 2097184 | tf_op jit(solution)/shard_map/all_to_all | solution.py:166
  64.8 1.3 convolution_bitcast_fusion
  66.0 0.1 slice_select_fusion.2
  66.1 0.1 maximum_maximum_fusion.local_ref
  66.2 0.0 copy-start
  66.2 2.7 %collective-permute-start = (f32[520,256]{1,0:T(8,128)S(1)}, f32[520,256]{1,0:T(8,128)S(1)}, u32[]{:S(2)}, u32[]{:S(2)}) collective-permute-start(f32[520,256]{1,0:T(8,128)S(1)} %maximum_maximum_fusion.local_ref), channel_id=1, source_target_pairs={{0,1},{1,0},{16,23},{23,16},{2,3},{3,2},{18,17},{17,18},{4,5},{5,4... | collective-permute-start | bytes 1597448 | tf_op jit(solution)/shard_map/ppermute | solution.py:40
  69.0 8.4 %collective-permute-done.received_ref = f32[520,256]{1,0:T(8,128)S(1)} collective-permute-done((f32[520,256]{1,0:T(8,128)S(1)}, f32[520,256]{1,0:T(8,128)S(1)}, u32[]{:S(2)}, u32[]{:S(2)}) %collective-permute-start) | collective-permute-done | bytes 532512 | tf_op jit(solution)/shard_map/ppermute | solution.py:40
  77.4 0.0 copy-done
  77.4 0.8 copy-done.7
  78.2 5.8 %shard_map.41 = bf16[512,512]{1,0:T(8,128)(2,1)} custom-call(f32[520,256]{1,0:T(8,128)} %copy-done, f32[520,256]{1,0:T(8,128)} %copy-done.7), custom_call_target="tpu_custom_call" | custom-call | flops 15728640 | bytes 1048576 | tf_op jit(solution)/shard_map/pallas_call | solution.py:138
  84.0 0.0 copy-start.3
  84.0 1.8 %convolution_convert_fusion.3 = bf16[2048,256]{0,1:T(8,128)(2,1)S(1)} fusion(bf16[2048,512]{1,0:T(8,128)(2,1)S(1)} %bitcast.12, pred[]{:T(512)S(6)} %eq.10, bf16[512,512]{1,0:T(8,128)(2,1)} %shard_map.41), kind=kOutput, calls=%fused_computation.4 | convolution fusion | flops 537526272 | bytes 3670017 | tf_op jit(solution)/shard_map/dot_general | solution.py:208
  85.9 1.9 %collective-permute-start.1 = (bf16[2048,256]{0,1:T(8,128)(2,1)S(1)}, bf16[2048,256]{0,1:T(8,128)(2,1)}, u32[]{:S(2)}, u32[]{:S(2)}) collective-permute-start(bf16[2048,256]{0,1:T(8,128)(2,1)S(1)} %convolution_convert_fusion.3), channel_id=1, source_target_pairs={{0,16},{16,32},{32,48},{48,64},{64,80},{80,96},{96,112},{112,128},... | collective-permute-start | bytes 3145736 | tf_op jit(solution)/shard_map/ppermute | solution.py:24
  87.8 0.0 copy-done.3
  87.8 1.8 convolution_convert_fusion.4
  89.6 10.2 %collective-permute-start.2 = (bf16[2048,256]{0,1:T(8,128)(2,1)}, bf16[2048,256]{0,1:T(8,128)(2,1)}, u32[]{:S(2)}, u32[]{:S(2)}) collective-permute-start(bf16[2048,256]{0,1:T(8,128)(2,1)} %convolution_convert_fusion.4), channel_id=1, source_target_pairs={{16,0},{32,16},{48,32},{64,48},{80,64},{96,80},{112,96},{128,112},... | collective-permute-start | bytes 3145736 | tf_op jit(solution)/shard_map/ppermute | solution.py:24
  99.8 8.9 %collective-permute-done.1 = bf16[2048,256]{0,1:T(8,128)(2,1)} collective-permute-done((bf16[2048,256]{0,1:T(8,128)(2,1)S(1)}, bf16[2048,256]{0,1:T(8,128)(2,1)}, u32[]{:S(2)}, u32[]{:S(2)}) %collective-permute-start.1) | collective-permute-done | bytes 1048608 | tf_op jit(solution)/shard_map/ppermute | solution.py:24
  108.6 1.3 broadcast_select_fusion.3
  110.0 2.4 %collective-permute-done.2 = bf16[2048,256]{0,1:T(8,128)(2,1)} collective-permute-done((bf16[2048,256]{0,1:T(8,128)(2,1)}, bf16[2048,256]{0,1:T(8,128)(2,1)}, u32[]{:S(2)}, u32[]{:S(2)}) %collective-permute-start.2) | collective-permute-done | bytes 1048608 | tf_op jit(solution)/shard_map/ppermute | solution.py:24
  112.4 1.3 broadcast_select_fusion.1
  113.7 0.0 copy-start.5
  113.7 1.3 fusion.1
  115.0 0.0 copy-done.5
  115.0 0.1 slice_select_fusion.1
  115.1 0.0 copy-start.6
  115.1 0.1 maximum_maximum_fusion.1.local_ref
  115.2 0.0 copy-start.2
  115.2 2.2 %collective-permute-start.3 = (f32[520,256]{1,0:T(8,128)S(1)}, f32[520,256]{1,0:T(8,128)S(1)}, u32[]{:S(2)}, u32[]{:S(2)}) collective-permute-start(f32[520,256]{1,0:T(8,128)S(1)} %maximum_maximum_fusion.1.local_ref), channel_id=1, source_target_pairs={{0,1},{1,0},{16,23},{23,16},{2,3},{3,2},{18,17},{17,18},{4,5},{5,4... | collective-permute-start | bytes 1597448 | tf_op jit(solution)/shard_map/ppermute | solution.py:40
  117.5 9.1 %collective-permute-done.3.received_ref = f32[520,256]{1,0:T(8,128)S(1)} collective-permute-done((f32[520,256]{1,0:T(8,128)S(1)}, f32[520,256]{1,0:T(8,128)S(1)}, u32[]{:S(2)}, u32[]{:S(2)}) %collective-permute-start.3) | collective-permute-done | bytes 532512 | tf_op jit(solution)/shard_map/ppermute | solution.py:40
  126.5 0.0 copy-done.2
  126.5 0.0 copy-start.9
  126.5 0.8 copy-done.9
  127.3 5.8 %shard_map.42 = bf16[512,512]{1,0:T(8,128)(2,1)} custom-call(f32[520,256]{1,0:T(8,128)} %copy-done.2, f32[520,256]{1,0:T(8,128)} %copy-done.9), custom_call_target="tpu_custom_call" | custom-call | flops 15728640 | bytes 1048576 | tf_op jit(solution)/shard_map/pallas_call | solution.py:138
  133.1 0.0 copy-done.6
  133.1 1.8 %convolution_convert_fusion.1 = bf16[2048,256]{0,1:T(8,128)(2,1)S(1)} fusion(bf16[2048,256]{0,1:T(8,128)(2,1)S(1)} %copy-done.6, bf16[2048,256]{0,1:T(8,128)(2,1)S(1)} %broadcast_select_fusion.3, pred[]{:T(512)S(6)} %eq.10, bf16[512,512]{1,0:T(8,128)(2,1)} %shard_map.42), kind=kOutput, calls=%fused_computation.2 | convolution fusion | flops 541720576 | bytes 3670017 | tf_op jit(solution)/shard_map/dot_general | solution.py:208
  135.0 1.9 %collective-permute-start.4 = (bf16[2048,256]{0,1:T(8,128)(2,1)S(1)}, bf16[2048,256]{0,1:T(8,128)(2,1)S(1)}, u32[]{:S(2)}, u32[]{:S(2)}) collective-permute-start(bf16[2048,256]{0,1:T(8,128)(2,1)S(1)} %convolution_convert_fusion.1), channel_id=1, source_target_pairs={{0,16},{16,32},{32,48},{48,64},{64,80},{80,96},{96,112},{112,128},... | collective-permute-start | bytes 3145736 | tf_op jit(solution)/shard_map/ppermute | solution.py:24
  136.9 0.0 copy-done.10
  136.9 0.8 convolution_convert_fusion.2
  137.7 6.0 %collective-permute-start.5 = (bf16[2048,256]{0,1:T(8,128)(2,1)S(1)}, bf16[2048,256]{0,1:T(8,128)(2,1)S(1)}, u32[]{:S(2)}, u32[]{:S(2)}) collective-permute-start(bf16[2048,256]{0,1:T(8,128)(2,1)S(1)} %convolution_convert_fusion.2), channel_id=1, source_target_pairs={{16,0},{32,16},{48,32},{64,48},{80,64},{96,80},{112,96},{128,112},... | collective-permute-start | bytes 3145736 | tf_op jit(solution)/shard_map/ppermute | solution.py:24
  143.7 9.8 %collective-permute-done.4 = bf16[2048,256]{0,1:T(8,128)(2,1)S(1)} collective-permute-done((bf16[2048,256]{0,1:T(8,128)(2,1)S(1)}, bf16[2048,256]{0,1:T(8,128)(2,1)S(1)}, u32[]{:S(2)}, u32[]{:S(2)}) %collective-permute-start.4) | collective-permute-done | bytes 1048608 | tf_op jit(solution)/shard_map/ppermute | solution.py:24
  153.4 0.1 broadcast_select_fusion.2
  153.5 2.4 %collective-permute-done.5 = bf16[2048,256]{0,1:T(8,128)(2,1)S(1)} collective-permute-done((bf16[2048,256]{0,1:T(8,128)(2,1)S(1)}, bf16[2048,256]{0,1:T(8,128)(2,1)S(1)}, u32[]{:S(2)}, u32[]{:S(2)}) %collective-permute-start.5) | collective-permute-done | bytes 1048608 | tf_op jit(solution)/shard_map/ppermute | solution.py:24
  156.0 0.1 broadcast_select_fusion
  156.1 1.3 fusion
  157.4 0.1 slice_select_fusion
  157.4 0.1 maximum_maximum_fusion.2.local_ref
  157.6 0.0 copy-start.1
  157.6 1.9 %collective-permute-start.6 = (f32[520,256]{1,0:T(8,128)S(1)}, f32[520,256]{1,0:T(8,128)S(1)}, u32[]{:S(2)}, u32[]{:S(2)}) collective-permute-start(f32[520,256]{1,0:T(8,128)S(1)} %maximum_maximum_fusion.2.local_ref), channel_id=1, source_target_pairs={{0,1},{1,0},{16,23},{23,16},{2,3},{3,2},{18,17},{17,18},{4,5},{5,4... | collective-permute-start | bytes 1597448 | tf_op jit(solution)/shard_map/ppermute | solution.py:40
  159.5 9.2 %collective-permute-done.6.received_ref = f32[520,256]{1,0:T(8,128)S(1)} collective-permute-done((f32[520,256]{1,0:T(8,128)S(1)}, f32[520,256]{1,0:T(8,128)S(1)}, u32[]{:S(2)}, u32[]{:S(2)}) %collective-permute-start.6) | collective-permute-done | bytes 532512 | tf_op jit(solution)/shard_map/ppermute | solution.py:40
  168.7 0.0 copy-done.1
  168.7 0.0 copy-start.8
  168.7 0.8 copy-done.8
  169.5 5.8 %shard_map.43 = bf16[512,512]{1,0:T(8,128)(2,1)} custom-call(f32[520,256]{1,0:T(8,128)} %copy-done.1, f32[520,256]{1,0:T(8,128)} %copy-done.8), custom_call_target="tpu_custom_call" | custom-call | flops 15728640 | bytes 1048576 | tf_op jit(solution)/shard_map/pallas_call | solution.py:138
  175.3 0.0 copy-start.4
  175.3 2.4 %multiply_reduce_fusion = f32[512]{0:T(512)S(1)} fusion(bf16[512,512]{1,0:T(8,128)(2,1)} %shard_map.43, bf16[2048,256]{0,1:T(8,128)(2,1)S(1)} %broadcast_select_fusion, bf16[2048,256]{0,1:T(8,128)(2,1)S(1)} %broadcast_select_fusion.2), kind=kOutput, calls=%fused_computation | convolution fusion | flops 1082129920 | bytes 2623488 | tf_op jit(solution)/shard_map/dot_general | solution.py:222
  177.8 1.9 %collective-permute-start.7 = (f32[512]{0:T(512)S(1)}, f32[512]{0:T(512)S(1)}, u32[]{:S(2)}, u32[]{:S(2)}) collective-permute-start(f32[512]{0:T(512)S(1)} %multiply_reduce_fusion), channel_id=1, source_target_pairs={{0,1},{1,0},{16,23},{23,16},{2,3},{3,2},{18,17},{17,18},{4,5},{5,4... | collective-permute-start | bytes 6152 | tf_op jit(solution)/shard_map/ppermute | solution.py:40
  179.7 0.0 copy-done.4
  179.7 1.0 convolution_convert_fusion.5
  180.7 2.5 %collective-permute-done.7 = f32[512]{0:T(512)S(1)} collective-permute-done((f32[512]{0:T(512)S(1)}, f32[512]{0:T(512)S(1)}, u32[]{:S(2)}, u32[]{:S(2)}) %collective-permute-start.7) | collective-permute-done | bytes 2080 | tf_op jit(solution)/shard_map/ppermute | solution.py:40
  183.2 0.6 add_sqrt_fusion
  (3 shorter events, 0.0 us)
Async XLA Ops:
  3.2 61.5 %all-to-all-start = ((bf16[8,256,512]{2,1,0:T(8,128)(2,1)}), bf16[8,256,512]{2,1,0:T(8,128)(2,1)S(1)}, u32[]{:S(2)}, u32[]{:S(2)}) async-start(bf16[8,256,512]{2,1,0:T(8,128)(2,1)} %broadcast_in_dim.22), calls=%async_computation | async-start | bytes 4194304 | tf_op jit(solution)/shard_map/all_to_all | solution.py:166
  66.2 11.2 %copy-start = (f32[520,256]{1,0:T(8,128)}, f32[520,256]{1,0:T(8,128)S(1)}, u32[]{:S(2)}) copy-start(f32[520,256]{1,0:T(8,128)S(1)} %maximum_maximum_fusion.local_ref) | copy-start | bytes 1597444
  66.2 11.2 %collective-permute-start = (f32[520,256]{1,0:T(8,128)S(1)}, f32[520,256]{1,0:T(8,128)S(1)}, u32[]{:S(2)}, u32[]{:S(2)}) collective-permute-start(f32[520,256]{1,0:T(8,128)S(1)} %maximum_maximum_fusion.local_ref), channel_id=1, source_target_pairs={{0,1},{1,0},{16,23},{23,16},{2,3},{3,2},{18,17},{17,18},{4,5},{5,4... | collective-permute-start | bytes 1597448 | tf_op jit(solution)/shard_map/ppermute | solution.py:40
  77.4 0.8 copy-start.7
  84.0 3.8 %copy-start.3 = (bf16[512,512]{1,0:T(8,128)(2,1)S(1)}, bf16[512,512]{1,0:T(8,128)(2,1)}, u32[]{:S(2)}) copy-start(bf16[512,512]{1,0:T(8,128)(2,1)} %shard_map.41) | copy-start | bytes 1572868
  85.9 22.8 %collective-permute-start.1 = (bf16[2048,256]{0,1:T(8,128)(2,1)S(1)}, bf16[2048,256]{0,1:T(8,128)(2,1)}, u32[]{:S(2)}, u32[]{:S(2)}) collective-permute-start(bf16[2048,256]{0,1:T(8,128)(2,1)S(1)} %convolution_convert_fusion.3), channel_id=1, source_target_pairs={{0,16},{16,32},{32,48},{48,64},{64,80},{80,96},{96,112},{112,128},... | collective-permute-start | bytes 3145736 | tf_op jit(solution)/shard_map/ppermute | solution.py:24
  89.6 22.8 %collective-permute-start.2 = (bf16[2048,256]{0,1:T(8,128)(2,1)}, bf16[2048,256]{0,1:T(8,128)(2,1)}, u32[]{:S(2)}, u32[]{:S(2)}) collective-permute-start(bf16[2048,256]{0,1:T(8,128)(2,1)} %convolution_convert_fusion.4), channel_id=1, source_target_pairs={{16,0},{32,16},{48,32},{64,48},{80,64},{96,80},{112,96},{128,112},... | collective-permute-start | bytes 3145736 | tf_op jit(solution)/shard_map/ppermute | solution.py:24
  113.7 1.3 copy-start.5
  115.1 18.0 %copy-start.6 = (bf16[2048,256]{0,1:T(8,128)(2,1)S(1)}, bf16[2048,256]{0,1:T(8,128)(2,1)}, u32[]{:S(2)}) copy-start(bf16[2048,256]{0,1:T(8,128)(2,1)} %copy-done.5) | copy-start | bytes 3145732
  115.2 11.3 %copy-start.2 = (f32[520,256]{1,0:T(8,128)}, f32[520,256]{1,0:T(8,128)S(1)}, u32[]{:S(2)}) copy-start(f32[520,256]{1,0:T(8,128)S(1)} %maximum_maximum_fusion.1.local_ref) | copy-start | bytes 1597444
  115.2 11.3 %collective-permute-start.3 = (f32[520,256]{1,0:T(8,128)S(1)}, f32[520,256]{1,0:T(8,128)S(1)}, u32[]{:S(2)}, u32[]{:S(2)}) collective-permute-start(f32[520,256]{1,0:T(8,128)S(1)} %maximum_maximum_fusion.1.local_ref), channel_id=1, source_target_pairs={{0,1},{1,0},{16,23},{23,16},{2,3},{3,2},{18,17},{17,18},{4,5},{5,4... | collective-permute-start | bytes 1597448 | tf_op jit(solution)/shard_map/ppermute | solution.py:40
  126.5 0.8 copy-start.9
  133.1 3.8 %copy-start.10 = (bf16[512,512]{1,0:T(8,128)(2,1)S(1)}, bf16[512,512]{1,0:T(8,128)(2,1)}, u32[]{:S(2)}) copy-start(bf16[512,512]{1,0:T(8,128)(2,1)} %shard_map.42) | copy-start | bytes 1572868
  135.0 18.5 %collective-permute-start.4 = (bf16[2048,256]{0,1:T(8,128)(2,1)S(1)}, bf16[2048,256]{0,1:T(8,128)(2,1)S(1)}, u32[]{:S(2)}, u32[]{:S(2)}) collective-permute-start(bf16[2048,256]{0,1:T(8,128)(2,1)S(1)} %convolution_convert_fusion.1), channel_id=1, source_target_pairs={{0,16},{16,32},{32,48},{48,64},{64,80},{80,96},{96,112},{112,128},... | collective-permute-start | bytes 3145736 | tf_op jit(solution)/shard_map/ppermute | solution.py:24
  137.7 18.3 %collective-permute-start.5 = (bf16[2048,256]{0,1:T(8,128)(2,1)S(1)}, bf16[2048,256]{0,1:T(8,128)(2,1)S(1)}, u32[]{:S(2)}, u32[]{:S(2)}) collective-permute-start(bf16[2048,256]{0,1:T(8,128)(2,1)S(1)} %convolution_convert_fusion.2), channel_id=1, source_target_pairs={{16,0},{32,16},{48,32},{64,48},{80,64},{96,80},{112,96},{128,112},... | collective-permute-start | bytes 3145736 | tf_op jit(solution)/shard_map/ppermute | solution.py:24
  157.6 11.2 %copy-start.1 = (f32[520,256]{1,0:T(8,128)}, f32[520,256]{1,0:T(8,128)S(1)}, u32[]{:S(2)}) copy-start(f32[520,256]{1,0:T(8,128)S(1)} %maximum_maximum_fusion.2.local_ref) | copy-start | bytes 1597444
  157.6 11.2 %collective-permute-start.6 = (f32[520,256]{1,0:T(8,128)S(1)}, f32[520,256]{1,0:T(8,128)S(1)}, u32[]{:S(2)}, u32[]{:S(2)}) collective-permute-start(f32[520,256]{1,0:T(8,128)S(1)} %maximum_maximum_fusion.2.local_ref), channel_id=1, source_target_pairs={{0,1},{1,0},{16,23},{23,16},{2,3},{3,2},{18,17},{17,18},{4,5},{5,4... | collective-permute-start | bytes 1597448 | tf_op jit(solution)/shard_map/ppermute | solution.py:40
  168.7 0.8 copy-start.8
  175.3 4.3 %copy-start.4 = (bf16[512,512]{1,0:T(8,128)(2,1)S(1)}, bf16[512,512]{1,0:T(8,128)(2,1)}, u32[]{:S(2)}) copy-start(bf16[512,512]{1,0:T(8,128)(2,1)} %shard_map.43) | copy-start | bytes 1572868
  177.8 5.5 %collective-permute-start.7 = (f32[512]{0:T(512)S(1)}, f32[512]{0:T(512)S(1)}, u32[]{:S(2)}, u32[]{:S(2)}) collective-permute-start(f32[512]{0:T(512)S(1)} %multiply_reduce_fusion), channel_id=1, source_target_pairs={{0,1},{1,0},{16,23},{23,16},{2,3},{3,2},{18,17},{17,18},{4,5},{5,4... | collective-permute-start | bytes 6152 | tf_op jit(solution)/shard_map/ppermute | solution.py:40

commit v14 on v10

--- a/solution.py
+++ b/solution.py
@@ -208,16 +208,18 @@
             break
         first_columns = rotation[:, :width]
         second_columns = rotation[:, width:]
-        going_right = jnp.dot(
-            pair_data,
-            jnp.where(position == 0, second_columns, first_columns),
-            preferred_element_type=jnp.float32,
-        ).astype(jnp.bfloat16)
-        going_left = jnp.dot(
-            pair_data,
-            jnp.where(position == 0, first_columns, second_columns),
-            preferred_element_type=jnp.float32,
-        ).astype(jnp.bfloat16)
+        chosen = jnp.concatenate(
+            [
+                jnp.where(position == 0, second_columns, first_columns),
+                jnp.where(position == 0, first_columns, second_columns),
+            ],
+            axis=1,
+        )
+        moving_blocks = jnp.dot(pair_data, chosen, preferred_element_type=jnp.float32).astype(
+            jnp.bfloat16
+        )
+        going_right = moving_blocks[:, :width]
+        going_left = moving_blocks[:, width:]
         from_left = send_right(going_right)
         from_right = send_left(going_left)
         upper_block = jnp.where(position == 0, going_left, from_left)

time: 184 us -> 187 us (1.016)
  local copies, waits for them, and re-layouts: 4.76 us -> 7.38 us
  matrix products: 12.4 us -> 10.4 us
    dot_general x4 -> x2, matrix products: 6.2 us -> 4.2 us  [local(): jnp.dot(pair_data, chosen, preferred_element_type=jnp.float32)]
  transfers between devices with their start and end apart: 9 -> 9, of which waited for: 9 -> 9; matrix products, arithmetic and copies ran while one was open for 3% -> 0% of each run, Pallas kernels for 0% -> 0%
where the time goes in v14:
time: 187 us; the launch traced here: 186 us
  waiting for transfers between devices  106 us (57%)
  starting transfers between devices  37.4 us (20%)
  Pallas kernels  17.3 us (9%)
  matrix products  10.4 us (6%)
  local copies, waits for them, and re-layouts  7.38 us (4%)
  other arithmetic  6.33 us (3%)
    all_to_all x1, waiting for transfers between devices, gathered_records(): gathered = lax.all_to_all(spread, GROUP_AXES, 0, 0, tiled=False)  52.8 us
    ppermute x4, waiting for transfers between devices, from_partner(): lax.ppermute(value, PARTNER_AXES, partner_pairs(lax.axis_size('y_hi')))  29.6 us
    ppermute x4, waiting for transfers between devices, from_behind(): lax.ppermute(value, COLUMN_AXES, [(source, source + steps) for source in...  23.9 us
    ppermute x4, starting transfers between devices, from_behind(): lax.ppermute(value, COLUMN_AXES, [(source, source + steps) for source in...  20 us
    pallas_call x3, Pallas kernels, rotation_of(): pl.pallas_call(sweeps_kernel, out_shape=jax.ShapeDtypeStruct((2 * width,...  17.3 us
    ppermute x4, starting transfers between devices, from_partner(): lax.ppermute(value, PARTNER_AXES, partner_pairs(lax.axis_size('y_hi')))  8.76 us
    all_to_all x1, starting transfers between devices, gathered_records(): gathered = lax.all_to_all(spread, GROUP_AXES, 0, 0, tiled=False)  8.66 us
    dot_general x2, matrix products, local(): jnp.dot(pair_data, chosen, preferred_element_type=jnp.float32)  4.2 us
  transfers between devices with their start and end apart: 9, of which 9 were waited for; matrix products, arithmetic and copies ran while one was open for 0% of the time, Pallas kernels for 0%

profile of v14, /device:TPU:2, one launch (start us, length us, event | category | flops | bytes accessed | tf_op | source)
XLA Modules:
  0.0 186.0 jit_solution(15308178966728891500)
XLA Ops:
  0.6 1.1 multiply_convert_fusion
  1.7 1.5 broadcast_in_dim.22
  3.2 8.7 %all-to-all-start = ((bf16[8,256,512]{2,1,0:T(8,128)(2,1)}), bf16[8,256,512]{2,1,0:T(8,128)(2,1)S(1)}, u32[]{:S(2)}, u32[]{:S(2)}) async-start(bf16[8,256,512]{2,1,0:T(8,128)(2,1)} %broadcast_in_dim.22), calls=%async_computation | async-start | bytes 4194304 | tf_op jit(solution)/shard_map/all_to_all | solution.py:166
  11.9 0.1 pad.19.clone
  12.0 52.8 %all-to-all-done = bf16[8,256,512]{2,1,0:T(8,128)(2,1)S(1)} async-done(((bf16[8,256,512]{2,1,0:T(8,128)(2,1)}), bf16[8,256,512]{2,1,0:T(8,128)(2,1)S(1)}, u32[]{:S(2)}, u32[]{:S(2)}) %all-to-all-start) | async-done | bytes 2097184 | tf_op jit(solution)/shard_map/all_to_all | solution.py:166
  64.8 0.0 copy-start.3
  64.8 1.3 convolution_bitcast_fusion
  66.0 0.1 copy-done.3
  66.1 0.1 slice_select_fusion.2
  66.2 0.1 maximum_maximum_fusion.local_ref
  66.3 0.0 copy-start
  66.3 2.7 %collective-permute-start = (f32[520,256]{1,0:T(8,128)S(1)}, f32[520,256]{1,0:T(8,128)S(1)}, u32[]{:S(2)}, u32[]{:S(2)}) collective-permute-start(f32[520,256]{1,0:T(8,128)S(1)} %maximum_maximum_fusion.local_ref), channel_id=1, source_target_pairs={{0,1},{1,0},{16,23},{23,16},{2,3},{3,2},{18,17},{17,18},{4,5},{5,4... | collective-permute-start | bytes 1597448 | tf_op jit(solution)/shard_map/ppermute | solution.py:40
  69.0 8.5 %collective-permute-done.received_ref = f32[520,256]{1,0:T(8,128)S(1)} collective-permute-done((f32[520,256]{1,0:T(8,128)S(1)}, f32[520,256]{1,0:T(8,128)S(1)}, u32[]{:S(2)}, u32[]{:S(2)}) %collective-permute-start) | collective-permute-done | bytes 532512 | tf_op jit(solution)/shard_map/ppermute | solution.py:40
  77.5 0.0 copy-done
  77.5 0.0 copy-start.7
  77.5 0.8 copy-done.7
  78.3 5.8 %shard_map.41 = bf16[512,512]{1,0:T(8,128)(2,1)} custom-call(f32[520,256]{1,0:T(8,128)} %copy-done, f32[520,256]{1,0:T(8,128)} %copy-done.7), custom_call_target="tpu_custom_call" | custom-call | flops 15728640 | bytes 1048576 | tf_op jit(solution)/shard_map/pallas_call | solution.py:138
  84.0 1.1 broadcast_select_fusion.7
  85.1 2.9 %convolution_convert_fusion.2 = bf16[2048,512]{0,1:T(8,128)(2,1)S(1)} fusion(bf16[2048,512]{1,0:T(8,128)(2,1)} %bitcast.10, bf16[512,256]{1,0:T(8,128)(2,1)S(1)} %get-tuple-element.22, bf16[512,256]{1,0:T(8,128)(2,1)S(1)} %get-tuple-element.21), kind=kOutput, calls=%fused_computation.3 | convolution fusion | flops 1075838976 | bytes 4718592 | tf_op jit(solution)/shard_map/dot_general | solution.py:218
  88.0 1.4 fusion.14
  89.4 1.9 %collective-permute-start.1 = (bf16[2048,256]{0,1:T(8,128)(2,1)}, bf16[2048,256]{0,1:T(8,128)(2,1)S(1)}, u32[]{:S(2)}, u32[]{:S(2)}) collective-permute-start(bf16[2048,256]{0,1:T(8,128)(2,1)} %get-tuple-element.8), channel_id=1, source_target_pairs={{0,16},{16,32},{32,48},{48,64},{64,80},{80,96},{96,112},{112,128},... | collective-permute-start | bytes 3145736 | tf_op jit(solution)/shard_map/ppermute | solution.py:24
  91.4 10.2 %collective-permute-start.2 = (bf16[2048,256]{0,1:T(8,128)(2,1)}, bf16[2048,256]{0,1:T(8,128)(2,1)}, u32[]{:S(2)}, u32[]{:S(2)}) collective-permute-start(bf16[2048,256]{0,1:T(8,128)(2,1)} %get-tuple-element.9), channel_id=1, source_target_pairs={{16,0},{32,16},{48,32},{64,48},{80,64},{96,80},{112,96},{128,112},... | collective-permute-start | bytes 3145736 | tf_op jit(solution)/shard_map/ppermute | solution.py:24
  101.6 10.7 %collective-permute-done.1 = bf16[2048,256]{0,1:T(8,128)(2,1)S(1)} collective-permute-done((bf16[2048,256]{0,1:T(8,128)(2,1)}, bf16[2048,256]{0,1:T(8,128)(2,1)S(1)}, u32[]{:S(2)}, u32[]{:S(2)}) %collective-permute-start.1) | collective-permute-done | bytes 1048608 | tf_op jit(solution)/shard_map/ppermute | solution.py:24
  112.3 0.0 copy-start.6
  112.3 1.0 copy-done.6
  113.3 0.9 collective-permute-done.2
  114.2 1.7 broadcast_select_fusion.3
  115.9 0.0 copy-start.4
  115.9 1.3 fusion.1
  117.2 0.0 copy-done.4
  117.2 0.1 slice_select_fusion.1
  117.3 0.0 copy-start.5
  117.3 0.1 maximum_maximum_fusion.1.local_ref
  117.4 0.0 copy-start.2
  117.4 2.2 %collective-permute-start.3 = (f32[520,256]{1,0:T(8,128)S(1)}, f32[520,256]{1,0:T(8,128)S(1)}, u32[]{:S(2)}, u32[]{:S(2)}) collective-permute-start(f32[520,256]{1,0:T(8,128)S(1)} %maximum_maximum_fusion.1.local_ref), channel_id=1, source_target_pairs={{0,1},{1,0},{16,23},{23,16},{2,3},{3,2},{18,17},{17,18},{4,5},{5,4... | collective-permute-start | bytes 1597448 | tf_op jit(solution)/shard_map/ppermute | solution.py:40
  119.7 9.1 %collective-permute-done.3.received_ref = f32[520,256]{1,0:T(8,128)S(1)} collective-permute-done((f32[520,256]{1,0:T(8,128)S(1)}, f32[520,256]{1,0:T(8,128)S(1)}, u32[]{:S(2)}, u32[]{:S(2)}) %collective-permute-start.3) | collective-permute-done | bytes 532512 | tf_op jit(solution)/shard_map/ppermute | solution.py:40
  128.7 0.0 copy-done.2
  128.7 0.0 copy-start.9
  128.7 0.8 copy-done.9
  129.6 5.8 %shard_map.42 = bf16[512,512]{1,0:T(8,128)(2,1)} custom-call(f32[520,256]{1,0:T(8,128)} %copy-done.2, f32[520,256]{1,0:T(8,128)} %copy-done.9), custom_call_target="tpu_custom_call" | custom-call | flops 15728640 | bytes 1048576 | tf_op jit(solution)/shard_map/pallas_call | solution.py:138
  135.3 1.1 broadcast_select_fusion.5
  136.4 0.0 copy-done.5
  136.4 1.3 convolution_convert_fusion.1
  137.7 0.1 fusion.13
  137.9 1.9 %collective-permute-start.4 = (bf16[2048,256]{0,1:T(8,128)(2,1)S(1)}, bf16[2048,256]{0,1:T(8,128)(2,1)S(1)}, u32[]{:S(2)}, u32[]{:S(2)}) collective-permute-start(bf16[2048,256]{0,1:T(8,128)(2,1)S(1)} %get-tuple-element.4), channel_id=1, source_target_pairs={{0,16},{16,32},{32,48},{48,64},{64,80},{80,96},{96,112},{112,128},... | collective-permute-start | bytes 3145736 | tf_op jit(solution)/shard_map/ppermute | solution.py:24
  139.8 6.0 %collective-permute-start.5 = (bf16[2048,256]{0,1:T(8,128)(2,1)S(1)}, bf16[2048,256]{0,1:T(8,128)(2,1)S(1)}, u32[]{:S(2)}, u32[]{:S(2)}) collective-permute-start(bf16[2048,256]{0,1:T(8,128)(2,1)S(1)} %get-tuple-element.5), channel_id=1, source_target_pairs={{16,0},{32,16},{48,32},{64,48},{80,64},{96,80},{112,96},{128,112},... | collective-permute-start | bytes 3145736 | tf_op jit(solution)/shard_map/ppermute | solution.py:24
  145.8 10.5 %collective-permute-done.4 = bf16[2048,256]{0,1:T(8,128)(2,1)S(1)} collective-permute-done((bf16[2048,256]{0,1:T(8,128)(2,1)S(1)}, bf16[2048,256]{0,1:T(8,128)(2,1)S(1)}, u32[]{:S(2)}, u32[]{:S(2)}) %collective-permute-start.4) | collective-permute-done | bytes 1048608 | tf_op jit(solution)/shard_map/ppermute | solution.py:24
  156.3 1.8 collective-permute-done.5
  158.1 0.2 broadcast_select_fusion.2
  158.3 1.3 fusion
  159.6 0.1 slice_select_fusion
  159.7 0.1 maximum_maximum_fusion.2.local_ref
  159.8 0.0 copy-start.1
  159.8 1.9 %collective-permute-start.6 = (f32[520,256]{1,0:T(8,128)S(1)}, f32[520,256]{1,0:T(8,128)S(1)}, u32[]{:S(2)}, u32[]{:S(2)}) collective-permute-start(f32[520,256]{1,0:T(8,128)S(1)} %maximum_maximum_fusion.2.local_ref), channel_id=1, source_target_pairs={{0,1},{1,0},{16,23},{23,16},{2,3},{3,2},{18,17},{17,18},{4,5},{5,4... | collective-permute-start | bytes 1597448 | tf_op jit(solution)/shard_map/ppermute | solution.py:40
  161.7 9.2 %collective-permute-done.6.received_ref = f32[520,256]{1,0:T(8,128)S(1)} collective-permute-done((f32[520,256]{1,0:T(8,128)S(1)}, f32[520,256]{1,0:T(8,128)S(1)}, u32[]{:S(2)}, u32[]{:S(2)}) %collective-permute-start.6) | collective-permute-done | bytes 532512 | tf_op jit(solution)/shard_map/ppermute | solution.py:40
  171.0 0.0 copy-done.1
  171.0 0.0 copy-start.8
  171.0 0.8 copy-done.8
  171.8 5.8 %shard_map.43 = bf16[512,512]{1,0:T(8,128)(2,1)} custom-call(f32[520,256]{1,0:T(8,128)} %copy-done.1, f32[520,256]{1,0:T(8,128)} %copy-done.8), custom_call_target="tpu_custom_call" | custom-call | flops 15728640 | bytes 1048576 | tf_op jit(solution)/shard_map/pallas_call | solution.py:138
  177.6 2.3 %multiply_reduce_fusion = (f32[512]{0:T(512)S(1)}, bf16[2048,512]{1,0:T(8,128)(2,1)S(1)}) fusion(bf16[512,512]{1,0:T(8,128)(2,1)} %shard_map.43, bf16[2048,256]{0,1:T(8,128)(2,1)S(1)} %get-tuple-element.3, bf16[2048,256]{0,1:T(8,128)(2,1)S(1)} %get-tuple-element.2), kind=kOutput, calls=%fused_computation | convolution fusion | flops 1082129920 | bytes 4720640 | tf_op jit(solution)/shard_map/dot_general | solution.py:205
  179.9 1.9 %collective-permute-start.7 = (f32[512]{0:T(512)S(1)}, f32[512]{0:T(512)S(1)}, u32[]{:S(2)}, u32[]{:S(2)}) collective-permute-start(f32[512]{0:T(512)S(1)} %get-tuple-element.23), channel_id=1, source_target_pairs={{0,1},{1,0},{16,23},{23,16},{2,3},{3,2},{18,17},{17,18},{4,5},{5,4... | collective-permute-start | bytes 6152 | tf_op jit(solution)/shard_map/ppermute | solution.py:40
  181.8 0.7 constant_dynamic-slice_fusion
  182.6 2.8 %collective-permute-done.7 = f32[512]{0:T(512)S(1)} collective-permute-done((f32[512]{0:T(512)S(1)}, f32[512]{0:T(512)S(1)}, u32[]{:S(2)}, u32[]{:S(2)}) %collective-permute-start.7) | collective-permute-done | bytes 2080 | tf_op jit(solution)/shard_map/ppermute | solution.py:40
  185.4 0.6 add_sqrt_fusion
  (1 shorter events, 0.0 us)
Async XLA Ops:
  3.2 61.5 %all-to-all-start = ((bf16[8,256,512]{2,1,0:T(8,128)(2,1)}), bf16[8,256,512]{2,1,0:T(8,128)(2,1)S(1)}, u32[]{:S(2)}, u32[]{:S(2)}) async-start(bf16[8,256,512]{2,1,0:T(8,128)(2,1)} %broadcast_in_dim.22), calls=%async_computation | async-start | bytes 4194304 | tf_op jit(solution)/shard_map/all_to_all | solution.py:166
  64.8 1.3 copy-start.3
  66.3 11.2 %copy-start = (f32[520,256]{1,0:T(8,128)}, f32[520,256]{1,0:T(8,128)S(1)}, u32[]{:S(2)}) copy-start(f32[520,256]{1,0:T(8,128)S(1)} %maximum_maximum_fusion.local_ref) | copy-start | bytes 1597444
  66.3 11.2 %collective-permute-start = (f32[520,256]{1,0:T(8,128)S(1)}, f32[520,256]{1,0:T(8,128)S(1)}, u32[]{:S(2)}, u32[]{:S(2)}) collective-permute-start(f32[520,256]{1,0:T(8,128)S(1)} %maximum_maximum_fusion.local_ref), channel_id=1, source_target_pairs={{0,1},{1,0},{16,23},{23,16},{2,3},{3,2},{18,17},{17,18},{4,5},{5,4... | collective-permute-start | bytes 1597448 | tf_op jit(solution)/shard_map/ppermute | solution.py:40
  77.5 0.8 copy-start.7
  89.4 22.9 %collective-permute-start.1 = (bf16[2048,256]{0,1:T(8,128)(2,1)}, bf16[2048,256]{0,1:T(8,128)(2,1)S(1)}, u32[]{:S(2)}, u32[]{:S(2)}) collective-permute-start(bf16[2048,256]{0,1:T(8,128)(2,1)} %get-tuple-element.8), channel_id=1, source_target_pairs={{0,16},{16,32},{32,48},{48,64},{64,80},{80,96},{96,112},{112,128},... | collective-permute-start | bytes 3145736 | tf_op jit(solution)/shard_map/ppermute | solution.py:24
  91.4 22.8 %collective-permute-start.2 = (bf16[2048,256]{0,1:T(8,128)(2,1)}, bf16[2048,256]{0,1:T(8,128)(2,1)}, u32[]{:S(2)}, u32[]{:S(2)}) collective-permute-start(bf16[2048,256]{0,1:T(8,128)(2,1)} %get-tuple-element.9), channel_id=1, source_target_pairs={{16,0},{32,16},{48,32},{64,48},{80,64},{96,80},{112,96},{128,112},... | collective-permute-start | bytes 3145736 | tf_op jit(solution)/shard_map/ppermute | solution.py:24
  112.3 1.0 copy-start.6
  115.9 1.3 copy-start.4
  117.3 19.1 %copy-start.5 = (bf16[2048,256]{0,1:T(8,128)(2,1)S(1)}, bf16[2048,256]{0,1:T(8,128)(2,1)}, u32[]{:S(2)}) copy-start(bf16[2048,256]{0,1:T(8,128)(2,1)} %copy-done.4) | copy-start | bytes 3145732
  117.4 11.3 %copy-start.2 = (f32[520,256]{1,0:T(8,128)}, f32[520,256]{1,0:T(8,128)S(1)}, u32[]{:S(2)}) copy-start(f32[520,256]{1,0:T(8,128)S(1)} %maximum_maximum_fusion.1.local_ref) | copy-start | bytes 1597444
  117.4 11.3 %collective-permute-start.3 = (f32[520,256]{1,0:T(8,128)S(1)}, f32[520,256]{1,0:T(8,128)S(1)}, u32[]{:S(2)}, u32[]{:S(2)}) collective-permute-start(f32[520,256]{1,0:T(8,128)S(1)} %maximum_maximum_fusion.1.local_ref), channel_id=1, source_target_pairs={{0,1},{1,0},{16,23},{23,16},{2,3},{3,2},{18,17},{17,18},{4,5},{5,4... | collective-permute-start | bytes 1597448 | tf_op jit(solution)/shard_map/ppermute | solution.py:40
  128.7 0.8 copy-start.9
  137.9 18.5 %collective-permute-start.4 = (bf16[2048,256]{0,1:T(8,128)(2,1)S(1)}, bf16[2048,256]{0,1:T(8,128)(2,1)S(1)}, u32[]{:S(2)}, u32[]{:S(2)}) collective-permute-start(bf16[2048,256]{0,1:T(8,128)(2,1)S(1)} %get-tuple-element.4), channel_id=1, source_target_pairs={{0,16},{16,32},{32,48},{48,64},{64,80},{80,96},{96,112},{112,128},... | collective-permute-start | bytes 3145736 | tf_op jit(solution)/shard_map/ppermute | solution.py:24
  139.8 18.3 %collective-permute-start.5 = (bf16[2048,256]{0,1:T(8,128)(2,1)S(1)}, bf16[2048,256]{0,1:T(8,128)(2,1)S(1)}, u32[]{:S(2)}, u32[]{:S(2)}) collective-permute-start(bf16[2048,256]{0,1:T(8,128)(2,1)S(1)} %get-tuple-element.5), channel_id=1, source_target_pairs={{16,0},{32,16},{48,32},{64,48},{80,64},{96,80},{112,96},{128,112},... | collective-permute-start | bytes 3145736 | tf_op jit(solution)/shard_map/ppermute | solution.py:24
  159.8 11.2 %copy-start.1 = (f32[520,256]{1,0:T(8,128)}, f32[520,256]{1,0:T(8,128)S(1)}, u32[]{:S(2)}) copy-start(f32[520,256]{1,0:T(8,128)S(1)} %maximum_maximum_fusion.2.local_ref) | copy-start | bytes 1597444
  159.8 11.2 %collective-permute-start.6 = (f32[520,256]{1,0:T(8,128)S(1)}, f32[520,256]{1,0:T(8,128)S(1)}, u32[]{:S(2)}, u32[]{:S(2)}) collective-permute-start(f32[520,256]{1,0:T(8,128)S(1)} %maximum_maximum_fusion.2.local_ref), channel_id=1, source_target_pairs={{0,1},{1,0},{16,23},{23,16},{2,3},{3,2},{18,17},{17,18},{4,5},{5,4... | collective-permute-start | bytes 1597448 | tf_op jit(solution)/shard_map/ppermute | solution.py:40
  171.0 0.8 copy-start.8
  179.9 5.5 %collective-permute-start.7 = (f32[512]{0:T(512)S(1)}, f32[512]{0:T(512)S(1)}, u32[]{:S(2)}, u32[]{:S(2)}) collective-permute-start(f32[512]{0:T(512)S(1)} %get-tuple-element.23), channel_id=1, source_target_pairs={{0,1},{1,0},{16,23},{23,16},{2,3},{3,2},{18,17},{17,18},{4,5},{5,4... | collective-permute-start | bytes 6152 | tf_op jit(solution)/shard_map/ppermute | solution.py:40

commit v15 on v10

--- a/solution.py
+++ b/solution.py
@@ -140,6 +140,7 @@
         out_shape=jax.ShapeDtypeStruct((2 * width, 2 * width), jnp.bfloat16),
         in_specs=[vmem, vmem],
         out_specs=vmem,
+        compiler_params=pltpu.CompilerParams(vmem_limit_bytes=16 * 1024 * 1024),
         cost_estimate=pl.CostEstimate(
             flops=SWEEPS * 40 * width * width, transcendentals=SWEEPS * 8 * width, bytes_accessed=4 * 4 * width * width
         ),

time: 184 us -> 171 us (0.929)
  Pallas kernels: 17.4 us -> 11.4 us
  matrix products: 12.4 us -> 9.18 us
  local copies, waits for them, and re-layouts: 4.76 us -> 2.32 us
    pallas_call x3, Pallas kernels: 17.4 us -> 11.4 us  [rotation_of(): pl.pallas_call(sweeps_kernel, out_shape=jax.ShapeDtypeStruct((2 * width,...]
    unnamed x20 -> x0, local copies, waits for them, and re-layouts: 2.45 us -> none
    dot_general x2, matrix products: 3.68 us -> 1.53 us  [local(): jnp.dot(pair_data, jnp.where(position == 0, second_columns, first_columns...]
where the time goes in v15:
time: 171 us
  waiting for transfers between devices  106 us (62%)
  starting transfers between devices  37.2 us (22%)
  Pallas kernels  11.4 us (7%)
  matrix products  9.18 us (5%)
  other arithmetic  3.91 us (2%)
  local copies, waits for them, and re-layouts  2.32 us (1%)
    all_to_all x1, waiting for transfers between devices, gathered_records(): gathered = lax.all_to_all(spread, GROUP_AXES, 0, 0, tiled=False)  52.8 us
    ppermute x4, waiting for transfers between devices, from_partner(): lax.ppermute(value, PARTNER_AXES, partner_pairs(lax.axis_size('y_hi')))  29.6 us
    ppermute x4, waiting for transfers between devices, from_behind(): lax.ppermute(value, COLUMN_AXES, [(source, source + steps) for source in...  23.4 us
    ppermute x4, starting transfers between devices, from_behind(): lax.ppermute(value, COLUMN_AXES, [(source, source + steps) for source in...  19.9 us
    pallas_call x3, Pallas kernels, rotation_of(): pl.pallas_call(sweeps_kernel, out_shape=jax.ShapeDtypeStruct((2 * width,...  11.4 us
    all_to_all x1, starting transfers between devices, gathered_records(): gathered = lax.all_to_all(spread, GROUP_AXES, 0, 0, tiled=False)  8.66 us
    ppermute x4, starting transfers between devices, from_partner(): lax.ppermute(value, PARTNER_AXES, partner_pairs(lax.axis_size('y_hi')))  8.64 us
    dot_general x3, matrix products, inner_products(): lax.dot_general(left_part, right_part, (((0,), (0,)), ((), ())), preferre...  3.84 us
  transfers between devices with their start and end apart: 9, of which 9 were waited for; matrix products, arithmetic and copies ran while one was open for 3% of the time, Pallas kernels for 0%

profile of v15, /device:TPU:2, one launch (start us, length us, event | category | flops | bytes accessed | tf_op | source)
XLA Modules:
  0.0 170.6 jit_solution(10198500443063464229)
XLA Ops:
  0.6 1.1 multiply_convert_fusion
  1.7 1.5 broadcast_in_dim.22
  3.2 8.7 %all-to-all-start = ((bf16[8,256,512]{2,1,0:T(8,128)(2,1)}), bf16[8,256,512]{2,1,0:T(8,128)(2,1)S(1)}, u32[]{:S(2)}, u32[]{:S(2)}) async-start(bf16[8,256,512]{2,1,0:T(8,128)(2,1)} %broadcast_in_dim.22), calls=%async_computation | async-start | bytes 4194304 | tf_op jit(solution)/shard_map/all_to_all | solution.py:167
  11.9 0.1 pad.15.clone
  12.0 52.8 %all-to-all-done = bf16[8,256,512]{2,1,0:T(8,128)(2,1)S(1)} async-done(((bf16[8,256,512]{2,1,0:T(8,128)(2,1)}), bf16[8,256,512]{2,1,0:T(8,128)(2,1)S(1)}, u32[]{:S(2)}, u32[]{:S(2)}) %all-to-all-start) | async-done | bytes 2097184 | tf_op jit(solution)/shard_map/all_to_all | solution.py:167
  64.8 1.3 convolution_bitcast_fusion
  66.0 0.1 slice_select_fusion.2
  66.1 0.1 maximum_maximum_fusion.local_ref
  66.2 2.7 %collective-permute-start = (f32[520,256]{1,0:T(8,128)S(1)}, f32[520,256]{1,0:T(8,128)S(1)}, u32[]{:S(2)}, u32[]{:S(2)}) collective-permute-start(f32[520,256]{1,0:T(8,128)S(1)} %maximum_maximum_fusion.local_ref), channel_id=1, source_target_pairs={{0,1},{1,0},{16,23},{23,16},{2,3},{3,2},{18,17},{17,18},{4,5},{5,4... | collective-permute-start | bytes 1597448 | tf_op jit(solution)/shard_map/ppermute | solution.py:40
  68.9 8.5 %collective-permute-done.received_ref = f32[520,256]{1,0:T(8,128)S(1)} collective-permute-done((f32[520,256]{1,0:T(8,128)S(1)}, f32[520,256]{1,0:T(8,128)S(1)}, u32[]{:S(2)}, u32[]{:S(2)}) %collective-permute-start) | collective-permute-done | bytes 532512 | tf_op jit(solution)/shard_map/ppermute | solution.py:40
  77.4 3.8 %shard_map.41 = bf16[512,512]{1,0:T(8,128)(2,1)S(1)} custom-call(f32[520,256]{1,0:T(8,128)S(1)} %maximum_maximum_fusion.local_ref, f32[520,256]{1,0:T(8,128)S(1)} %collective-permute-done.received_ref), custom_call_target="tpu_custom_call" | custom-call | flops 15728640 | bytes 1048576 | tf_op jit(solution)/shard_map/pallas_call | solution.py:138
  81.2 0.8 convolution_convert_fusion.3
  82.0 1.9 %collective-permute-start.1 = (bf16[2048,256]{0,1:T(8,128)(2,1)S(1)}, bf16[2048,256]{0,1:T(8,128)(2,1)}, u32[]{:S(2)}, u32[]{:S(2)}) collective-permute-start(bf16[2048,256]{0,1:T(8,128)(2,1)S(1)} %convolution_convert_fusion.3), channel_id=1, source_target_pairs={{0,16},{16,32},{32,48},{48,64},{64,80},{80,96},{96,112},{112,128},... | collective-permute-start | bytes 3145736 | tf_op jit(solution)/shard_map/ppermute | solution.py:24
  83.9 1.7 %convolution_convert_fusion.4 = bf16[2048,256]{0,1:T(8,128)(2,1)} fusion(bf16[2048,512]{1,0:T(8,128)(2,1)S(1)} %bitcast.12, pred[]{:T(512)S(6)} %eq.10, bf16[512,512]{1,0:T(8,128)(2,1)S(1)} %shard_map.41), kind=kOutput, calls=%fused_computation.5 | convolution fusion | flops 537526272 | bytes 3670017 | tf_op jit(solution)/shard_map/dot_general | solution.py:217
  85.6 10.2 %collective-permute-start.2 = (bf16[2048,256]{0,1:T(8,128)(2,1)}, bf16[2048,256]{0,1:T(8,128)(2,1)S(1)}, u32[]{:S(2)}, u32[]{:S(2)}) collective-permute-start(bf16[2048,256]{0,1:T(8,128)(2,1)} %convolution_convert_fusion.4), channel_id=1, source_target_pairs={{16,0},{32,16},{48,32},{64,48},{80,64},{96,80},{112,96},{128,112},... | collective-permute-start | bytes 3145736 | tf_op jit(solution)/shard_map/ppermute | solution.py:24
  95.8 8.9 %collective-permute-done.1 = bf16[2048,256]{0,1:T(8,128)(2,1)} collective-permute-done((bf16[2048,256]{0,1:T(8,128)(2,1)S(1)}, bf16[2048,256]{0,1:T(8,128)(2,1)}, u32[]{:S(2)}, u32[]{:S(2)}) %collective-permute-start.1) | collective-permute-done | bytes 1048608 | tf_op jit(solution)/shard_map/ppermute | solution.py:24
  104.7 1.3 broadcast_select_fusion.3
  106.1 2.3 %collective-permute-done.2 = bf16[2048,256]{0,1:T(8,128)(2,1)S(1)} collective-permute-done((bf16[2048,256]{0,1:T(8,128)(2,1)}, bf16[2048,256]{0,1:T(8,128)(2,1)S(1)}, u32[]{:S(2)}, u32[]{:S(2)}) %collective-permute-start.2) | collective-permute-done | bytes 1048608 | tf_op jit(solution)/shard_map/ppermute | solution.py:24
  108.4 0.1 broadcast_select_fusion.1
  108.5 1.3 fusion.1
  109.8 0.1 slice_select_fusion.1
  109.9 0.1 maximum_maximum_fusion.1.local_ref
  110.0 2.1 %collective-permute-start.3 = (f32[520,256]{1,0:T(8,128)S(1)}, f32[520,256]{1,0:T(8,128)S(1)}, u32[]{:S(2)}, u32[]{:S(2)}) collective-permute-start(f32[520,256]{1,0:T(8,128)S(1)} %maximum_maximum_fusion.1.local_ref), channel_id=1, source_target_pairs={{0,1},{1,0},{16,23},{23,16},{2,3},{3,2},{18,17},{17,18},{4,5},{5,4... | collective-permute-start | bytes 1597448 | tf_op jit(solution)/shard_map/ppermute | solution.py:40
  112.1 9.1 %collective-permute-done.3.received_ref = f32[520,256]{1,0:T(8,128)S(1)} collective-permute-done((f32[520,256]{1,0:T(8,128)S(1)}, f32[520,256]{1,0:T(8,128)S(1)}, u32[]{:S(2)}, u32[]{:S(2)}) %collective-permute-start.3) | collective-permute-done | bytes 532512 | tf_op jit(solution)/shard_map/ppermute | solution.py:40
  121.2 3.8 %shard_map.42 = bf16[512,512]{1,0:T(8,128)(2,1)S(1)} custom-call(f32[520,256]{1,0:T(8,128)S(1)} %maximum_maximum_fusion.1.local_ref, f32[520,256]{1,0:T(8,128)S(1)} %collective-permute-done.3.received_ref), custom_call_target="tpu_custom_call" | custom-call | flops 15728640 | bytes 1048576 | tf_op jit(solution)/shard_map/pallas_call | solution.py:138
  125.0 0.8 convolution_convert_fusion.1
  125.7 1.9 %collective-permute-start.4 = (bf16[2048,256]{0,1:T(8,128)(2,1)S(1)}, bf16[2048,256]{0,1:T(8,128)(2,1)S(1)}, u32[]{:S(2)}, u32[]{:S(2)}) collective-permute-start(bf16[2048,256]{0,1:T(8,128)(2,1)S(1)} %convolution_convert_fusion.1), channel_id=1, source_target_pairs={{0,16},{16,32},{32,48},{48,64},{64,80},{80,96},{96,112},{112,128},... | collective-permute-start | bytes 3145736 | tf_op jit(solution)/shard_map/ppermute | solution.py:24
  127.7 0.8 convolution_convert_fusion.2
  128.4 5.9 %collective-permute-start.5 = (bf16[2048,256]{0,1:T(8,128)(2,1)S(1)}, bf16[2048,256]{0,1:T(8,128)(2,1)S(1)}, u32[]{:S(2)}, u32[]{:S(2)}) collective-permute-start(bf16[2048,256]{0,1:T(8,128)(2,1)S(1)} %convolution_convert_fusion.2), channel_id=1, source_target_pairs={{16,0},{32,16},{48,32},{64,48},{80,64},{96,80},{112,96},{128,112},... | collective-permute-start | bytes 3145736 | tf_op jit(solution)/shard_map/ppermute | solution.py:24
  134.3 9.8 %collective-permute-done.4 = bf16[2048,256]{0,1:T(8,128)(2,1)S(1)} collective-permute-done((bf16[2048,256]{0,1:T(8,128)(2,1)S(1)}, bf16[2048,256]{0,1:T(8,128)(2,1)S(1)}, u32[]{:S(2)}, u32[]{:S(2)}) %collective-permute-start.4) | collective-permute-done | bytes 1048608 | tf_op jit(solution)/shard_map/ppermute | solution.py:24
  144.1 0.1 broadcast_select_fusion.2
  144.2 2.4 %collective-permute-done.5 = bf16[2048,256]{0,1:T(8,128)(2,1)S(1)} collective-permute-done((bf16[2048,256]{0,1:T(8,128)(2,1)S(1)}, bf16[2048,256]{0,1:T(8,128)(2,1)S(1)}, u32[]{:S(2)}, u32[]{:S(2)}) %collective-permute-start.5) | collective-permute-done | bytes 1048608 | tf_op jit(solution)/shard_map/ppermute | solution.py:24
  146.6 0.1 broadcast_select_fusion
  146.7 1.3 fusion
  148.0 0.1 slice_select_fusion
  148.1 0.1 maximum_maximum_fusion.2.local_ref
  148.2 1.9 %collective-permute-start.6 = (f32[520,256]{1,0:T(8,128)S(1)}, f32[520,256]{1,0:T(8,128)S(1)}, u32[]{:S(2)}, u32[]{:S(2)}) collective-permute-start(f32[520,256]{1,0:T(8,128)S(1)} %maximum_maximum_fusion.2.local_ref), channel_id=1, source_target_pairs={{0,1},{1,0},{16,23},{23,16},{2,3},{3,2},{18,17},{17,18},{4,5},{5,4... | collective-permute-start | bytes 1597448 | tf_op jit(solution)/shard_map/ppermute | solution.py:40
  150.2 9.2 %collective-permute-done.6.received_ref = f32[520,256]{1,0:T(8,128)S(1)} collective-permute-done((f32[520,256]{1,0:T(8,128)S(1)}, f32[520,256]{1,0:T(8,128)S(1)}, u32[]{:S(2)}, u32[]{:S(2)}) %collective-permute-start.6) | collective-permute-done | bytes 532512 | tf_op jit(solution)/shard_map/ppermute | solution.py:40
  159.4 3.8 %shard_map.43 = bf16[512,512]{1,0:T(8,128)(2,1)S(1)} custom-call(f32[520,256]{1,0:T(8,128)S(1)} %maximum_maximum_fusion.2.local_ref, f32[520,256]{1,0:T(8,128)S(1)} %collective-permute-done.6.received_ref), custom_call_target="tpu_custom_call" | custom-call | flops 15728640 | bytes 1048576 | tf_op jit(solution)/shard_map/pallas_call | solution.py:138
  163.2 1.3 multiply_reduce_fusion
  164.5 1.9 %collective-permute-start.7 = (f32[512]{0:T(512)S(1)}, f32[512]{0:T(512)S(1)}, u32[]{:S(2)}, u32[]{:S(2)}) collective-permute-start(f32[512]{0:T(512)S(1)} %get-tuple-element.11), channel_id=1, source_target_pairs={{0,1},{1,0},{16,23},{23,16},{2,3},{3,2},{18,17},{17,18},{4,5},{5,4... | collective-permute-start | bytes 6152 | tf_op jit(solution)/shard_map/ppermute | solution.py:40
  166.4 0.7 constant_dynamic-slice_fusion
  167.2 2.8 %collective-permute-done.7 = f32[512]{0:T(512)S(1)} collective-permute-done((f32[512]{0:T(512)S(1)}, f32[512]{0:T(512)S(1)}, u32[]{:S(2)}, u32[]{:S(2)}) %collective-permute-start.7) | collective-permute-done | bytes 2080 | tf_op jit(solution)/shard_map/ppermute | solution.py:40
  170.0 0.6 add_sqrt_fusion
  (1 shorter events, 0.0 us)
Async XLA Ops:
  3.2 61.5 %all-to-all-start = ((bf16[8,256,512]{2,1,0:T(8,128)(2,1)}), bf16[8,256,512]{2,1,0:T(8,128)(2,1)S(1)}, u32[]{:S(2)}, u32[]{:S(2)}) async-start(bf16[8,256,512]{2,1,0:T(8,128)(2,1)} %broadcast_in_dim.22), calls=%async_computation | async-start | bytes 4194304 | tf_op jit(solution)/shard_map/all_to_all | solution.py:167
  66.2 11.2 %collective-permute-start = (f32[520,256]{1,0:T(8,128)S(1)}, f32[520,256]{1,0:T(8,128)S(1)}, u32[]{:S(2)}, u32[]{:S(2)}) collective-permute-start(f32[520,256]{1,0:T(8,128)S(1)} %maximum_maximum_fusion.local_ref), channel_id=1, source_target_pairs={{0,1},{1,0},{16,23},{23,16},{2,3},{3,2},{18,17},{17,18},{4,5},{5,4... | collective-permute-start | bytes 1597448 | tf_op jit(solution)/shard_map/ppermute | solution.py:40
  82.0 22.8 %collective-permute-start.1 = (bf16[2048,256]{0,1:T(8,128)(2,1)S(1)}, bf16[2048,256]{0,1:T(8,128)(2,1)}, u32[]{:S(2)}, u32[]{:S(2)}) collective-permute-start(bf16[2048,256]{0,1:T(8,128)(2,1)S(1)} %convolution_convert_fusion.3), channel_id=1, source_target_pairs={{0,16},{16,32},{32,48},{48,64},{64,80},{80,96},{96,112},{112,128},... | collective-permute-start | bytes 3145736 | tf_op jit(solution)/shard_map/ppermute | solution.py:24
  85.6 22.8 %collective-permute-start.2 = (bf16[2048,256]{0,1:T(8,128)(2,1)}, bf16[2048,256]{0,1:T(8,128)(2,1)S(1)}, u32[]{:S(2)}, u32[]{:S(2)}) collective-permute-start(bf16[2048,256]{0,1:T(8,128)(2,1)} %convolution_convert_fusion.4), channel_id=1, source_target_pairs={{16,0},{32,16},{48,32},{64,48},{80,64},{96,80},{112,96},{128,112},... | collective-permute-start | bytes 3145736 | tf_op jit(solution)/shard_map/ppermute | solution.py:24
  110.0 11.2 %collective-permute-start.3 = (f32[520,256]{1,0:T(8,128)S(1)}, f32[520,256]{1,0:T(8,128)S(1)}, u32[]{:S(2)}, u32[]{:S(2)}) collective-permute-start(f32[520,256]{1,0:T(8,128)S(1)} %maximum_maximum_fusion.1.local_ref), channel_id=1, source_target_pairs={{0,1},{1,0},{16,23},{23,16},{2,3},{3,2},{18,17},{17,18},{4,5},{5,4... | collective-permute-start | bytes 1597448 | tf_op jit(solution)/shard_map/ppermute | solution.py:40
  125.7 18.3 %collective-permute-start.4 = (bf16[2048,256]{0,1:T(8,128)(2,1)S(1)}, bf16[2048,256]{0,1:T(8,128)(2,1)S(1)}, u32[]{:S(2)}, u32[]{:S(2)}) collective-permute-start(bf16[2048,256]{0,1:T(8,128)(2,1)S(1)} %convolution_convert_fusion.1), channel_id=1, source_target_pairs={{0,16},{16,32},{32,48},{48,64},{64,80},{80,96},{96,112},{112,128},... | collective-permute-start | bytes 3145736 | tf_op jit(solution)/shard_map/ppermute | solution.py:24
  128.4 18.2 %collective-permute-start.5 = (bf16[2048,256]{0,1:T(8,128)(2,1)S(1)}, bf16[2048,256]{0,1:T(8,128)(2,1)S(1)}, u32[]{:S(2)}, u32[]{:S(2)}) collective-permute-start(bf16[2048,256]{0,1:T(8,128)(2,1)S(1)} %convolution_convert_fusion.2), channel_id=1, source_target_pairs={{16,0},{32,16},{48,32},{64,48},{80,64},{96,80},{112,96},{128,112},... | collective-permute-start | bytes 3145736 | tf_op jit(solution)/shard_map/ppermute | solution.py:24
  148.2 11.2 %collective-permute-start.6 = (f32[520,256]{1,0:T(8,128)S(1)}, f32[520,256]{1,0:T(8,128)S(1)}, u32[]{:S(2)}, u32[]{:S(2)}) collective-permute-start(f32[520,256]{1,0:T(8,128)S(1)} %maximum_maximum_fusion.2.local_ref), channel_id=1, source_target_pairs={{0,1},{1,0},{16,23},{23,16},{2,3},{3,2},{18,17},{17,18},{4,5},{5,4... | collective-permute-start | bytes 1597448 | tf_op jit(solution)/shard_map/ppermute | solution.py:40
  164.5 5.5 %collective-permute-start.7 = (f32[512]{0:T(512)S(1)}, f32[512]{0:T(512)S(1)}, u32[]{:S(2)}, u32[]{:S(2)}) collective-permute-start(f32[512]{0:T(512)S(1)} %get-tuple-element.11), channel_id=1, source_target_pairs={{0,1},{1,0},{16,23},{23,16},{2,3},{3,2},{18,17},{17,18},{4,5},{5,4... | collective-permute-start | bytes 6152 | tf_op jit(solution)/shard_map/ppermute | solution.py:40

commit v16 on v15

--- a/solution.py
+++ b/solution.py
@@ -80,7 +80,6 @@
     mirrored = folded.T
     top_left = jnp.where(rows <= cols, folded, mirrored)
     low_right = jnp.where(rows > cols, folded, jnp.where(rows < cols, mirrored, low_diag))
-    low_left = top_right.T
     first_top = jnp.where(on_diagonal, 1.0, 0.0).astype(jnp.float32)
     first_low = jnp.zeros((width, width), jnp.float32)
     second_top = jnp.zeros((width, width), jnp.float32)
@@ -98,10 +97,10 @@
     for sweep_index in range(SWEEPS):
         if sweep_index > 0:
             top_right = to_left(top_right, 1)
-            low_left = to_left(low_left, 0)
             low_right = to_left(to_left(low_right, 0), 1)
             second_top = to_left(second_top, 1)
             second_low = to_left(second_low, 1)
+        low_left = top_right.T
         cos_col, sin_col = half_angle_terms(
             diagonal_row(top_left), diagonal_row(low_right), diagonal_row(top_right)
         )
@@ -112,7 +111,6 @@
         left_b = low_left * cos_col - low_right * sin_col
         right_b = low_left * sin_col + low_right * cos_col
         top_left = cos_row * left_a - sin_row * left_b
-        low_left = sin_row * left_a + cos_row * left_b
         top_right = cos_row * right_a - sin_row * right_b
         low_right = sin_row * right_a + cos_row * right_b
         first_top, second_top = (

time: 171 us -> 171 us (level)
  no operation moved by 1% of the time
where the time goes in v16:
time: 171 us
  waiting for transfers between devices  106 us (62%)
  starting transfers between devices  37.2 us (22%)
  Pallas kernels  11.3 us (7%)
  matrix products  9.17 us (5%)
  other arithmetic  3.91 us (2%)
  local copies, waits for them, and re-layouts  2.32 us (1%)
    all_to_all x1, waiting for transfers between devices, gathered_records(): gathered = lax.all_to_all(spread, GROUP_AXES, 0, 0, tiled=False)  52.8 us
    ppermute x4, waiting for transfers between devices, from_partner(): lax.ppermute(value, PARTNER_AXES, partner_pairs(lax.axis_size('y_hi')))  29.6 us
    ppermute x4, waiting for transfers between devices, from_behind(): lax.ppermute(value, COLUMN_AXES, [(source, source + steps) for source in...  23.4 us
    ppermute x4, starting transfers between devices, from_behind(): lax.ppermute(value, COLUMN_AXES, [(source, source + steps) for source in...  19.9 us
    pallas_call x3, Pallas kernels, rotation_of(): pl.pallas_call(sweeps_kernel, out_shape=jax.ShapeDtypeStruct((2 * width,...  11.3 us
    all_to_all x1, starting transfers between devices, gathered_records(): gathered = lax.all_to_all(spread, GROUP_AXES, 0, 0, tiled=False)  8.66 us
    ppermute x4, starting transfers between devices, from_partner(): lax.ppermute(value, PARTNER_AXES, partner_pairs(lax.axis_size('y_hi')))  8.63 us
    dot_general x3, matrix products, inner_products(): lax.dot_general(left_part, right_part, (((0,), (0,)), ((), ())), preferre...  3.83 us
  transfers between devices with their start and end apart: 9, of which 9 were waited for; matrix products, arithmetic and copies ran while one was open for 3% of the time, Pallas kernels for 0%

profile of v16, /device:TPU:2, one launch (start us, length us, event | category | flops | bytes accessed | tf_op | source)
XLA Modules:
  0.0 170.6 jit_solution(2860341341894394915)
XLA Ops:
  0.6 1.1 multiply_convert_fusion
  1.7 1.5 broadcast_in_dim.22
  3.2 8.7 %all-to-all-start = ((bf16[8,256,512]{2,1,0:T(8,128)(2,1)}), bf16[8,256,512]{2,1,0:T(8,128)(2,1)S(1)}, u32[]{:S(2)}, u32[]{:S(2)}) async-start(bf16[8,256,512]{2,1,0:T(8,128)(2,1)} %broadcast_in_dim.22), calls=%async_computation | async-start | bytes 4194304 | tf_op jit(solution)/shard_map/all_to_all | solution.py:165
  11.9 0.1 pad.15.clone
  12.0 52.8 %all-to-all-done = bf16[8,256,512]{2,1,0:T(8,128)(2,1)S(1)} async-done(((bf16[8,256,512]{2,1,0:T(8,128)(2,1)}), bf16[8,256,512]{2,1,0:T(8,128)(2,1)S(1)}, u32[]{:S(2)}, u32[]{:S(2)}) %all-to-all-start) | async-done | bytes 2097184 | tf_op jit(solution)/shard_map/all_to_all | solution.py:165
  64.8 1.3 convolution_bitcast_fusion
  66.0 0.1 slice_select_fusion.2
  66.1 0.1 maximum_maximum_fusion.local_ref
  66.2 2.7 %collective-permute-start = (f32[520,256]{1,0:T(8,128)S(1)}, f32[520,256]{1,0:T(8,128)S(1)}, u32[]{:S(2)}, u32[]{:S(2)}) collective-permute-start(f32[520,256]{1,0:T(8,128)S(1)} %maximum_maximum_fusion.local_ref), channel_id=1, source_target_pairs={{0,1},{1,0},{16,23},{23,16},{2,3},{3,2},{18,17},{17,18},{4,5},{5,4... | collective-permute-start | bytes 1597448 | tf_op jit(solution)/shard_map/ppermute | solution.py:40
  68.9 8.5 %collective-permute-done.received_ref = f32[520,256]{1,0:T(8,128)S(1)} collective-permute-done((f32[520,256]{1,0:T(8,128)S(1)}, f32[520,256]{1,0:T(8,128)S(1)}, u32[]{:S(2)}, u32[]{:S(2)}) %collective-permute-start) | collective-permute-done | bytes 532512 | tf_op jit(solution)/shard_map/ppermute | solution.py:40
  77.4 3.8 %shard_map.41 = bf16[512,512]{1,0:T(8,128)(2,1)S(1)} custom-call(f32[520,256]{1,0:T(8,128)S(1)} %maximum_maximum_fusion.local_ref, f32[520,256]{1,0:T(8,128)S(1)} %collective-permute-done.received_ref), custom_call_target="tpu_custom_call" | custom-call | flops 15728640 | bytes 1048576 | tf_op jit(solution)/shard_map/pallas_call | solution.py:136
  81.2 0.8 convolution_convert_fusion.3
  82.0 1.9 %collective-permute-start.1 = (bf16[2048,256]{0,1:T(8,128)(2,1)S(1)}, bf16[2048,256]{0,1:T(8,128)(2,1)}, u32[]{:S(2)}, u32[]{:S(2)}) collective-permute-start(bf16[2048,256]{0,1:T(8,128)(2,1)S(1)} %convolution_convert_fusion.3), channel_id=1, source_target_pairs={{0,16},{16,32},{32,48},{48,64},{64,80},{80,96},{96,112},{112,128},... | collective-permute-start | bytes 3145736 | tf_op jit(solution)/shard_map/ppermute | solution.py:24
  83.9 1.7 %convolution_convert_fusion.4 = bf16[2048,256]{0,1:T(8,128)(2,1)} fusion(bf16[2048,512]{1,0:T(8,128)(2,1)S(1)} %bitcast.12, pred[]{:T(512)S(6)} %eq.10, bf16[512,512]{1,0:T(8,128)(2,1)S(1)} %shard_map.41), kind=kOutput, calls=%fused_computation.5 | convolution fusion | flops 537526272 | bytes 3670017 | tf_op jit(solution)/shard_map/dot_general | solution.py:215
  85.6 10.2 %collective-permute-start.2 = (bf16[2048,256]{0,1:T(8,128)(2,1)}, bf16[2048,256]{0,1:T(8,128)(2,1)S(1)}, u32[]{:S(2)}, u32[]{:S(2)}) collective-permute-start(bf16[2048,256]{0,1:T(8,128)(2,1)} %convolution_convert_fusion.4), channel_id=1, source_target_pairs={{16,0},{32,16},{48,32},{64,48},{80,64},{96,80},{112,96},{128,112},... | collective-permute-start | bytes 3145736 | tf_op jit(solution)/shard_map/ppermute | solution.py:24
  95.8 8.9 %collective-permute-done.1 = bf16[2048,256]{0,1:T(8,128)(2,1)} collective-permute-done((bf16[2048,256]{0,1:T(8,128)(2,1)S(1)}, bf16[2048,256]{0,1:T(8,128)(2,1)}, u32[]{:S(2)}, u32[]{:S(2)}) %collective-permute-start.1) | collective-permute-done | bytes 1048608 | tf_op jit(solution)/shard_map/ppermute | solution.py:24
  104.7 1.3 broadcast_select_fusion.3
  106.1 2.3 %collective-permute-done.2 = bf16[2048,256]{0,1:T(8,128)(2,1)S(1)} collective-permute-done((bf16[2048,256]{0,1:T(8,128)(2,1)}, bf16[2048,256]{0,1:T(8,128)(2,1)S(1)}, u32[]{:S(2)}, u32[]{:S(2)}) %collective-permute-start.2) | collective-permute-done | bytes 1048608 | tf_op jit(solution)/shard_map/ppermute | solution.py:24
  108.4 0.1 broadcast_select_fusion.1
  108.5 1.3 fusion.1
  109.8 0.1 slice_select_fusion.1
  109.9 0.1 maximum_maximum_fusion.1.local_ref
  110.0 2.1 %collective-permute-start.3 = (f32[520,256]{1,0:T(8,128)S(1)}, f32[520,256]{1,0:T(8,128)S(1)}, u32[]{:S(2)}, u32[]{:S(2)}) collective-permute-start(f32[520,256]{1,0:T(8,128)S(1)} %maximum_maximum_fusion.1.local_ref), channel_id=1, source_target_pairs={{0,1},{1,0},{16,23},{23,16},{2,3},{3,2},{18,17},{17,18},{4,5},{5,4... | collective-permute-start | bytes 1597448 | tf_op jit(solution)/shard_map/ppermute | solution.py:40
  112.1 9.1 %collective-permute-done.3.received_ref = f32[520,256]{1,0:T(8,128)S(1)} collective-permute-done((f32[520,256]{1,0:T(8,128)S(1)}, f32[520,256]{1,0:T(8,128)S(1)}, u32[]{:S(2)}, u32[]{:S(2)}) %collective-permute-start.3) | collective-permute-done | bytes 532512 | tf_op jit(solution)/shard_map/ppermute | solution.py:40
  121.2 3.8 %shard_map.42 = bf16[512,512]{1,0:T(8,128)(2,1)S(1)} custom-call(f32[520,256]{1,0:T(8,128)S(1)} %maximum_maximum_fusion.1.local_ref, f32[520,256]{1,0:T(8,128)S(1)} %collective-permute-done.3.received_ref), custom_call_target="tpu_custom_call" | custom-call | flops 15728640 | bytes 1048576 | tf_op jit(solution)/shard_map/pallas_call | solution.py:136
  125.0 0.8 convolution_convert_fusion.1
  125.7 1.9 %collective-permute-start.4 = (bf16[2048,256]{0,1:T(8,128)(2,1)S(1)}, bf16[2048,256]{0,1:T(8,128)(2,1)S(1)}, u32[]{:S(2)}, u32[]{:S(2)}) collective-permute-start(bf16[2048,256]{0,1:T(8,128)(2,1)S(1)} %convolution_convert_fusion.1), channel_id=1, source_target_pairs={{0,16},{16,32},{32,48},{48,64},{64,80},{80,96},{96,112},{112,128},... | collective-permute-start | bytes 3145736 | tf_op jit(solution)/shard_map/ppermute | solution.py:24
  127.7 0.8 convolution_convert_fusion.2
  128.4 5.9 %collective-permute-start.5 = (bf16[2048,256]{0,1:T(8,128)(2,1)S(1)}, bf16[2048,256]{0,1:T(8,128)(2,1)S(1)}, u32[]{:S(2)}, u32[]{:S(2)}) collective-permute-start(bf16[2048,256]{0,1:T(8,128)(2,1)S(1)} %convolution_convert_fusion.2), channel_id=1, source_target_pairs={{16,0},{32,16},{48,32},{64,48},{80,64},{96,80},{112,96},{128,112},... | collective-permute-start | bytes 3145736 | tf_op jit(solution)/shard_map/ppermute | solution.py:24
  134.3 9.8 %collective-permute-done.4 = bf16[2048,256]{0,1:T(8,128)(2,1)S(1)} collective-permute-done((bf16[2048,256]{0,1:T(8,128)(2,1)S(1)}, bf16[2048,256]{0,1:T(8,128)(2,1)S(1)}, u32[]{:S(2)}, u32[]{:S(2)}) %collective-permute-start.4) | collective-permute-done | bytes 1048608 | tf_op jit(solution)/shard_map/ppermute | solution.py:24
  144.1 0.1 broadcast_select_fusion.2
  144.2 2.4 %collective-permute-done.5 = bf16[2048,256]{0,1:T(8,128)(2,1)S(1)} collective-permute-done((bf16[2048,256]{0,1:T(8,128)(2,1)S(1)}, bf16[2048,256]{0,1:T(8,128)(2,1)S(1)}, u32[]{:S(2)}, u32[]{:S(2)}) %collective-permute-start.5) | collective-permute-done | bytes 1048608 | tf_op jit(solution)/shard_map/ppermute | solution.py:24
  146.6 0.1 broadcast_select_fusion
  146.7 1.3 fusion
  148.0 0.1 slice_select_fusion
  148.1 0.1 maximum_maximum_fusion.2.local_ref
  148.2 1.9 %collective-permute-start.6 = (f32[520,256]{1,0:T(8,128)S(1)}, f32[520,256]{1,0:T(8,128)S(1)}, u32[]{:S(2)}, u32[]{:S(2)}) collective-permute-start(f32[520,256]{1,0:T(8,128)S(1)} %maximum_maximum_fusion.2.local_ref), channel_id=1, source_target_pairs={{0,1},{1,0},{16,23},{23,16},{2,3},{3,2},{18,17},{17,18},{4,5},{5,4... | collective-permute-start | bytes 1597448 | tf_op jit(solution)/shard_map/ppermute | solution.py:40
  150.2 9.2 %collective-permute-done.6.received_ref = f32[520,256]{1,0:T(8,128)S(1)} collective-permute-done((f32[520,256]{1,0:T(8,128)S(1)}, f32[520,256]{1,0:T(8,128)S(1)}, u32[]{:S(2)}, u32[]{:S(2)}) %collective-permute-start.6) | collective-permute-done | bytes 532512 | tf_op jit(solution)/shard_map/ppermute | solution.py:40
  159.4 3.8 %shard_map.43 = bf16[512,512]{1,0:T(8,128)(2,1)S(1)} custom-call(f32[520,256]{1,0:T(8,128)S(1)} %maximum_maximum_fusion.2.local_ref, f32[520,256]{1,0:T(8,128)S(1)} %collective-permute-done.6.received_ref), custom_call_target="tpu_custom_call" | custom-call | flops 15728640 | bytes 1048576 | tf_op jit(solution)/shard_map/pallas_call | solution.py:136
  163.2 1.3 multiply_reduce_fusion
  164.5 1.9 %collective-permute-start.7 = (f32[512]{0:T(512)S(1)}, f32[512]{0:T(512)S(1)}, u32[]{:S(2)}, u32[]{:S(2)}) collective-permute-start(f32[512]{0:T(512)S(1)} %get-tuple-element.11), channel_id=1, source_target_pairs={{0,1},{1,0},{16,23},{23,16},{2,3},{3,2},{18,17},{17,18},{4,5},{5,4... | collective-permute-start | bytes 6152 | tf_op jit(solution)/shard_map/ppermute | solution.py:40
  166.4 0.7 constant_dynamic-slice_fusion
  167.1 2.8 %collective-permute-done.7 = f32[512]{0:T(512)S(1)} collective-permute-done((f32[512]{0:T(512)S(1)}, f32[512]{0:T(512)S(1)}, u32[]{:S(2)}, u32[]{:S(2)}) %collective-permute-start.7) | collective-permute-done | bytes 2080 | tf_op jit(solution)/shard_map/ppermute | solution.py:40
  170.0 0.6 add_sqrt_fusion
  (1 shorter events, 0.0 us)
Async XLA Ops:
  3.2 61.5 %all-to-all-start = ((bf16[8,256,512]{2,1,0:T(8,128)(2,1)}), bf16[8,256,512]{2,1,0:T(8,128)(2,1)S(1)}, u32[]{:S(2)}, u32[]{:S(2)}) async-start(bf16[8,256,512]{2,1,0:T(8,128)(2,1)} %broadcast_in_dim.22), calls=%async_computation | async-start | bytes 4194304 | tf_op jit(solution)/shard_map/all_to_all | solution.py:165
  66.2 11.2 %collective-permute-start = (f32[520,256]{1,0:T(8,128)S(1)}, f32[520,256]{1,0:T(8,128)S(1)}, u32[]{:S(2)}, u32[]{:S(2)}) collective-permute-start(f32[520,256]{1,0:T(8,128)S(1)} %maximum_maximum_fusion.local_ref), channel_id=1, source_target_pairs={{0,1},{1,0},{16,23},{23,16},{2,3},{3,2},{18,17},{17,18},{4,5},{5,4... | collective-permute-start | bytes 1597448 | tf_op jit(solution)/shard_map/ppermute | solution.py:40
  82.0 22.8 %collective-permute-start.1 = (bf16[2048,256]{0,1:T(8,128)(2,1)S(1)}, bf16[2048,256]{0,1:T(8,128)(2,1)}, u32[]{:S(2)}, u32[]{:S(2)}) collective-permute-start(bf16[2048,256]{0,1:T(8,128)(2,1)S(1)} %convolution_convert_fusion.3), channel_id=1, source_target_pairs={{0,16},{16,32},{32,48},{48,64},{64,80},{80,96},{96,112},{112,128},... | collective-permute-start | bytes 3145736 | tf_op jit(solution)/shard_map/ppermute | solution.py:24
  85.6 22.8 %collective-permute-start.2 = (bf16[2048,256]{0,1:T(8,128)(2,1)}, bf16[2048,256]{0,1:T(8,128)(2,1)S(1)}, u32[]{:S(2)}, u32[]{:S(2)}) collective-permute-start(bf16[2048,256]{0,1:T(8,128)(2,1)} %convolution_convert_fusion.4), channel_id=1, source_target_pairs={{16,0},{32,16},{48,32},{64,48},{80,64},{96,80},{112,96},{128,112},... | collective-permute-start | bytes 3145736 | tf_op jit(solution)/shard_map/ppermute | solution.py:24
  110.0 11.2 %collective-permute-start.3 = (f32[520,256]{1,0:T(8,128)S(1)}, f32[520,256]{1,0:T(8,128)S(1)}, u32[]{:S(2)}, u32[]{:S(2)}) collective-permute-start(f32[520,256]{1,0:T(8,128)S(1)} %maximum_maximum_fusion.1.local_ref), channel_id=1, source_target_pairs={{0,1},{1,0},{16,23},{23,16},{2,3},{3,2},{18,17},{17,18},{4,5},{5,4... | collective-permute-start | bytes 1597448 | tf_op jit(solution)/shard_map/ppermute | solution.py:40
  125.7 18.4 %collective-permute-start.4 = (bf16[2048,256]{0,1:T(8,128)(2,1)S(1)}, bf16[2048,256]{0,1:T(8,128)(2,1)S(1)}, u32[]{:S(2)}, u32[]{:S(2)}) collective-permute-start(bf16[2048,256]{0,1:T(8,128)(2,1)S(1)} %convolution_convert_fusion.1), channel_id=1, source_target_pairs={{0,16},{16,32},{32,48},{48,64},{64,80},{80,96},{96,112},{112,128},... | collective-permute-start | bytes 3145736 | tf_op jit(solution)/shard_map/ppermute | solution.py:24
  128.4 18.2 %collective-permute-start.5 = (bf16[2048,256]{0,1:T(8,128)(2,1)S(1)}, bf16[2048,256]{0,1:T(8,128)(2,1)S(1)}, u32[]{:S(2)}, u32[]{:S(2)}) collective-permute-start(bf16[2048,256]{0,1:T(8,128)(2,1)S(1)} %convolution_convert_fusion.2), channel_id=1, source_target_pairs={{16,0},{32,16},{48,32},{64,48},{80,64},{96,80},{112,96},{128,112},... | collective-permute-start | bytes 3145736 | tf_op jit(solution)/shard_map/ppermute | solution.py:24
  148.2 11.2 %collective-permute-start.6 = (f32[520,256]{1,0:T(8,128)S(1)}, f32[520,256]{1,0:T(8,128)S(1)}, u32[]{:S(2)}, u32[]{:S(2)}) collective-permute-start(f32[520,256]{1,0:T(8,128)S(1)} %maximum_maximum_fusion.2.local_ref), channel_id=1, source_target_pairs={{0,1},{1,0},{16,23},{23,16},{2,3},{3,2},{18,17},{17,18},{4,5},{5,4... | collective-permute-start | bytes 1597448 | tf_op jit(solution)/shard_map/ppermute | solution.py:40
  164.5 5.5 %collective-permute-start.7 = (f32[512]{0:T(512)S(1)}, f32[512]{0:T(512)S(1)}, u32[]{:S(2)}, u32[]{:S(2)}) collective-permute-start(f32[512]{0:T(512)S(1)} %get-tuple-element.11), channel_id=1, source_target_pairs={{0,1},{1,0},{16,23},{23,16},{2,3},{3,2},{18,17},{17,18},{4,5},{5,4... | collective-permute-start | bytes 6152 | tf_op jit(solution)/shard_map/ppermute | solution.py:40

commit v17 on v16

--- a/solution.py
+++ b/solution.py
@@ -113,14 +113,18 @@
         top_left = cos_row * left_a - sin_row * left_b
         top_right = cos_row * right_a - sin_row * right_b
         low_right = sin_row * right_a + cos_row * right_b
-        first_top, second_top = (
-            first_top * cos_col - second_top * sin_col,
-            first_top * sin_col + second_top * cos_col,
-        )
-        first_low, second_low = (
-            first_low * cos_col - second_low * sin_col,
-            first_low * sin_col + second_low * cos_col,
-        )
+        if sweep_index == 0:
+            first_top, second_top = first_top * cos_col, first_top * sin_col
+            first_low, second_low = -(second_low * sin_col), second_low * cos_col
+        else:
+            first_top, second_top = (
+                first_top * cos_col - second_top * sin_col,
+                first_top * sin_col + second_top * cos_col,
+            )
+            first_low, second_low = (
+                first_low * cos_col - second_low * sin_col,
+                first_low * sin_col + second_low * cos_col,
+            )
     second_top = pltpu.roll(second_top, SWEEPS - 1, 1)
     second_low = pltpu.roll(second_low, SWEEPS - 1, 1)
     out = rotation_ref.dtype

time: 171 us -> 171 us (level)
  no operation moved by 1% of the time
where the time goes in v17:
time: 171 us
  waiting for transfers between devices  106 us (62%)
  starting transfers between devices  37.2 us (22%)
  Pallas kernels  11.4 us (7%)
  matrix products  9.17 us (5%)
  other arithmetic  3.91 us (2%)
  local copies, waits for them, and re-layouts  2.32 us (1%)
    all_to_all x1, waiting for transfers between devices, gathered_records(): gathered = lax.all_to_all(spread, GROUP_AXES, 0, 0, tiled=False)  52.8 us
    ppermute x4, waiting for transfers between devices, from_partner(): lax.ppermute(value, PARTNER_AXES, partner_pairs(lax.axis_size('y_hi')))  29.5 us
    ppermute x4, waiting for transfers between devices, from_behind(): lax.ppermute(value, COLUMN_AXES, [(source, source + steps) for source in...  23.4 us
    ppermute x4, starting transfers between devices, from_behind(): lax.ppermute(value, COLUMN_AXES, [(source, source + steps) for source in...  19.9 us
    pallas_call x3, Pallas kernels, rotation_of(): pl.pallas_call(sweeps_kernel, out_shape=jax.ShapeDtypeStruct((2 * width,...  11.4 us
    all_to_all x1, starting transfers between devices, gathered_records(): gathered = lax.all_to_all(spread, GROUP_AXES, 0, 0, tiled=False)  8.66 us
    ppermute x4, starting transfers between devices, from_partner(): lax.ppermute(value, PARTNER_AXES, partner_pairs(lax.axis_size('y_hi')))  8.64 us
    dot_general x3, matrix products, inner_products(): lax.dot_general(left_part, right_part, (((0,), (0,)), ((), ())), preferre...  3.83 us
  transfers between devices with their start and end apart: 9, of which 9 were waited for; matrix products, arithmetic and copies ran while one was open for 3% of the time, Pallas kernels for 0%

profile of v17, /device:TPU:2, one launch (start us, length us, event | category | flops | bytes accessed | tf_op | source)
XLA Modules:
  0.0 170.6 jit_solution(14759824493454029196)
XLA Ops:
  0.6 1.1 multiply_convert_fusion
  1.7 1.5 broadcast_in_dim.22
  3.2 8.7 %all-to-all-start = ((bf16[8,256,512]{2,1,0:T(8,128)(2,1)}), bf16[8,256,512]{2,1,0:T(8,128)(2,1)S(1)}, u32[]{:S(2)}, u32[]{:S(2)}) async-start(bf16[8,256,512]{2,1,0:T(8,128)(2,1)} %broadcast_in_dim.22), calls=%async_computation | async-start | bytes 4194304 | tf_op jit(solution)/shard_map/all_to_all | solution.py:169
  11.9 0.1 pad.15.clone
  12.0 52.8 %all-to-all-done = bf16[8,256,512]{2,1,0:T(8,128)(2,1)S(1)} async-done(((bf16[8,256,512]{2,1,0:T(8,128)(2,1)}), bf16[8,256,512]{2,1,0:T(8,128)(2,1)S(1)}, u32[]{:S(2)}, u32[]{:S(2)}) %all-to-all-start) | async-done | bytes 2097184 | tf_op jit(solution)/shard_map/all_to_all | solution.py:169
  64.8 1.3 convolution_bitcast_fusion
  66.0 0.1 slice_select_fusion.2
  66.1 0.1 maximum_maximum_fusion.local_ref
  66.2 2.7 %collective-permute-start = (f32[520,256]{1,0:T(8,128)S(1)}, f32[520,256]{1,0:T(8,128)S(1)}, u32[]{:S(2)}, u32[]{:S(2)}) collective-permute-start(f32[520,256]{1,0:T(8,128)S(1)} %maximum_maximum_fusion.local_ref), channel_id=1, source_target_pairs={{0,1},{1,0},{16,23},{23,16},{2,3},{3,2},{18,17},{17,18},{4,5},{5,4... | collective-permute-start | bytes 1597448 | tf_op jit(solution)/shard_map/ppermute | solution.py:40
  68.9 8.5 %collective-permute-done.received_ref = f32[520,256]{1,0:T(8,128)S(1)} collective-permute-done((f32[520,256]{1,0:T(8,128)S(1)}, f32[520,256]{1,0:T(8,128)S(1)}, u32[]{:S(2)}, u32[]{:S(2)}) %collective-permute-start) | collective-permute-done | bytes 532512 | tf_op jit(solution)/shard_map/ppermute | solution.py:40
  77.4 3.8 %shard_map.41 = bf16[512,512]{1,0:T(8,128)(2,1)S(1)} custom-call(f32[520,256]{1,0:T(8,128)S(1)} %maximum_maximum_fusion.local_ref, f32[520,256]{1,0:T(8,128)S(1)} %collective-permute-done.received_ref), custom_call_target="tpu_custom_call" | custom-call | flops 15728640 | bytes 1048576 | tf_op jit(solution)/shard_map/pallas_call | solution.py:140
  81.2 0.8 convolution_convert_fusion.3
  82.0 1.9 %collective-permute-start.1 = (bf16[2048,256]{0,1:T(8,128)(2,1)S(1)}, bf16[2048,256]{0,1:T(8,128)(2,1)}, u32[]{:S(2)}, u32[]{:S(2)}) collective-permute-start(bf16[2048,256]{0,1:T(8,128)(2,1)S(1)} %convolution_convert_fusion.3), channel_id=1, source_target_pairs={{0,16},{16,32},{32,48},{48,64},{64,80},{80,96},{96,112},{112,128},... | collective-permute-start | bytes 3145736 | tf_op jit(solution)/shard_map/ppermute | solution.py:24
  83.9 1.7 %convolution_convert_fusion.4 = bf16[2048,256]{0,1:T(8,128)(2,1)} fusion(bf16[2048,512]{1,0:T(8,128)(2,1)S(1)} %bitcast.12, pred[]{:T(512)S(6)} %eq.10, bf16[512,512]{1,0:T(8,128)(2,1)S(1)} %shard_map.41), kind=kOutput, calls=%fused_computation.5 | convolution fusion | flops 537526272 | bytes 3670017 | tf_op jit(solution)/shard_map/dot_general | solution.py:219
  85.6 10.2 %collective-permute-start.2 = (bf16[2048,256]{0,1:T(8,128)(2,1)}, bf16[2048,256]{0,1:T(8,128)(2,1)S(1)}, u32[]{:S(2)}, u32[]{:S(2)}) collective-permute-start(bf16[2048,256]{0,1:T(8,128)(2,1)} %convolution_convert_fusion.4), channel_id=1, source_target_pairs={{16,0},{32,16},{48,32},{64,48},{80,64},{96,80},{112,96},{128,112},... | collective-permute-start | bytes 3145736 | tf_op jit(solution)/shard_map/ppermute | solution.py:24
  95.8 8.9 %collective-permute-done.1 = bf16[2048,256]{0,1:T(8,128)(2,1)} collective-permute-done((bf16[2048,256]{0,1:T(8,128)(2,1)S(1)}, bf16[2048,256]{0,1:T(8,128)(2,1)}, u32[]{:S(2)}, u32[]{:S(2)}) %collective-permute-start.1) | collective-permute-done | bytes 1048608 | tf_op jit(solution)/shard_map/ppermute | solution.py:24
  104.7 1.3 broadcast_select_fusion.3
  106.1 2.3 %collective-permute-done.2 = bf16[2048,256]{0,1:T(8,128)(2,1)S(1)} collective-permute-done((bf16[2048,256]{0,1:T(8,128)(2,1)}, bf16[2048,256]{0,1:T(8,128)(2,1)S(1)}, u32[]{:S(2)}, u32[]{:S(2)}) %collective-permute-start.2) | collective-permute-done | bytes 1048608 | tf_op jit(solution)/shard_map/ppermute | solution.py:24
  108.4 0.1 broadcast_select_fusion.1
  108.5 1.3 fusion.1
  109.8 0.1 slice_select_fusion.1
  109.9 0.1 maximum_maximum_fusion.1.local_ref
  110.0 2.1 %collective-permute-start.3 = (f32[520,256]{1,0:T(8,128)S(1)}, f32[520,256]{1,0:T(8,128)S(1)}, u32[]{:S(2)}, u32[]{:S(2)}) collective-permute-start(f32[520,256]{1,0:T(8,128)S(1)} %maximum_maximum_fusion.1.local_ref), channel_id=1, source_target_pairs={{0,1},{1,0},{16,23},{23,16},{2,3},{3,2},{18,17},{17,18},{4,5},{5,4... | collective-permute-start | bytes 1597448 | tf_op jit(solution)/shard_map/ppermute | solution.py:40
  112.1 9.1 %collective-permute-done.3.received_ref = f32[520,256]{1,0:T(8,128)S(1)} collective-permute-done((f32[520,256]{1,0:T(8,128)S(1)}, f32[520,256]{1,0:T(8,128)S(1)}, u32[]{:S(2)}, u32[]{:S(2)}) %collective-permute-start.3) | collective-permute-done | bytes 532512 | tf_op jit(solution)/shard_map/ppermute | solution.py:40
  121.2 3.8 %shard_map.42 = bf16[512,512]{1,0:T(8,128)(2,1)S(1)} custom-call(f32[520,256]{1,0:T(8,128)S(1)} %maximum_maximum_fusion.1.local_ref, f32[520,256]{1,0:T(8,128)S(1)} %collective-permute-done.3.received_ref), custom_call_target="tpu_custom_call" | custom-call | flops 15728640 | bytes 1048576 | tf_op jit(solution)/shard_map/pallas_call | solution.py:140
  125.0 0.8 convolution_convert_fusion.1
  125.7 1.9 %collective-permute-start.4 = (bf16[2048,256]{0,1:T(8,128)(2,1)S(1)}, bf16[2048,256]{0,1:T(8,128)(2,1)S(1)}, u32[]{:S(2)}, u32[]{:S(2)}) collective-permute-start(bf16[2048,256]{0,1:T(8,128)(2,1)S(1)} %convolution_convert_fusion.1), channel_id=1, source_target_pairs={{0,16},{16,32},{32,48},{48,64},{64,80},{80,96},{96,112},{112,128},... | collective-permute-start | bytes 3145736 | tf_op jit(solution)/shard_map/ppermute | solution.py:24
  127.7 0.8 convolution_convert_fusion.2
  128.4 5.9 %collective-permute-start.5 = (bf16[2048,256]{0,1:T(8,128)(2,1)S(1)}, bf16[2048,256]{0,1:T(8,128)(2,1)S(1)}, u32[]{:S(2)}, u32[]{:S(2)}) collective-permute-start(bf16[2048,256]{0,1:T(8,128)(2,1)S(1)} %convolution_convert_fusion.2), channel_id=1, source_target_pairs={{16,0},{32,16},{48,32},{64,48},{80,64},{96,80},{112,96},{128,112},... | collective-permute-start | bytes 3145736 | tf_op jit(solution)/shard_map/ppermute | solution.py:24
  134.3 9.8 %collective-permute-done.4 = bf16[2048,256]{0,1:T(8,128)(2,1)S(1)} collective-permute-done((bf16[2048,256]{0,1:T(8,128)(2,1)S(1)}, bf16[2048,256]{0,1:T(8,128)(2,1)S(1)}, u32[]{:S(2)}, u32[]{:S(2)}) %collective-permute-start.4) | collective-permute-done | bytes 1048608 | tf_op jit(solution)/shard_map/ppermute | solution.py:24
  144.1 0.1 broadcast_select_fusion.2
  144.2 2.4 %collective-permute-done.5 = bf16[2048,256]{0,1:T(8,128)(2,1)S(1)} collective-permute-done((bf16[2048,256]{0,1:T(8,128)(2,1)S(1)}, bf16[2048,256]{0,1:T(8,128)(2,1)S(1)}, u32[]{:S(2)}, u32[]{:S(2)}) %collective-permute-start.5) | collective-permute-done | bytes 1048608 | tf_op jit(solution)/shard_map/ppermute | solution.py:24
  146.6 0.1 broadcast_select_fusion
  146.7 1.3 fusion
  148.0 0.1 slice_select_fusion
  148.1 0.1 maximum_maximum_fusion.2.local_ref
  148.2 1.9 %collective-permute-start.6 = (f32[520,256]{1,0:T(8,128)S(1)}, f32[520,256]{1,0:T(8,128)S(1)}, u32[]{:S(2)}, u32[]{:S(2)}) collective-permute-start(f32[520,256]{1,0:T(8,128)S(1)} %maximum_maximum_fusion.2.local_ref), channel_id=1, source_target_pairs={{0,1},{1,0},{16,23},{23,16},{2,3},{3,2},{18,17},{17,18},{4,5},{5,4... | collective-permute-start | bytes 1597448 | tf_op jit(solution)/shard_map/ppermute | solution.py:40
  150.2 9.2 %collective-permute-done.6.received_ref = f32[520,256]{1,0:T(8,128)S(1)} collective-permute-done((f32[520,256]{1,0:T(8,128)S(1)}, f32[520,256]{1,0:T(8,128)S(1)}, u32[]{:S(2)}, u32[]{:S(2)}) %collective-permute-start.6) | collective-permute-done | bytes 532512 | tf_op jit(solution)/shard_map/ppermute | solution.py:40
  159.4 3.8 %shard_map.43 = bf16[512,512]{1,0:T(8,128)(2,1)S(1)} custom-call(f32[520,256]{1,0:T(8,128)S(1)} %maximum_maximum_fusion.2.local_ref, f32[520,256]{1,0:T(8,128)S(1)} %collective-permute-done.6.received_ref), custom_call_target="tpu_custom_call" | custom-call | flops 15728640 | bytes 1048576 | tf_op jit(solution)/shard_map/pallas_call | solution.py:140
  163.2 1.3 multiply_reduce_fusion
  164.5 1.9 %collective-permute-start.7 = (f32[512]{0:T(512)S(1)}, f32[512]{0:T(512)S(1)}, u32[]{:S(2)}, u32[]{:S(2)}) collective-permute-start(f32[512]{0:T(512)S(1)} %get-tuple-element.11), channel_id=1, source_target_pairs={{0,1},{1,0},{16,23},{23,16},{2,3},{3,2},{18,17},{17,18},{4,5},{5,4... | collective-permute-start | bytes 6152 | tf_op jit(solution)/shard_map/ppermute | solution.py:40
  166.4 0.7 constant_dynamic-slice_fusion
  167.2 2.8 %collective-permute-done.7 = f32[512]{0:T(512)S(1)} collective-permute-done((f32[512]{0:T(512)S(1)}, f32[512]{0:T(512)S(1)}, u32[]{:S(2)}, u32[]{:S(2)}) %collective-permute-start.7) | collective-permute-done | bytes 2080 | tf_op jit(solution)/shard_map/ppermute | solution.py:40
  170.0 0.6 add_sqrt_fusion
  (1 shorter events, 0.0 us)
Async XLA Ops:
  3.2 61.5 %all-to-all-start = ((bf16[8,256,512]{2,1,0:T(8,128)(2,1)}), bf16[8,256,512]{2,1,0:T(8,128)(2,1)S(1)}, u32[]{:S(2)}, u32[]{:S(2)}) async-start(bf16[8,256,512]{2,1,0:T(8,128)(2,1)} %broadcast_in_dim.22), calls=%async_computation | async-start | bytes 4194304 | tf_op jit(solution)/shard_map/all_to_all | solution.py:169
  66.2 11.2 %collective-permute-start = (f32[520,256]{1,0:T(8,128)S(1)}, f32[520,256]{1,0:T(8,128)S(1)}, u32[]{:S(2)}, u32[]{:S(2)}) collective-permute-start(f32[520,256]{1,0:T(8,128)S(1)} %maximum_maximum_fusion.local_ref), channel_id=1, source_target_pairs={{0,1},{1,0},{16,23},{23,16},{2,3},{3,2},{18,17},{17,18},{4,5},{5,4... | collective-permute-start | bytes 1597448 | tf_op jit(solution)/shard_map/ppermute | solution.py:40
  82.0 22.8 %collective-permute-start.1 = (bf16[2048,256]{0,1:T(8,128)(2,1)S(1)}, bf16[2048,256]{0,1:T(8,128)(2,1)}, u32[]{:S(2)}, u32[]{:S(2)}) collective-permute-start(bf16[2048,256]{0,1:T(8,128)(2,1)S(1)} %convolution_convert_fusion.3), channel_id=1, source_target_pairs={{0,16},{16,32},{32,48},{48,64},{64,80},{80,96},{96,112},{112,128},... | collective-permute-start | bytes 3145736 | tf_op jit(solution)/shard_map/ppermute | solution.py:24
  85.6 22.8 %collective-permute-start.2 = (bf16[2048,256]{0,1:T(8,128)(2,1)}, bf16[2048,256]{0,1:T(8,128)(2,1)S(1)}, u32[]{:S(2)}, u32[]{:S(2)}) collective-permute-start(bf16[2048,256]{0,1:T(8,128)(2,1)} %convolution_convert_fusion.4), channel_id=1, source_target_pairs={{16,0},{32,16},{48,32},{64,48},{80,64},{96,80},{112,96},{128,112},... | collective-permute-start | bytes 3145736 | tf_op jit(solution)/shard_map/ppermute | solution.py:24
  110.0 11.2 %collective-permute-start.3 = (f32[520,256]{1,0:T(8,128)S(1)}, f32[520,256]{1,0:T(8,128)S(1)}, u32[]{:S(2)}, u32[]{:S(2)}) collective-permute-start(f32[520,256]{1,0:T(8,128)S(1)} %maximum_maximum_fusion.1.local_ref), channel_id=1, source_target_pairs={{0,1},{1,0},{16,23},{23,16},{2,3},{3,2},{18,17},{17,18},{4,5},{5,4... | collective-permute-start | bytes 1597448 | tf_op jit(solution)/shard_map/ppermute | solution.py:40
  125.7 18.4 %collective-permute-start.4 = (bf16[2048,256]{0,1:T(8,128)(2,1)S(1)}, bf16[2048,256]{0,1:T(8,128)(2,1)S(1)}, u32[]{:S(2)}, u32[]{:S(2)}) collective-permute-start(bf16[2048,256]{0,1:T(8,128)(2,1)S(1)} %convolution_convert_fusion.1), channel_id=1, source_target_pairs={{0,16},{16,32},{32,48},{48,64},{64,80},{80,96},{96,112},{112,128},... | collective-permute-start | bytes 3145736 | tf_op jit(solution)/shard_map/ppermute | solution.py:24
  128.4 18.2 %collective-permute-start.5 = (bf16[2048,256]{0,1:T(8,128)(2,1)S(1)}, bf16[2048,256]{0,1:T(8,128)(2,1)S(1)}, u32[]{:S(2)}, u32[]{:S(2)}) collective-permute-start(bf16[2048,256]{0,1:T(8,128)(2,1)S(1)} %convolution_convert_fusion.2), channel_id=1, source_target_pairs={{16,0},{32,16},{48,32},{64,48},{80,64},{96,80},{112,96},{128,112},... | collective-permute-start | bytes 3145736 | tf_op jit(solution)/shard_map/ppermute | solution.py:24
  148.2 11.2 %collective-permute-start.6 = (f32[520,256]{1,0:T(8,128)S(1)}, f32[520,256]{1,0:T(8,128)S(1)}, u32[]{:S(2)}, u32[]{:S(2)}) collective-permute-start(f32[520,256]{1,0:T(8,128)S(1)} %maximum_maximum_fusion.2.local_ref), channel_id=1, source_target_pairs={{0,1},{1,0},{16,23},{23,16},{2,3},{3,2},{18,17},{17,18},{4,5},{5,4... | collective-permute-start | bytes 1597448 | tf_op jit(solution)/shard_map/ppermute | solution.py:40
  164.5 5.5 %collective-permute-start.7 = (f32[512]{0:T(512)S(1)}, f32[512]{0:T(512)S(1)}, u32[]{:S(2)}, u32[]{:S(2)}) collective-permute-start(f32[512]{0:T(512)S(1)} %get-tuple-element.11), channel_id=1, source_target_pairs={{0,1},{1,0},{16,23},{23,16},{2,3},{3,2},{18,17},{17,18},{4,5},{5,4... | collective-permute-start | bytes 6152 | tf_op jit(solution)/shard_map/ppermute | solution.py:40

commit v18 on v13

--- a/solution.py
+++ b/solution.py
@@ -80,7 +80,6 @@
     mirrored = folded.T
     top_left = jnp.where(rows <= cols, folded, mirrored)
     low_right = jnp.where(rows > cols, folded, jnp.where(rows < cols, mirrored, low_diag))
-    low_left = top_right.T
     first_top = jnp.where(on_diagonal, 1.0, 0.0).astype(jnp.float32)
     first_low = jnp.zeros((width, width), jnp.float32)
     second_top = jnp.zeros((width, width), jnp.float32)
@@ -98,10 +97,10 @@
     for sweep_index in range(SWEEPS):
         if sweep_index > 0:
             top_right = to_left(top_right, 1)
-            low_left = to_left(low_left, 0)
             low_right = to_left(to_left(low_right, 0), 1)
             second_top = to_left(second_top, 1)
             second_low = to_left(second_low, 1)
+        low_left = top_right.T
         cos_col, sin_col = half_angle_terms(
             diagonal_row(top_left), diagonal_row(low_right), diagonal_row(top_right)
         )
@@ -112,7 +111,6 @@
         left_b = low_left * cos_col - low_right * sin_col
         right_b = low_left * sin_col + low_right * cos_col
         top_left = cos_row * left_a - sin_row * left_b
-        low_left = sin_row * left_a + cos_row * left_b
         top_right = cos_row * right_a - sin_row * right_b
         low_right = sin_row * right_a + cos_row * right_b
         first_top, second_top = (
@@ -140,6 +138,7 @@
         out_shape=jax.ShapeDtypeStruct((2 * width, 2 * width), jnp.bfloat16),
         in_specs=[vmem, vmem],
         out_specs=vmem,
+        compiler_params=pltpu.CompilerParams(vmem_limit_bytes=16 * 1024 * 1024),
         cost_estimate=pl.CostEstimate(
             flops=SWEEPS * 40 * width * width, transcendentals=SWEEPS * 8 * width, bytes_accessed=4 * 4 * width * width
         ),

time: 184 us -> 171 us (0.929)
  Pallas kernels: 17.4 us -> 11.3 us
  matrix products: 13.5 us -> 10.2 us
  local copies, waits for them, and re-layouts: 4.04 us -> 1.6 us
    pallas_call x3, Pallas kernels: 17.4 us -> 11.3 us  [rotation_of(): pl.pallas_call(sweeps_kernel, out_shape=jax.ShapeDtypeStruct((2 * width,...]
    unnamed x22 -> x0, local copies, waits for them, and re-layouts: 2.45 us -> none
    dot_general x2, matrix products: 3.68 us -> 1.52 us  [local(): jnp.dot(pair_data, jnp.where(position == 0, second_columns, first_columns...]
where the time goes in v18:
time: 171 us
  waiting for transfers between devices  105 us (61%)
  starting transfers between devices  37.2 us (22%)
  Pallas kernels  11.3 us (7%)
  matrix products  10.2 us (6%)
  other arithmetic  3.91 us (2%)
    all_to_all x1, waiting for transfers between devices, gathered_records(): gathered = lax.all_to_all(spread, GROUP_AXES, 0, 0, tiled=False)  52.8 us
    ppermute x4, waiting for transfers between devices, from_partner(): lax.ppermute(value, PARTNER_AXES, partner_pairs(lax.axis_size('y_hi')))  29.2 us
    ppermute x4, waiting for transfers between devices, from_behind(): lax.ppermute(value, COLUMN_AXES, [(source, source + steps) for source in...  23.4 us
    ppermute x4, starting transfers between devices, from_behind(): lax.ppermute(value, COLUMN_AXES, [(source, source + steps) for source in...  19.9 us
    pallas_call x3, Pallas kernels, rotation_of(): pl.pallas_call(sweeps_kernel, out_shape=jax.ShapeDtypeStruct((2 * width,...  11.3 us
    all_to_all x1, starting transfers between devices, gathered_records(): gathered = lax.all_to_all(spread, GROUP_AXES, 0, 0, tiled=False)  8.66 us
    ppermute x4, starting transfers between devices, from_partner(): lax.ppermute(value, PARTNER_AXES, partner_pairs(lax.axis_size('y_hi')))  8.63 us
    dot_general x3, matrix products, inner_products(): lax.dot_general(left_part, right_part, (((0,), (0,)), ((), ())), preferre...  3.84 us
  transfers between devices with their start and end apart: 9, of which 9 were waited for; matrix products, arithmetic and copies ran while one was open for 3% of the time, Pallas kernels for 0%

profile of v18, /device:TPU:2, one launch (start us, length us, event | category | flops | bytes accessed | tf_op | source)
XLA Modules:
  0.0 170.6 jit_solution(11006022693378391709)
XLA Ops:
  0.6 1.1 multiply_convert_fusion
  1.7 1.5 broadcast_in_dim.22
  3.2 8.7 %all-to-all-start = ((bf16[8,256,512]{2,1,0:T(8,128)(2,1)}), bf16[8,256,512]{2,1,0:T(8,128)(2,1)S(1)}, u32[]{:S(2)}, u32[]{:S(2)}) async-start(bf16[8,256,512]{2,1,0:T(8,128)(2,1)} %broadcast_in_dim.22), calls=%async_computation | async-start | bytes 4194304 | tf_op jit(solution)/shard_map/all_to_all | solution.py:165
  11.9 0.1 pad.15.clone
  12.0 52.8 %all-to-all-done = bf16[8,256,512]{2,1,0:T(8,128)(2,1)S(1)} async-done(((bf16[8,256,512]{2,1,0:T(8,128)(2,1)}), bf16[8,256,512]{2,1,0:T(8,128)(2,1)S(1)}, u32[]{:S(2)}, u32[]{:S(2)}) %all-to-all-start) | async-done | bytes 2097184 | tf_op jit(solution)/shard_map/all_to_all | solution.py:165
  64.8 1.3 convolution_bitcast_fusion
  66.0 0.1 slice_select_fusion.2
  66.1 0.1 maximum_maximum_fusion.local_ref
  66.2 2.7 %collective-permute-start = (f32[520,256]{1,0:T(8,128)S(1)}, f32[520,256]{1,0:T(8,128)S(1)}, u32[]{:S(2)}, u32[]{:S(2)}) collective-permute-start(f32[520,256]{1,0:T(8,128)S(1)} %maximum_maximum_fusion.local_ref), channel_id=1, source_target_pairs={{0,1},{1,0},{16,23},{23,16},{2,3},{3,2},{18,17},{17,18},{4,5},{5,4... | collective-permute-start | bytes 1597448 | tf_op jit(solution)/shard_map/ppermute | solution.py:40
  69.0 8.5 %collective-permute-done.received_ref = f32[520,256]{1,0:T(8,128)S(1)} collective-permute-done((f32[520,256]{1,0:T(8,128)S(1)}, f32[520,256]{1,0:T(8,128)S(1)}, u32[]{:S(2)}, u32[]{:S(2)}) %collective-permute-start) | collective-permute-done | bytes 532512 | tf_op jit(solution)/shard_map/ppermute | solution.py:40
  77.4 3.8 %shard_map.41 = bf16[512,512]{1,0:T(8,128)(2,1)S(1)} custom-call(f32[520,256]{1,0:T(8,128)S(1)} %maximum_maximum_fusion.local_ref, f32[520,256]{1,0:T(8,128)S(1)} %collective-permute-done.received_ref), custom_call_target="tpu_custom_call" | custom-call | flops 15728640 | bytes 1048576 | tf_op jit(solution)/shard_map/pallas_call | solution.py:136
  81.2 0.8 convolution_convert_fusion.3
  82.0 1.9 %collective-permute-start.1 = (bf16[2048,256]{0,1:T(8,128)(2,1)S(1)}, bf16[2048,256]{0,1:T(8,128)(2,1)}, u32[]{:S(2)}, u32[]{:S(2)}) collective-permute-start(bf16[2048,256]{0,1:T(8,128)(2,1)S(1)} %convolution_convert_fusion.3), channel_id=1, source_target_pairs={{0,16},{16,32},{32,48},{48,64},{64,80},{80,96},{96,112},{112,128},... | collective-permute-start | bytes 3145736 | tf_op jit(solution)/shard_map/ppermute | solution.py:24
  83.9 1.7 %convolution_convert_fusion.4 = bf16[2048,256]{0,1:T(8,128)(2,1)} fusion(bf16[2048,512]{1,0:T(8,128)(2,1)S(1)} %bitcast.13, pred[]{:T(512)S(6)} %eq.10, bf16[512,512]{1,0:T(8,128)(2,1)S(1)} %shard_map.41), kind=kOutput, calls=%fused_computation.5 | convolution fusion | flops 537526272 | bytes 3670017 | tf_op jit(solution)/shard_map/dot_general | solution.py:212
  85.6 10.2 %collective-permute-start.2 = (bf16[2048,256]{0,1:T(8,128)(2,1)}, bf16[2048,256]{0,1:T(8,128)(2,1)S(1)}, u32[]{:S(2)}, u32[]{:S(2)}) collective-permute-start(bf16[2048,256]{0,1:T(8,128)(2,1)} %convolution_convert_fusion.4), channel_id=1, source_target_pairs={{16,0},{32,16},{48,32},{64,48},{80,64},{96,80},{112,96},{128,112},... | collective-permute-start | bytes 3145736 | tf_op jit(solution)/shard_map/ppermute | solution.py:24
  95.8 8.9 %collective-permute-done.1 = bf16[2048,256]{0,1:T(8,128)(2,1)} collective-permute-done((bf16[2048,256]{0,1:T(8,128)(2,1)S(1)}, bf16[2048,256]{0,1:T(8,128)(2,1)}, u32[]{:S(2)}, u32[]{:S(2)}) %collective-permute-start.1) | collective-permute-done | bytes 1048608 | tf_op jit(solution)/shard_map/ppermute | solution.py:24
  104.7 1.3 broadcast_select_fusion.3
  106.1 2.4 %collective-permute-done.2 = bf16[2048,256]{0,1:T(8,128)(2,1)S(1)} collective-permute-done((bf16[2048,256]{0,1:T(8,128)(2,1)}, bf16[2048,256]{0,1:T(8,128)(2,1)S(1)}, u32[]{:S(2)}, u32[]{:S(2)}) %collective-permute-start.2) | collective-permute-done | bytes 1048608 | tf_op jit(solution)/shard_map/ppermute | solution.py:24
  108.4 0.1 broadcast_select_fusion.1
  108.5 1.3 fusion.1
  109.8 0.1 slice_select_fusion.1
  109.9 0.1 maximum_maximum_fusion.1.local_ref
  110.0 2.1 %collective-permute-start.3 = (f32[520,256]{1,0:T(8,128)S(1)}, f32[520,256]{1,0:T(8,128)S(1)}, u32[]{:S(2)}, u32[]{:S(2)}) collective-permute-start(f32[520,256]{1,0:T(8,128)S(1)} %maximum_maximum_fusion.1.local_ref), channel_id=1, source_target_pairs={{0,1},{1,0},{16,23},{23,16},{2,3},{3,2},{18,17},{17,18},{4,5},{5,4... | collective-permute-start | bytes 1597448 | tf_op jit(solution)/shard_map/ppermute | solution.py:40
  112.1 9.1 %collective-permute-done.3.received_ref = f32[520,256]{1,0:T(8,128)S(1)} collective-permute-done((f32[520,256]{1,0:T(8,128)S(1)}, f32[520,256]{1,0:T(8,128)S(1)}, u32[]{:S(2)}, u32[]{:S(2)}) %collective-permute-start.3) | collective-permute-done | bytes 532512 | tf_op jit(solution)/shard_map/ppermute | solution.py:40
  121.2 3.8 %shard_map.42 = bf16[512,512]{1,0:T(8,128)(2,1)S(1)} custom-call(f32[520,256]{1,0:T(8,128)S(1)} %maximum_maximum_fusion.1.local_ref, f32[520,256]{1,0:T(8,128)S(1)} %collective-permute-done.3.received_ref), custom_call_target="tpu_custom_call" | custom-call | flops 15728640 | bytes 1048576 | tf_op jit(solution)/shard_map/pallas_call | solution.py:136
  125.0 0.8 convolution_convert_fusion.1
  125.7 1.9 %collective-permute-start.4 = (bf16[2048,256]{0,1:T(8,128)(2,1)S(1)}, bf16[2048,256]{0,1:T(8,128)(2,1)S(1)}, u32[]{:S(2)}, u32[]{:S(2)}) collective-permute-start(bf16[2048,256]{0,1:T(8,128)(2,1)S(1)} %convolution_convert_fusion.1), channel_id=1, source_target_pairs={{0,16},{16,32},{32,48},{48,64},{64,80},{80,96},{96,112},{112,128},... | collective-permute-start | bytes 3145736 | tf_op jit(solution)/shard_map/ppermute | solution.py:24
  127.7 0.8 convolution_convert_fusion.2
  128.4 5.9 %collective-permute-start.5 = (bf16[2048,256]{0,1:T(8,128)(2,1)S(1)}, bf16[2048,256]{0,1:T(8,128)(2,1)S(1)}, u32[]{:S(2)}, u32[]{:S(2)}) collective-permute-start(bf16[2048,256]{0,1:T(8,128)(2,1)S(1)} %convolution_convert_fusion.2), channel_id=1, source_target_pairs={{16,0},{32,16},{48,32},{64,48},{80,64},{96,80},{112,96},{128,112},... | collective-permute-start | bytes 3145736 | tf_op jit(solution)/shard_map/ppermute | solution.py:24
  134.3 9.8 %collective-permute-done.4 = bf16[2048,256]{0,1:T(8,128)(2,1)S(1)} collective-permute-done((bf16[2048,256]{0,1:T(8,128)(2,1)S(1)}, bf16[2048,256]{0,1:T(8,128)(2,1)S(1)}, u32[]{:S(2)}, u32[]{:S(2)}) %collective-permute-start.4) | collective-permute-done | bytes 1048608 | tf_op jit(solution)/shard_map/ppermute | solution.py:24
  144.1 0.1 broadcast_select_fusion.2
  144.2 2.4 %collective-permute-done.5 = bf16[2048,256]{0,1:T(8,128)(2,1)S(1)} collective-permute-done((bf16[2048,256]{0,1:T(8,128)(2,1)S(1)}, bf16[2048,256]{0,1:T(8,128)(2,1)S(1)}, u32[]{:S(2)}, u32[]{:S(2)}) %collective-permute-start.5) | collective-permute-done | bytes 1048608 | tf_op jit(solution)/shard_map/ppermute | solution.py:24
  146.6 0.1 broadcast_select_fusion
  146.7 1.3 fusion
  148.0 0.1 slice_select_fusion
  148.1 0.1 maximum_maximum_fusion.2.local_ref
  148.2 1.9 %collective-permute-start.6 = (f32[520,256]{1,0:T(8,128)S(1)}, f32[520,256]{1,0:T(8,128)S(1)}, u32[]{:S(2)}, u32[]{:S(2)}) collective-permute-start(f32[520,256]{1,0:T(8,128)S(1)} %maximum_maximum_fusion.2.local_ref), channel_id=1, source_target_pairs={{0,1},{1,0},{16,23},{23,16},{2,3},{3,2},{18,17},{17,18},{4,5},{5,4... | collective-permute-start | bytes 1597448 | tf_op jit(solution)/shard_map/ppermute | solution.py:40
  150.2 9.2 %collective-permute-done.6.received_ref = f32[520,256]{1,0:T(8,128)S(1)} collective-permute-done((f32[520,256]{1,0:T(8,128)S(1)}, f32[520,256]{1,0:T(8,128)S(1)}, u32[]{:S(2)}, u32[]{:S(2)}) %collective-permute-start.6) | collective-permute-done | bytes 532512 | tf_op jit(solution)/shard_map/ppermute | solution.py:40
  159.4 3.8 %shard_map.43 = bf16[512,512]{1,0:T(8,128)(2,1)S(1)} custom-call(f32[520,256]{1,0:T(8,128)S(1)} %maximum_maximum_fusion.2.local_ref, f32[520,256]{1,0:T(8,128)S(1)} %collective-permute-done.6.received_ref), custom_call_target="tpu_custom_call" | custom-call | flops 15728640 | bytes 1048576 | tf_op jit(solution)/shard_map/pallas_call | solution.py:136
  163.2 1.3 multiply_reduce_fusion
  164.5 1.9 %collective-permute-start.7 = (f32[512]{0:T(512)S(1)}, f32[512]{0:T(512)S(1)}, u32[]{:S(2)}, u32[]{:S(2)}) collective-permute-start(f32[512]{0:T(512)S(1)} %multiply_reduce_fusion), channel_id=1, source_target_pairs={{0,1},{1,0},{16,23},{23,16},{2,3},{3,2},{18,17},{17,18},{4,5},{5,4... | collective-permute-start | bytes 6152 | tf_op jit(solution)/shard_map/ppermute | solution.py:40
  166.4 1.0 convolution_convert_fusion.5
  167.5 2.5 %collective-permute-done.7 = f32[512]{0:T(512)S(1)} collective-permute-done((f32[512]{0:T(512)S(1)}, f32[512]{0:T(512)S(1)}, u32[]{:S(2)}, u32[]{:S(2)}) %collective-permute-start.7) | collective-permute-done | bytes 2080 | tf_op jit(solution)/shard_map/ppermute | solution.py:40
  170.0 0.6 add_sqrt_fusion
  (1 shorter events, 0.0 us)
Async XLA Ops:
  3.2 61.5 %all-to-all-start = ((bf16[8,256,512]{2,1,0:T(8,128)(2,1)}), bf16[8,256,512]{2,1,0:T(8,128)(2,1)S(1)}, u32[]{:S(2)}, u32[]{:S(2)}) async-start(bf16[8,256,512]{2,1,0:T(8,128)(2,1)} %broadcast_in_dim.22), calls=%async_computation | async-start | bytes 4194304 | tf_op jit(solution)/shard_map/all_to_all | solution.py:165
  66.2 11.2 %collective-permute-start = (f32[520,256]{1,0:T(8,128)S(1)}, f32[520,256]{1,0:T(8,128)S(1)}, u32[]{:S(2)}, u32[]{:S(2)}) collective-permute-start(f32[520,256]{1,0:T(8,128)S(1)} %maximum_maximum_fusion.local_ref), channel_id=1, source_target_pairs={{0,1},{1,0},{16,23},{23,16},{2,3},{3,2},{18,17},{17,18},{4,5},{5,4... | collective-permute-start | bytes 1597448 | tf_op jit(solution)/shard_map/ppermute | solution.py:40
  82.0 22.8 %collective-permute-start.1 = (bf16[2048,256]{0,1:T(8,128)(2,1)S(1)}, bf16[2048,256]{0,1:T(8,128)(2,1)}, u32[]{:S(2)}, u32[]{:S(2)}) collective-permute-start(bf16[2048,256]{0,1:T(8,128)(2,1)S(1)} %convolution_convert_fusion.3), channel_id=1, source_target_pairs={{0,16},{16,32},{32,48},{48,64},{64,80},{80,96},{96,112},{112,128},... | collective-permute-start | bytes 3145736 | tf_op jit(solution)/shard_map/ppermute | solution.py:24
  85.6 22.8 %collective-permute-start.2 = (bf16[2048,256]{0,1:T(8,128)(2,1)}, bf16[2048,256]{0,1:T(8,128)(2,1)S(1)}, u32[]{:S(2)}, u32[]{:S(2)}) collective-permute-start(bf16[2048,256]{0,1:T(8,128)(2,1)} %convolution_convert_fusion.4), channel_id=1, source_target_pairs={{16,0},{32,16},{48,32},{64,48},{80,64},{96,80},{112,96},{128,112},... | collective-permute-start | bytes 3145736 | tf_op jit(solution)/shard_map/ppermute | solution.py:24
  110.0 11.2 %collective-permute-start.3 = (f32[520,256]{1,0:T(8,128)S(1)}, f32[520,256]{1,0:T(8,128)S(1)}, u32[]{:S(2)}, u32[]{:S(2)}) collective-permute-start(f32[520,256]{1,0:T(8,128)S(1)} %maximum_maximum_fusion.1.local_ref), channel_id=1, source_target_pairs={{0,1},{1,0},{16,23},{23,16},{2,3},{3,2},{18,17},{17,18},{4,5},{5,4... | collective-permute-start | bytes 1597448 | tf_op jit(solution)/shard_map/ppermute | solution.py:40
  125.7 18.4 %collective-permute-start.4 = (bf16[2048,256]{0,1:T(8,128)(2,1)S(1)}, bf16[2048,256]{0,1:T(8,128)(2,1)S(1)}, u32[]{:S(2)}, u32[]{:S(2)}) collective-permute-start(bf16[2048,256]{0,1:T(8,128)(2,1)S(1)} %convolution_convert_fusion.1), channel_id=1, source_target_pairs={{0,16},{16,32},{32,48},{48,64},{64,80},{80,96},{96,112},{112,128},... | collective-permute-start | bytes 3145736 | tf_op jit(solution)/shard_map/ppermute | solution.py:24
  128.4 18.2 %collective-permute-start.5 = (bf16[2048,256]{0,1:T(8,128)(2,1)S(1)}, bf16[2048,256]{0,1:T(8,128)(2,1)S(1)}, u32[]{:S(2)}, u32[]{:S(2)}) collective-permute-start(bf16[2048,256]{0,1:T(8,128)(2,1)S(1)} %convolution_convert_fusion.2), channel_id=1, source_target_pairs={{16,0},{32,16},{48,32},{64,48},{80,64},{96,80},{112,96},{128,112},... | collective-permute-start | bytes 3145736 | tf_op jit(solution)/shard_map/ppermute | solution.py:24
  148.2 11.2 %collective-permute-start.6 = (f32[520,256]{1,0:T(8,128)S(1)}, f32[520,256]{1,0:T(8,128)S(1)}, u32[]{:S(2)}, u32[]{:S(2)}) collective-permute-start(f32[520,256]{1,0:T(8,128)S(1)} %maximum_maximum_fusion.2.local_ref), channel_id=1, source_target_pairs={{0,1},{1,0},{16,23},{23,16},{2,3},{3,2},{18,17},{17,18},{4,5},{5,4... | collective-permute-start | bytes 1597448 | tf_op jit(solution)/shard_map/ppermute | solution.py:40
  164.5 5.5 %collective-permute-start.7 = (f32[512]{0:T(512)S(1)}, f32[512]{0:T(512)S(1)}, u32[]{:S(2)}, u32[]{:S(2)}) collective-permute-start(f32[512]{0:T(512)S(1)} %multiply_reduce_fusion), channel_id=1, source_target_pairs={{0,1},{1,0},{16,23},{23,16},{2,3},{3,2},{18,17},{17,18},{4,5},{5,4... | collective-permute-start | bytes 6152 | tf_op jit(solution)/shard_map/ppermute | solution.py:40
